TPU v7x, 768 devices: a whole 4x8x12 slice. The times are simulated.
768 devices in a mesh: rows: 384 (over x, z, y_lo, core), rep: 2 (over y_hi).
Axes of the slice: x: 4, y: 8 (y_hi: 2, y_lo: 4; y = y_hi * 4 + y_lo), z: 12, core: 2. Of those that a mesh axis runs over, the one named last changes fastest.
Arguments:
- features: bfloat16 [294912, 256], P('rows'), may hold values from -6 to 6
- tiles: bfloat16 [2304, 12, 128, 128], P('rows', 'rep'), may hold values from -0.21875 to 0.21875
- columns: int32 [2304, 12], P('rows', 'rep'), may hold values from 0 to 2303, as said below
- live: int32 [2304, 2], P('rows', 'rep'), may hold values from 1 to 6, as said below
- weight: bfloat16 [256, 256], replicated, may hold values from -0.375 to 0.375
- bias: float32 [256], replicated, may hold values from -3 to 3
- cotangent: bfloat16 [294912, 256], P('rows'), may hold values from -6 to 6
Outputs:
- activations: bfloat16 [294912, 256], P('rows')
- feature_grad: bfloat16 [294912, 256], P('rows')
- weight_grad: float32 [256, 256], replicated
- bias_grad: float32 [256], replicated
Inputs may be any that keep to these rules, and one draw needn't show every extreme that they name: `columns`: the 12 slots of row block g name, in some order, each of the blocks s to s + 2 * 6 - 1 once, where s = g - 6 clipped to 0 .. 2292. `live`: 1 to 6 live slots in each half of a row block's slots; some row block in every draw has all 6 live in its first half.
All inputs are finite; a program needn't handle non-finite values.
Results may differ from a plain program's by a relative error of at most 0.0061.
Values may be sent and summed in bfloat16 or wider, within the bound.
No kernel may reach another device: no remote copies, remote signals or barrier semaphores. Data moves between devices by JAX's collectives and lax.ppermute only.
A program may use at most 32 MiB of HBM per device.

v0:
```python
import math

import jax
import jax.numpy as jnp
from jax import lax
from jax.sharding import PartitionSpec as P


def extended(block, sides, width):
    for axis, dim in sides:
        count = lax.axis_size(axis)
        forward = [(i, i + 1) for i in range(count - 1)]
        backward = [(target, source) for source, target in forward]
        low = lax.ppermute(
            lax.slice_in_dim(block, block.shape[dim] - width, None, axis=dim), axis, forward
        )
        high = lax.ppermute(lax.slice_in_dim(block, 0, width, axis=dim), axis, backward)
        block = jnp.concatenate([low, block, high], axis=dim)
    return block


def from_behind(x, axis, by):
    count = lax.axis_size(axis)
    pairs = [(i, i + by) for i in range(count) if 0 <= i + by < count]
    return lax.ppermute(x, axis, pairs)


def dense_part(aggregated, grad_input, weight, bias):
    pre_act = jnp.dot(aggregated, weight, preferred_element_type=jnp.float32) + bias
    outputs = jax.nn.silu(pre_act).astype(jnp.bfloat16)
    sigmoid_pre = jax.nn.sigmoid(pre_act)
    pre_grad = (
        grad_input.astype(jnp.float32) * sigmoid_pre * (1.0 + pre_act * (1.0 - sigmoid_pre))
    ).astype(jnp.bfloat16)
    agg_grad = jnp.dot(pre_grad, weight.T, preferred_element_type=jnp.float32).astype(jnp.bfloat16)
    return (outputs, pre_grad, agg_grad)


def local(features, tiles, columns, live, weight, bias, cotangent):
    num_blocks = tiles.shape[0]
    slot_count = tiles.shape[1]
    tile_size = tiles.shape[2]
    feat_width = features.shape[1]
    rows_here = num_blocks * tile_size
    half_rows = rows_here // 2
    row_index = lax.axis_index("rows")
    partner = lax.axis_index("rep")
    node_count = rows_here * lax.axis_size("rows")
    padded = extended(features, (("rows", 0),), rows_here)
    padded_blocks = padded.reshape(3 * num_blocks, tile_size, feat_width)
    local_cols = columns - (row_index - 1) * num_blocks
    live_mask = jnp.arange(slot_count, dtype=jnp.int32)[None, :] < live
    targets = jnp.arange(3 * num_blocks, dtype=jnp.int32)
    selector = (local_cols[:, :, None] == targets[None, None, :]) & live_mask[:, :, None]
    selector = selector.astype(jnp.bfloat16)
    band_tiles = jnp.einsum(
        "bks,bkij->bsij", selector, tiles, preferred_element_type=jnp.float32
    ).astype(jnp.bfloat16)
    partial_sum = jnp.einsum(
        "bsij,sjf->bif", band_tiles, padded_blocks, preferred_element_type=jnp.float32
    )
    partial_sum = partial_sum.reshape(rows_here, feat_width)
    aggregate = lax.psum(partial_sum, "rep").astype(jnp.bfloat16)
    activations, pre_grad, agg_grad = dense_part(aggregate, cotangent, weight, bias)
    agg_half = lax.dynamic_slice_in_dim(aggregate, partner * half_rows, half_rows, 0)
    grad_half = lax.dynamic_slice_in_dim(pre_grad, partner * half_rows, half_rows, 0)
    weight_part = lax.dot_general(
        agg_half, grad_half, (((0,), (0,)), ((), ())), preferred_element_type=jnp.float32
    )
    bias_part = jnp.sum(grad_half.astype(jnp.float32), axis=0)
    weight_total, bias_total = lax.psum((weight_part, bias_part), ("rows", "rep"))
    scale = 1.0 / math.sqrt(node_count)
    weight_grad = weight_total * scale
    bias_grad = bias_total * scale
    grad_blocks = agg_grad.reshape(num_blocks, tile_size, feat_width)
    spread = jnp.einsum(
        "bsij,bif->sjf", band_tiles, grad_blocks, preferred_element_type=jnp.float32
    )
    from_above = from_behind(spread[:num_blocks], "rows", -1)
    from_below = from_behind(spread[2 * num_blocks :].astype(jnp.bfloat16), "rows", 1).astype(
        jnp.float32
    )
    own_terms = spread[num_blocks : 2 * num_blocks] + from_above + from_below
    own_total = lax.psum(own_terms, "rep")
    feature_grad = own_total.reshape(rows_here, feat_width).astype(jnp.bfloat16)
    return (activations, feature_grad, weight_grad, bias_grad)


def solution(mesh):
    placed = (
        P("rows", None),
        P("rows", "rep", None, None),
        P("rows", "rep"),
        P("rows", "rep"),
        P(),
        P(),
        P("rows", None),
    )
    return jax.shard_map(
        local,
        mesh=mesh,
        in_specs=placed,
        out_specs=(P("rows", None), P("rows", None), P(), P()),
        check_vma=False,
    )
```

profile of v0, /device:TPU:6, one launch (start us, length us, event | category | flops | bytes accessed | tf_op | source)
XLA Modules:
  0.0 607.5 jit_solution(9612222282030963014)
XLA Ops:
  7.2 0.0 copy-start
  7.2 0.0 all-reduce.4.cloned.1.call-start
  7.2 2.1 collective-permute-start
  9.3 17.3 %collective-permute-start.1 = (bf16[768,256]{1,0:T(8,128)(2,1)}, bf16[768,256]{1,0:T(8,128)(2,1)S(1)}, u32[]{:S(2)}, u32[]{:S(2)}) collective-permute-start(bf16[768,256]{1,0:T(8,128)(2,1)} %param.7), channel_id=1, source_target_pairs={{2,0},{4,2},{6,4},{8,6},{10,8},{12,10},{14,12},{16,14},{18,16},{20... | collective-permute-start | bytes 1179656 | tf_op jit(solution)/shard_map/ppermute | solution.py:17
  26.6 0.7 broadcast_subtract_fusion
  27.3 0.7 iota_compare_fusion.1
  28.1 0.0 copy-done
  28.1 0.0 copy-start.5
  28.1 2.2 convolution_convert_fusion
  30.3 0.0 copy-start.1
  30.3 0.1 collective-permute-done
  30.4 1.8 collective-permute-done.1
  32.2 0.0 copy-done.5
  32.2 0.1 pad_maximum_fusion
  32.3 0.1 copy-done.1
  32.4 0.0 copy-start.6
  32.4 0.0 copy-start.7
  32.4 1.1 fusion.8
  33.5 35.1 %all-reduce.5 = bf16[768,256]{1,0:T(8,128)(2,1)S(1)} all-reduce(f32[768,256]{1,0:T(8,128)S(1)} %fusion.8), channel_id=1, replica_groups=mesh['rows'=384,'rep'=2] {'rep'}, use_global_device_ids=true, to_apply=%region_0.0 | all-reduce | flops 196608 | bytes 1179648 | tf_op jit(solution)/shard_map/psum | solution.py:63
  68.6 0.0 copy-done.6
  68.6 0.0 copy-done.7
  68.6 0.0 copy-start.4
  68.6 0.0 copy-start.2
  68.6 2.5 multiply_convert_fusion
  71.1 0.0 copy-done.4
  71.1 0.0 copy-start.3
  71.1 0.3 convolution_convert_fusion.1
  71.4 0.5 copy-done.3
  71.8 0.0 copy-done.2
  71.8 1.2 fusion.4
  73.0 1.0 slice.14
  74.0 19.4 %collective-permute-start.2 = (f32[6,128,256]{2,1,0:T(8,128)}, f32[6,128,256]{2,1,0:T(8,128)}, u32[]{:S(2)}, u32[]{:S(2)}) collective-permute-start(f32[6,128,256]{2,1,0:T(8,128)} %slice.14), channel_id=1, source_target_pairs={{2,0},{4,2},{6,4},{8,6},{10,8},{12,10},{14,12},{16,14},{18,16},{20... | collective-permute-start | bytes 2359304 | tf_op jit(solution)/shard_map/ppermute | solution.py:25
  93.4 0.8 slice.20
  94.2 2.0 fusion.12
  96.2 0.0 all-reduce.4.cloned.1.call-update
  96.2 1.9 collective-permute-start.3
  98.1 1.0 convert_reduce_fusion
  99.1 105.1 %psum.31 = f32[256]{0:T(256)S(1)} all-reduce(f32[256]{0:T(256)S(1)} %convert_reduce_fusion), channel_id=1, replica_groups=mesh['rows'=384,'rep'=2] {'rows','rep'}, use_global_device_ids=true, to_apply=%region_4.5 | all-reduce | flops 256 | bytes 2048 | tf_op jit(solution)/shard_map/psum | solution.py:71
  204.2 0.6 broadcast_multiply_fusion.1
  204.7 342.6 %all-reduce.4.cloned.1.call-done = f32[256,256]{1,0:T(8,128)} async-done(((f32[256,256]{1,0:T(8,128)}), f32[256,256]{1,0:T(8,128)}) %all-reduce.4.cloned.1.call-update) | async-done | bytes 262160 | tf_op jit(solution)/shard_map/psum | solution.py:71
  547.3 1.7 broadcast_multiply_fusion
  549.0 0.0 collective-permute-done.3
  549.0 0.0 collective-permute-done.2
  549.0 2.3 fusion.11
  551.3 49.4 %all-reduce.6 = bf16[6,128,256]{2,1,0:T(8,128)(2,1)} all-reduce(f32[6,128,256]{2,1,0:T(8,128)} %fusion.11), channel_id=1, replica_groups=mesh['rows'=384,'rep'=2] {'rep'}, use_global_device_ids=true, to_apply=%region_1.2 | all-reduce | flops 196608 | bytes 1179648 | tf_op jit(solution)/shard_map/psum | solution.py:84
Async XLA Ops:
  7.2 20.9 %copy-start = (bf16[6,6,128,128]{3,2,1,0:T(8,128)(2,1)S(1)}, bf16[6,6,128,128]{3,2,1,0:T(8,128)(2,1)}, u32[]{:S(2)}) copy-start(bf16[6,6,128,128]{3,2,1,0:T(8,128)(2,1)} %param.8) | copy-start | bytes 3538948
  7.2 540.1 %all-reduce.4.cloned.1.call-start = ((), (), s32[]{:S(2)}) async-start(), calls=%async_computation | async-start | bytes 524288 | tf_op jit(solution)/shard_map/psum | solution.py:71
  7.2 23.2 %collective-permute-start = (bf16[768,256]{1,0:T(8,128)(2,1)}, bf16[768,256]{1,0:T(8,128)(2,1)S(1)}, u32[]{:S(2)}, u32[]{:S(2)}) collective-permute-start(bf16[768,256]{1,0:T(8,128)(2,1)} %param.7), channel_id=1, source_target_pairs={{0,2},{2,4},{4,6},{6,8},{8,10},{10,12},{12,14},{14,16},{16,18},{18... | collective-permute-start | bytes 1179656 | tf_op jit(solution)/shard_map/ppermute | solution.py:14
  9.3 22.9 %collective-permute-start.1 = (bf16[768,256]{1,0:T(8,128)(2,1)}, bf16[768,256]{1,0:T(8,128)(2,1)S(1)}, u32[]{:S(2)}, u32[]{:S(2)}) collective-permute-start(bf16[768,256]{1,0:T(8,128)(2,1)} %param.7), channel_id=1, source_target_pairs={{2,0},{4,2},{6,4},{8,6},{10,8},{12,10},{14,12},{16,14},{18,16},{20... | collective-permute-start | bytes 1179656 | tf_op jit(solution)/shard_map/ppermute | solution.py:17
  28.1 4.2 copy-start.5
  30.3 2.1 copy-start.1
  32.4 36.2 %copy-start.6 = (bf16[256,256]{1,0:T(8,128)(2,1)S(1)}, bf16[256,256]{1,0:T(8,128)(2,1)}, u32[]{:S(2)}) copy-start(bf16[256,256]{1,0:T(8,128)(2,1)} %param.11) | copy-start | bytes 393220
  32.4 36.2 %copy-start.7 = (f32[256]{0:T(256)S(1)}, f32[256]{0:T(256)}, u32[]{:S(2)}) copy-start(f32[256]{0:T(256)} %param.12) | copy-start | bytes 3076
  68.6 2.5 copy-start.4
  68.6 3.2 copy-start.2
  71.1 0.8 copy-start.3
  74.0 475.0 %collective-permute-start.2 = (f32[6,128,256]{2,1,0:T(8,128)}, f32[6,128,256]{2,1,0:T(8,128)}, u32[]{:S(2)}, u32[]{:S(2)}) collective-permute-start(f32[6,128,256]{2,1,0:T(8,128)} %slice.14), channel_id=1, source_target_pairs={{2,0},{4,2},{6,4},{8,6},{10,8},{12,10},{14,12},{16,14},{18,16},{20... | collective-permute-start | bytes 2359304 | tf_op jit(solution)/shard_map/ppermute | solution.py:25
  96.2 452.8 %collective-permute-start.3 = (bf16[6,128,256]{2,1,0:T(8,128)(2,1)}, bf16[6,128,256]{2,1,0:T(8,128)(2,1)}, u32[]{:S(2)}, u32[]{:S(2)}) collective-permute-start(bf16[6,128,256]{2,1,0:T(8,128)(2,1)} %slice.20), channel_id=1, source_target_pairs={{0,2},{2,4},{4,6},{6,8},{8,10},{10,12},{12,14},{14,16},{16,18},{18... | collective-permute-start | bytes 1179656 | tf_op jit(solution)/shard_map/ppermute | solution.py:25
Sparse Core Ops, SparseCore 0:
  96.3 450.9 all-reduce.3
where the time goes:
time: 608 us
  waiting for transfers between devices  345 us (57%)
  blocking collectives  190 us (31%)
  starting transfers between devices  40.7 us (7%)
  between operations  14.2 us (2%)
  matrix products  9.21 us (2%)
  other arithmetic  6.99 us (1%)
    psum x1, waiting for transfers between devices, local(): lax.psum((weight_part, bias_part), ('rows', 'rep'))  343 us
    psum x1, blocking collectives, local(): lax.psum((weight_part, bias_part), ('rows', 'rep'))  105 us
    psum x1, blocking collectives, local(): own_total = lax.psum(own_terms, 'rep')  49.4 us
    psum x1, blocking collectives, local(): aggregate = lax.psum(partial_sum, 'rep').astype(jnp.bfloat16)  35.1 us
    ppermute x2, starting transfers between devices, from_behind(): return lax.ppermute(x, axis, pairs)  21.3 us
    ppermute x1, starting transfers between devices, extended(): lax.ppermute(lax.slice_in_dim(block, 0, width, axis=dim), axis, backward)  17.3 us
  transfers between devices with their start and end apart: 5, of which 3 were waited for; matrix products, arithmetic and copies ran while one was open for 2% of the time, Pallas kernels for 0%

commit v1 on v0

--- a/solution.py
+++ b/solution.py
@@ -23,6 +23,52 @@
     count = lax.axis_size(axis)
     pairs = [(i, i + by) for i in range(count) if 0 <= i + by < count]
     return lax.ppermute(x, axis, pairs)
+
+
+ROW_AXES = {384: ((96, 4), (8, 12), (2, 4), (1, 2))}
+
+
+def moved(x, axis, count, stride, size, target):
+    pairs = []
+    for index in range(count):
+        coord = (index // stride) % size
+        pairs.append((index, index + (target(coord) - coord) * stride))
+    return lax.ppermute(x, axis, pairs)
+
+
+def swapped_sum(x, axis, count, stride, size, bit):
+    return x + moved(x, axis, count, stride, size, lambda c: c ^ bit)
+
+
+def three_way_sum(x, axis, count, stride, size):
+    third = size // 3
+    ahead = moved(x, axis, count, stride, size, lambda c: (c + third) % size)
+    behind = moved(x, axis, count, stride, size, lambda c: (c - third) % size)
+    group = (lax.axis_index(axis) // stride) % size // third
+    first = jnp.where(group == 0, x, jnp.where(group == 1, ahead, behind))
+    second = jnp.where(group == 0, behind, jnp.where(group == 1, x, ahead))
+    third_part = jnp.where(group == 0, ahead, jnp.where(group == 1, behind, x))
+    return (first + second) + third_part
+
+
+def global_sum(x):
+    count = lax.axis_size("rows")
+    if count not in ROW_AXES or lax.axis_size("rep") != 2:
+        return lax.psum(x, ("rows", "rep"))
+    (x_stride, x_size), (z_stride, z_size), (y_stride, y_size), (c_stride, c_size) = ROW_AXES[count]
+    x = swapped_sum(x, "rows", count, c_stride, c_size, 1)
+    x = swapped_sum(x, "rows", count, y_stride, y_size, 1)
+    x = swapped_sum(x, "rows", count, y_stride, y_size, 2)
+    x = x + lax.ppermute(x, "rep", [(0, 1), (1, 0)])
+    x = swapped_sum(x, "rows", count, x_stride, x_size, 1)
+    x = swapped_sum(x, "rows", count, x_stride, x_size, 2)
+    x = swapped_sum(x, "rows", count, z_stride, z_size, 1)
+    x = swapped_sum(x, "rows", count, z_stride, z_size, 2)
+    return three_way_sum(x, "rows", count, z_stride, z_size)
+
+
+def partner_sum(x):
+    return x + lax.ppermute(x, "rep", [(0, 1), (1, 0)])
 
 
 def dense_part(aggregated, grad_input, weight, bias):
@@ -60,7 +106,7 @@
         "bsij,sjf->bif", band_tiles, padded_blocks, preferred_element_type=jnp.float32
     )
     partial_sum = partial_sum.reshape(rows_here, feat_width)
-    aggregate = lax.psum(partial_sum, "rep").astype(jnp.bfloat16)
+    aggregate = partner_sum(partial_sum).astype(jnp.bfloat16)
     activations, pre_grad, agg_grad = dense_part(aggregate, cotangent, weight, bias)
     agg_half = lax.dynamic_slice_in_dim(aggregate, partner * half_rows, half_rows, 0)
     grad_half = lax.dynamic_slice_in_dim(pre_grad, partner * half_rows, half_rows, 0)
@@ -68,7 +114,9 @@
         agg_half, grad_half, (((0,), (0,)), ((), ())), preferred_element_type=jnp.float32
     )
     bias_part = jnp.sum(grad_half.astype(jnp.float32), axis=0)
-    weight_total, bias_total = lax.psum((weight_part, bias_part), ("rows", "rep"))
+    grad_terms = global_sum(jnp.concatenate([weight_part, bias_part[None, :]], axis=0))
+    weight_total = grad_terms[:feat_width]
+    bias_total = grad_terms[feat_width]
     scale = 1.0 / math.sqrt(node_count)
     weight_grad = weight_total * scale
     bias_grad = bias_total * scale
@@ -81,7 +129,7 @@
         jnp.float32
     )
     own_terms = spread[num_blocks : 2 * num_blocks] + from_above + from_below
-    own_total = lax.psum(own_terms, "rep")
+    own_total = partner_sum(own_terms)
     feature_grad = own_total.reshape(rows_here, feat_width).astype(jnp.bfloat16)
     return (activations, feature_grad, weight_grad, bias_grad)
 

time: 608 us -> 220 us (0.36)
  the two profiles are of different devices: /device:TPU:6 before, /device:TPU:8 now
where the time goes in v1:
time: 220 us
  waiting for transfers between devices  128 us (58%)
  starting transfers between devices  79.8 us (36%)
  matrix products  6.35 us (3%)
  other arithmetic  4.35 us (2%)
    ppermute x9, waiting for transfers between devices, moved(): return lax.ppermute(x, axis, pairs)  68.9 us
    ppermute x9, starting transfers between devices, moved(): return lax.ppermute(x, axis, pairs)  58.8 us
    ppermute x2, waiting for transfers between devices, partner_sum(): return x + lax.ppermute(x, 'rep', [(0, 1), (1, 0)])  38.8 us
    ppermute x1, waiting for transfers between devices, global_sum(): x = x + lax.ppermute(x, 'rep', [(0, 1), (1, 0)])  18.4 us
    ppermute x2, starting transfers between devices, partner_sum(): return x + lax.ppermute(x, 'rep', [(0, 1), (1, 0)])  8.84 us
    ppermute x2, starting transfers between devices, from_behind(): return lax.ppermute(x, axis, pairs)  4.47 us
  transfers between devices with their start and end apart: 16, of which 12 were waited for; matrix products, arithmetic and copies ran while one was open for 3% of the time, Pallas kernels for 0%

profile of v1, /device:TPU:8, one launch (start us, length us, event | category | flops | bytes accessed | tf_op | source)
XLA Modules:
  0.0 219.7 jit_solution(8682997428949854971)
XLA Ops:
  0.6 0.0 copy-start
  0.6 2.1 collective-permute-start
  2.7 3.6 %collective-permute-start.1 = (bf16[768,256]{1,0:T(8,128)(2,1)}, bf16[768,256]{1,0:T(8,128)(2,1)S(1)}, u32[]{:S(2)}, u32[]{:S(2)}) collective-permute-start(bf16[768,256]{1,0:T(8,128)(2,1)} %param.7), channel_id=1, source_target_pairs={{2,0},{4,2},{6,4},{8,6},{10,8},{12,10},{14,12},{16,14},{18,16},{20... | collective-permute-start | bytes 1179656 | tf_op jit(solution)/shard_map/ppermute | solution.py:17
  6.4 0.7 broadcast_subtract_fusion
  7.1 0.7 iota_compare_fusion.1
  7.8 0.0 copy-done
  7.8 0.0 copy-start.2
  7.8 2.2 %convolution_convert_fusion = bf16[6,18,128,128]{3,1,2,0:T(8,128)(2,1)S(1)} fusion(bf16[6,6,128,128]{3,2,1,0:T(8,128)(2,1)S(1)} %copy-done, s32[6,6]{1,0:T(8,128)S(1)} %broadcast_subtract_fusion, pred[6,6]{1,0:T(8,128)(4,1)S(1)} %iota_compare_fusion.1), kind=kOutput, calls=%fused_computation.4 | convolution fusion | flops 23004432 | bytes 4718772 | tf_op jit(solution)/shard_map/bks,bkij->bsij/dot_general | solution.py:102
  10.0 0.0 copy-start.1
  10.0 0.0 collective-permute-done
  10.1 1.9 collective-permute-done.1
  11.9 0.0 copy-done.2
  12.0 0.1 pad_maximum_fusion
  12.0 0.0 copy-start.3
  12.0 0.0 copy-start.4
  12.1 0.0 copy-start.5
  12.1 1.1 fusion.8
  13.2 0.0 copy-done.1
  13.2 6.8 %collective-permute-start.2 = (f32[768,256]{1,0:T(8,128)S(1)}, f32[768,256]{1,0:T(8,128)S(1)}, u32[]{:S(2)}, u32[]{:S(2)}) collective-permute-start(f32[768,256]{1,0:T(8,128)S(1)} %fusion.8), channel_id=1, source_target_pairs={{0,1},{1,0},{2,3},{3,2},{4,5},{5,4},{6,7},{7,6},{8,9},{9,8},{10,11... | collective-permute-start | bytes 2359304 | tf_op jit(solution)/shard_map/ppermute | solution.py:71
  20.0 38.8 %collective-permute-done.2 = f32[768,256]{1,0:T(8,128)S(1)} collective-permute-done((f32[768,256]{1,0:T(8,128)S(1)}, f32[768,256]{1,0:T(8,128)S(1)}, u32[]{:S(2)}, u32[]{:S(2)}) %collective-permute-start.2) | collective-permute-done | bytes 786464 | tf_op jit(solution)/shard_map/ppermute | solution.py:71
  58.8 0.1 add_convert_fusion.1
  58.9 0.0 copy-done.3
  58.9 0.0 copy-done.4
  58.9 0.0 copy-done.5
  58.9 0.0 slice-start.1
  58.9 1.3 multiply_convert_fusion
  60.2 0.3 fusion.12
  60.5 0.1 convert_reduce_fusion
  60.6 1.9 collective-permute-start.6
  62.5 1.5 collective-permute-done.6
  64.1 3.8 %collective-permute-start.7 = (f32[257,256]{1,0:T(8,128)S(1)}, f32[257,256]{1,0:T(8,128)S(1)}, u32[]{:S(2)}, u32[]{:S(2)}) collective-permute-start(f32[257,256]{1,0:T(8,128)S(1)} %fusion.21), channel_id=1, source_target_pairs={{0,4},{2,6},{4,0},{6,2},{8,12},{10,14},{12,8},{14,10},{16,20},{18,... | collective-permute-start | bytes 789512 | tf_op jit(solution)/shard_map/ppermute | solution.py:36
  67.9 0.3 convolution_convert_fusion.1
  68.2 6.5 %collective-permute-done.7 = f32[257,256]{1,0:T(8,128)S(1)} collective-permute-done((f32[257,256]{1,0:T(8,128)S(1)}, f32[257,256]{1,0:T(8,128)S(1)}, u32[]{:S(2)}, u32[]{:S(2)}) %collective-permute-start.7) | collective-permute-done | bytes 263200 | tf_op jit(solution)/shard_map/ppermute | solution.py:36
  74.7 1.9 collective-permute-start.8
  76.6 0.0 slice-done
  76.6 0.0 slice-done.1
  76.6 1.2 fusion.4
  77.8 0.1 slice.22
  77.9 2.6 %collective-permute-start.3 = (f32[6,128,256]{2,1,0:T(8,128)S(1)}, f32[6,128,256]{2,1,0:T(8,128)S(1)}, u32[]{:S(2)}, u32[]{:S(2)}) collective-permute-start(f32[6,128,256]{2,1,0:T(8,128)S(1)} %slice.22), channel_id=1, source_target_pairs={{2,0},{4,2},{6,4},{8,6},{10,8},{12,10},{14,12},{16,14},{18,16},{20... | collective-permute-start | bytes 2359304 | tf_op jit(solution)/shard_map/ppermute | solution.py:25
  80.5 23.4 %collective-permute-done.8 = f32[257,256]{1,0:T(8,128)S(1)} collective-permute-done((f32[257,256]{1,0:T(8,128)S(1)}, f32[257,256]{1,0:T(8,128)S(1)}, u32[]{:S(2)}, u32[]{:S(2)}) %collective-permute-start.8) | collective-permute-done | bytes 263200 | tf_op jit(solution)/shard_map/ppermute | solution.py:36
  103.9 1.9 collective-permute-start.9
  105.8 1.9 collective-permute-start.4
  107.8 18.4 %collective-permute-done.9 = f32[257,256]{1,0:T(8,128)S(1)} collective-permute-done((f32[257,256]{1,0:T(8,128)S(1)}, f32[257,256]{1,0:T(8,128)S(1)}, u32[]{:S(2)}, u32[]{:S(2)}) %collective-permute-start.9) | collective-permute-done | bytes 263200 | tf_op jit(solution)/shard_map/ppermute | solution.py:62
  126.2 1.9 collective-permute-start.10
  128.1 6.4 %collective-permute-done.10 = f32[257,256]{1,0:T(8,128)S(1)} collective-permute-done((f32[257,256]{1,0:T(8,128)S(1)}, f32[257,256]{1,0:T(8,128)S(1)}, u32[]{:S(2)}, u32[]{:S(2)}) %collective-permute-start.10) | collective-permute-done | bytes 263200 | tf_op jit(solution)/shard_map/ppermute | solution.py:36
  134.6 1.9 collective-permute-start.11
  136.5 0.0 collective-permute-done.4
  136.5 0.0 collective-permute-done.3
  136.5 0.1 fusion.11
  136.7 2.0 collective-permute-start.5
  138.7 5.8 %collective-permute-done.11 = f32[257,256]{1,0:T(8,128)S(1)} collective-permute-done((f32[257,256]{1,0:T(8,128)S(1)}, f32[257,256]{1,0:T(8,128)S(1)}, u32[]{:S(2)}, u32[]{:S(2)}) %collective-permute-start.11) | collective-permute-done | bytes 263200 | tf_op jit(solution)/shard_map/ppermute | solution.py:36
  144.5 6.9 %collective-permute-start.12 = (f32[257,256]{1,0:T(8,128)S(1)}, f32[257,256]{1,0:T(8,128)S(1)}, u32[]{:S(2)}, u32[]{:S(2)}) collective-permute-start(f32[257,256]{1,0:T(8,128)S(1)} %add.84), channel_id=1, source_target_pairs={{0,16},{2,18},{4,20},{6,22},{8,24},{10,26},{12,28},{14,30},{16,0},... | collective-permute-start | bytes 789512 | tf_op jit(solution)/shard_map/ppermute | solution.py:36
  151.4 5.0 %collective-permute-done.12 = f32[257,256]{1,0:T(8,128)S(1)} collective-permute-done((f32[257,256]{1,0:T(8,128)S(1)}, f32[257,256]{1,0:T(8,128)S(1)}, u32[]{:S(2)}, u32[]{:S(2)}) %collective-permute-start.12) | collective-permute-done | bytes 263200 | tf_op jit(solution)/shard_map/ppermute | solution.py:36
  156.4 13.0 %collective-permute-start.13 = (f32[257,256]{1,0:T(8,128)S(1)}, f32[257,256]{1,0:T(8,128)S(1)}, u32[]{:S(2)}, u32[]{:S(2)}) collective-permute-start(f32[257,256]{1,0:T(8,128)S(1)} %add.85), channel_id=1, source_target_pairs={{0,32},{2,34},{4,36},{6,38},{8,40},{10,42},{12,44},{14,46},{16,48}... | collective-permute-start | bytes 789512 | tf_op jit(solution)/shard_map/ppermute | solution.py:36
  169.5 7.3 %collective-permute-done.13 = f32[257,256]{1,0:T(8,128)S(1)} collective-permute-done((f32[257,256]{1,0:T(8,128)S(1)}, f32[257,256]{1,0:T(8,128)S(1)}, u32[]{:S(2)}, u32[]{:S(2)}) %collective-permute-start.13) | collective-permute-done | bytes 263200 | tf_op jit(solution)/shard_map/ppermute | solution.py:36
  176.8 16.2 %collective-permute-start.14 = (f32[257,256]{1,0:T(8,128)S(1)}, f32[257,256]{1,0:T(8,128)S(1)}, u32[]{:S(2)}, u32[]{:S(2)}) collective-permute-start(f32[257,256]{1,0:T(8,128)S(1)} %add.86), channel_id=1, source_target_pairs={{0,64},{2,66},{4,68},{6,70},{8,72},{10,74},{12,76},{14,78},{16,80}... | collective-permute-start | bytes 789512 | tf_op jit(solution)/shard_map/ppermute | solution.py:36
  192.9 11.3 %collective-permute-start.15 = (f32[257,256]{1,0:T(8,128)S(1)}, f32[257,256]{1,0:T(8,128)S(1)}, u32[]{:S(2)}, u32[]{:S(2)}) collective-permute-start(f32[257,256]{1,0:T(8,128)S(1)} %add.86), channel_id=1, source_target_pairs={{0,128},{2,130},{4,132},{6,134},{8,136},{10,138},{12,140},{14,142}... | collective-permute-start | bytes 789512 | tf_op jit(solution)/shard_map/ppermute | solution.py:36
  204.2 0.0 collective-permute-done.5
  204.2 0.9 add_convert_fusion
  205.1 9.2 %collective-permute-done.14 = f32[257,256]{1,0:T(8,128)S(1)} collective-permute-done((f32[257,256]{1,0:T(8,128)S(1)}, f32[257,256]{1,0:T(8,128)S(1)}, u32[]{:S(2)}, u32[]{:S(2)}) %collective-permute-start.14) | collective-permute-done | bytes 263200 | tf_op jit(solution)/shard_map/ppermute | solution.py:36
  214.3 3.9 %collective-permute-done.15 = f32[257,256]{1,0:T(8,128)S(1)} collective-permute-done((f32[257,256]{1,0:T(8,128)S(1)}, f32[257,256]{1,0:T(8,128)S(1)}, u32[]{:S(2)}, u32[]{:S(2)}) %collective-permute-start.15) | collective-permute-done | bytes 263200 | tf_op jit(solution)/shard_map/ppermute | solution.py:36
  218.3 0.1 select_add_fusion
  218.4 0.7 slice_multiply_fusion
  219.1 0.6 slice_multiply_fusion.1
  (12 shorter events, 0.3 us)
Async XLA Ops:
  0.6 7.2 %copy-start = (bf16[6,6,128,128]{3,2,1,0:T(8,128)(2,1)S(1)}, bf16[6,6,128,128]{3,2,1,0:T(8,128)(2,1)}, u32[]{:S(2)}) copy-start(bf16[6,6,128,128]{3,2,1,0:T(8,128)(2,1)} %param.8) | copy-start | bytes 3538948
  0.6 9.4 %collective-permute-start = (bf16[768,256]{1,0:T(8,128)(2,1)}, bf16[768,256]{1,0:T(8,128)(2,1)S(1)}, u32[]{:S(2)}, u32[]{:S(2)}) collective-permute-start(bf16[768,256]{1,0:T(8,128)(2,1)} %param.7), channel_id=1, source_target_pairs={{0,2},{2,4},{4,6},{6,8},{8,10},{10,12},{12,14},{14,16},{16,18},{18... | collective-permute-start | bytes 1179656 | tf_op jit(solution)/shard_map/ppermute | solution.py:14
  2.7 9.2 %collective-permute-start.1 = (bf16[768,256]{1,0:T(8,128)(2,1)}, bf16[768,256]{1,0:T(8,128)(2,1)S(1)}, u32[]{:S(2)}, u32[]{:S(2)}) collective-permute-start(bf16[768,256]{1,0:T(8,128)(2,1)} %param.7), channel_id=1, source_target_pairs={{2,0},{4,2},{6,4},{8,6},{10,8},{12,10},{14,12},{16,14},{18,16},{20... | collective-permute-start | bytes 1179656 | tf_op jit(solution)/shard_map/ppermute | solution.py:17
  7.8 4.2 %copy-start.2 = (bf16[768,256]{1,0:T(8,128)(2,1)S(1)}, bf16[768,256]{1,0:T(8,128)(2,1)}, u32[]{:S(2)}) copy-start(bf16[768,256]{1,0:T(8,128)(2,1)} %param.7) | copy-start | bytes 1179652
  10.0 3.1 %copy-start.1 = (bf16[6,18,128,128]{3,1,2,0:T(8,128)(2,1)}, bf16[6,18,128,128]{3,1,2,0:T(8,128)(2,1)S(1)}, u32[]{:S(2)}) copy-start(bf16[6,18,128,128]{3,1,2,0:T(8,128)(2,1)S(1)} %convolution_convert_fusion) | copy-start | bytes 10616836
  12.0 46.9 %copy-start.3 = (bf16[256,256]{1,0:T(8,128)(2,1)S(1)}, bf16[256,256]{1,0:T(8,128)(2,1)}, u32[]{:S(2)}) copy-start(bf16[256,256]{1,0:T(8,128)(2,1)} %param.11) | copy-start | bytes 393220
  12.0 46.9 %copy-start.4 = (bf16[768,256]{1,0:T(8,128)(2,1)S(1)}, bf16[768,256]{1,0:T(8,128)(2,1)}, u32[]{:S(2)}) copy-start(bf16[768,256]{1,0:T(8,128)(2,1)} %param.13) | copy-start | bytes 1179652
  12.1 46.9 %copy-start.5 = (f32[256]{0:T(256)S(1)}, f32[256]{0:T(256)}, u32[]{:S(2)}) copy-start(f32[256]{0:T(256)} %param.12) | copy-start | bytes 3076
  13.2 45.6 %collective-permute-start.2 = (f32[768,256]{1,0:T(8,128)S(1)}, f32[768,256]{1,0:T(8,128)S(1)}, u32[]{:S(2)}, u32[]{:S(2)}) collective-permute-start(f32[768,256]{1,0:T(8,128)S(1)} %fusion.8), channel_id=1, source_target_pairs={{0,1},{1,0},{2,3},{3,2},{4,5},{5,4},{6,7},{7,6},{8,9},{9,8},{10,11... | collective-permute-start | bytes 2359304 | tf_op jit(solution)/shard_map/ppermute | solution.py:71
  58.8 17.8 %slice-start = ((s8[4718592]{0:T(1024)(128)(4,1)}), s8[4194304]{0:T(1024)(128)(4,1)S(1)}, s32[]{:S(2)}) async-start(s8[4718592]{0:T(1024)(128)(4,1)} %bitcast.28), calls=%async_computation | async-start | bytes 8388608
  58.9 17.7 %slice-start.1 = ((s8[4718592]{0:T(1024)(128)(4,1)}), s8[524288]{0:T(1024)(128)(4,1)S(1)}, s32[]{:S(2)}) async-start(s8[4718592]{0:T(1024)(128)(4,1)} %bitcast.28), calls=%async_computation.1 | async-start | bytes 1048576
  60.6 3.4 %collective-permute-start.6 = (f32[257,256]{1,0:T(8,128)S(1)}, f32[257,256]{1,0:T(8,128)S(1)}, u32[]{:S(2)}, u32[]{:S(2)}) collective-permute-start(f32[257,256]{1,0:T(8,128)S(1)} %pad_maximum_fusion.1), channel_id=1, source_target_pairs={{0,2},{2,0},{4,6},{6,4},{8,10},{10,8},{12,14},{14,12},{16,18},{18,... | collective-permute-start | bytes 789512 | tf_op jit(solution)/shard_map/ppermute | solution.py:36
  64.1 10.5 %collective-permute-start.7 = (f32[257,256]{1,0:T(8,128)S(1)}, f32[257,256]{1,0:T(8,128)S(1)}, u32[]{:S(2)}, u32[]{:S(2)}) collective-permute-start(f32[257,256]{1,0:T(8,128)S(1)} %fusion.21), channel_id=1, source_target_pairs={{0,4},{2,6},{4,0},{6,2},{8,12},{10,14},{12,8},{14,10},{16,20},{18,... | collective-permute-start | bytes 789512 | tf_op jit(solution)/shard_map/ppermute | solution.py:36
  74.7 29.2 %collective-permute-start.8 = (f32[257,256]{1,0:T(8,128)S(1)}, f32[257,256]{1,0:T(8,128)S(1)}, u32[]{:S(2)}, u32[]{:S(2)}) collective-permute-start(f32[257,256]{1,0:T(8,128)S(1)} %add.80), channel_id=1, source_target_pairs={{0,8},{2,10},{4,12},{6,14},{8,0},{10,2},{12,4},{14,6},{16,24},{18,... | collective-permute-start | bytes 789512 | tf_op jit(solution)/shard_map/ppermute | solution.py:36
  77.9 58.6 %collective-permute-start.3 = (f32[6,128,256]{2,1,0:T(8,128)S(1)}, f32[6,128,256]{2,1,0:T(8,128)S(1)}, u32[]{:S(2)}, u32[]{:S(2)}) collective-permute-start(f32[6,128,256]{2,1,0:T(8,128)S(1)} %slice.22), channel_id=1, source_target_pairs={{2,0},{4,2},{6,4},{8,6},{10,8},{12,10},{14,12},{16,14},{18,16},{20... | collective-permute-start | bytes 2359304 | tf_op jit(solution)/shard_map/ppermute | solution.py:25
  103.9 22.3 %collective-permute-start.9 = (f32[257,256]{1,0:T(8,128)S(1)}, f32[257,256]{1,0:T(8,128)S(1)}, u32[]{:S(2)}, u32[]{:S(2)}) collective-permute-start(f32[257,256]{1,0:T(8,128)S(1)} %add.81), channel_id=1, source_target_pairs={{0,1},{1,0},{2,3},{3,2},{4,5},{5,4},{6,7},{7,6},{8,9},{9,8},{10,11... | collective-permute-start | bytes 789512 | tf_op jit(solution)/shard_map/ppermute | solution.py:62
  105.8 30.7 %collective-permute-start.4 = (bf16[6,128,256]{2,1,0:T(8,128)(2,1)S(1)}, bf16[6,128,256]{2,1,0:T(8,128)(2,1)S(1)}, u32[]{:S(2)}, u32[]{:S(2)}) collective-permute-start(bf16[6,128,256]{2,1,0:T(8,128)(2,1)S(1)} %slice.32), channel_id=1, source_target_pairs={{0,2},{2,4},{4,6},{6,8},{8,10},{10,12},{12,14},{14,16},{16,18},{18... | collective-permute-start | bytes 1179656 | tf_op jit(solution)/shard_map/ppermute | solution.py:25
  126.2 8.4 %collective-permute-start.10 = (f32[257,256]{1,0:T(8,128)S(1)}, f32[257,256]{1,0:T(8,128)S(1)}, u32[]{:S(2)}, u32[]{:S(2)}) collective-permute-start(f32[257,256]{1,0:T(8,128)S(1)} %add.82), channel_id=1, source_target_pairs={{0,192},{2,194},{4,196},{6,198},{8,200},{10,202},{12,204},{14,206}... | collective-permute-start | bytes 789512 | tf_op jit(solution)/shard_map/ppermute | solution.py:36
  134.6 9.9 %collective-permute-start.11 = (f32[257,256]{1,0:T(8,128)S(1)}, f32[257,256]{1,0:T(8,128)S(1)}, u32[]{:S(2)}, u32[]{:S(2)}) collective-permute-start(f32[257,256]{1,0:T(8,128)S(1)} %add.83), channel_id=1, source_target_pairs={{0,384},{2,386},{4,388},{6,390},{8,392},{10,394},{12,396},{14,398}... | collective-permute-start | bytes 789512 | tf_op jit(solution)/shard_map/ppermute | solution.py:36
  136.7 67.6 %collective-permute-start.5 = (f32[6,128,256]{2,1,0:T(8,128)S(1)}, f32[6,128,256]{2,1,0:T(8,128)S(1)}, u32[]{:S(2)}, u32[]{:S(2)}) collective-permute-start(f32[6,128,256]{2,1,0:T(8,128)S(1)} %fusion.11), channel_id=1, source_target_pairs={{0,1},{1,0},{2,3},{3,2},{4,5},{5,4},{6,7},{7,6},{8,9},{9,8},{10,11... | collective-permute-start | bytes 2359304 | tf_op jit(solution)/shard_map/ppermute | solution.py:71
  144.5 11.9 %collective-permute-start.12 = (f32[257,256]{1,0:T(8,128)S(1)}, f32[257,256]{1,0:T(8,128)S(1)}, u32[]{:S(2)}, u32[]{:S(2)}) collective-permute-start(f32[257,256]{1,0:T(8,128)S(1)} %add.84), channel_id=1, source_target_pairs={{0,16},{2,18},{4,20},{6,22},{8,24},{10,26},{12,28},{14,30},{16,0},... | collective-permute-start | bytes 789512 | tf_op jit(solution)/shard_map/ppermute | solution.py:36
  156.4 20.3 %collective-permute-start.13 = (f32[257,256]{1,0:T(8,128)S(1)}, f32[257,256]{1,0:T(8,128)S(1)}, u32[]{:S(2)}, u32[]{:S(2)}) collective-permute-start(f32[257,256]{1,0:T(8,128)S(1)} %add.85), channel_id=1, source_target_pairs={{0,32},{2,34},{4,36},{6,38},{8,40},{10,42},{12,44},{14,46},{16,48}... | collective-permute-start | bytes 789512 | tf_op jit(solution)/shard_map/ppermute | solution.py:36
  176.8 37.6 %collective-permute-start.14 = (f32[257,256]{1,0:T(8,128)S(1)}, f32[257,256]{1,0:T(8,128)S(1)}, u32[]{:S(2)}, u32[]{:S(2)}) collective-permute-start(f32[257,256]{1,0:T(8,128)S(1)} %add.86), channel_id=1, source_target_pairs={{0,64},{2,66},{4,68},{6,70},{8,72},{10,74},{12,76},{14,78},{16,80}... | collective-permute-start | bytes 789512 | tf_op jit(solution)/shard_map/ppermute | solution.py:36
  192.9 25.3 %collective-permute-start.15 = (f32[257,256]{1,0:T(8,128)S(1)}, f32[257,256]{1,0:T(8,128)S(1)}, u32[]{:S(2)}, u32[]{:S(2)}) collective-permute-start(f32[257,256]{1,0:T(8,128)S(1)} %add.86), channel_id=1, source_target_pairs={{0,128},{2,130},{4,132},{6,134},{8,136},{10,138},{12,140},{14,142}... | collective-permute-start | bytes 789512 | tf_op jit(solution)/shard_map/ppermute | solution.py:36

commit v2 on v1

--- a/solution.py
+++ b/solution.py
@@ -56,7 +56,11 @@
     if count not in ROW_AXES or lax.axis_size("rep") != 2:
         return lax.psum(x, ("rows", "rep"))
     (x_stride, x_size), (z_stride, z_size), (y_stride, y_size), (c_stride, c_size) = ROW_AXES[count]
-    x = swapped_sum(x, "rows", count, c_stride, c_size, 1)
+    core = (lax.axis_index("rows") // c_stride) % c_size
+    width = x.shape[1] // 2
+    keep = lax.dynamic_slice_in_dim(x, core * width, width, 1)
+    give = lax.dynamic_slice_in_dim(x, (1 - core) * width, width, 1)
+    x = keep + moved(give, "rows", count, c_stride, c_size, lambda c: c ^ 1)
     x = swapped_sum(x, "rows", count, y_stride, y_size, 1)
     x = swapped_sum(x, "rows", count, y_stride, y_size, 2)
     x = x + lax.ppermute(x, "rep", [(0, 1), (1, 0)])
@@ -64,7 +68,19 @@
     x = swapped_sum(x, "rows", count, x_stride, x_size, 2)
     x = swapped_sum(x, "rows", count, z_stride, z_size, 1)
     x = swapped_sum(x, "rows", count, z_stride, z_size, 2)
-    return three_way_sum(x, "rows", count, z_stride, z_size)
+    x = three_way_sum(x, "rows", count, z_stride, z_size)
+    other = moved(x, "rows", count, c_stride, c_size, lambda c: c ^ 1)
+    return jnp.where(core == 0, jnp.concatenate([x, other], 1), jnp.concatenate([other, x], 1))
+
+
+def partner_swap(x):
+    return lax.ppermute(x, "rep", [(0, 1), (1, 0)])
+
+
+def in_order(mine, theirs, partner):
+    return jnp.where(
+        partner == 0, jnp.concatenate([mine, theirs], 0), jnp.concatenate([theirs, mine], 0)
+    )
 
 
 def partner_sum(x):
@@ -106,10 +122,14 @@
         "bsij,sjf->bif", band_tiles, padded_blocks, preferred_element_type=jnp.float32
     )
     partial_sum = partial_sum.reshape(rows_here, feat_width)
-    aggregate = partner_sum(partial_sum).astype(jnp.bfloat16)
-    activations, pre_grad, agg_grad = dense_part(aggregate, cotangent, weight, bias)
-    agg_half = lax.dynamic_slice_in_dim(aggregate, partner * half_rows, half_rows, 0)
-    grad_half = lax.dynamic_slice_in_dim(pre_grad, partner * half_rows, half_rows, 0)
+    own_part = lax.dynamic_slice_in_dim(partial_sum, partner * half_rows, half_rows, 0)
+    their_part = lax.dynamic_slice_in_dim(partial_sum, (1 - partner) * half_rows, half_rows, 0)
+    agg_half = (own_part + partner_swap(their_part)).astype(jnp.bfloat16)
+    grad_in = lax.dynamic_slice_in_dim(cotangent, partner * half_rows, half_rows, 0)
+    act_half, grad_half, agg_grad_half = dense_part(agg_half, grad_in, weight, bias)
+    sent = partner_swap(jnp.concatenate([act_half, agg_grad_half], 1))
+    activations = in_order(act_half, sent[:, :feat_width], partner)
+    agg_grad = in_order(agg_grad_half, sent[:, feat_width:], partner)
     weight_part = lax.dot_general(
         agg_half, grad_half, (((0,), (0,)), ((), ())), preferred_element_type=jnp.float32
     )

time: 220 us -> 203 us (0.923)
  the two profiles are of different devices: /device:TPU:8 before, /device:TPU:56 now
where the time goes in v2:
time: 203 us; the launch traced here: 202 us
  starting transfers between devices  99.3 us (49%)
  waiting for transfers between devices  80.1 us (39%)
  other arithmetic  11.2 us (6%)
  matrix products  7.69 us (4%)
  local copies, waits for them, and re-layouts  2.53 us (1%)
    ppermute x10, starting transfers between devices, moved(): return lax.ppermute(x, axis, pairs)  72.6 us
    ppermute x10, waiting for transfers between devices, moved(): return lax.ppermute(x, axis, pairs)  28.5 us
    ppermute x1, waiting for transfers between devices, partner_sum(): return x + lax.ppermute(x, 'rep', [(0, 1), (1, 0)])  26.6 us
    ppermute x1, waiting for transfers between devices, global_sum(): x = x + lax.ppermute(x, 'rep', [(0, 1), (1, 0)])  14 us
    ppermute x2, waiting for transfers between devices, partner_swap(): return lax.ppermute(x, 'rep', [(0, 1), (1, 0)])  9.07 us
    ppermute x2, starting transfers between devices, partner_swap(): return lax.ppermute(x, 'rep', [(0, 1), (1, 0)])  7.53 us
    ppermute x1, starting transfers between devices, global_sum(): x = x + lax.ppermute(x, 'rep', [(0, 1), (1, 0)])  6.95 us
    ppermute x2, starting transfers between devices, from_behind(): return lax.ppermute(x, axis, pairs)  4.59 us
  transfers between devices with their start and end apart: 18, of which 11 were waited for; matrix products, arithmetic and copies ran while one was open for 9% of the time, Pallas kernels for 0%

profile of v2, /device:TPU:56, one launch (start us, length us, event | category | flops | bytes accessed | tf_op | source)
XLA Modules:
  0.0 202.0 jit_solution(14151513521726244512)
XLA Ops:
  0.6 0.0 copy-start
  0.6 2.1 %collective-permute-start = (bf16[768,256]{1,0:T(8,128)(2,1)}, bf16[768,256]{1,0:T(8,128)(2,1)S(1)}, u32[]{:S(2)}, u32[]{:S(2)}) collective-permute-start(bf16[768,256]{1,0:T(8,128)(2,1)} %param.7), channel_id=1, source_target_pairs={{0,2},{2,4},{4,6},{6,8},{8,10},{10,12},{12,14},{14,16},{16,18},{18... | collective-permute-start | bytes 1179656 | tf_op jit(solution)/shard_map/ppermute | solution.py:14
  2.7 3.6 %collective-permute-start.1 = (bf16[768,256]{1,0:T(8,128)(2,1)}, bf16[768,256]{1,0:T(8,128)(2,1)S(1)}, u32[]{:S(2)}, u32[]{:S(2)}) collective-permute-start(bf16[768,256]{1,0:T(8,128)(2,1)} %param.7), channel_id=1, source_target_pairs={{2,0},{4,2},{6,4},{8,6},{10,8},{12,10},{14,12},{16,14},{18,16},{20... | collective-permute-start | bytes 1179656 | tf_op jit(solution)/shard_map/ppermute | solution.py:17
  6.4 0.7 broadcast_subtract_fusion
  7.1 0.7 iota_compare_fusion.1
  7.8 2.2 %convolution_convert_fusion = bf16[6,18,128,128]{3,1,2,0:T(8,128)(2,1)S(1)} fusion(bf16[6,6,128,128]{3,2,1,0:T(8,128)(2,1)S(1)} %copy-done, s32[6,6]{1,0:T(8,128)S(1)} %broadcast_subtract_fusion, pred[6,6]{1,0:T(8,128)(4,1)S(1)} %iota_compare_fusion.1), kind=kOutput, calls=%fused_computation.4 | convolution fusion | flops 23004432 | bytes 4718772 | tf_op jit(solution)/shard_map/bks,bkij->bsij/dot_general | solution.py:118
  10.0 0.0 copy-start.1
  10.0 0.0 collective-permute-done
  10.1 1.9 collective-permute-done.1
  12.0 0.1 pad_maximum_fusion
  12.0 0.0 copy-start.4
  12.0 0.0 copy-start.5
  12.1 0.0 copy-start.6
  12.1 1.1 fusion.8
  13.2 0.0 copy-done.1
  13.2 4.7 %collective-permute-start.2 = (f32[384,256]{1,0:T(8,128)S(1)}, f32[384,256]{1,0:T(8,128)S(1)}, u32[]{:S(2)}, u32[]{:S(2)}) collective-permute-start(f32[384,256]{1,0:T(8,128)S(1)} %constant_dynamic-slice_fusion), channel_id=1, source_target_pairs={{0,1},{1,0},{2,3},{3,2},{4,5},{5,4},{6,7},{7,6},{8,9},{9,8},{10,11... | collective-permute-start | bytes 1179656 | tf_op jit(solution)/shard_map/ppermute | solution.py:77
  18.0 9.1 %collective-permute-done.2 = f32[384,256]{1,0:T(8,128)S(1)} collective-permute-done((f32[384,256]{1,0:T(8,128)S(1)}, f32[384,256]{1,0:T(8,128)S(1)}, u32[]{:S(2)}, u32[]{:S(2)}) %collective-permute-start.2) | collective-permute-done | bytes 393248 | tf_op jit(solution)/shard_map/ppermute | solution.py:77
  27.0 0.1 add_convert_fusion.1
  27.1 0.0 copy-done.4
  27.1 0.4 convert_reduce_fusion
  27.5 0.3 fusion.21
  27.8 0.2 convolution_convert_fusion.1
  28.0 10.6 %collective-permute-start.7 = (f32[257,128]{1,0:T(8,128)S(1)}, f32[257,128]{1,0:T(8,128)S(1)}, u32[]{:S(2)}, u32[]{:S(2)}) collective-permute-start(f32[257,128]{1,0:T(8,128)S(1)} %fusion.12), channel_id=1, source_target_pairs={{0,2},{2,0},{4,6},{6,4},{8,10},{10,8},{12,14},{14,12},{16,18},{18,... | collective-permute-start | bytes 394760 | tf_op jit(solution)/shard_map/ppermute | solution.py:36
  38.7 2.8 %collective-permute-start.3 = (bf16[384,512]{1,0:T(8,128)(2,1)S(1)}, bf16[384,512]{1,0:T(8,128)(2,1)S(1)}, u32[]{:S(2)}, u32[]{:S(2)}) collective-permute-start(bf16[384,512]{1,0:T(8,128)(2,1)S(1)} %pad_maximum_fusion.1), channel_id=1, source_target_pairs={{0,1},{1,0},{2,3},{3,2},{4,5},{5,4},{6,7},{7,6},{8,9},{9,8},{10,11... | collective-permute-start | bytes 1179656 | tf_op jit(solution)/shard_map/ppermute | solution.py:77
  41.5 0.0 collective-permute-done.7
  41.5 1.9 collective-permute-start.8
  43.5 9.5 %collective-permute-done.8 = f32[257,128]{1,0:T(8,128)S(1)} collective-permute-done((f32[257,128]{1,0:T(8,128)S(1)}, f32[257,128]{1,0:T(8,128)S(1)}, u32[]{:S(2)}, u32[]{:S(2)}) %collective-permute-start.8) | collective-permute-done | bytes 131616 | tf_op jit(solution)/shard_map/ppermute | solution.py:36
  53.0 13.7 %collective-permute-start.9 = (f32[257,128]{1,0:T(8,128)S(1)}, f32[257,128]{1,0:T(8,128)S(1)}, u32[]{:S(2)}, u32[]{:S(2)}) collective-permute-start(f32[257,128]{1,0:T(8,128)S(1)} %add.97), channel_id=1, source_target_pairs={{0,8},{2,10},{4,12},{6,14},{8,0},{10,2},{12,4},{14,6},{16,24},{18,... | collective-permute-start | bytes 394760 | tf_op jit(solution)/shard_map/ppermute | solution.py:36
  66.7 0.0 collective-permute-done.3
  66.7 0.7 fusion.20
  67.4 0.2 maximum_select_fusion.1
  67.6 3.5 %fusion.4 = f32[18,128,256]{2,1,0:T(8,128)S(1)} fusion(bf16[6,128,256,1]{2,1,0,3:T(8,128)(2,1)S(1)} %bitcast.30, bf16[6,18,128,128]{3,1,2,0:T(8,128)(2,1)} %copy-done.1), kind=kOutput, calls=%fused_computation.5 | convolution fusion | flops 905969664 | bytes 6291456 | tf_op jit(solution)/shard_map/bsij,bif->sjf/dot_general | solution.py:144
  71.1 1.0 slice.32
  72.1 2.7 %collective-permute-start.4 = (f32[6,128,256]{2,1,0:T(8,128)}, f32[6,128,256]{2,1,0:T(8,128)}, u32[]{:S(2)}, u32[]{:S(2)}) collective-permute-start(f32[6,128,256]{2,1,0:T(8,128)} %slice.32), channel_id=1, source_target_pairs={{2,0},{4,2},{6,4},{8,6},{10,8},{12,10},{14,12},{16,14},{18,16},{20... | collective-permute-start | bytes 2359304 | tf_op jit(solution)/shard_map/ppermute | solution.py:25
  74.8 0.0 collective-permute-done.9
  74.8 6.9 %collective-permute-start.10 = (f32[257,128]{1,0:T(8,128)S(1)}, f32[257,128]{1,0:T(8,128)S(1)}, u32[]{:S(2)}, u32[]{:S(2)}) collective-permute-start(f32[257,128]{1,0:T(8,128)S(1)} %add.98), channel_id=1, source_target_pairs={{0,1},{1,0},{2,3},{3,2},{4,5},{5,4},{6,7},{7,6},{8,9},{9,8},{10,11... | collective-permute-start | bytes 394760 | tf_op jit(solution)/shard_map/ppermute | solution.py:66
  81.8 14.0 %collective-permute-done.10 = f32[257,128]{1,0:T(8,128)S(1)} collective-permute-done((f32[257,128]{1,0:T(8,128)S(1)}, f32[257,128]{1,0:T(8,128)S(1)}, u32[]{:S(2)}, u32[]{:S(2)}) %collective-permute-start.10) | collective-permute-done | bytes 131616 | tf_op jit(solution)/shard_map/ppermute | solution.py:66
  95.8 3.4 %collective-permute-start.11 = (f32[257,128]{1,0:T(8,128)S(1)}, f32[257,128]{1,0:T(8,128)S(1)}, u32[]{:S(2)}, u32[]{:S(2)}) collective-permute-start(f32[257,128]{1,0:T(8,128)S(1)} %add.99), channel_id=1, source_target_pairs={{0,192},{2,194},{4,196},{6,198},{8,200},{10,202},{12,204},{14,206}... | collective-permute-start | bytes 394760 | tf_op jit(solution)/shard_map/ppermute | solution.py:36
  99.2 3.7 %collective-permute-done.11 = f32[257,128]{1,0:T(8,128)S(1)} collective-permute-done((f32[257,128]{1,0:T(8,128)S(1)}, f32[257,128]{1,0:T(8,128)S(1)}, u32[]{:S(2)}, u32[]{:S(2)}) %collective-permute-start.11) | collective-permute-done | bytes 131616 | tf_op jit(solution)/shard_map/ppermute | solution.py:36
  102.9 6.6 %collective-permute-start.12 = (f32[257,128]{1,0:T(8,128)S(1)}, f32[257,128]{1,0:T(8,128)S(1)}, u32[]{:S(2)}, u32[]{:S(2)}) collective-permute-start(f32[257,128]{1,0:T(8,128)S(1)} %add.100), channel_id=1, source_target_pairs={{0,384},{2,386},{4,388},{6,390},{8,392},{10,394},{12,396},{14,398}... | collective-permute-start | bytes 394760 | tf_op jit(solution)/shard_map/ppermute | solution.py:36
  109.5 0.8 slice.42
  110.3 1.9 collective-permute-start.5
  112.2 0.3 collective-permute-done.12
  112.5 10.1 %collective-permute-start.13 = (f32[257,128]{1,0:T(8,128)S(1)}, f32[257,128]{1,0:T(8,128)S(1)}, u32[]{:S(2)}, u32[]{:S(2)}) collective-permute-start(f32[257,128]{1,0:T(8,128)S(1)} %add.101), channel_id=1, source_target_pairs={{0,16},{2,18},{4,20},{6,22},{8,24},{10,26},{12,28},{14,30},{16,0},... | collective-permute-start | bytes 394760 | tf_op jit(solution)/shard_map/ppermute | solution.py:36
  122.6 4.0 %collective-permute-done.13 = f32[257,128]{1,0:T(8,128)S(1)} collective-permute-done((f32[257,128]{1,0:T(8,128)S(1)}, f32[257,128]{1,0:T(8,128)S(1)}, u32[]{:S(2)}, u32[]{:S(2)}) %collective-permute-start.13) | collective-permute-done | bytes 131616 | tf_op jit(solution)/shard_map/ppermute | solution.py:36
  126.7 0.7 add.102
  127.3 5.1 %collective-permute-start.14 = (f32[257,128]{1,0:T(8,128)}, f32[257,128]{1,0:T(8,128)}, u32[]{:S(2)}, u32[]{:S(2)}) collective-permute-start(f32[257,128]{1,0:T(8,128)} %add.102), channel_id=1, source_target_pairs={{0,32},{2,34},{4,36},{6,38},{8,40},{10,42},{12,44},{14,46},{16,48}... | collective-permute-start | bytes 394760 | tf_op jit(solution)/shard_map/ppermute | solution.py:36
  132.5 3.2 %collective-permute-done.14 = f32[257,128]{1,0:T(8,128)} collective-permute-done((f32[257,128]{1,0:T(8,128)}, f32[257,128]{1,0:T(8,128)}, u32[]{:S(2)}, u32[]{:S(2)}) %collective-permute-start.14) | collective-permute-done | bytes 131616 | tf_op jit(solution)/shard_map/ppermute | solution.py:36
  135.7 1.0 add.103
  136.7 17.4 %collective-permute-start.16 = (f32[257,128]{1,0:T(8,128)S(1)}, f32[257,128]{1,0:T(8,128)S(1)}, u32[]{:S(2)}, u32[]{:S(2)}) collective-permute-start(f32[257,128]{1,0:T(8,128)S(1)} %add.103), channel_id=1, source_target_pairs={{0,128},{2,130},{4,132},{6,134},{8,136},{10,138},{12,140},{14,142}... | collective-permute-start | bytes 394760 | tf_op jit(solution)/shard_map/ppermute | solution.py:36
  154.1 1.9 collective-permute-start.15
  156.0 0.0 collective-permute-done.5
  156.1 0.0 collective-permute-done.4
  156.1 2.3 %fusion.11 = f32[6,128,256]{2,1,0:T(8,128)} fusion(f32[6,128,256]{2,1,0:T(8,128)} %collective-permute-done.4, f32[18,128,256]{2,1,0:T(8,128)S(1)} %fusion.4, bf16[6,128,256]{2,1,0:T(8,128)(2,1)} %collective-permute-done.5), kind=kLoop, calls=%fused_computation.13 | loop fusion | flops 589824 | bytes 2752512 | tf_op jit(solution)/shard_map/add | solution.py:151
  158.3 1.9 collective-permute-start.6
  160.3 5.8 %collective-permute-done.16 = f32[257,128]{1,0:T(8,128)S(1)} collective-permute-done((f32[257,128]{1,0:T(8,128)S(1)}, f32[257,128]{1,0:T(8,128)S(1)}, u32[]{:S(2)}, u32[]{:S(2)}) %collective-permute-start.16) | collective-permute-done | bytes 131616 | tf_op jit(solution)/shard_map/ppermute | solution.py:36
  166.1 1.9 collective-permute-done.15
  168.0 1.9 collective-permute-start.17
  170.0 2.1 %maximum_select_fusion = bf16[768,256]{1,0:T(8,128)(2,1)} fusion(bf16[384,256]{1,0:T(8,128)(2,1)} %get-tuple-element.7, bf16[384,256]{1,0:T(8,128)(2,1)} %copy-done.2, pred[]{:T(512)S(6)} %eq.17), kind=kLoop, calls=%fused_computation.16 | loop fusion | flops 1769472 | bytes 786433 | tf_op jit(solution)/shard_map/jit(_where)/select_n | solution.py:81
  172.0 0.0 collective-permute-done.17
  172.1 0.6 slice_multiply_fusion.1
  172.6 0.7 slice_multiply_fusion
  173.4 26.6 %collective-permute-done.6 = f32[6,128,256]{2,1,0:T(8,128)S(1)} collective-permute-done((f32[6,128,256]{2,1,0:T(8,128)}, f32[6,128,256]{2,1,0:T(8,128)S(1)}, u32[]{:S(2)}, u32[]{:S(2)}) %collective-permute-start.6) | collective-permute-done | bytes 786464 | tf_op jit(solution)/shard_map/ppermute | solution.py:87
  200.0 2.0 add_convert_fusion
  (18 shorter events, 0.3 us)
Async XLA Ops:
  0.6 7.2 %copy-start = (bf16[6,6,128,128]{3,2,1,0:T(8,128)(2,1)S(1)}, bf16[6,6,128,128]{3,2,1,0:T(8,128)(2,1)}, u32[]{:S(2)}) copy-start(bf16[6,6,128,128]{3,2,1,0:T(8,128)(2,1)} %param.8) | copy-start | bytes 3538948
  0.6 9.4 %collective-permute-start = (bf16[768,256]{1,0:T(8,128)(2,1)}, bf16[768,256]{1,0:T(8,128)(2,1)S(1)}, u32[]{:S(2)}, u32[]{:S(2)}) collective-permute-start(bf16[768,256]{1,0:T(8,128)(2,1)} %param.7), channel_id=1, source_target_pairs={{0,2},{2,4},{4,6},{6,8},{8,10},{10,12},{12,14},{14,16},{16,18},{18... | collective-permute-start | bytes 1179656 | tf_op jit(solution)/shard_map/ppermute | solution.py:14
  2.7 9.2 %collective-permute-start.1 = (bf16[768,256]{1,0:T(8,128)(2,1)}, bf16[768,256]{1,0:T(8,128)(2,1)S(1)}, u32[]{:S(2)}, u32[]{:S(2)}) collective-permute-start(bf16[768,256]{1,0:T(8,128)(2,1)} %param.7), channel_id=1, source_target_pairs={{2,0},{4,2},{6,4},{8,6},{10,8},{12,10},{14,12},{16,14},{18,16},{20... | collective-permute-start | bytes 1179656 | tf_op jit(solution)/shard_map/ppermute | solution.py:17
  7.8 4.2 %copy-start.3 = (bf16[768,256]{1,0:T(8,128)(2,1)S(1)}, bf16[768,256]{1,0:T(8,128)(2,1)}, u32[]{:S(2)}) copy-start(bf16[768,256]{1,0:T(8,128)(2,1)} %param.7) | copy-start | bytes 1179652
  10.0 3.1 %copy-start.1 = (bf16[6,18,128,128]{3,1,2,0:T(8,128)(2,1)}, bf16[6,18,128,128]{3,1,2,0:T(8,128)(2,1)S(1)}, u32[]{:S(2)}) copy-start(bf16[6,18,128,128]{3,1,2,0:T(8,128)(2,1)S(1)} %convolution_convert_fusion) | copy-start | bytes 10616836
  12.0 15.0 %copy-start.4 = (bf16[256,256]{1,0:T(8,128)(2,1)S(1)}, bf16[256,256]{1,0:T(8,128)(2,1)}, u32[]{:S(2)}) copy-start(bf16[256,256]{1,0:T(8,128)(2,1)} %param.11) | copy-start | bytes 393220
  12.0 15.0 %copy-start.5 = (bf16[768,256]{1,0:T(8,128)(2,1)S(1)}, bf16[768,256]{1,0:T(8,128)(2,1)}, u32[]{:S(2)}) copy-start(bf16[768,256]{1,0:T(8,128)(2,1)} %param.13) | copy-start | bytes 1179652
  12.1 15.0 %copy-start.6 = (f32[256]{0:T(256)S(1)}, f32[256]{0:T(256)}, u32[]{:S(2)}) copy-start(f32[256]{0:T(256)} %param.12) | copy-start | bytes 3076
  13.2 13.8 %collective-permute-start.2 = (f32[384,256]{1,0:T(8,128)S(1)}, f32[384,256]{1,0:T(8,128)S(1)}, u32[]{:S(2)}, u32[]{:S(2)}) collective-permute-start(f32[384,256]{1,0:T(8,128)S(1)} %constant_dynamic-slice_fusion), channel_id=1, source_target_pairs={{0,1},{1,0},{2,3},{3,2},{4,5},{5,4},{6,7},{7,6},{8,9},{9,8},{10,11... | collective-permute-start | bytes 1179656 | tf_op jit(solution)/shard_map/ppermute | solution.py:77
  27.5 11.2 %copy-start.2 = (bf16[384,256]{1,0:T(8,128)(2,1)}, bf16[384,256]{1,0:T(8,128)(2,1)S(1)}, u32[]{:S(2)}) copy-start(bf16[384,256]{1,0:T(8,128)(2,1)S(1)} %get-tuple-element.8) | copy-start | bytes 589828
  28.0 13.5 %collective-permute-start.7 = (f32[257,128]{1,0:T(8,128)S(1)}, f32[257,128]{1,0:T(8,128)S(1)}, u32[]{:S(2)}, u32[]{:S(2)}) collective-permute-start(f32[257,128]{1,0:T(8,128)S(1)} %fusion.12), channel_id=1, source_target_pairs={{0,2},{2,0},{4,6},{6,4},{8,10},{10,8},{12,14},{14,12},{16,18},{18,... | collective-permute-start | bytes 394760 | tf_op jit(solution)/shard_map/ppermute | solution.py:36
  38.7 28.0 %collective-permute-start.3 = (bf16[384,512]{1,0:T(8,128)(2,1)S(1)}, bf16[384,512]{1,0:T(8,128)(2,1)S(1)}, u32[]{:S(2)}, u32[]{:S(2)}) collective-permute-start(bf16[384,512]{1,0:T(8,128)(2,1)S(1)} %pad_maximum_fusion.1), channel_id=1, source_target_pairs={{0,1},{1,0},{2,3},{3,2},{4,5},{5,4},{6,7},{7,6},{8,9},{9,8},{10,11... | collective-permute-start | bytes 1179656 | tf_op jit(solution)/shard_map/ppermute | solution.py:77
  41.5 11.5 %collective-permute-start.8 = (f32[257,128]{1,0:T(8,128)S(1)}, f32[257,128]{1,0:T(8,128)S(1)}, u32[]{:S(2)}, u32[]{:S(2)}) collective-permute-start(f32[257,128]{1,0:T(8,128)S(1)} %fusion.14), channel_id=1, source_target_pairs={{0,4},{2,6},{4,0},{6,2},{8,12},{10,14},{12,8},{14,10},{16,20},{18,... | collective-permute-start | bytes 394760 | tf_op jit(solution)/shard_map/ppermute | solution.py:36
  53.0 21.7 %collective-permute-start.9 = (f32[257,128]{1,0:T(8,128)S(1)}, f32[257,128]{1,0:T(8,128)S(1)}, u32[]{:S(2)}, u32[]{:S(2)}) collective-permute-start(f32[257,128]{1,0:T(8,128)S(1)} %add.97), channel_id=1, source_target_pairs={{0,8},{2,10},{4,12},{6,14},{8,0},{10,2},{12,4},{14,6},{16,24},{18,... | collective-permute-start | bytes 394760 | tf_op jit(solution)/shard_map/ppermute | solution.py:36
  72.1 84.0 %collective-permute-start.4 = (f32[6,128,256]{2,1,0:T(8,128)}, f32[6,128,256]{2,1,0:T(8,128)}, u32[]{:S(2)}, u32[]{:S(2)}) collective-permute-start(f32[6,128,256]{2,1,0:T(8,128)} %slice.32), channel_id=1, source_target_pairs={{2,0},{4,2},{6,4},{8,6},{10,8},{12,10},{14,12},{16,14},{18,16},{20... | collective-permute-start | bytes 2359304 | tf_op jit(solution)/shard_map/ppermute | solution.py:25
  74.8 20.9 %collective-permute-start.10 = (f32[257,128]{1,0:T(8,128)S(1)}, f32[257,128]{1,0:T(8,128)S(1)}, u32[]{:S(2)}, u32[]{:S(2)}) collective-permute-start(f32[257,128]{1,0:T(8,128)S(1)} %add.98), channel_id=1, source_target_pairs={{0,1},{1,0},{2,3},{3,2},{4,5},{5,4},{6,7},{7,6},{8,9},{9,8},{10,11... | collective-permute-start | bytes 394760 | tf_op jit(solution)/shard_map/ppermute | solution.py:66
  95.8 7.1 %collective-permute-start.11 = (f32[257,128]{1,0:T(8,128)S(1)}, f32[257,128]{1,0:T(8,128)S(1)}, u32[]{:S(2)}, u32[]{:S(2)}) collective-permute-start(f32[257,128]{1,0:T(8,128)S(1)} %add.99), channel_id=1, source_target_pairs={{0,192},{2,194},{4,196},{6,198},{8,200},{10,202},{12,204},{14,206}... | collective-permute-start | bytes 394760 | tf_op jit(solution)/shard_map/ppermute | solution.py:36
  102.9 9.6 %collective-permute-start.12 = (f32[257,128]{1,0:T(8,128)S(1)}, f32[257,128]{1,0:T(8,128)S(1)}, u32[]{:S(2)}, u32[]{:S(2)}) collective-permute-start(f32[257,128]{1,0:T(8,128)S(1)} %add.100), channel_id=1, source_target_pairs={{0,384},{2,386},{4,388},{6,390},{8,392},{10,394},{12,396},{14,398}... | collective-permute-start | bytes 394760 | tf_op jit(solution)/shard_map/ppermute | solution.py:36
  110.3 45.7 %collective-permute-start.5 = (bf16[6,128,256]{2,1,0:T(8,128)(2,1)}, bf16[6,128,256]{2,1,0:T(8,128)(2,1)}, u32[]{:S(2)}, u32[]{:S(2)}) collective-permute-start(bf16[6,128,256]{2,1,0:T(8,128)(2,1)} %slice.42), channel_id=1, source_target_pairs={{0,2},{2,4},{4,6},{6,8},{8,10},{10,12},{12,14},{14,16},{16,18},{18... | collective-permute-start | bytes 1179656 | tf_op jit(solution)/shard_map/ppermute | solution.py:25
  112.5 14.1 %collective-permute-start.13 = (f32[257,128]{1,0:T(8,128)S(1)}, f32[257,128]{1,0:T(8,128)S(1)}, u32[]{:S(2)}, u32[]{:S(2)}) collective-permute-start(f32[257,128]{1,0:T(8,128)S(1)} %add.101), channel_id=1, source_target_pairs={{0,16},{2,18},{4,20},{6,22},{8,24},{10,26},{12,28},{14,30},{16,0},... | collective-permute-start | bytes 394760 | tf_op jit(solution)/shard_map/ppermute | solution.py:36
  127.3 8.4 %collective-permute-start.14 = (f32[257,128]{1,0:T(8,128)}, f32[257,128]{1,0:T(8,128)}, u32[]{:S(2)}, u32[]{:S(2)}) collective-permute-start(f32[257,128]{1,0:T(8,128)} %add.102), channel_id=1, source_target_pairs={{0,32},{2,34},{4,36},{6,38},{8,40},{10,42},{12,44},{14,46},{16,48}... | collective-permute-start | bytes 394760 | tf_op jit(solution)/shard_map/ppermute | solution.py:36
  136.7 29.3 %collective-permute-start.16 = (f32[257,128]{1,0:T(8,128)S(1)}, f32[257,128]{1,0:T(8,128)S(1)}, u32[]{:S(2)}, u32[]{:S(2)}) collective-permute-start(f32[257,128]{1,0:T(8,128)S(1)} %add.103), channel_id=1, source_target_pairs={{0,128},{2,130},{4,132},{6,134},{8,136},{10,138},{12,140},{14,142}... | collective-permute-start | bytes 394760 | tf_op jit(solution)/shard_map/ppermute | solution.py:36
  154.1 13.9 %collective-permute-start.15 = (f32[257,128]{1,0:T(8,128)S(1)}, f32[257,128]{1,0:T(8,128)S(1)}, u32[]{:S(2)}, u32[]{:S(2)}) collective-permute-start(f32[257,128]{1,0:T(8,128)S(1)} %add.103), channel_id=1, source_target_pairs={{0,64},{2,66},{4,68},{6,70},{8,72},{10,74},{12,76},{14,78},{16,80}... | collective-permute-start | bytes 394760 | tf_op jit(solution)/shard_map/ppermute | solution.py:36
  158.3 41.6 %collective-permute-start.6 = (f32[6,128,256]{2,1,0:T(8,128)}, f32[6,128,256]{2,1,0:T(8,128)S(1)}, u32[]{:S(2)}, u32[]{:S(2)}) collective-permute-start(f32[6,128,256]{2,1,0:T(8,128)} %fusion.11), channel_id=1, source_target_pairs={{0,1},{1,0},{2,3},{3,2},{4,5},{5,4},{6,7},{7,6},{8,9},{9,8},{10,11... | collective-permute-start | bytes 2359304 | tf_op jit(solution)/shard_map/ppermute | solution.py:87
  168.0 4.0 %collective-permute-start.17 = (f32[257,128]{1,0:T(8,128)S(1)}, f32[257,128]{1,0:T(8,128)S(1)}, u32[]{:S(2)}, u32[]{:S(2)}) collective-permute-start(f32[257,128]{1,0:T(8,128)S(1)} %select_add_fusion), channel_id=1, source_target_pairs={{0,2},{2,0},{4,6},{6,4},{8,10},{10,8},{12,14},{14,12},{16,18},{18,... | collective-permute-start | bytes 394760 | tf_op jit(solution)/shard_map/ppermute | solution.py:36

commit v3 on v2

--- a/solution.py
+++ b/solution.py
@@ -51,10 +51,10 @@
     return (first + second) + third_part
 
 
-def global_sum(x):
+def global_sum(x, tie):
     count = lax.axis_size("rows")
     if count not in ROW_AXES or lax.axis_size("rep") != 2:
-        return lax.psum(x, ("rows", "rep"))
+        return lax.psum(x, ("rows", "rep")), tie
     (x_stride, x_size), (z_stride, z_size), (y_stride, y_size), (c_stride, c_size) = ROW_AXES[count]
     core = (lax.axis_index("rows") // c_stride) % c_size
     width = x.shape[1] // 2
@@ -66,11 +66,13 @@
     x = x + lax.ppermute(x, "rep", [(0, 1), (1, 0)])
     x = swapped_sum(x, "rows", count, x_stride, x_size, 1)
     x = swapped_sum(x, "rows", count, x_stride, x_size, 2)
+    x, tie = lax.optimization_barrier((x, tie))
     x = swapped_sum(x, "rows", count, z_stride, z_size, 1)
     x = swapped_sum(x, "rows", count, z_stride, z_size, 2)
     x = three_way_sum(x, "rows", count, z_stride, z_size)
     other = moved(x, "rows", count, c_stride, c_size, lambda c: c ^ 1)
-    return jnp.where(core == 0, jnp.concatenate([x, other], 1), jnp.concatenate([other, x], 1))
+    joined = jnp.where(core == 0, jnp.concatenate([x, other], 1), jnp.concatenate([other, x], 1))
+    return joined, tie
 
 
 def partner_swap(x):
@@ -134,12 +136,6 @@
         agg_half, grad_half, (((0,), (0,)), ((), ())), preferred_element_type=jnp.float32
     )
     bias_part = jnp.sum(grad_half.astype(jnp.float32), axis=0)
-    grad_terms = global_sum(jnp.concatenate([weight_part, bias_part[None, :]], axis=0))
-    weight_total = grad_terms[:feat_width]
-    bias_total = grad_terms[feat_width]
-    scale = 1.0 / math.sqrt(node_count)
-    weight_grad = weight_total * scale
-    bias_grad = bias_total * scale
     grad_blocks = agg_grad.reshape(num_blocks, tile_size, feat_width)
     spread = jnp.einsum(
         "bsij,bif->sjf", band_tiles, grad_blocks, preferred_element_type=jnp.float32
@@ -150,6 +146,14 @@
     )
     own_terms = spread[num_blocks : 2 * num_blocks] + from_above + from_below
     own_total = partner_sum(own_terms)
+    grad_terms, own_total = global_sum(
+        jnp.concatenate([weight_part, bias_part[None, :]], axis=0), own_total
+    )
+    weight_total = grad_terms[:feat_width]
+    bias_total = grad_terms[feat_width]
+    scale = 1.0 / math.sqrt(node_count)
+    weight_grad = weight_total * scale
+    bias_grad = bias_total * scale
     feature_grad = own_total.reshape(rows_here, feat_width).astype(jnp.bfloat16)
     return (activations, feature_grad, weight_grad, bias_grad)
 

time: 203 us -> 228 us (1.12)
  the two profiles are of different devices: /device:TPU:56 before, /device:TPU:1 now
where the time goes in v3:
time: 228 us; the launch traced here: 226 us
  waiting for transfers between devices  113 us (50%)
  starting transfers between devices  92.6 us (41%)
  matrix products  8.71 us (4%)
  other arithmetic  6.36 us (3%)
  local copies, waits for them, and re-layouts  4.37 us (2%)
    ppermute x10, waiting for transfers between devices, moved(): return lax.ppermute(x, axis, pairs)  63.9 us
    ppermute x10, starting transfers between devices, moved(): return lax.ppermute(x, axis, pairs)  58.7 us
    ppermute x2, waiting for transfers between devices, partner_swap(): return lax.ppermute(x, 'rep', [(0, 1), (1, 0)])  36.2 us
    ppermute x1, waiting for transfers between devices, global_sum(): x = x + lax.ppermute(x, 'rep', [(0, 1), (1, 0)])  9.19 us
    ppermute x1, starting transfers between devices, extended(): lax.ppermute(lax.slice_in_dim(block, 0, width, axis=dim), axis, backward)  9.15 us
    ppermute x2, starting transfers between devices, from_behind(): return lax.ppermute(x, axis, pairs)  5.54 us
    ppermute x1, starting transfers between devices, partner_sum(): return x + lax.ppermute(x, 'rep', [(0, 1), (1, 0)])  5.36 us
    ppermute x1, starting transfers between devices, extended(): lax.ppermute(lax.slice_in_dim(block, block.shape[dim] - width, None, axis...  4.73 us
  transfers between devices with their start and end apart: 18, of which 12 were waited for; matrix products, arithmetic and copies ran while one was open for 4% of the time, Pallas kernels for 0%

profile of v3, /device:TPU:1, one launch (start us, length us, event | category | flops | bytes accessed | tf_op | source)
XLA Modules:
  0.0 226.1 jit_solution(8585604935816331536)
XLA Ops:
  0.6 0.0 copy-start
  0.6 4.7 %collective-permute-start = (bf16[768,256]{1,0:T(8,128)(2,1)}, bf16[768,256]{1,0:T(8,128)(2,1)S(1)}, u32[]{:S(2)}, u32[]{:S(2)}) collective-permute-start(bf16[768,256]{1,0:T(8,128)(2,1)} %param.7), channel_id=1, source_target_pairs={{0,2},{2,4},{4,6},{6,8},{8,10},{10,12},{12,14},{14,16},{16,18},{18... | collective-permute-start | bytes 1179656 | tf_op jit(solution)/shard_map/ppermute | solution.py:14
  5.4 9.1 %collective-permute-start.1 = (bf16[768,256]{1,0:T(8,128)(2,1)}, bf16[768,256]{1,0:T(8,128)(2,1)S(1)}, u32[]{:S(2)}, u32[]{:S(2)}) collective-permute-start(bf16[768,256]{1,0:T(8,128)(2,1)} %param.7), channel_id=1, source_target_pairs={{2,0},{4,2},{6,4},{8,6},{10,8},{12,10},{14,12},{16,14},{18,16},{20... | collective-permute-start | bytes 1179656 | tf_op jit(solution)/shard_map/ppermute | solution.py:17
  14.5 0.7 broadcast_subtract_fusion
  15.2 0.7 iota_compare_fusion.1
  16.0 2.2 convolution_convert_fusion
  18.2 0.0 collective-permute-done
  18.2 0.0 collective-permute-done.1
  18.2 0.1 pad_maximum_fusion
  18.3 0.0 copy-start.8
  18.3 0.0 copy-start.9
  18.4 0.0 copy-start.10
  18.4 1.1 fusion.8
  19.5 0.9 copy-done.1
  20.4 2.1 collective-permute-start.2
  22.5 21.9 %collective-permute-done.2 = f32[384,256]{1,0:T(8,128)S(1)} collective-permute-done((f32[384,256]{1,0:T(8,128)S(1)}, f32[384,256]{1,0:T(8,128)S(1)}, u32[]{:S(2)}, u32[]{:S(2)}) %collective-permute-start.2) | collective-permute-done | bytes 393248 | tf_op jit(solution)/shard_map/ppermute | solution.py:79
  44.4 0.1 add_convert_fusion
  44.5 0.4 convert_reduce_fusion
  44.9 0.3 copy-done.2
  45.2 0.7 copy-done.6
  45.8 0.2 convolution_convert_fusion.1
  46.1 2.5 %collective-permute-start.3 = (bf16[384,512]{1,0:T(8,128)(2,1)S(1)}, bf16[384,512]{1,0:T(8,128)(2,1)S(1)}, u32[]{:S(2)}, u32[]{:S(2)}) collective-permute-start(bf16[384,512]{1,0:T(8,128)(2,1)S(1)} %pad_maximum_fusion.1), channel_id=1, source_target_pairs={{0,1},{1,0},{2,3},{3,2},{4,5},{5,4},{6,7},{7,6},{8,9},{9,8},{10,11... | collective-permute-start | bytes 1179656 | tf_op jit(solution)/shard_map/ppermute | solution.py:79
  48.7 14.3 %collective-permute-done.3 = bf16[384,512]{1,0:T(8,128)(2,1)S(1)} collective-permute-done((bf16[384,512]{1,0:T(8,128)(2,1)S(1)}, bf16[384,512]{1,0:T(8,128)(2,1)S(1)}, u32[]{:S(2)}, u32[]{:S(2)}) %collective-permute-start.3) | collective-permute-done | bytes 393248 | tf_op jit(solution)/shard_map/ppermute | solution.py:79
  63.0 0.7 fusion.20
  63.7 0.2 maximum_select_fusion.1
  63.9 3.5 %fusion.4 = f32[18,128,256]{2,1,0:T(8,128)S(1)} fusion(bf16[6,128,256,1]{2,1,0,3:T(8,128)(2,1)S(1)} %bitcast.30, bf16[6,18,128,128]{3,1,2,0:T(8,128)(2,1)} %copy-done.1), kind=kOutput, calls=%fused_computation.5 | convolution fusion | flops 905969664 | bytes 6291456 | tf_op jit(solution)/shard_map/bsij,bif->sjf/dot_general | solution.py:140
  67.4 0.9 slice.32
  68.3 2.8 %collective-permute-start.10 = (f32[6,128,256]{2,1,0:T(8,128)}, f32[6,128,256]{2,1,0:T(8,128)}, u32[]{:S(2)}, u32[]{:S(2)}) collective-permute-start(f32[6,128,256]{2,1,0:T(8,128)} %slice.32), channel_id=1, source_target_pairs={{2,0},{4,2},{6,4},{8,6},{10,8},{12,10},{14,12},{16,14},{18,16},{20... | collective-permute-start | bytes 2359304 | tf_op jit(solution)/shard_map/ppermute | solution.py:25
  71.1 0.8 slice.42
  71.9 2.7 %collective-permute-start.11 = (bf16[6,128,256]{2,1,0:T(8,128)(2,1)}, bf16[6,128,256]{2,1,0:T(8,128)(2,1)}, u32[]{:S(2)}, u32[]{:S(2)}) collective-permute-start(bf16[6,128,256]{2,1,0:T(8,128)(2,1)} %slice.42), channel_id=1, source_target_pairs={{0,2},{2,4},{4,6},{6,8},{8,10},{10,12},{12,14},{14,16},{16,18},{18... | collective-permute-start | bytes 1179656 | tf_op jit(solution)/shard_map/ppermute | solution.py:25
  74.7 1.3 fusion.21
  76.0 2.3 %collective-permute-start.4 = (f32[257,128]{1,0:T(8,128)S(1)}, f32[257,128]{1,0:T(8,128)S(1)}, u32[]{:S(2)}, u32[]{:S(2)}) collective-permute-start(f32[257,128]{1,0:T(8,128)S(1)} %fusion.12), channel_id=1, source_target_pairs={{0,2},{2,0},{4,6},{6,4},{8,10},{10,8},{12,14},{14,12},{16,18},{18,... | collective-permute-start | bytes 394760 | tf_op jit(solution)/shard_map/ppermute | solution.py:36
  78.3 1.3 collective-permute-done.11
  79.7 2.3 collective-permute-done.10
  81.9 1.4 fusion.11
  83.3 5.4 %collective-permute-start.12 = (f32[6,128,256]{2,1,0:T(8,128)S(1)}, f32[6,128,256]{2,1,0:T(8,128)S(1)}, u32[]{:S(2)}, u32[]{:S(2)}) collective-permute-start(f32[6,128,256]{2,1,0:T(8,128)S(1)} %fusion.11), channel_id=1, source_target_pairs={{0,1},{1,0},{2,3},{3,2},{4,5},{5,4},{6,7},{7,6},{8,9},{9,8},{10,11... | collective-permute-start | bytes 2359304 | tf_op jit(solution)/shard_map/ppermute | solution.py:89
  88.7 0.0 collective-permute-done.4
  88.7 1.9 collective-permute-start.5
  90.6 33.9 %collective-permute-done.5 = f32[257,128]{1,0:T(8,128)S(1)} collective-permute-done((f32[257,128]{1,0:T(8,128)S(1)}, f32[257,128]{1,0:T(8,128)S(1)}, u32[]{:S(2)}, u32[]{:S(2)}) %collective-permute-start.5) | collective-permute-done | bytes 131616 | tf_op jit(solution)/shard_map/ppermute | solution.py:36
  124.6 1.9 collective-permute-start.6
  126.5 8.8 %collective-permute-done.6 = f32[257,128]{1,0:T(8,128)S(1)} collective-permute-done((f32[257,128]{1,0:T(8,128)S(1)}, f32[257,128]{1,0:T(8,128)S(1)}, u32[]{:S(2)}, u32[]{:S(2)}) %collective-permute-start.6) | collective-permute-done | bytes 131616 | tf_op jit(solution)/shard_map/ppermute | solution.py:36
  135.3 0.0 copy-start.4
  135.3 0.0 copy-start.5
  135.4 4.5 %collective-permute-start.7 = (f32[257,128]{1,0:T(8,128)S(1)}, f32[257,128]{1,0:T(8,128)S(1)}, u32[]{:S(2)}, u32[]{:S(2)}) collective-permute-start(f32[257,128]{1,0:T(8,128)S(1)} %add.94), channel_id=1, source_target_pairs={{0,1},{1,0},{2,3},{3,2},{4,5},{5,4},{6,7},{7,6},{8,9},{9,8},{10,11... | collective-permute-start | bytes 394760 | tf_op jit(solution)/shard_map/ppermute | solution.py:66
  139.9 9.2 %collective-permute-done.7 = f32[257,128]{1,0:T(8,128)S(1)} collective-permute-done((f32[257,128]{1,0:T(8,128)S(1)}, f32[257,128]{1,0:T(8,128)S(1)}, u32[]{:S(2)}, u32[]{:S(2)}) %collective-permute-start.7) | collective-permute-done | bytes 131616 | tf_op jit(solution)/shard_map/ppermute | solution.py:66
  149.1 2.5 %collective-permute-start.8 = (f32[257,128]{1,0:T(8,128)S(1)}, f32[257,128]{1,0:T(8,128)S(1)}, u32[]{:S(2)}, u32[]{:S(2)}) collective-permute-start(f32[257,128]{1,0:T(8,128)S(1)} %add.95), channel_id=1, source_target_pairs={{0,192},{2,194},{4,196},{6,198},{8,200},{10,202},{12,204},{14,206}... | collective-permute-start | bytes 394760 | tf_op jit(solution)/shard_map/ppermute | solution.py:36
  151.6 4.0 %collective-permute-done.8 = f32[257,128]{1,0:T(8,128)S(1)} collective-permute-done((f32[257,128]{1,0:T(8,128)S(1)}, f32[257,128]{1,0:T(8,128)S(1)}, u32[]{:S(2)}, u32[]{:S(2)}) %collective-permute-start.8) | collective-permute-done | bytes 131616 | tf_op jit(solution)/shard_map/ppermute | solution.py:36
  155.7 4.1 %collective-permute-start.9 = (f32[257,128]{1,0:T(8,128)S(1)}, f32[257,128]{1,0:T(8,128)S(1)}, u32[]{:S(2)}, u32[]{:S(2)}) collective-permute-start(f32[257,128]{1,0:T(8,128)S(1)} %add.96), channel_id=1, source_target_pairs={{0,384},{2,386},{4,388},{6,390},{8,392},{10,394},{12,396},{14,398}... | collective-permute-start | bytes 394760 | tf_op jit(solution)/shard_map/ppermute | solution.py:36
  159.7 3.2 %collective-permute-done.9 = f32[257,128]{1,0:T(8,128)S(1)} collective-permute-done((f32[257,128]{1,0:T(8,128)S(1)}, f32[257,128]{1,0:T(8,128)S(1)}, u32[]{:S(2)}, u32[]{:S(2)}) %collective-permute-start.9) | collective-permute-done | bytes 131616 | tf_op jit(solution)/shard_map/ppermute | solution.py:36
  163.0 0.0 collective-permute-done.12
  163.0 0.8 add.100
  163.8 10.5 %collective-permute-start.13 = (f32[257,128]{1,0:T(8,128)S(1)}, f32[257,128]{1,0:T(8,128)S(1)}, u32[]{:S(2)}, u32[]{:S(2)}) collective-permute-start(f32[257,128]{1,0:T(8,128)S(1)} %add.97), channel_id=1, source_target_pairs={{0,16},{2,18},{4,20},{6,22},{8,24},{10,26},{12,28},{14,30},{16,0},... | collective-permute-start | bytes 394760 | tf_op jit(solution)/shard_map/ppermute | solution.py:36
  174.3 2.4 %collective-permute-done.13 = f32[257,128]{1,0:T(8,128)S(1)} collective-permute-done((f32[257,128]{1,0:T(8,128)S(1)}, f32[257,128]{1,0:T(8,128)S(1)}, u32[]{:S(2)}, u32[]{:S(2)}) %collective-permute-start.13) | collective-permute-done | bytes 131616 | tf_op jit(solution)/shard_map/ppermute | solution.py:36
  176.7 7.7 %collective-permute-start.14 = (f32[257,128]{1,0:T(8,128)S(1)}, f32[257,128]{1,0:T(8,128)S(1)}, u32[]{:S(2)}, u32[]{:S(2)}) collective-permute-start(f32[257,128]{1,0:T(8,128)S(1)} %add.102), channel_id=1, source_target_pairs={{0,32},{2,34},{4,36},{6,38},{8,40},{10,42},{12,44},{14,46},{16,48}... | collective-permute-start | bytes 394760 | tf_op jit(solution)/shard_map/ppermute | solution.py:36
  184.4 2.7 %collective-permute-done.14 = f32[257,128]{1,0:T(8,128)S(1)} collective-permute-done((f32[257,128]{1,0:T(8,128)S(1)}, f32[257,128]{1,0:T(8,128)S(1)}, u32[]{:S(2)}, u32[]{:S(2)}) %collective-permute-start.14) | collective-permute-done | bytes 131616 | tf_op jit(solution)/shard_map/ppermute | solution.py:36
  187.1 12.4 %collective-permute-start.16 = (f32[257,128]{1,0:T(8,128)S(1)}, f32[257,128]{1,0:T(8,128)S(1)}, u32[]{:S(2)}, u32[]{:S(2)}) collective-permute-start(f32[257,128]{1,0:T(8,128)S(1)} %add.103), channel_id=1, source_target_pairs={{0,128},{2,130},{4,132},{6,134},{8,136},{10,138},{12,140},{14,142}... | collective-permute-start | bytes 394760 | tf_op jit(solution)/shard_map/ppermute | solution.py:36
  199.4 3.7 %collective-permute-start.15 = (f32[257,128]{1,0:T(8,128)S(1)}, f32[257,128]{1,0:T(8,128)S(1)}, u32[]{:S(2)}, u32[]{:S(2)}) collective-permute-start(f32[257,128]{1,0:T(8,128)S(1)} %add.103), channel_id=1, source_target_pairs={{0,64},{2,66},{4,68},{6,70},{8,72},{10,74},{12,76},{14,78},{16,80}... | collective-permute-start | bytes 394760 | tf_op jit(solution)/shard_map/ppermute | solution.py:36
  203.2 8.8 %collective-permute-done.16 = f32[257,128]{1,0:T(8,128)S(1)} collective-permute-done((f32[257,128]{1,0:T(8,128)S(1)}, f32[257,128]{1,0:T(8,128)S(1)}, u32[]{:S(2)}, u32[]{:S(2)}) %collective-permute-start.16) | collective-permute-done | bytes 131616 | tf_op jit(solution)/shard_map/ppermute | solution.py:36
  212.0 0.0 collective-permute-done.15
  212.0 11.8 %collective-permute-start.17 = (f32[257,128]{1,0:T(8,128)S(1)}, f32[257,128]{1,0:T(8,128)S(1)}, u32[]{:S(2)}, u32[]{:S(2)}) collective-permute-start(f32[257,128]{1,0:T(8,128)S(1)} %select_add_fusion), channel_id=1, source_target_pairs={{0,2},{2,0},{4,6},{6,4},{8,10},{10,8},{12,14},{14,12},{16,18},{18,... | collective-permute-start | bytes 394760 | tf_op jit(solution)/shard_map/ppermute | solution.py:36
  223.8 0.9 maximum_select_fusion
  224.7 0.0 collective-permute-done.17
  224.8 0.6 slice_multiply_fusion.1
  225.4 0.7 slice_multiply_fusion
  (26 shorter events, 0.3 us)
Async XLA Ops:
  0.6 15.3 %copy-start = (bf16[6,6,128,128]{3,2,1,0:T(8,128)(2,1)S(1)}, bf16[6,6,128,128]{3,2,1,0:T(8,128)(2,1)}, u32[]{:S(2)}) copy-start(bf16[6,6,128,128]{3,2,1,0:T(8,128)(2,1)} %param.8) | copy-start | bytes 3538948
  0.6 17.6 %collective-permute-start = (bf16[768,256]{1,0:T(8,128)(2,1)}, bf16[768,256]{1,0:T(8,128)(2,1)S(1)}, u32[]{:S(2)}, u32[]{:S(2)}) collective-permute-start(bf16[768,256]{1,0:T(8,128)(2,1)} %param.7), channel_id=1, source_target_pairs={{0,2},{2,4},{4,6},{6,8},{8,10},{10,12},{12,14},{14,16},{16,18},{18... | collective-permute-start | bytes 1179656 | tf_op jit(solution)/shard_map/ppermute | solution.py:14
  5.4 12.8 %collective-permute-start.1 = (bf16[768,256]{1,0:T(8,128)(2,1)}, bf16[768,256]{1,0:T(8,128)(2,1)S(1)}, u32[]{:S(2)}, u32[]{:S(2)}) collective-permute-start(bf16[768,256]{1,0:T(8,128)(2,1)} %param.7), channel_id=1, source_target_pairs={{2,0},{4,2},{6,4},{8,6},{10,8},{12,10},{14,12},{16,14},{18,16},{20... | collective-permute-start | bytes 1179656 | tf_op jit(solution)/shard_map/ppermute | solution.py:17
  16.0 2.3 %copy-start.7 = (bf16[768,256]{1,0:T(8,128)(2,1)S(1)}, bf16[768,256]{1,0:T(8,128)(2,1)}, u32[]{:S(2)}) copy-start(bf16[768,256]{1,0:T(8,128)(2,1)} %param.7) | copy-start | bytes 1179652
  18.2 2.2 copy-start.1
  18.3 26.1 %copy-start.8 = (bf16[256,256]{1,0:T(8,128)(2,1)S(1)}, bf16[256,256]{1,0:T(8,128)(2,1)}, u32[]{:S(2)}) copy-start(bf16[256,256]{1,0:T(8,128)(2,1)} %param.11) | copy-start | bytes 393220
  18.3 26.1 %copy-start.9 = (bf16[768,256]{1,0:T(8,128)(2,1)S(1)}, bf16[768,256]{1,0:T(8,128)(2,1)}, u32[]{:S(2)}) copy-start(bf16[768,256]{1,0:T(8,128)(2,1)} %param.13) | copy-start | bytes 1179652
  18.4 26.1 %copy-start.10 = (f32[256]{0:T(256)S(1)}, f32[256]{0:T(256)}, u32[]{:S(2)}) copy-start(f32[256]{0:T(256)} %param.12) | copy-start | bytes 3076
  20.4 24.0 %collective-permute-start.2 = (f32[384,256]{1,0:T(8,128)S(1)}, f32[384,256]{1,0:T(8,128)S(1)}, u32[]{:S(2)}, u32[]{:S(2)}) collective-permute-start(f32[384,256]{1,0:T(8,128)S(1)} %constant_dynamic-slice_fusion), channel_id=1, source_target_pairs={{0,1},{1,0},{2,3},{3,2},{4,5},{5,4},{6,7},{7,6},{8,9},{9,8},{10,11... | collective-permute-start | bytes 1179656 | tf_op jit(solution)/shard_map/ppermute | solution.py:79
  44.5 0.7 copy-start.2
  45.2 0.7 copy-start.6
  45.2 0.9 copy-start.3
  46.1 16.9 %collective-permute-start.3 = (bf16[384,512]{1,0:T(8,128)(2,1)S(1)}, bf16[384,512]{1,0:T(8,128)(2,1)S(1)}, u32[]{:S(2)}, u32[]{:S(2)}) collective-permute-start(bf16[384,512]{1,0:T(8,128)(2,1)S(1)} %pad_maximum_fusion.1), channel_id=1, source_target_pairs={{0,1},{1,0},{2,3},{3,2},{4,5},{5,4},{6,7},{7,6},{8,9},{9,8},{10,11... | collective-permute-start | bytes 1179656 | tf_op jit(solution)/shard_map/ppermute | solution.py:79
  68.3 13.6 %collective-permute-start.10 = (f32[6,128,256]{2,1,0:T(8,128)}, f32[6,128,256]{2,1,0:T(8,128)}, u32[]{:S(2)}, u32[]{:S(2)}) collective-permute-start(f32[6,128,256]{2,1,0:T(8,128)} %slice.32), channel_id=1, source_target_pairs={{2,0},{4,2},{6,4},{8,6},{10,8},{12,10},{14,12},{16,14},{18,16},{20... | collective-permute-start | bytes 2359304 | tf_op jit(solution)/shard_map/ppermute | solution.py:25
  71.9 7.8 %collective-permute-start.11 = (bf16[6,128,256]{2,1,0:T(8,128)(2,1)}, bf16[6,128,256]{2,1,0:T(8,128)(2,1)}, u32[]{:S(2)}, u32[]{:S(2)}) collective-permute-start(bf16[6,128,256]{2,1,0:T(8,128)(2,1)} %slice.42), channel_id=1, source_target_pairs={{0,2},{2,4},{4,6},{6,8},{8,10},{10,12},{12,14},{14,16},{16,18},{18... | collective-permute-start | bytes 1179656 | tf_op jit(solution)/shard_map/ppermute | solution.py:25
  76.0 12.7 %collective-permute-start.4 = (f32[257,128]{1,0:T(8,128)S(1)}, f32[257,128]{1,0:T(8,128)S(1)}, u32[]{:S(2)}, u32[]{:S(2)}) collective-permute-start(f32[257,128]{1,0:T(8,128)S(1)} %fusion.12), channel_id=1, source_target_pairs={{0,2},{2,0},{4,6},{6,4},{8,10},{10,8},{12,14},{14,12},{16,18},{18,... | collective-permute-start | bytes 394760 | tf_op jit(solution)/shard_map/ppermute | solution.py:36
  83.3 79.7 %collective-permute-start.12 = (f32[6,128,256]{2,1,0:T(8,128)S(1)}, f32[6,128,256]{2,1,0:T(8,128)S(1)}, u32[]{:S(2)}, u32[]{:S(2)}) collective-permute-start(f32[6,128,256]{2,1,0:T(8,128)S(1)} %fusion.11), channel_id=1, source_target_pairs={{0,1},{1,0},{2,3},{3,2},{4,5},{5,4},{6,7},{7,6},{8,9},{9,8},{10,11... | collective-permute-start | bytes 2359304 | tf_op jit(solution)/shard_map/ppermute | solution.py:89
  88.7 35.9 %collective-permute-start.5 = (f32[257,128]{1,0:T(8,128)S(1)}, f32[257,128]{1,0:T(8,128)S(1)}, u32[]{:S(2)}, u32[]{:S(2)}) collective-permute-start(f32[257,128]{1,0:T(8,128)S(1)} %fusion.14), channel_id=1, source_target_pairs={{0,4},{2,6},{4,0},{6,2},{8,12},{10,14},{12,8},{14,10},{16,20},{18,... | collective-permute-start | bytes 394760 | tf_op jit(solution)/shard_map/ppermute | solution.py:36
  124.6 10.7 %collective-permute-start.6 = (f32[257,128]{1,0:T(8,128)S(1)}, f32[257,128]{1,0:T(8,128)S(1)}, u32[]{:S(2)}, u32[]{:S(2)}) collective-permute-start(f32[257,128]{1,0:T(8,128)S(1)} %add.93), channel_id=1, source_target_pairs={{0,8},{2,10},{4,12},{6,14},{8,0},{10,2},{12,4},{14,6},{16,24},{18,... | collective-permute-start | bytes 394760 | tf_op jit(solution)/shard_map/ppermute | solution.py:36
  135.3 88.5 %copy-start.4 = (bf16[384,256]{1,0:T(8,128)(2,1)S(1)}, bf16[384,256]{1,0:T(8,128)(2,1)}, u32[]{:S(2)}) copy-start(bf16[384,256]{1,0:T(8,128)(2,1)} %copy-done.3) | copy-start | bytes 589828
  135.3 88.5 %copy-start.5 = (bf16[384,256]{1,0:T(8,128)(2,1)S(1)}, bf16[384,256]{1,0:T(8,128)(2,1)}, u32[]{:S(2)}) copy-start(bf16[384,256]{1,0:T(8,128)(2,1)} %get-tuple-element.11) | copy-start | bytes 589828
  135.4 13.7 %collective-permute-start.7 = (f32[257,128]{1,0:T(8,128)S(1)}, f32[257,128]{1,0:T(8,128)S(1)}, u32[]{:S(2)}, u32[]{:S(2)}) collective-permute-start(f32[257,128]{1,0:T(8,128)S(1)} %add.94), channel_id=1, source_target_pairs={{0,1},{1,0},{2,3},{3,2},{4,5},{5,4},{6,7},{7,6},{8,9},{9,8},{10,11... | collective-permute-start | bytes 394760 | tf_op jit(solution)/shard_map/ppermute | solution.py:66
  149.1 6.6 %collective-permute-start.8 = (f32[257,128]{1,0:T(8,128)S(1)}, f32[257,128]{1,0:T(8,128)S(1)}, u32[]{:S(2)}, u32[]{:S(2)}) collective-permute-start(f32[257,128]{1,0:T(8,128)S(1)} %add.95), channel_id=1, source_target_pairs={{0,192},{2,194},{4,196},{6,198},{8,200},{10,202},{12,204},{14,206}... | collective-permute-start | bytes 394760 | tf_op jit(solution)/shard_map/ppermute | solution.py:36
  155.7 7.3 %collective-permute-start.9 = (f32[257,128]{1,0:T(8,128)S(1)}, f32[257,128]{1,0:T(8,128)S(1)}, u32[]{:S(2)}, u32[]{:S(2)}) collective-permute-start(f32[257,128]{1,0:T(8,128)S(1)} %add.96), channel_id=1, source_target_pairs={{0,384},{2,386},{4,388},{6,390},{8,392},{10,394},{12,396},{14,398}... | collective-permute-start | bytes 394760 | tf_op jit(solution)/shard_map/ppermute | solution.py:36
  163.8 12.9 %collective-permute-start.13 = (f32[257,128]{1,0:T(8,128)S(1)}, f32[257,128]{1,0:T(8,128)S(1)}, u32[]{:S(2)}, u32[]{:S(2)}) collective-permute-start(f32[257,128]{1,0:T(8,128)S(1)} %add.97), channel_id=1, source_target_pairs={{0,16},{2,18},{4,20},{6,22},{8,24},{10,26},{12,28},{14,30},{16,0},... | collective-permute-start | bytes 394760 | tf_op jit(solution)/shard_map/ppermute | solution.py:36
  176.7 10.3 %collective-permute-start.14 = (f32[257,128]{1,0:T(8,128)S(1)}, f32[257,128]{1,0:T(8,128)S(1)}, u32[]{:S(2)}, u32[]{:S(2)}) collective-permute-start(f32[257,128]{1,0:T(8,128)S(1)} %add.102), channel_id=1, source_target_pairs={{0,32},{2,34},{4,36},{6,38},{8,40},{10,42},{12,44},{14,46},{16,48}... | collective-permute-start | bytes 394760 | tf_op jit(solution)/shard_map/ppermute | solution.py:36
  187.1 24.9 %collective-permute-start.16 = (f32[257,128]{1,0:T(8,128)S(1)}, f32[257,128]{1,0:T(8,128)S(1)}, u32[]{:S(2)}, u32[]{:S(2)}) collective-permute-start(f32[257,128]{1,0:T(8,128)S(1)} %add.103), channel_id=1, source_target_pairs={{0,128},{2,130},{4,132},{6,134},{8,136},{10,138},{12,140},{14,142}... | collective-permute-start | bytes 394760 | tf_op jit(solution)/shard_map/ppermute | solution.py:36
  199.4 12.6 %collective-permute-start.15 = (f32[257,128]{1,0:T(8,128)S(1)}, f32[257,128]{1,0:T(8,128)S(1)}, u32[]{:S(2)}, u32[]{:S(2)}) collective-permute-start(f32[257,128]{1,0:T(8,128)S(1)} %add.103), channel_id=1, source_target_pairs={{0,64},{2,66},{4,68},{6,70},{8,72},{10,74},{12,76},{14,78},{16,80}... | collective-permute-start | bytes 394760 | tf_op jit(solution)/shard_map/ppermute | solution.py:36
  212.0 12.7 %collective-permute-start.17 = (f32[257,128]{1,0:T(8,128)S(1)}, f32[257,128]{1,0:T(8,128)S(1)}, u32[]{:S(2)}, u32[]{:S(2)}) collective-permute-start(f32[257,128]{1,0:T(8,128)S(1)} %select_add_fusion), channel_id=1, source_target_pairs={{0,2},{2,0},{4,6},{6,4},{8,10},{10,8},{12,14},{14,12},{16,18},{18,... | collective-permute-start | bytes 394760 | tf_op jit(solution)/shard_map/ppermute | solution.py:36

commit v4 on v2

--- a/solution.py
+++ b/solution.py
@@ -61,14 +61,14 @@
     keep = lax.dynamic_slice_in_dim(x, core * width, width, 1)
     give = lax.dynamic_slice_in_dim(x, (1 - core) * width, width, 1)
     x = keep + moved(give, "rows", count, c_stride, c_size, lambda c: c ^ 1)
-    x = swapped_sum(x, "rows", count, y_stride, y_size, 1)
-    x = swapped_sum(x, "rows", count, y_stride, y_size, 2)
-    x = x + lax.ppermute(x, "rep", [(0, 1), (1, 0)])
     x = swapped_sum(x, "rows", count, x_stride, x_size, 1)
     x = swapped_sum(x, "rows", count, x_stride, x_size, 2)
     x = swapped_sum(x, "rows", count, z_stride, z_size, 1)
     x = swapped_sum(x, "rows", count, z_stride, z_size, 2)
     x = three_way_sum(x, "rows", count, z_stride, z_size)
+    x = swapped_sum(x, "rows", count, y_stride, y_size, 1)
+    x = swapped_sum(x, "rows", count, y_stride, y_size, 2)
+    x = x + lax.ppermute(x, "rep", [(0, 1), (1, 0)])
     other = moved(x, "rows", count, c_stride, c_size, lambda c: c ^ 1)
     return jnp.where(core == 0, jnp.concatenate([x, other], 1), jnp.concatenate([other, x], 1))
 

time: 203 us -> 201 us (level)
  the two profiles are of different devices: /device:TPU:56 before, /device:TPU:1 now
where the time goes in v4:
time: 201 us; the launch traced here: 199 us
  starting transfers between devices  101 us (50%)
  waiting for transfers between devices  75.4 us (38%)
  other arithmetic  11.2 us (6%)
  matrix products  7.69 us (4%)
  local copies, waits for them, and re-layouts  2.66 us (1%)
    ppermute x10, starting transfers between devices, moved(): return lax.ppermute(x, axis, pairs)  56 us
    ppermute x1, waiting for transfers between devices, partner_sum(): return x + lax.ppermute(x, 'rep', [(0, 1), (1, 0)])  30.8 us
    ppermute x2, waiting for transfers between devices, partner_swap(): return lax.ppermute(x, 'rep', [(0, 1), (1, 0)])  24.4 us
    ppermute x10, waiting for transfers between devices, moved(): return lax.ppermute(x, axis, pairs)  20.2 us
    ppermute x1, starting transfers between devices, global_sum(): x = x + lax.ppermute(x, 'rep', [(0, 1), (1, 0)])  13 us
    ppermute x2, starting transfers between devices, from_behind(): return lax.ppermute(x, axis, pairs)  11.8 us
    ppermute x1, starting transfers between devices, extended(): lax.ppermute(lax.slice_in_dim(block, 0, width, axis=dim), axis, backward)  9.15 us
    ppermute x1, starting transfers between devices, extended(): lax.ppermute(lax.slice_in_dim(block, block.shape[dim] - width, None, axis...  4.73 us
  transfers between devices with their start and end apart: 18, of which 8 were waited for; matrix products, arithmetic and copies ran while one was open for 8% of the time, Pallas kernels for 0%

profile of v4, /device:TPU:1, one launch (start us, length us, event | category | flops | bytes accessed | tf_op | source)
XLA Modules:
  0.0 198.9 jit_solution(2755467272334883897)
XLA Ops:
  0.6 0.0 copy-start
  0.6 4.7 %collective-permute-start = (bf16[768,256]{1,0:T(8,128)(2,1)}, bf16[768,256]{1,0:T(8,128)(2,1)S(1)}, u32[]{:S(2)}, u32[]{:S(2)}) collective-permute-start(bf16[768,256]{1,0:T(8,128)(2,1)} %param.7), channel_id=1, source_target_pairs={{0,2},{2,4},{4,6},{6,8},{8,10},{10,12},{12,14},{14,16},{16,18},{18... | collective-permute-start | bytes 1179656 | tf_op jit(solution)/shard_map/ppermute | solution.py:14
  5.4 9.1 %collective-permute-start.1 = (bf16[768,256]{1,0:T(8,128)(2,1)}, bf16[768,256]{1,0:T(8,128)(2,1)S(1)}, u32[]{:S(2)}, u32[]{:S(2)}) collective-permute-start(bf16[768,256]{1,0:T(8,128)(2,1)} %param.7), channel_id=1, source_target_pairs={{2,0},{4,2},{6,4},{8,6},{10,8},{12,10},{14,12},{16,14},{18,16},{20... | collective-permute-start | bytes 1179656 | tf_op jit(solution)/shard_map/ppermute | solution.py:17
  14.5 0.7 broadcast_subtract_fusion
  15.2 0.7 iota_compare_fusion.1
  16.0 0.0 copy-done
  16.0 2.2 %convolution_convert_fusion = bf16[6,18,128,128]{3,1,2,0:T(8,128)(2,1)S(1)} fusion(bf16[6,6,128,128]{3,2,1,0:T(8,128)(2,1)S(1)} %copy-done, s32[6,6]{1,0:T(8,128)S(1)} %broadcast_subtract_fusion, pred[6,6]{1,0:T(8,128)(4,1)S(1)} %iota_compare_fusion.1), kind=kOutput, calls=%fused_computation.4 | convolution fusion | flops 23004432 | bytes 4718772 | tf_op jit(solution)/shard_map/bks,bkij->bsij/dot_general | solution.py:118
  18.2 0.0 copy-start.1
  18.2 0.0 collective-permute-done
  18.2 0.0 collective-permute-done.1
  18.2 0.0 copy-done.3
  18.2 0.1 pad_maximum_fusion
  18.3 0.0 copy-start.4
  18.3 0.0 copy-start.5
  18.4 0.0 copy-start.6
  18.4 1.1 fusion.8
  19.5 0.9 copy-done.1
  20.4 2.1 %collective-permute-start.2 = (f32[384,256]{1,0:T(8,128)S(1)}, f32[384,256]{1,0:T(8,128)S(1)}, u32[]{:S(2)}, u32[]{:S(2)}) collective-permute-start(f32[384,256]{1,0:T(8,128)S(1)} %constant_dynamic-slice_fusion), channel_id=1, source_target_pairs={{0,1},{1,0},{2,3},{3,2},{4,5},{5,4},{6,7},{7,6},{8,9},{9,8},{10,11... | collective-permute-start | bytes 1179656 | tf_op jit(solution)/shard_map/ppermute | solution.py:77
  22.5 21.9 %collective-permute-done.2 = f32[384,256]{1,0:T(8,128)S(1)} collective-permute-done((f32[384,256]{1,0:T(8,128)S(1)}, f32[384,256]{1,0:T(8,128)S(1)}, u32[]{:S(2)}, u32[]{:S(2)}) %collective-permute-start.2) | collective-permute-done | bytes 393248 | tf_op jit(solution)/shard_map/ppermute | solution.py:77
  44.4 0.1 add_convert_fusion.1
  44.5 0.4 convert_reduce_fusion
  44.9 0.3 fusion.21
  45.1 0.2 convolution_convert_fusion.1
  45.4 2.4 %collective-permute-start.7 = (f32[257,128]{1,0:T(8,128)S(1)}, f32[257,128]{1,0:T(8,128)S(1)}, u32[]{:S(2)}, u32[]{:S(2)}) collective-permute-start(f32[257,128]{1,0:T(8,128)S(1)} %fusion.12), channel_id=1, source_target_pairs={{0,2},{2,0},{4,6},{6,4},{8,10},{10,8},{12,14},{14,12},{16,18},{18,... | collective-permute-start | bytes 394760 | tf_op jit(solution)/shard_map/ppermute | solution.py:36
  47.8 2.2 %collective-permute-start.3 = (bf16[384,512]{1,0:T(8,128)(2,1)S(1)}, bf16[384,512]{1,0:T(8,128)(2,1)S(1)}, u32[]{:S(2)}, u32[]{:S(2)}) collective-permute-start(bf16[384,512]{1,0:T(8,128)(2,1)S(1)} %pad_maximum_fusion.1), channel_id=1, source_target_pairs={{0,1},{1,0},{2,3},{3,2},{4,5},{5,4},{6,7},{7,6},{8,9},{9,8},{10,11... | collective-permute-start | bytes 1179656 | tf_op jit(solution)/shard_map/ppermute | solution.py:77
  50.0 0.0 collective-permute-done.7
  50.0 4.3 %collective-permute-start.8 = (f32[257,128]{1,0:T(8,128)S(1)}, f32[257,128]{1,0:T(8,128)S(1)}, u32[]{:S(2)}, u32[]{:S(2)}) collective-permute-start(f32[257,128]{1,0:T(8,128)S(1)} %fusion.14), channel_id=1, source_target_pairs={{0,192},{2,194},{4,196},{6,198},{8,200},{10,202},{12,204},{14,206}... | collective-permute-start | bytes 394760 | tf_op jit(solution)/shard_map/ppermute | solution.py:36
  54.4 3.7 %collective-permute-done.8 = f32[257,128]{1,0:T(8,128)S(1)} collective-permute-done((f32[257,128]{1,0:T(8,128)S(1)}, f32[257,128]{1,0:T(8,128)S(1)}, u32[]{:S(2)}, u32[]{:S(2)}) %collective-permute-start.8) | collective-permute-done | bytes 131616 | tf_op jit(solution)/shard_map/ppermute | solution.py:36
  58.1 4.6 %collective-permute-start.9 = (f32[257,128]{1,0:T(8,128)S(1)}, f32[257,128]{1,0:T(8,128)S(1)}, u32[]{:S(2)}, u32[]{:S(2)}) collective-permute-start(f32[257,128]{1,0:T(8,128)S(1)} %add.97), channel_id=1, source_target_pairs={{0,384},{2,386},{4,388},{6,390},{8,392},{10,394},{12,396},{14,398}... | collective-permute-start | bytes 394760 | tf_op jit(solution)/shard_map/ppermute | solution.py:36
  62.7 2.6 %collective-permute-done.3 = bf16[384,512]{1,0:T(8,128)(2,1)S(1)} collective-permute-done((bf16[384,512]{1,0:T(8,128)(2,1)S(1)}, bf16[384,512]{1,0:T(8,128)(2,1)S(1)}, u32[]{:S(2)}, u32[]{:S(2)}) %collective-permute-start.3) | collective-permute-done | bytes 393248 | tf_op jit(solution)/shard_map/ppermute | solution.py:77
  65.3 0.7 fusion.20
  66.0 0.2 maximum_select_fusion.1
  66.2 0.0 collective-permute-done.9
  66.2 4.3 %collective-permute-start.10 = (f32[257,128]{1,0:T(8,128)S(1)}, f32[257,128]{1,0:T(8,128)S(1)}, u32[]{:S(2)}, u32[]{:S(2)}) collective-permute-start(f32[257,128]{1,0:T(8,128)S(1)} %add.98), channel_id=1, source_target_pairs={{0,16},{2,18},{4,20},{6,22},{8,24},{10,26},{12,28},{14,30},{16,0},... | collective-permute-start | bytes 394760 | tf_op jit(solution)/shard_map/ppermute | solution.py:36
  70.5 3.5 %fusion.4 = f32[18,128,256]{2,1,0:T(8,128)S(1)} fusion(bf16[6,128,256,1]{2,1,0,3:T(8,128)(2,1)S(1)} %bitcast.30, bf16[6,18,128,128]{3,1,2,0:T(8,128)(2,1)} %copy-done.1), kind=kOutput, calls=%fused_computation.5 | convolution fusion | flops 905969664 | bytes 6291456 | tf_op jit(solution)/shard_map/bsij,bif->sjf/dot_general | solution.py:144
  74.1 1.0 slice.32
  75.0 5.0 %collective-permute-start.4 = (f32[6,128,256]{2,1,0:T(8,128)}, f32[6,128,256]{2,1,0:T(8,128)}, u32[]{:S(2)}, u32[]{:S(2)}) collective-permute-start(f32[6,128,256]{2,1,0:T(8,128)} %slice.32), channel_id=1, source_target_pairs={{2,0},{4,2},{6,4},{8,6},{10,8},{12,10},{14,12},{16,14},{18,16},{20... | collective-permute-start | bytes 2359304 | tf_op jit(solution)/shard_map/ppermute | solution.py:25
  80.0 0.0 collective-permute-done.10
  80.1 6.1 %collective-permute-start.11 = (f32[257,128]{1,0:T(8,128)S(1)}, f32[257,128]{1,0:T(8,128)S(1)}, u32[]{:S(2)}, u32[]{:S(2)}) collective-permute-start(f32[257,128]{1,0:T(8,128)S(1)} %add.99), channel_id=1, source_target_pairs={{0,32},{2,34},{4,36},{6,38},{8,40},{10,42},{12,44},{14,46},{16,48}... | collective-permute-start | bytes 394760 | tf_op jit(solution)/shard_map/ppermute | solution.py:36
  86.1 5.1 %collective-permute-done.11 = f32[257,128]{1,0:T(8,128)S(1)} collective-permute-done((f32[257,128]{1,0:T(8,128)S(1)}, f32[257,128]{1,0:T(8,128)S(1)}, u32[]{:S(2)}, u32[]{:S(2)}) %collective-permute-start.11) | collective-permute-done | bytes 131616 | tf_op jit(solution)/shard_map/ppermute | solution.py:36
  91.2 0.7 add.100
  91.9 14.2 %collective-permute-start.13 = (f32[257,128]{1,0:T(8,128)}, f32[257,128]{1,0:T(8,128)}, u32[]{:S(2)}, u32[]{:S(2)}) collective-permute-start(f32[257,128]{1,0:T(8,128)} %add.100), channel_id=1, source_target_pairs={{0,128},{2,130},{4,132},{6,134},{8,136},{10,138},{12,140},{14,142}... | collective-permute-start | bytes 394760 | tf_op jit(solution)/shard_map/ppermute | solution.py:36
  106.0 1.9 collective-permute-start.12
  108.1 6.8 %collective-permute-start.5 = (bf16[6,128,256]{2,1,0:T(8,128)(2,1)S(1)}, bf16[6,128,256]{2,1,0:T(8,128)(2,1)S(1)}, u32[]{:S(2)}, u32[]{:S(2)}) collective-permute-start(bf16[6,128,256]{2,1,0:T(8,128)(2,1)S(1)} %slice.42), channel_id=1, source_target_pairs={{0,2},{2,4},{4,6},{6,8},{8,10},{10,12},{12,14},{14,16},{16,18},{18... | collective-permute-start | bytes 1179656 | tf_op jit(solution)/shard_map/ppermute | solution.py:25
  114.9 0.0 collective-permute-done.13
  114.9 4.8 %collective-permute-done.12 = f32[257,128]{1,0:T(8,128)} collective-permute-done((f32[257,128]{1,0:T(8,128)}, f32[257,128]{1,0:T(8,128)}, u32[]{:S(2)}, u32[]{:S(2)}) %collective-permute-start.12) | collective-permute-done | bytes 131616 | tf_op jit(solution)/shard_map/ppermute | solution.py:36
  119.7 1.1 select_add_fusion
  120.7 11.0 %collective-permute-start.14 = (f32[257,128]{1,0:T(8,128)S(1)}, f32[257,128]{1,0:T(8,128)S(1)}, u32[]{:S(2)}, u32[]{:S(2)}) collective-permute-start(f32[257,128]{1,0:T(8,128)S(1)} %select_add_fusion), channel_id=1, source_target_pairs={{0,4},{2,6},{4,0},{6,2},{8,12},{10,14},{12,8},{14,10},{16,20},{18,... | collective-permute-start | bytes 394760 | tf_op jit(solution)/shard_map/ppermute | solution.py:36
  131.8 2.8 %collective-permute-done.14 = f32[257,128]{1,0:T(8,128)S(1)} collective-permute-done((f32[257,128]{1,0:T(8,128)S(1)}, f32[257,128]{1,0:T(8,128)S(1)}, u32[]{:S(2)}, u32[]{:S(2)}) %collective-permute-start.14) | collective-permute-done | bytes 131616 | tf_op jit(solution)/shard_map/ppermute | solution.py:36
  134.6 2.9 %collective-permute-start.15 = (f32[257,128]{1,0:T(8,128)S(1)}, f32[257,128]{1,0:T(8,128)S(1)}, u32[]{:S(2)}, u32[]{:S(2)}) collective-permute-start(f32[257,128]{1,0:T(8,128)S(1)} %add.103), channel_id=1, source_target_pairs={{0,8},{2,10},{4,12},{6,14},{8,0},{10,2},{12,4},{14,6},{16,24},{18,... | collective-permute-start | bytes 394760 | tf_op jit(solution)/shard_map/ppermute | solution.py:36
  137.5 3.7 %collective-permute-done.15 = f32[257,128]{1,0:T(8,128)S(1)} collective-permute-done((f32[257,128]{1,0:T(8,128)S(1)}, f32[257,128]{1,0:T(8,128)S(1)}, u32[]{:S(2)}, u32[]{:S(2)}) %collective-permute-start.15) | collective-permute-done | bytes 131616 | tf_op jit(solution)/shard_map/ppermute | solution.py:36
  141.3 13.0 %collective-permute-start.16 = (f32[257,128]{1,0:T(8,128)S(1)}, f32[257,128]{1,0:T(8,128)S(1)}, u32[]{:S(2)}, u32[]{:S(2)}) collective-permute-start(f32[257,128]{1,0:T(8,128)S(1)} %add.104), channel_id=1, source_target_pairs={{0,1},{1,0},{2,3},{3,2},{4,5},{5,4},{6,7},{7,6},{8,9},{9,8},{10,11... | collective-permute-start | bytes 394760 | tf_op jit(solution)/shard_map/ppermute | solution.py:71
  154.3 0.0 collective-permute-done.5
  154.3 0.0 collective-permute-done.4
  154.3 2.2 %fusion.11 = f32[6,128,256]{2,1,0:T(8,128)} fusion(f32[6,128,256]{2,1,0:T(8,128)} %collective-permute-done.4, f32[18,128,256]{2,1,0:T(8,128)S(1)} %fusion.4, bf16[6,128,256]{2,1,0:T(8,128)(2,1)S(1)} %collective-permute-done.5), kind=kLoop, calls=%fused_computation.13 | loop fusion | flops 589824 | bytes 2752512 | tf_op jit(solution)/shard_map/add | solution.py:151
  156.5 1.9 collective-permute-start.6
  158.4 0.0 collective-permute-done.16
  158.5 4.3 %collective-permute-start.17 = (f32[257,128]{1,0:T(8,128)S(1)}, f32[257,128]{1,0:T(8,128)S(1)}, u32[]{:S(2)}, u32[]{:S(2)}) collective-permute-start(f32[257,128]{1,0:T(8,128)S(1)} %add.105), channel_id=1, source_target_pairs={{0,2},{2,0},{4,6},{6,4},{8,10},{10,8},{12,14},{14,12},{16,18},{18,... | collective-permute-start | bytes 394760 | tf_op jit(solution)/shard_map/ppermute | solution.py:36
  162.8 2.1 %maximum_select_fusion = bf16[768,256]{1,0:T(8,128)(2,1)} fusion(bf16[384,256]{1,0:T(8,128)(2,1)} %get-tuple-element.7, bf16[384,256]{1,0:T(8,128)(2,1)} %copy-done.2, pred[]{:T(512)S(6)} %eq.17), kind=kLoop, calls=%fused_computation.16 | loop fusion | flops 1769472 | bytes 786433 | tf_op jit(solution)/shard_map/jit(_where)/select_n | solution.py:81
  164.8 0.0 collective-permute-done.17
  164.9 0.6 slice_multiply_fusion.1
  165.5 0.7 slice_multiply_fusion
  166.2 30.8 %collective-permute-done.6 = f32[6,128,256]{2,1,0:T(8,128)S(1)} collective-permute-done((f32[6,128,256]{2,1,0:T(8,128)}, f32[6,128,256]{2,1,0:T(8,128)S(1)}, u32[]{:S(2)}, u32[]{:S(2)}) %collective-permute-start.6) | collective-permute-done | bytes 786464 | tf_op jit(solution)/shard_map/ppermute | solution.py:87
  196.9 2.0 add_convert_fusion
  (18 shorter events, 0.3 us)
Async XLA Ops:
  0.6 15.3 %copy-start = (bf16[6,6,128,128]{3,2,1,0:T(8,128)(2,1)S(1)}, bf16[6,6,128,128]{3,2,1,0:T(8,128)(2,1)}, u32[]{:S(2)}) copy-start(bf16[6,6,128,128]{3,2,1,0:T(8,128)(2,1)} %param.8) | copy-start | bytes 3538948
  0.6 17.6 %collective-permute-start = (bf16[768,256]{1,0:T(8,128)(2,1)}, bf16[768,256]{1,0:T(8,128)(2,1)S(1)}, u32[]{:S(2)}, u32[]{:S(2)}) collective-permute-start(bf16[768,256]{1,0:T(8,128)(2,1)} %param.7), channel_id=1, source_target_pairs={{0,2},{2,4},{4,6},{6,8},{8,10},{10,12},{12,14},{14,16},{16,18},{18... | collective-permute-start | bytes 1179656 | tf_op jit(solution)/shard_map/ppermute | solution.py:14
  5.4 12.8 %collective-permute-start.1 = (bf16[768,256]{1,0:T(8,128)(2,1)}, bf16[768,256]{1,0:T(8,128)(2,1)S(1)}, u32[]{:S(2)}, u32[]{:S(2)}) collective-permute-start(bf16[768,256]{1,0:T(8,128)(2,1)} %param.7), channel_id=1, source_target_pairs={{2,0},{4,2},{6,4},{8,6},{10,8},{12,10},{14,12},{16,14},{18,16},{20... | collective-permute-start | bytes 1179656 | tf_op jit(solution)/shard_map/ppermute | solution.py:17
  16.0 2.3 %copy-start.3 = (bf16[768,256]{1,0:T(8,128)(2,1)S(1)}, bf16[768,256]{1,0:T(8,128)(2,1)}, u32[]{:S(2)}) copy-start(bf16[768,256]{1,0:T(8,128)(2,1)} %param.7) | copy-start | bytes 1179652
  18.2 2.1 %copy-start.1 = (bf16[6,18,128,128]{3,1,2,0:T(8,128)(2,1)}, bf16[6,18,128,128]{3,1,2,0:T(8,128)(2,1)S(1)}, u32[]{:S(2)}) copy-start(bf16[6,18,128,128]{3,1,2,0:T(8,128)(2,1)S(1)} %convolution_convert_fusion) | copy-start | bytes 10616836
  18.3 26.1 %copy-start.4 = (bf16[256,256]{1,0:T(8,128)(2,1)S(1)}, bf16[256,256]{1,0:T(8,128)(2,1)}, u32[]{:S(2)}) copy-start(bf16[256,256]{1,0:T(8,128)(2,1)} %param.11) | copy-start | bytes 393220
  18.3 26.1 %copy-start.5 = (bf16[768,256]{1,0:T(8,128)(2,1)S(1)}, bf16[768,256]{1,0:T(8,128)(2,1)}, u32[]{:S(2)}) copy-start(bf16[768,256]{1,0:T(8,128)(2,1)} %param.13) | copy-start | bytes 1179652
  18.4 26.1 %copy-start.6 = (f32[256]{0:T(256)S(1)}, f32[256]{0:T(256)}, u32[]{:S(2)}) copy-start(f32[256]{0:T(256)} %param.12) | copy-start | bytes 3076
  20.4 24.0 %collective-permute-start.2 = (f32[384,256]{1,0:T(8,128)S(1)}, f32[384,256]{1,0:T(8,128)S(1)}, u32[]{:S(2)}, u32[]{:S(2)}) collective-permute-start(f32[384,256]{1,0:T(8,128)S(1)} %constant_dynamic-slice_fusion), channel_id=1, source_target_pairs={{0,1},{1,0},{2,3},{3,2},{4,5},{5,4},{6,7},{7,6},{8,9},{9,8},{10,11... | collective-permute-start | bytes 1179656 | tf_op jit(solution)/shard_map/ppermute | solution.py:77
  44.9 2.9 %copy-start.2 = (bf16[384,256]{1,0:T(8,128)(2,1)}, bf16[384,256]{1,0:T(8,128)(2,1)S(1)}, u32[]{:S(2)}) copy-start(bf16[384,256]{1,0:T(8,128)(2,1)S(1)} %get-tuple-element.8) | copy-start | bytes 589828
  45.4 4.6 %collective-permute-start.7 = (f32[257,128]{1,0:T(8,128)S(1)}, f32[257,128]{1,0:T(8,128)S(1)}, u32[]{:S(2)}, u32[]{:S(2)}) collective-permute-start(f32[257,128]{1,0:T(8,128)S(1)} %fusion.12), channel_id=1, source_target_pairs={{0,2},{2,0},{4,6},{6,4},{8,10},{10,8},{12,14},{14,12},{16,18},{18,... | collective-permute-start | bytes 394760 | tf_op jit(solution)/shard_map/ppermute | solution.py:36
  47.8 17.5 %collective-permute-start.3 = (bf16[384,512]{1,0:T(8,128)(2,1)S(1)}, bf16[384,512]{1,0:T(8,128)(2,1)S(1)}, u32[]{:S(2)}, u32[]{:S(2)}) collective-permute-start(bf16[384,512]{1,0:T(8,128)(2,1)S(1)} %pad_maximum_fusion.1), channel_id=1, source_target_pairs={{0,1},{1,0},{2,3},{3,2},{4,5},{5,4},{6,7},{7,6},{8,9},{9,8},{10,11... | collective-permute-start | bytes 1179656 | tf_op jit(solution)/shard_map/ppermute | solution.py:77
  50.0 8.1 %collective-permute-start.8 = (f32[257,128]{1,0:T(8,128)S(1)}, f32[257,128]{1,0:T(8,128)S(1)}, u32[]{:S(2)}, u32[]{:S(2)}) collective-permute-start(f32[257,128]{1,0:T(8,128)S(1)} %fusion.14), channel_id=1, source_target_pairs={{0,192},{2,194},{4,196},{6,198},{8,200},{10,202},{12,204},{14,206}... | collective-permute-start | bytes 394760 | tf_op jit(solution)/shard_map/ppermute | solution.py:36
  58.1 8.0 %collective-permute-start.9 = (f32[257,128]{1,0:T(8,128)S(1)}, f32[257,128]{1,0:T(8,128)S(1)}, u32[]{:S(2)}, u32[]{:S(2)}) collective-permute-start(f32[257,128]{1,0:T(8,128)S(1)} %add.97), channel_id=1, source_target_pairs={{0,384},{2,386},{4,388},{6,390},{8,392},{10,394},{12,396},{14,398}... | collective-permute-start | bytes 394760 | tf_op jit(solution)/shard_map/ppermute | solution.py:36
  66.2 13.8 %collective-permute-start.10 = (f32[257,128]{1,0:T(8,128)S(1)}, f32[257,128]{1,0:T(8,128)S(1)}, u32[]{:S(2)}, u32[]{:S(2)}) collective-permute-start(f32[257,128]{1,0:T(8,128)S(1)} %add.98), channel_id=1, source_target_pairs={{0,16},{2,18},{4,20},{6,22},{8,24},{10,26},{12,28},{14,30},{16,0},... | collective-permute-start | bytes 394760 | tf_op jit(solution)/shard_map/ppermute | solution.py:36
  75.0 79.3 %collective-permute-start.4 = (f32[6,128,256]{2,1,0:T(8,128)}, f32[6,128,256]{2,1,0:T(8,128)}, u32[]{:S(2)}, u32[]{:S(2)}) collective-permute-start(f32[6,128,256]{2,1,0:T(8,128)} %slice.32), channel_id=1, source_target_pairs={{2,0},{4,2},{6,4},{8,6},{10,8},{12,10},{14,12},{16,14},{18,16},{20... | collective-permute-start | bytes 2359304 | tf_op jit(solution)/shard_map/ppermute | solution.py:25
  80.1 11.1 %collective-permute-start.11 = (f32[257,128]{1,0:T(8,128)S(1)}, f32[257,128]{1,0:T(8,128)S(1)}, u32[]{:S(2)}, u32[]{:S(2)}) collective-permute-start(f32[257,128]{1,0:T(8,128)S(1)} %add.99), channel_id=1, source_target_pairs={{0,32},{2,34},{4,36},{6,38},{8,40},{10,42},{12,44},{14,46},{16,48}... | collective-permute-start | bytes 394760 | tf_op jit(solution)/shard_map/ppermute | solution.py:36
  91.9 23.0 %collective-permute-start.13 = (f32[257,128]{1,0:T(8,128)}, f32[257,128]{1,0:T(8,128)}, u32[]{:S(2)}, u32[]{:S(2)}) collective-permute-start(f32[257,128]{1,0:T(8,128)} %add.100), channel_id=1, source_target_pairs={{0,128},{2,130},{4,132},{6,134},{8,136},{10,138},{12,140},{14,142}... | collective-permute-start | bytes 394760 | tf_op jit(solution)/shard_map/ppermute | solution.py:36
  106.0 13.6 %collective-permute-start.12 = (f32[257,128]{1,0:T(8,128)}, f32[257,128]{1,0:T(8,128)}, u32[]{:S(2)}, u32[]{:S(2)}) collective-permute-start(f32[257,128]{1,0:T(8,128)} %add.100), channel_id=1, source_target_pairs={{0,64},{2,66},{4,68},{6,70},{8,72},{10,74},{12,76},{14,78},{16,80}... | collective-permute-start | bytes 394760 | tf_op jit(solution)/shard_map/ppermute | solution.py:36
  108.1 46.2 %collective-permute-start.5 = (bf16[6,128,256]{2,1,0:T(8,128)(2,1)S(1)}, bf16[6,128,256]{2,1,0:T(8,128)(2,1)S(1)}, u32[]{:S(2)}, u32[]{:S(2)}) collective-permute-start(bf16[6,128,256]{2,1,0:T(8,128)(2,1)S(1)} %slice.42), channel_id=1, source_target_pairs={{0,2},{2,4},{4,6},{6,8},{8,10},{10,12},{12,14},{14,16},{16,18},{18... | collective-permute-start | bytes 1179656 | tf_op jit(solution)/shard_map/ppermute | solution.py:25
  120.7 13.9 %collective-permute-start.14 = (f32[257,128]{1,0:T(8,128)S(1)}, f32[257,128]{1,0:T(8,128)S(1)}, u32[]{:S(2)}, u32[]{:S(2)}) collective-permute-start(f32[257,128]{1,0:T(8,128)S(1)} %select_add_fusion), channel_id=1, source_target_pairs={{0,4},{2,6},{4,0},{6,2},{8,12},{10,14},{12,8},{14,10},{16,20},{18,... | collective-permute-start | bytes 394760 | tf_op jit(solution)/shard_map/ppermute | solution.py:36
  134.6 6.7 %collective-permute-start.15 = (f32[257,128]{1,0:T(8,128)S(1)}, f32[257,128]{1,0:T(8,128)S(1)}, u32[]{:S(2)}, u32[]{:S(2)}) collective-permute-start(f32[257,128]{1,0:T(8,128)S(1)} %add.103), channel_id=1, source_target_pairs={{0,8},{2,10},{4,12},{6,14},{8,0},{10,2},{12,4},{14,6},{16,24},{18,... | collective-permute-start | bytes 394760 | tf_op jit(solution)/shard_map/ppermute | solution.py:36
  141.3 17.1 %collective-permute-start.16 = (f32[257,128]{1,0:T(8,128)S(1)}, f32[257,128]{1,0:T(8,128)S(1)}, u32[]{:S(2)}, u32[]{:S(2)}) collective-permute-start(f32[257,128]{1,0:T(8,128)S(1)} %add.104), channel_id=1, source_target_pairs={{0,1},{1,0},{2,3},{3,2},{4,5},{5,4},{6,7},{7,6},{8,9},{9,8},{10,11... | collective-permute-start | bytes 394760 | tf_op jit(solution)/shard_map/ppermute | solution.py:71
  156.5 40.4 %collective-permute-start.6 = (f32[6,128,256]{2,1,0:T(8,128)}, f32[6,128,256]{2,1,0:T(8,128)S(1)}, u32[]{:S(2)}, u32[]{:S(2)}) collective-permute-start(f32[6,128,256]{2,1,0:T(8,128)} %fusion.11), channel_id=1, source_target_pairs={{0,1},{1,0},{2,3},{3,2},{4,5},{5,4},{6,7},{7,6},{8,9},{9,8},{10,11... | collective-permute-start | bytes 2359304 | tf_op jit(solution)/shard_map/ppermute | solution.py:87
  158.5 6.4 %collective-permute-start.17 = (f32[257,128]{1,0:T(8,128)S(1)}, f32[257,128]{1,0:T(8,128)S(1)}, u32[]{:S(2)}, u32[]{:S(2)}) collective-permute-start(f32[257,128]{1,0:T(8,128)S(1)} %add.105), channel_id=1, source_target_pairs={{0,2},{2,0},{4,6},{6,4},{8,10},{10,8},{12,14},{14,12},{16,18},{18,... | collective-permute-start | bytes 394760 | tf_op jit(solution)/shard_map/ppermute | solution.py:36

commit v5 on v4

--- a/solution.py
+++ b/solution.py
@@ -51,26 +51,45 @@
     return (first + second) + third_part
 
 
-def global_sum(x):
+def chain_start(x, early):
     count = lax.axis_size("rows")
     if count not in ROW_AXES or lax.axis_size("rep") != 2:
-        return lax.psum(x, ("rows", "rep"))
-    (x_stride, x_size), (z_stride, z_size), (y_stride, y_size), (c_stride, c_size) = ROW_AXES[count]
+        return x, early
+    c_stride, c_size = ROW_AXES[count][3]
     core = (lax.axis_index("rows") // c_stride) % c_size
     width = x.shape[1] // 2
     keep = lax.dynamic_slice_in_dim(x, core * width, width, 1)
     give = lax.dynamic_slice_in_dim(x, (1 - core) * width, width, 1)
     x = keep + moved(give, "rows", count, c_stride, c_size, lambda c: c ^ 1)
+    return lax.optimization_barrier((x, early))
+
+
+def chain_next(x, mid):
+    count = lax.axis_size("rows")
+    if count not in ROW_AXES or lax.axis_size("rep") != 2:
+        return x, mid
+    x_stride, x_size = ROW_AXES[count][0]
     x = swapped_sum(x, "rows", count, x_stride, x_size, 1)
+    return lax.optimization_barrier((x, mid))
+
+
+def chain_rest(x, tie):
+    count = lax.axis_size("rows")
+    if count not in ROW_AXES or lax.axis_size("rep") != 2:
+        return lax.psum(x, ("rows", "rep")), tie
+    (x_stride, x_size), (z_stride, z_size), (y_stride, y_size), (c_stride, c_size) = ROW_AXES[count]
+    core = (lax.axis_index("rows") // c_stride) % c_size
     x = swapped_sum(x, "rows", count, x_stride, x_size, 2)
     x = swapped_sum(x, "rows", count, z_stride, z_size, 1)
     x = swapped_sum(x, "rows", count, z_stride, z_size, 2)
     x = three_way_sum(x, "rows", count, z_stride, z_size)
+    x, tie = lax.optimization_barrier((x, tie))
     x = swapped_sum(x, "rows", count, y_stride, y_size, 1)
     x = swapped_sum(x, "rows", count, y_stride, y_size, 2)
     x = x + lax.ppermute(x, "rep", [(0, 1), (1, 0)])
     other = moved(x, "rows", count, c_stride, c_size, lambda c: c ^ 1)
-    return jnp.where(core == 0, jnp.concatenate([x, other], 1), jnp.concatenate([other, x], 1))
+    joined = jnp.where(core == 0, jnp.concatenate([x, other], 1), jnp.concatenate([other, x], 1))
+    return joined, tie
 
 
 def partner_swap(x):
@@ -127,19 +146,17 @@
     agg_half = (own_part + partner_swap(their_part)).astype(jnp.bfloat16)
     grad_in = lax.dynamic_slice_in_dim(cotangent, partner * half_rows, half_rows, 0)
     act_half, grad_half, agg_grad_half = dense_part(agg_half, grad_in, weight, bias)
-    sent = partner_swap(jnp.concatenate([act_half, agg_grad_half], 1))
-    activations = in_order(act_half, sent[:, :feat_width], partner)
-    agg_grad = in_order(agg_grad_half, sent[:, feat_width:], partner)
     weight_part = lax.dot_general(
         agg_half, grad_half, (((0,), (0,)), ((), ())), preferred_element_type=jnp.float32
     )
     bias_part = jnp.sum(grad_half.astype(jnp.float32), axis=0)
-    grad_terms = global_sum(jnp.concatenate([weight_part, bias_part[None, :]], axis=0))
-    weight_total = grad_terms[:feat_width]
-    bias_total = grad_terms[feat_width]
-    scale = 1.0 / math.sqrt(node_count)
-    weight_grad = weight_total * scale
-    bias_grad = bias_total * scale
+    chain, payload = chain_start(
+        jnp.concatenate([weight_part, bias_part[None, :]], axis=0),
+        jnp.concatenate([act_half, agg_grad_half], 1),
+    )
+    chain, sent = chain_next(chain, partner_swap(payload))
+    activations = in_order(payload[:, :feat_width], sent[:, :feat_width], partner)
+    agg_grad = in_order(payload[:, feat_width:], sent[:, feat_width:], partner)
     grad_blocks = agg_grad.reshape(num_blocks, tile_size, feat_width)
     spread = jnp.einsum(
         "bsij,bif->sjf", band_tiles, grad_blocks, preferred_element_type=jnp.float32
@@ -150,6 +167,12 @@
     )
     own_terms = spread[num_blocks : 2 * num_blocks] + from_above + from_below
     own_total = partner_sum(own_terms)
+    grad_terms, own_total = chain_rest(chain, own_total)
+    weight_total = grad_terms[:feat_width]
+    bias_total = grad_terms[feat_width]
+    scale = 1.0 / math.sqrt(node_count)
+    weight_grad = weight_total * scale
+    bias_grad = bias_total * scale
     feature_grad = own_total.reshape(rows_here, feat_width).astype(jnp.bfloat16)
     return (activations, feature_grad, weight_grad, bias_grad)
 

time: 201 us -> 203 us (level)
  waiting for transfers between devices: 75.4 us -> 106 us
  starting transfers between devices: 101 us -> 79.8 us
  other arithmetic: 11.2 us -> 5.17 us
  local copies, waits for them, and re-layouts: 2.66 us -> 0.22 us
    ppermute x1, waiting for transfers between devices: 30.8 us -> 0.01 us  [partner_sum(): return x + lax.ppermute(x, 'rep', [(0, 1), (1, 0)])]
    ppermute x2, waiting for transfers between devices: 0.01 us -> 28.7 us  [from_behind(): return lax.ppermute(x, axis, pairs)]
    ppermute x10, waiting for transfers between devices: 20.2 us -> 37.2 us  [moved(): return lax.ppermute(x, axis, pairs)]
    ppermute x1, starting transfers between devices: 13 us -> 2.64 us  [chain_rest(): x = x + lax.ppermute(x, 'rep', [(0, 1), (1, 0)])]
    ppermute x1, waiting for transfers between devices: 0.01 us -> 7.11 us  [chain_rest(): x = x + lax.ppermute(x, 'rep', [(0, 1), (1, 0)])]
    ppermute x2, waiting for transfers between devices: 24.4 us -> 31.2 us  [partner_swap(): return lax.ppermute(x, 'rep', [(0, 1), (1, 0)])]
    ppermute x2, starting transfers between devices: 11.8 us -> 5.56 us  [from_behind(): return lax.ppermute(x, axis, pairs)]
    ppermute x10, starting transfers between devices: 56 us -> 49.9 us  [moved(): return lax.ppermute(x, axis, pairs)]
  transfers between devices with their start and end apart: 18 -> 18, of which waited for: 8 -> 16; matrix products, arithmetic and copies ran while one was open for 8% -> 3% of each run, Pallas kernels for 0% -> 0%
where the time goes in v5:
time: 203 us; the launch traced here: 200 us
  waiting for transfers between devices  106 us (52%)
  starting transfers between devices  79.8 us (39%)
  matrix products  7.71 us (4%)
  other arithmetic  5.17 us (3%)
    ppermute x10, starting transfers between devices, moved(): return lax.ppermute(x, axis, pairs)  49.9 us
    ppermute x10, waiting for transfers between devices, moved(): return lax.ppermute(x, axis, pairs)  37.2 us
    ppermute x2, waiting for transfers between devices, partner_swap(): return lax.ppermute(x, 'rep', [(0, 1), (1, 0)])  31.2 us
    ppermute x2, waiting for transfers between devices, from_behind(): return lax.ppermute(x, axis, pairs)  28.7 us
    ppermute x1, starting transfers between devices, extended(): lax.ppermute(lax.slice_in_dim(block, 0, width, axis=dim), axis, backward)  12.6 us
    ppermute x1, waiting for transfers between devices, chain_rest(): x = x + lax.ppermute(x, 'rep', [(0, 1), (1, 0)])  7.11 us
    ppermute x2, starting transfers between devices, from_behind(): return lax.ppermute(x, axis, pairs)  5.56 us
    ppermute x2, starting transfers between devices, partner_swap(): return lax.ppermute(x, 'rep', [(0, 1), (1, 0)])  4.69 us
  transfers between devices with their start and end apart: 18, of which 16 were waited for; matrix products, arithmetic and copies ran while one was open for 3% of the time, Pallas kernels for 0%

profile of v5, /device:TPU:1, one launch (start us, length us, event | category | flops | bytes accessed | tf_op | source)
XLA Modules:
  0.0 199.6 jit_solution(17373841916428754632)
XLA Ops:
  0.6 0.0 copy-start
  0.6 12.6 %collective-permute-start.1 = (bf16[768,256]{1,0:T(8,128)(2,1)}, bf16[768,256]{1,0:T(8,128)(2,1)S(1)}, u32[]{:S(2)}, u32[]{:S(2)}) collective-permute-start(bf16[768,256]{1,0:T(8,128)(2,1)} %param.7), channel_id=1, source_target_pairs={{2,0},{4,2},{6,4},{8,6},{10,8},{12,10},{14,12},{16,14},{18,16},{20... | collective-permute-start | bytes 1179656 | tf_op jit(solution)/shard_map/ppermute | solution.py:17
  13.2 1.9 collective-permute-start
  15.2 0.7 broadcast_subtract_fusion
  15.8 0.7 iota_compare_fusion.1
  16.6 0.0 copy-done
  16.6 2.2 %convolution_convert_fusion = bf16[6,18,128,128]{3,1,2,0:T(8,128)(2,1)S(1)} fusion(bf16[6,6,128,128]{3,2,1,0:T(8,128)(2,1)S(1)} %copy-done, s32[6,6]{1,0:T(8,128)S(1)} %broadcast_subtract_fusion, pred[6,6]{1,0:T(8,128)(4,1)S(1)} %iota_compare_fusion.1), kind=kOutput, calls=%fused_computation.4 | convolution fusion | flops 23004432 | bytes 4718772 | tf_op jit(solution)/shard_map/bks,bkij->bsij/dot_general | solution.py:137
  18.8 0.0 copy-start.1
  18.8 0.0 collective-permute-done.1
  18.8 1.3 collective-permute-done
  20.2 0.0 copy-done.2
  20.2 0.1 pad_maximum_fusion
  20.2 0.0 copy-start.3
  20.3 0.0 copy-start.4
  20.3 0.0 copy-start.5
  20.3 1.1 fusion.8
  21.4 0.0 copy-done.1
  21.4 2.7 %collective-permute-start.2 = (f32[384,256]{1,0:T(8,128)S(1)}, f32[384,256]{1,0:T(8,128)S(1)}, u32[]{:S(2)}, u32[]{:S(2)}) collective-permute-start(f32[384,256]{1,0:T(8,128)S(1)} %constant_dynamic-slice_fusion), channel_id=1, source_target_pairs={{0,1},{1,0},{2,3},{3,2},{4,5},{5,4},{6,7},{7,6},{8,9},{9,8},{10,11... | collective-permute-start | bytes 1179656 | tf_op jit(solution)/shard_map/ppermute | solution.py:96
  24.2 22.2 %collective-permute-done.2 = f32[384,256]{1,0:T(8,128)S(1)} collective-permute-done((f32[384,256]{1,0:T(8,128)S(1)}, f32[384,256]{1,0:T(8,128)S(1)}, u32[]{:S(2)}, u32[]{:S(2)}) %collective-permute-start.2) | collective-permute-done | bytes 393248 | tf_op jit(solution)/shard_map/ppermute | solution.py:96
  46.4 0.1 add_convert_fusion
  46.5 0.0 copy-done.3
  46.5 0.0 copy-done.4
  46.5 0.0 copy-done.5
  46.5 0.4 convert_reduce_fusion
  46.9 0.3 fusion.22
  47.2 2.7 %collective-permute-start.3 = (f32[257,128]{1,0:T(8,128)S(1)}, f32[257,128]{1,0:T(8,128)S(1)}, u32[]{:S(2)}, u32[]{:S(2)}) collective-permute-start(f32[257,128]{1,0:T(8,128)S(1)} %fusion.12), channel_id=1, source_target_pairs={{0,2},{2,0},{4,6},{6,4},{8,10},{10,8},{12,14},{14,12},{16,18},{18,... | collective-permute-start | bytes 394760 | tf_op jit(solution)/shard_map/ppermute | solution.py:36
  49.9 0.2 convolution_convert_fusion.1
  50.2 0.7 collective-permute-done.3
  50.9 2.0 collective-permute-start.5
  52.9 7.6 %collective-permute-start.4 = (f32[257,128]{1,0:T(8,128)S(1)}, f32[257,128]{1,0:T(8,128)S(1)}, u32[]{:S(2)}, u32[]{:S(2)}) collective-permute-start(f32[257,128]{1,0:T(8,128)S(1)} %fusion.14), channel_id=1, source_target_pairs={{0,192},{2,194},{4,196},{6,198},{8,200},{10,202},{12,204},{14,206}... | collective-permute-start | bytes 394760 | tf_op jit(solution)/shard_map/ppermute | solution.py:36
  60.5 3.3 %collective-permute-done.4 = f32[257,128]{1,0:T(8,128)S(1)} collective-permute-done((f32[257,128]{1,0:T(8,128)S(1)}, f32[257,128]{1,0:T(8,128)S(1)}, u32[]{:S(2)}, u32[]{:S(2)}) %collective-permute-start.4) | collective-permute-done | bytes 131616 | tf_op jit(solution)/shard_map/ppermute | solution.py:36
  63.8 9.0 %collective-permute-done.5 = bf16[384,512]{1,0:T(8,128)(2,1)S(1)} collective-permute-done((bf16[384,512]{1,0:T(8,128)(2,1)S(1)}, bf16[384,512]{1,0:T(8,128)(2,1)S(1)}, u32[]{:S(2)}, u32[]{:S(2)}) %collective-permute-start.5) | collective-permute-done | bytes 393248 | tf_op jit(solution)/shard_map/ppermute | solution.py:96
  72.8 0.2 maximum_select_fusion.1
  73.0 3.5 %fusion.4 = f32[18,128,256]{2,1,0:T(8,128)S(1)} fusion(bf16[6,128,256,1]{2,1,0,3:T(8,128)(2,1)S(1)} %bitcast.30, bf16[6,18,128,128]{3,1,2,0:T(8,128)(2,1)} %copy-done.1), kind=kOutput, calls=%fused_computation.5 | convolution fusion | flops 905969664 | bytes 6291456 | tf_op jit(solution)/shard_map/bsij,bif->sjf/dot_general | solution.py:161
  76.5 0.1 slice.38
  76.6 2.4 %collective-permute-start.11 = (f32[6,128,256]{2,1,0:T(8,128)S(1)}, f32[6,128,256]{2,1,0:T(8,128)S(1)}, u32[]{:S(2)}, u32[]{:S(2)}) collective-permute-start(f32[6,128,256]{2,1,0:T(8,128)S(1)} %slice.38), channel_id=1, source_target_pairs={{2,0},{4,2},{6,4},{8,6},{10,8},{12,10},{14,12},{16,14},{18,16},{20... | collective-permute-start | bytes 2359304 | tf_op jit(solution)/shard_map/ppermute | solution.py:25
  79.1 3.1 %collective-permute-start.12 = (bf16[6,128,256]{2,1,0:T(8,128)(2,1)S(1)}, bf16[6,128,256]{2,1,0:T(8,128)(2,1)S(1)}, u32[]{:S(2)}, u32[]{:S(2)}) collective-permute-start(bf16[6,128,256]{2,1,0:T(8,128)(2,1)S(1)} %slice.48), channel_id=1, source_target_pairs={{0,2},{2,4},{4,6},{6,8},{8,10},{10,12},{12,14},{14,16},{16,18},{18... | collective-permute-start | bytes 1179656 | tf_op jit(solution)/shard_map/ppermute | solution.py:25
  82.2 5.4 %collective-permute-done.12 = bf16[6,128,256]{2,1,0:T(8,128)(2,1)S(1)} collective-permute-done((bf16[6,128,256]{2,1,0:T(8,128)(2,1)S(1)}, bf16[6,128,256]{2,1,0:T(8,128)(2,1)S(1)}, u32[]{:S(2)}, u32[]{:S(2)}) %collective-permute-start.12) | collective-permute-done | bytes 393248 | tf_op jit(solution)/shard_map/ppermute | solution.py:25
  87.6 23.3 %collective-permute-done.11 = f32[6,128,256]{2,1,0:T(8,128)S(1)} collective-permute-done((f32[6,128,256]{2,1,0:T(8,128)S(1)}, f32[6,128,256]{2,1,0:T(8,128)S(1)}, u32[]{:S(2)}, u32[]{:S(2)}) %collective-permute-start.11) | collective-permute-done | bytes 786464 | tf_op jit(solution)/shard_map/ppermute | solution.py:25
  111.0 0.2 fusion.11
  111.1 2.5 %collective-permute-start.13 = (f32[6,128,256]{2,1,0:T(8,128)S(1)}, f32[6,128,256]{2,1,0:T(8,128)S(1)}, u32[]{:S(2)}, u32[]{:S(2)}) collective-permute-start(f32[6,128,256]{2,1,0:T(8,128)S(1)} %fusion.11), channel_id=1, source_target_pairs={{0,1},{1,0},{2,3},{3,2},{4,5},{5,4},{6,7},{7,6},{8,9},{9,8},{10,11... | collective-permute-start | bytes 2359304 | tf_op jit(solution)/shard_map/ppermute | solution.py:106
  113.6 4.7 %collective-permute-start.6 = (f32[257,128]{1,0:T(8,128)S(1)}, f32[257,128]{1,0:T(8,128)S(1)}, u32[]{:S(2)}, u32[]{:S(2)}) collective-permute-start(f32[257,128]{1,0:T(8,128)S(1)} %add.94), channel_id=1, source_target_pairs={{0,384},{2,386},{4,388},{6,390},{8,392},{10,394},{12,396},{14,398}... | collective-permute-start | bytes 394760 | tf_op jit(solution)/shard_map/ppermute | solution.py:36
  118.4 2.5 %collective-permute-done.6 = f32[257,128]{1,0:T(8,128)S(1)} collective-permute-done((f32[257,128]{1,0:T(8,128)S(1)}, f32[257,128]{1,0:T(8,128)S(1)}, u32[]{:S(2)}, u32[]{:S(2)}) %collective-permute-start.6) | collective-permute-done | bytes 131616 | tf_op jit(solution)/shard_map/ppermute | solution.py:36
  120.9 1.9 collective-permute-start.7
  122.9 3.8 %collective-permute-done.7 = f32[257,128]{1,0:T(8,128)S(1)} collective-permute-done((f32[257,128]{1,0:T(8,128)S(1)}, f32[257,128]{1,0:T(8,128)S(1)}, u32[]{:S(2)}, u32[]{:S(2)}) %collective-permute-start.7) | collective-permute-done | bytes 131616 | tf_op jit(solution)/shard_map/ppermute | solution.py:36
  126.7 1.9 collective-permute-start.8
  128.6 6.9 %collective-permute-done.8 = f32[257,128]{1,0:T(8,128)S(1)} collective-permute-done((f32[257,128]{1,0:T(8,128)S(1)}, f32[257,128]{1,0:T(8,128)S(1)}, u32[]{:S(2)}, u32[]{:S(2)}) %collective-permute-start.8) | collective-permute-done | bytes 131616 | tf_op jit(solution)/shard_map/ppermute | solution.py:36
  135.5 1.9 collective-permute-start.9
  137.5 23.4 %collective-permute-start.10 = (f32[257,128]{1,0:T(8,128)S(1)}, f32[257,128]{1,0:T(8,128)S(1)}, u32[]{:S(2)}, u32[]{:S(2)}) collective-permute-start(f32[257,128]{1,0:T(8,128)S(1)} %add.98), channel_id=1, source_target_pairs={{0,128},{2,130},{4,132},{6,134},{8,136},{10,138},{12,140},{14,142}... | collective-permute-start | bytes 394760 | tf_op jit(solution)/shard_map/ppermute | solution.py:36
  160.9 0.5 collective-permute-done.9
  161.4 8.0 %collective-permute-done.10 = f32[257,128]{1,0:T(8,128)S(1)} collective-permute-done((f32[257,128]{1,0:T(8,128)S(1)}, f32[257,128]{1,0:T(8,128)S(1)}, u32[]{:S(2)}, u32[]{:S(2)}) %collective-permute-start.10) | collective-permute-done | bytes 131616 | tf_op jit(solution)/shard_map/ppermute | solution.py:36
  169.5 0.0 collective-permute-done.13
  169.5 0.8 add.103
  170.3 1.9 collective-permute-start.14
  172.2 3.8 %collective-permute-done.14 = f32[257,128]{1,0:T(8,128)S(1)} collective-permute-done((f32[257,128]{1,0:T(8,128)S(1)}, f32[257,128]{1,0:T(8,128)S(1)}, u32[]{:S(2)}, u32[]{:S(2)}) %collective-permute-start.14) | collective-permute-done | bytes 131616 | tf_op jit(solution)/shard_map/ppermute | solution.py:36
  176.1 1.9 collective-permute-start.15
  178.0 7.2 %collective-permute-done.15 = f32[257,128]{1,0:T(8,128)S(1)} collective-permute-done((f32[257,128]{1,0:T(8,128)S(1)}, f32[257,128]{1,0:T(8,128)S(1)}, u32[]{:S(2)}, u32[]{:S(2)}) %collective-permute-start.15) | collective-permute-done | bytes 131616 | tf_op jit(solution)/shard_map/ppermute | solution.py:36
  185.2 2.6 %collective-permute-start.16 = (f32[257,128]{1,0:T(8,128)S(1)}, f32[257,128]{1,0:T(8,128)S(1)}, u32[]{:S(2)}, u32[]{:S(2)}) collective-permute-start(f32[257,128]{1,0:T(8,128)S(1)} %add.105), channel_id=1, source_target_pairs={{0,1},{1,0},{2,3},{3,2},{4,5},{5,4},{6,7},{7,6},{8,9},{9,8},{10,11... | collective-permute-start | bytes 394760 | tf_op jit(solution)/shard_map/ppermute | solution.py:89
  187.9 7.1 %collective-permute-done.16 = f32[257,128]{1,0:T(8,128)S(1)} collective-permute-done((f32[257,128]{1,0:T(8,128)S(1)}, f32[257,128]{1,0:T(8,128)S(1)}, u32[]{:S(2)}, u32[]{:S(2)}) %collective-permute-start.16) | collective-permute-done | bytes 131616 | tf_op jit(solution)/shard_map/ppermute | solution.py:89
  195.0 1.9 collective-permute-start.17
  196.9 0.9 maximum_select_fusion
  197.8 0.4 collective-permute-done.17
  198.3 0.7 slice_multiply_fusion
  199.0 0.6 slice_multiply_fusion.1
  (17 shorter events, 0.4 us)
Async XLA Ops:
  0.6 15.9 %copy-start = (bf16[6,6,128,128]{3,2,1,0:T(8,128)(2,1)S(1)}, bf16[6,6,128,128]{3,2,1,0:T(8,128)(2,1)}, u32[]{:S(2)}) copy-start(bf16[6,6,128,128]{3,2,1,0:T(8,128)(2,1)} %param.8) | copy-start | bytes 3538948
  0.6 18.2 %collective-permute-start.1 = (bf16[768,256]{1,0:T(8,128)(2,1)}, bf16[768,256]{1,0:T(8,128)(2,1)S(1)}, u32[]{:S(2)}, u32[]{:S(2)}) collective-permute-start(bf16[768,256]{1,0:T(8,128)(2,1)} %param.7), channel_id=1, source_target_pairs={{2,0},{4,2},{6,4},{8,6},{10,8},{12,10},{14,12},{16,14},{18,16},{20... | collective-permute-start | bytes 1179656 | tf_op jit(solution)/shard_map/ppermute | solution.py:17
  13.2 6.9 %collective-permute-start = (bf16[768,256]{1,0:T(8,128)(2,1)}, bf16[768,256]{1,0:T(8,128)(2,1)S(1)}, u32[]{:S(2)}, u32[]{:S(2)}) collective-permute-start(bf16[768,256]{1,0:T(8,128)(2,1)} %param.7), channel_id=1, source_target_pairs={{0,2},{2,4},{4,6},{6,8},{8,10},{10,12},{12,14},{14,16},{16,18},{18... | collective-permute-start | bytes 1179656 | tf_op jit(solution)/shard_map/ppermute | solution.py:14
  16.6 3.6 %copy-start.2 = (bf16[768,256]{1,0:T(8,128)(2,1)S(1)}, bf16[768,256]{1,0:T(8,128)(2,1)}, u32[]{:S(2)}) copy-start(bf16[768,256]{1,0:T(8,128)(2,1)} %param.7) | copy-start | bytes 1179652
  18.8 2.6 %copy-start.1 = (bf16[6,18,128,128]{3,1,2,0:T(8,128)(2,1)}, bf16[6,18,128,128]{3,1,2,0:T(8,128)(2,1)S(1)}, u32[]{:S(2)}) copy-start(bf16[6,18,128,128]{3,1,2,0:T(8,128)(2,1)S(1)} %convolution_convert_fusion) | copy-start | bytes 10616836
  20.2 26.2 %copy-start.3 = (bf16[256,256]{1,0:T(8,128)(2,1)S(1)}, bf16[256,256]{1,0:T(8,128)(2,1)}, u32[]{:S(2)}) copy-start(bf16[256,256]{1,0:T(8,128)(2,1)} %param.11) | copy-start | bytes 393220
  20.3 26.2 %copy-start.4 = (bf16[768,256]{1,0:T(8,128)(2,1)S(1)}, bf16[768,256]{1,0:T(8,128)(2,1)}, u32[]{:S(2)}) copy-start(bf16[768,256]{1,0:T(8,128)(2,1)} %param.13) | copy-start | bytes 1179652
  20.3 26.2 %copy-start.5 = (f32[256]{0:T(256)S(1)}, f32[256]{0:T(256)}, u32[]{:S(2)}) copy-start(f32[256]{0:T(256)} %param.12) | copy-start | bytes 3076
  21.4 25.0 %collective-permute-start.2 = (f32[384,256]{1,0:T(8,128)S(1)}, f32[384,256]{1,0:T(8,128)S(1)}, u32[]{:S(2)}, u32[]{:S(2)}) collective-permute-start(f32[384,256]{1,0:T(8,128)S(1)} %constant_dynamic-slice_fusion), channel_id=1, source_target_pairs={{0,1},{1,0},{2,3},{3,2},{4,5},{5,4},{6,7},{7,6},{8,9},{9,8},{10,11... | collective-permute-start | bytes 1179656 | tf_op jit(solution)/shard_map/ppermute | solution.py:96
  47.2 3.7 %collective-permute-start.3 = (f32[257,128]{1,0:T(8,128)S(1)}, f32[257,128]{1,0:T(8,128)S(1)}, u32[]{:S(2)}, u32[]{:S(2)}) collective-permute-start(f32[257,128]{1,0:T(8,128)S(1)} %fusion.12), channel_id=1, source_target_pairs={{0,2},{2,0},{4,6},{6,4},{8,10},{10,8},{12,14},{14,12},{16,18},{18,... | collective-permute-start | bytes 394760 | tf_op jit(solution)/shard_map/ppermute | solution.py:36
  50.9 21.9 %collective-permute-start.5 = (bf16[384,512]{1,0:T(8,128)(2,1)S(1)}, bf16[384,512]{1,0:T(8,128)(2,1)S(1)}, u32[]{:S(2)}, u32[]{:S(2)}) collective-permute-start(bf16[384,512]{1,0:T(8,128)(2,1)S(1)} %pad_maximum_fusion.1), channel_id=1, source_target_pairs={{0,1},{1,0},{2,3},{3,2},{4,5},{5,4},{6,7},{7,6},{8,9},{9,8},{10,11... | collective-permute-start | bytes 1179656 | tf_op jit(solution)/shard_map/ppermute | solution.py:96
  52.9 10.9 %collective-permute-start.4 = (f32[257,128]{1,0:T(8,128)S(1)}, f32[257,128]{1,0:T(8,128)S(1)}, u32[]{:S(2)}, u32[]{:S(2)}) collective-permute-start(f32[257,128]{1,0:T(8,128)S(1)} %fusion.14), channel_id=1, source_target_pairs={{0,192},{2,194},{4,196},{6,198},{8,200},{10,202},{12,204},{14,206}... | collective-permute-start | bytes 394760 | tf_op jit(solution)/shard_map/ppermute | solution.py:36
  76.6 34.4 %collective-permute-start.11 = (f32[6,128,256]{2,1,0:T(8,128)S(1)}, f32[6,128,256]{2,1,0:T(8,128)S(1)}, u32[]{:S(2)}, u32[]{:S(2)}) collective-permute-start(f32[6,128,256]{2,1,0:T(8,128)S(1)} %slice.38), channel_id=1, source_target_pairs={{2,0},{4,2},{6,4},{8,6},{10,8},{12,10},{14,12},{16,14},{18,16},{20... | collective-permute-start | bytes 2359304 | tf_op jit(solution)/shard_map/ppermute | solution.py:25
  79.1 8.6 %collective-permute-start.12 = (bf16[6,128,256]{2,1,0:T(8,128)(2,1)S(1)}, bf16[6,128,256]{2,1,0:T(8,128)(2,1)S(1)}, u32[]{:S(2)}, u32[]{:S(2)}) collective-permute-start(bf16[6,128,256]{2,1,0:T(8,128)(2,1)S(1)} %slice.48), channel_id=1, source_target_pairs={{0,2},{2,4},{4,6},{6,8},{8,10},{10,12},{12,14},{14,16},{16,18},{18... | collective-permute-start | bytes 1179656 | tf_op jit(solution)/shard_map/ppermute | solution.py:25
  111.1 58.3 %collective-permute-start.13 = (f32[6,128,256]{2,1,0:T(8,128)S(1)}, f32[6,128,256]{2,1,0:T(8,128)S(1)}, u32[]{:S(2)}, u32[]{:S(2)}) collective-permute-start(f32[6,128,256]{2,1,0:T(8,128)S(1)} %fusion.11), channel_id=1, source_target_pairs={{0,1},{1,0},{2,3},{3,2},{4,5},{5,4},{6,7},{7,6},{8,9},{9,8},{10,11... | collective-permute-start | bytes 2359304 | tf_op jit(solution)/shard_map/ppermute | solution.py:106
  113.6 7.3 %collective-permute-start.6 = (f32[257,128]{1,0:T(8,128)S(1)}, f32[257,128]{1,0:T(8,128)S(1)}, u32[]{:S(2)}, u32[]{:S(2)}) collective-permute-start(f32[257,128]{1,0:T(8,128)S(1)} %add.94), channel_id=1, source_target_pairs={{0,384},{2,386},{4,388},{6,390},{8,392},{10,394},{12,396},{14,398}... | collective-permute-start | bytes 394760 | tf_op jit(solution)/shard_map/ppermute | solution.py:36
  120.9 5.8 %collective-permute-start.7 = (f32[257,128]{1,0:T(8,128)S(1)}, f32[257,128]{1,0:T(8,128)S(1)}, u32[]{:S(2)}, u32[]{:S(2)}) collective-permute-start(f32[257,128]{1,0:T(8,128)S(1)} %add.96), channel_id=1, source_target_pairs={{0,16},{2,18},{4,20},{6,22},{8,24},{10,26},{12,28},{14,30},{16,0},... | collective-permute-start | bytes 394760 | tf_op jit(solution)/shard_map/ppermute | solution.py:36
  126.7 8.8 %collective-permute-start.8 = (f32[257,128]{1,0:T(8,128)S(1)}, f32[257,128]{1,0:T(8,128)S(1)}, u32[]{:S(2)}, u32[]{:S(2)}) collective-permute-start(f32[257,128]{1,0:T(8,128)S(1)} %add.97), channel_id=1, source_target_pairs={{0,32},{2,34},{4,36},{6,38},{8,40},{10,42},{12,44},{14,46},{16,48}... | collective-permute-start | bytes 394760 | tf_op jit(solution)/shard_map/ppermute | solution.py:36
  135.5 25.9 %collective-permute-start.9 = (f32[257,128]{1,0:T(8,128)S(1)}, f32[257,128]{1,0:T(8,128)S(1)}, u32[]{:S(2)}, u32[]{:S(2)}) collective-permute-start(f32[257,128]{1,0:T(8,128)S(1)} %add.98), channel_id=1, source_target_pairs={{0,64},{2,66},{4,68},{6,70},{8,72},{10,74},{12,76},{14,78},{16,80}... | collective-permute-start | bytes 394760 | tf_op jit(solution)/shard_map/ppermute | solution.py:36
  137.5 31.9 %collective-permute-start.10 = (f32[257,128]{1,0:T(8,128)S(1)}, f32[257,128]{1,0:T(8,128)S(1)}, u32[]{:S(2)}, u32[]{:S(2)}) collective-permute-start(f32[257,128]{1,0:T(8,128)S(1)} %add.98), channel_id=1, source_target_pairs={{0,128},{2,130},{4,132},{6,134},{8,136},{10,138},{12,140},{14,142}... | collective-permute-start | bytes 394760 | tf_op jit(solution)/shard_map/ppermute | solution.py:36
  170.3 5.7 %collective-permute-start.14 = (f32[257,128]{1,0:T(8,128)S(1)}, f32[257,128]{1,0:T(8,128)S(1)}, u32[]{:S(2)}, u32[]{:S(2)}) collective-permute-start(f32[257,128]{1,0:T(8,128)S(1)} %select_add_fusion), channel_id=1, source_target_pairs={{0,4},{2,6},{4,0},{6,2},{8,12},{10,14},{12,8},{14,10},{16,20},{18,... | collective-permute-start | bytes 394760 | tf_op jit(solution)/shard_map/ppermute | solution.py:36
  176.1 9.1 %collective-permute-start.15 = (f32[257,128]{1,0:T(8,128)S(1)}, f32[257,128]{1,0:T(8,128)S(1)}, u32[]{:S(2)}, u32[]{:S(2)}) collective-permute-start(f32[257,128]{1,0:T(8,128)S(1)} %add.104), channel_id=1, source_target_pairs={{0,8},{2,10},{4,12},{6,14},{8,0},{10,2},{12,4},{14,6},{16,24},{18,... | collective-permute-start | bytes 394760 | tf_op jit(solution)/shard_map/ppermute | solution.py:36
  185.2 9.8 %collective-permute-start.16 = (f32[257,128]{1,0:T(8,128)S(1)}, f32[257,128]{1,0:T(8,128)S(1)}, u32[]{:S(2)}, u32[]{:S(2)}) collective-permute-start(f32[257,128]{1,0:T(8,128)S(1)} %add.105), channel_id=1, source_target_pairs={{0,1},{1,0},{2,3},{3,2},{4,5},{5,4},{6,7},{7,6},{8,9},{9,8},{10,11... | collective-permute-start | bytes 394760 | tf_op jit(solution)/shard_map/ppermute | solution.py:89
  195.0 3.2 %collective-permute-start.17 = (f32[257,128]{1,0:T(8,128)S(1)}, f32[257,128]{1,0:T(8,128)S(1)}, u32[]{:S(2)}, u32[]{:S(2)}) collective-permute-start(f32[257,128]{1,0:T(8,128)S(1)} %add.106), channel_id=1, source_target_pairs={{0,2},{2,0},{4,6},{6,4},{8,10},{10,8},{12,14},{14,12},{16,18},{18,... | collective-permute-start | bytes 394760 | tf_op jit(solution)/shard_map/ppermute | solution.py:36

commit v6 on v4

--- a/solution.py
+++ b/solution.py
@@ -149,8 +149,12 @@
         jnp.float32
     )
     own_terms = spread[num_blocks : 2 * num_blocks] + from_above + from_below
-    own_total = partner_sum(own_terms)
-    feature_grad = own_total.reshape(rows_here, feat_width).astype(jnp.bfloat16)
+    half_blocks = num_blocks // 2
+    own_half = lax.dynamic_slice_in_dim(own_terms, partner * half_blocks, half_blocks, 0)
+    their_half = lax.dynamic_slice_in_dim(own_terms, (1 - partner) * half_blocks, half_blocks, 0)
+    total_half = (own_half + partner_swap(their_half)).astype(jnp.bfloat16)
+    feature_grad = in_order(total_half, partner_swap(total_half), partner)
+    feature_grad = feature_grad.reshape(rows_here, feat_width)
     return (activations, feature_grad, weight_grad, bias_grad)
 
 

time: 201 us -> 206 us (1.025)
  waiting for transfers between devices: 75.4 us -> 81.9 us
    ppermute x1 -> x0, waiting for transfers between devices: 30.8 us -> none  [partner_sum(): return x + lax.ppermute(x, 'rep', [(0, 1), (1, 0)])]
    ppermute x2 -> x4, waiting for transfers between devices: 24.4 us -> 49.1 us  [partner_swap(): return lax.ppermute(x, 'rep', [(0, 1), (1, 0)])]
    ppermute x1, starting transfers between devices: 13 us -> 2.04 us  [global_sum(): x = x + lax.ppermute(x, 'rep', [(0, 1), (1, 0)])]
    ppermute x2 -> x4, starting transfers between devices: 4.31 us -> 13.1 us  [partner_swap(): return lax.ppermute(x, 'rep', [(0, 1), (1, 0)])]
    ppermute x1, waiting for transfers between devices: 0.01 us -> 6.31 us  [global_sum(): x = x + lax.ppermute(x, 'rep', [(0, 1), (1, 0)])]
    ppermute x10, waiting for transfers between devices: 20.2 us -> 26.4 us  [moved(): return lax.ppermute(x, axis, pairs)]
    ppermute x10, starting transfers between devices: 56 us -> 60.9 us  [moved(): return lax.ppermute(x, axis, pairs)]
  transfers between devices with their start and end apart: 18 -> 19, of which waited for: 8 -> 10; matrix products, arithmetic and copies ran while one was open for 8% -> 8% of each run, Pallas kernels for 0% -> 0%
where the time goes in v6:
time: 206 us
  starting transfers between devices  102 us (50%)
  waiting for transfers between devices  81.9 us (40%)
  other arithmetic  9.64 us (5%)
  matrix products  7.69 us (4%)
  local copies, waits for them, and re-layouts  3.42 us (2%)
    ppermute x10, starting transfers between devices, moved(): return lax.ppermute(x, axis, pairs)  60.9 us
    ppermute x4, waiting for transfers between devices, partner_swap(): return lax.ppermute(x, 'rep', [(0, 1), (1, 0)])  49.1 us
    ppermute x10, waiting for transfers between devices, moved(): return lax.ppermute(x, axis, pairs)  26.4 us
    ppermute x4, starting transfers between devices, partner_swap(): return lax.ppermute(x, 'rep', [(0, 1), (1, 0)])  13.1 us
    ppermute x2, starting transfers between devices, from_behind(): return lax.ppermute(x, axis, pairs)  11.8 us
    ppermute x1, starting transfers between devices, extended(): lax.ppermute(lax.slice_in_dim(block, 0, width, axis=dim), axis, backward)  9.15 us
    ppermute x1, waiting for transfers between devices, global_sum(): x = x + lax.ppermute(x, 'rep', [(0, 1), (1, 0)])  6.31 us
    ppermute x1, starting transfers between devices, extended(): lax.ppermute(lax.slice_in_dim(block, block.shape[dim] - width, None, axis...  4.73 us
  transfers between devices with their start and end apart: 19, of which 10 were waited for; matrix products, arithmetic and copies ran while one was open for 8% of the time, Pallas kernels for 0%

profile of v6, /device:TPU:1, one launch (start us, length us, event | category | flops | bytes accessed | tf_op | source)
XLA Modules:
  0.0 205.5 jit_solution(6064066076445971358)
XLA Ops:
  0.6 0.0 copy-start
  0.6 4.7 %collective-permute-start = (bf16[768,256]{1,0:T(8,128)(2,1)}, bf16[768,256]{1,0:T(8,128)(2,1)S(1)}, u32[]{:S(2)}, u32[]{:S(2)}) collective-permute-start(bf16[768,256]{1,0:T(8,128)(2,1)} %param.7), channel_id=1, source_target_pairs={{0,2},{2,4},{4,6},{6,8},{8,10},{10,12},{12,14},{14,16},{16,18},{18... | collective-permute-start | bytes 1179656 | tf_op jit(solution)/shard_map/ppermute | solution.py:14
  5.4 9.1 %collective-permute-start.1 = (bf16[768,256]{1,0:T(8,128)(2,1)}, bf16[768,256]{1,0:T(8,128)(2,1)S(1)}, u32[]{:S(2)}, u32[]{:S(2)}) collective-permute-start(bf16[768,256]{1,0:T(8,128)(2,1)} %param.7), channel_id=1, source_target_pairs={{2,0},{4,2},{6,4},{8,6},{10,8},{12,10},{14,12},{16,14},{18,16},{20... | collective-permute-start | bytes 1179656 | tf_op jit(solution)/shard_map/ppermute | solution.py:17
  14.5 0.7 broadcast_subtract_fusion
  15.2 0.7 iota_compare_fusion.1
  16.0 2.2 %convolution_convert_fusion = bf16[6,18,128,128]{3,1,2,0:T(8,128)(2,1)S(1)} fusion(bf16[6,6,128,128]{3,2,1,0:T(8,128)(2,1)S(1)} %copy-done, s32[6,6]{1,0:T(8,128)S(1)} %broadcast_subtract_fusion, pred[6,6]{1,0:T(8,128)(4,1)S(1)} %iota_compare_fusion.1), kind=kOutput, calls=%fused_computation.4 | convolution fusion | flops 23004432 | bytes 4718772 | tf_op jit(solution)/shard_map/bks,bkij->bsij/dot_general | solution.py:118
  18.2 0.0 collective-permute-done
  18.2 0.1 pad_maximum_fusion
  18.3 0.0 copy-start.6
  18.3 0.0 copy-start.7
  18.4 0.0 copy-start.8
  18.4 1.1 fusion.8
  19.5 0.9 copy-done.1
  20.4 2.1 %collective-permute-start.2 = (f32[384,256]{1,0:T(8,128)S(1)}, f32[384,256]{1,0:T(8,128)S(1)}, u32[]{:S(2)}, u32[]{:S(2)}) collective-permute-start(f32[384,256]{1,0:T(8,128)S(1)} %constant_dynamic-slice_fusion.1), channel_id=1, source_target_pairs={{0,1},{1,0},{2,3},{3,2},{4,5},{5,4},{6,7},{7,6},{8,9},{9,8},{10,11... | collective-permute-start | bytes 1179656 | tf_op jit(solution)/shard_map/ppermute | solution.py:77
  22.5 21.9 %collective-permute-done.2 = f32[384,256]{1,0:T(8,128)S(1)} collective-permute-done((f32[384,256]{1,0:T(8,128)S(1)}, f32[384,256]{1,0:T(8,128)S(1)}, u32[]{:S(2)}, u32[]{:S(2)}) %collective-permute-start.2) | collective-permute-done | bytes 393248 | tf_op jit(solution)/shard_map/ppermute | solution.py:77
  44.4 0.1 add_convert_fusion.1
  44.5 0.4 convert_reduce_fusion
  44.9 0.3 fusion.21
  45.1 0.2 convolution_convert_fusion.1
  45.4 2.4 %collective-permute-start.8 = (f32[257,128]{1,0:T(8,128)S(1)}, f32[257,128]{1,0:T(8,128)S(1)}, u32[]{:S(2)}, u32[]{:S(2)}) collective-permute-start(f32[257,128]{1,0:T(8,128)S(1)} %fusion.12), channel_id=1, source_target_pairs={{0,2},{2,0},{4,6},{6,4},{8,10},{10,8},{12,14},{14,12},{16,18},{18,... | collective-permute-start | bytes 394760 | tf_op jit(solution)/shard_map/ppermute | solution.py:36
  47.8 2.2 %collective-permute-start.3 = (bf16[384,512]{1,0:T(8,128)(2,1)S(1)}, bf16[384,512]{1,0:T(8,128)(2,1)S(1)}, u32[]{:S(2)}, u32[]{:S(2)}) collective-permute-start(bf16[384,512]{1,0:T(8,128)(2,1)S(1)} %pad_maximum_fusion.1), channel_id=1, source_target_pairs={{0,1},{1,0},{2,3},{3,2},{4,5},{5,4},{6,7},{7,6},{8,9},{9,8},{10,11... | collective-permute-start | bytes 1179656 | tf_op jit(solution)/shard_map/ppermute | solution.py:77
  50.1 4.3 %collective-permute-start.9 = (f32[257,128]{1,0:T(8,128)S(1)}, f32[257,128]{1,0:T(8,128)S(1)}, u32[]{:S(2)}, u32[]{:S(2)}) collective-permute-start(f32[257,128]{1,0:T(8,128)S(1)} %fusion.14), channel_id=1, source_target_pairs={{0,192},{2,194},{4,196},{6,198},{8,200},{10,202},{12,204},{14,206}... | collective-permute-start | bytes 394760 | tf_op jit(solution)/shard_map/ppermute | solution.py:36
  54.4 3.7 %collective-permute-done.9 = f32[257,128]{1,0:T(8,128)S(1)} collective-permute-done((f32[257,128]{1,0:T(8,128)S(1)}, f32[257,128]{1,0:T(8,128)S(1)}, u32[]{:S(2)}, u32[]{:S(2)}) %collective-permute-start.9) | collective-permute-done | bytes 131616 | tf_op jit(solution)/shard_map/ppermute | solution.py:36
  58.1 4.6 %collective-permute-start.10 = (f32[257,128]{1,0:T(8,128)S(1)}, f32[257,128]{1,0:T(8,128)S(1)}, u32[]{:S(2)}, u32[]{:S(2)}) collective-permute-start(f32[257,128]{1,0:T(8,128)S(1)} %add.105), channel_id=1, source_target_pairs={{0,384},{2,386},{4,388},{6,390},{8,392},{10,394},{12,396},{14,398}... | collective-permute-start | bytes 394760 | tf_op jit(solution)/shard_map/ppermute | solution.py:36
  62.7 2.6 %collective-permute-done.3 = bf16[384,512]{1,0:T(8,128)(2,1)S(1)} collective-permute-done((bf16[384,512]{1,0:T(8,128)(2,1)S(1)}, bf16[384,512]{1,0:T(8,128)(2,1)S(1)}, u32[]{:S(2)}, u32[]{:S(2)}) %collective-permute-start.3) | collective-permute-done | bytes 393248 | tf_op jit(solution)/shard_map/ppermute | solution.py:77
  65.3 0.7 fusion.20
  66.0 0.2 maximum_select_fusion.1
  66.2 0.0 collective-permute-done.10
  66.2 4.3 %collective-permute-start.11 = (f32[257,128]{1,0:T(8,128)S(1)}, f32[257,128]{1,0:T(8,128)S(1)}, u32[]{:S(2)}, u32[]{:S(2)}) collective-permute-start(f32[257,128]{1,0:T(8,128)S(1)} %add.106), channel_id=1, source_target_pairs={{0,16},{2,18},{4,20},{6,22},{8,24},{10,26},{12,28},{14,30},{16,0},... | collective-permute-start | bytes 394760 | tf_op jit(solution)/shard_map/ppermute | solution.py:36
  70.5 3.5 %fusion.4 = f32[18,128,256]{2,1,0:T(8,128)S(1)} fusion(bf16[6,128,256,1]{2,1,0,3:T(8,128)(2,1)S(1)} %bitcast.30, bf16[6,18,128,128]{3,1,2,0:T(8,128)(2,1)} %copy-done.1), kind=kOutput, calls=%fused_computation.5 | convolution fusion | flops 905969664 | bytes 6291456 | tf_op jit(solution)/shard_map/bsij,bif->sjf/dot_general | solution.py:144
  74.1 0.9 slice.32
  75.0 5.0 %collective-permute-start.4 = (f32[6,128,256]{2,1,0:T(8,128)}, f32[6,128,256]{2,1,0:T(8,128)}, u32[]{:S(2)}, u32[]{:S(2)}) collective-permute-start(f32[6,128,256]{2,1,0:T(8,128)} %slice.32), channel_id=1, source_target_pairs={{2,0},{4,2},{6,4},{8,6},{10,8},{12,10},{14,12},{16,14},{18,16},{20... | collective-permute-start | bytes 2359304 | tf_op jit(solution)/shard_map/ppermute | solution.py:25
  80.0 0.0 collective-permute-done.11
  80.0 6.1 %collective-permute-start.12 = (f32[257,128]{1,0:T(8,128)S(1)}, f32[257,128]{1,0:T(8,128)S(1)}, u32[]{:S(2)}, u32[]{:S(2)}) collective-permute-start(f32[257,128]{1,0:T(8,128)S(1)} %add.107), channel_id=1, source_target_pairs={{0,32},{2,34},{4,36},{6,38},{8,40},{10,42},{12,44},{14,46},{16,48}... | collective-permute-start | bytes 394760 | tf_op jit(solution)/shard_map/ppermute | solution.py:36
  86.1 5.1 %collective-permute-done.12 = f32[257,128]{1,0:T(8,128)S(1)} collective-permute-done((f32[257,128]{1,0:T(8,128)S(1)}, f32[257,128]{1,0:T(8,128)S(1)}, u32[]{:S(2)}, u32[]{:S(2)}) %collective-permute-start.12) | collective-permute-done | bytes 131616 | tf_op jit(solution)/shard_map/ppermute | solution.py:36
  91.2 0.7 add.108
  91.8 14.2 %collective-permute-start.14 = (f32[257,128]{1,0:T(8,128)}, f32[257,128]{1,0:T(8,128)}, u32[]{:S(2)}, u32[]{:S(2)}) collective-permute-start(f32[257,128]{1,0:T(8,128)} %add.108), channel_id=1, source_target_pairs={{0,128},{2,130},{4,132},{6,134},{8,136},{10,138},{12,140},{14,142}... | collective-permute-start | bytes 394760 | tf_op jit(solution)/shard_map/ppermute | solution.py:36
  106.0 1.9 collective-permute-start.13
  108.0 0.8 slice.42
  108.8 6.8 %collective-permute-start.5 = (bf16[6,128,256]{2,1,0:T(8,128)(2,1)}, bf16[6,128,256]{2,1,0:T(8,128)(2,1)}, u32[]{:S(2)}, u32[]{:S(2)}) collective-permute-start(bf16[6,128,256]{2,1,0:T(8,128)(2,1)} %slice.42), channel_id=1, source_target_pairs={{0,2},{2,4},{4,6},{6,8},{8,10},{10,12},{12,14},{14,16},{16,18},{18... | collective-permute-start | bytes 1179656 | tf_op jit(solution)/shard_map/ppermute | solution.py:25
  115.6 4.1 %collective-permute-done.13 = f32[257,128]{1,0:T(8,128)} collective-permute-done((f32[257,128]{1,0:T(8,128)}, f32[257,128]{1,0:T(8,128)}, u32[]{:S(2)}, u32[]{:S(2)}) %collective-permute-start.13) | collective-permute-done | bytes 131616 | tf_op jit(solution)/shard_map/ppermute | solution.py:36
  119.6 1.1 select_add_fusion
  120.7 11.0 %collective-permute-start.15 = (f32[257,128]{1,0:T(8,128)S(1)}, f32[257,128]{1,0:T(8,128)S(1)}, u32[]{:S(2)}, u32[]{:S(2)}) collective-permute-start(f32[257,128]{1,0:T(8,128)S(1)} %select_add_fusion), channel_id=1, source_target_pairs={{0,4},{2,6},{4,0},{6,2},{8,12},{10,14},{12,8},{14,10},{16,20},{18,... | collective-permute-start | bytes 394760 | tf_op jit(solution)/shard_map/ppermute | solution.py:36
  131.7 4.5 %collective-permute-done.15 = f32[257,128]{1,0:T(8,128)S(1)} collective-permute-done((f32[257,128]{1,0:T(8,128)S(1)}, f32[257,128]{1,0:T(8,128)S(1)}, u32[]{:S(2)}, u32[]{:S(2)}) %collective-permute-start.15) | collective-permute-done | bytes 131616 | tf_op jit(solution)/shard_map/ppermute | solution.py:36
  136.2 0.7 add.111
  136.9 2.2 %collective-permute-start.16 = (f32[257,128]{1,0:T(8,128)}, f32[257,128]{1,0:T(8,128)}, u32[]{:S(2)}, u32[]{:S(2)}) collective-permute-start(f32[257,128]{1,0:T(8,128)} %add.111), channel_id=1, source_target_pairs={{0,8},{2,10},{4,12},{6,14},{8,0},{10,2},{12,4},{14,6},{16,24},{18,... | collective-permute-start | bytes 394760 | tf_op jit(solution)/shard_map/ppermute | solution.py:36
  139.0 0.0 copy-start.3
  139.1 0.0 copy-start.4
  139.1 9.1 %collective-permute-done.16 = f32[257,128]{1,0:T(8,128)} collective-permute-done((f32[257,128]{1,0:T(8,128)}, f32[257,128]{1,0:T(8,128)}, u32[]{:S(2)}, u32[]{:S(2)}) %collective-permute-start.16) | collective-permute-done | bytes 131616 | tf_op jit(solution)/shard_map/ppermute | solution.py:36
  148.2 1.0 add.112
  149.2 2.0 collective-permute-start.17
  151.2 0.0 collective-permute-done.4
  151.3 1.4 fusion.11
  152.6 6.3 %collective-permute-done.17 = f32[257,128]{1,0:T(8,128)S(1)} collective-permute-done((f32[257,128]{1,0:T(8,128)S(1)}, f32[257,128]{1,0:T(8,128)S(1)}, u32[]{:S(2)}, u32[]{:S(2)}) %collective-permute-start.17) | collective-permute-done | bytes 131616 | tf_op jit(solution)/shard_map/ppermute | solution.py:71
  159.0 9.9 %collective-permute-start.18 = (f32[257,128]{1,0:T(8,128)S(1)}, f32[257,128]{1,0:T(8,128)S(1)}, u32[]{:S(2)}, u32[]{:S(2)}) collective-permute-start(f32[257,128]{1,0:T(8,128)S(1)} %add.113), channel_id=1, source_target_pairs={{0,2},{2,0},{4,6},{6,4},{8,10},{10,8},{12,14},{14,12},{16,18},{18,... | collective-permute-start | bytes 394760 | tf_op jit(solution)/shard_map/ppermute | solution.py:36
  168.9 6.4 %collective-permute-start.6 = (f32[3,128,256]{2,1,0:T(8,128)S(1)}, f32[3,128,256]{2,1,0:T(8,128)S(1)}, u32[]{:S(2)}, u32[]{:S(2)}) collective-permute-start(f32[3,128,256]{2,1,0:T(8,128)S(1)} %constant_dynamic-slice_fusion), channel_id=1, source_target_pairs={{0,1},{1,0},{2,3},{3,2},{4,5},{5,4},{6,7},{7,6},{8,9},{9,8},{10,11... | collective-permute-start | bytes 1179656 | tf_op jit(solution)/shard_map/ppermute | solution.py:77
  175.4 0.9 maximum_select_fusion
  176.3 0.7 slice_multiply_fusion
  177.0 15.9 %collective-permute-done.6 = f32[3,128,256]{2,1,0:T(8,128)S(1)} collective-permute-done((f32[3,128,256]{2,1,0:T(8,128)S(1)}, f32[3,128,256]{2,1,0:T(8,128)S(1)}, u32[]{:S(2)}, u32[]{:S(2)}) %collective-permute-start.6) | collective-permute-done | bytes 393248 | tf_op jit(solution)/shard_map/ppermute | solution.py:77
  192.9 0.1 add_convert_fusion
  193.0 2.4 %collective-permute-start.7 = (bf16[3,128,256]{2,1,0:T(8,128)(2,1)S(1)}, bf16[3,128,256]{2,1,0:T(8,128)(2,1)S(1)}, u32[]{:S(2)}, u32[]{:S(2)}) collective-permute-start(bf16[3,128,256]{2,1,0:T(8,128)(2,1)S(1)} %add_convert_fusion), channel_id=1, source_target_pairs={{0,1},{1,0},{2,3},{3,2},{4,5},{5,4},{6,7},{7,6},{8,9},{9,8},{10,11... | collective-permute-start | bytes 589832 | tf_op jit(solution)/shard_map/ppermute | solution.py:77
  195.4 0.6 slice_multiply_fusion.1
  195.9 8.8 %collective-permute-done.7 = bf16[3,128,256]{2,1,0:T(8,128)(2,1)S(1)} collective-permute-done((bf16[3,128,256]{2,1,0:T(8,128)(2,1)S(1)}, bf16[3,128,256]{2,1,0:T(8,128)(2,1)S(1)}, u32[]{:S(2)}, u32[]{:S(2)}) %collective-permute-start.7) | collective-permute-done | bytes 196640 | tf_op jit(solution)/shard_map/ppermute | solution.py:77
  204.7 0.8 maximum_select_fusion.2
  (26 shorter events, 0.3 us)
Async XLA Ops:
  0.6 15.3 %copy-start = (bf16[6,6,128,128]{3,2,1,0:T(8,128)(2,1)S(1)}, bf16[6,6,128,128]{3,2,1,0:T(8,128)(2,1)}, u32[]{:S(2)}) copy-start(bf16[6,6,128,128]{3,2,1,0:T(8,128)(2,1)} %param.8) | copy-start | bytes 3538948
  0.6 17.6 %collective-permute-start = (bf16[768,256]{1,0:T(8,128)(2,1)}, bf16[768,256]{1,0:T(8,128)(2,1)S(1)}, u32[]{:S(2)}, u32[]{:S(2)}) collective-permute-start(bf16[768,256]{1,0:T(8,128)(2,1)} %param.7), channel_id=1, source_target_pairs={{0,2},{2,4},{4,6},{6,8},{8,10},{10,12},{12,14},{14,16},{16,18},{18... | collective-permute-start | bytes 1179656 | tf_op jit(solution)/shard_map/ppermute | solution.py:14
  5.4 12.8 %collective-permute-start.1 = (bf16[768,256]{1,0:T(8,128)(2,1)}, bf16[768,256]{1,0:T(8,128)(2,1)S(1)}, u32[]{:S(2)}, u32[]{:S(2)}) collective-permute-start(bf16[768,256]{1,0:T(8,128)(2,1)} %param.7), channel_id=1, source_target_pairs={{2,0},{4,2},{6,4},{8,6},{10,8},{12,10},{14,12},{16,14},{18,16},{20... | collective-permute-start | bytes 1179656 | tf_op jit(solution)/shard_map/ppermute | solution.py:17
  16.0 2.3 %copy-start.5 = (bf16[768,256]{1,0:T(8,128)(2,1)S(1)}, bf16[768,256]{1,0:T(8,128)(2,1)}, u32[]{:S(2)}) copy-start(bf16[768,256]{1,0:T(8,128)(2,1)} %param.7) | copy-start | bytes 1179652
  18.2 2.1 %copy-start.1 = (bf16[6,18,128,128]{3,1,2,0:T(8,128)(2,1)}, bf16[6,18,128,128]{3,1,2,0:T(8,128)(2,1)S(1)}, u32[]{:S(2)}) copy-start(bf16[6,18,128,128]{3,1,2,0:T(8,128)(2,1)S(1)} %convolution_convert_fusion) | copy-start | bytes 10616836
  18.3 26.1 %copy-start.6 = (bf16[256,256]{1,0:T(8,128)(2,1)S(1)}, bf16[256,256]{1,0:T(8,128)(2,1)}, u32[]{:S(2)}) copy-start(bf16[256,256]{1,0:T(8,128)(2,1)} %param.11) | copy-start | bytes 393220
  18.3 26.1 %copy-start.7 = (bf16[768,256]{1,0:T(8,128)(2,1)S(1)}, bf16[768,256]{1,0:T(8,128)(2,1)}, u32[]{:S(2)}) copy-start(bf16[768,256]{1,0:T(8,128)(2,1)} %param.13) | copy-start | bytes 1179652
  18.4 26.1 %copy-start.8 = (f32[256]{0:T(256)S(1)}, f32[256]{0:T(256)}, u32[]{:S(2)}) copy-start(f32[256]{0:T(256)} %param.12) | copy-start | bytes 3076
  20.4 24.0 %collective-permute-start.2 = (f32[384,256]{1,0:T(8,128)S(1)}, f32[384,256]{1,0:T(8,128)S(1)}, u32[]{:S(2)}, u32[]{:S(2)}) collective-permute-start(f32[384,256]{1,0:T(8,128)S(1)} %constant_dynamic-slice_fusion.1), channel_id=1, source_target_pairs={{0,1},{1,0},{2,3},{3,2},{4,5},{5,4},{6,7},{7,6},{8,9},{9,8},{10,11... | collective-permute-start | bytes 1179656 | tf_op jit(solution)/shard_map/ppermute | solution.py:77
  44.9 2.9 %copy-start.2 = (bf16[384,256]{1,0:T(8,128)(2,1)}, bf16[384,256]{1,0:T(8,128)(2,1)S(1)}, u32[]{:S(2)}) copy-start(bf16[384,256]{1,0:T(8,128)(2,1)S(1)} %get-tuple-element.8) | copy-start | bytes 589828
  45.4 4.6 %collective-permute-start.8 = (f32[257,128]{1,0:T(8,128)S(1)}, f32[257,128]{1,0:T(8,128)S(1)}, u32[]{:S(2)}, u32[]{:S(2)}) collective-permute-start(f32[257,128]{1,0:T(8,128)S(1)} %fusion.12), channel_id=1, source_target_pairs={{0,2},{2,0},{4,6},{6,4},{8,10},{10,8},{12,14},{14,12},{16,18},{18,... | collective-permute-start | bytes 394760 | tf_op jit(solution)/shard_map/ppermute | solution.py:36
  47.8 17.5 %collective-permute-start.3 = (bf16[384,512]{1,0:T(8,128)(2,1)S(1)}, bf16[384,512]{1,0:T(8,128)(2,1)S(1)}, u32[]{:S(2)}, u32[]{:S(2)}) collective-permute-start(bf16[384,512]{1,0:T(8,128)(2,1)S(1)} %pad_maximum_fusion.1), channel_id=1, source_target_pairs={{0,1},{1,0},{2,3},{3,2},{4,5},{5,4},{6,7},{7,6},{8,9},{9,8},{10,11... | collective-permute-start | bytes 1179656 | tf_op jit(solution)/shard_map/ppermute | solution.py:77
  50.1 8.1 %collective-permute-start.9 = (f32[257,128]{1,0:T(8,128)S(1)}, f32[257,128]{1,0:T(8,128)S(1)}, u32[]{:S(2)}, u32[]{:S(2)}) collective-permute-start(f32[257,128]{1,0:T(8,128)S(1)} %fusion.14), channel_id=1, source_target_pairs={{0,192},{2,194},{4,196},{6,198},{8,200},{10,202},{12,204},{14,206}... | collective-permute-start | bytes 394760 | tf_op jit(solution)/shard_map/ppermute | solution.py:36
  58.1 8.0 %collective-permute-start.10 = (f32[257,128]{1,0:T(8,128)S(1)}, f32[257,128]{1,0:T(8,128)S(1)}, u32[]{:S(2)}, u32[]{:S(2)}) collective-permute-start(f32[257,128]{1,0:T(8,128)S(1)} %add.105), channel_id=1, source_target_pairs={{0,384},{2,386},{4,388},{6,390},{8,392},{10,394},{12,396},{14,398}... | collective-permute-start | bytes 394760 | tf_op jit(solution)/shard_map/ppermute | solution.py:36
  66.2 13.8 %collective-permute-start.11 = (f32[257,128]{1,0:T(8,128)S(1)}, f32[257,128]{1,0:T(8,128)S(1)}, u32[]{:S(2)}, u32[]{:S(2)}) collective-permute-start(f32[257,128]{1,0:T(8,128)S(1)} %add.106), channel_id=1, source_target_pairs={{0,16},{2,18},{4,20},{6,22},{8,24},{10,26},{12,28},{14,30},{16,0},... | collective-permute-start | bytes 394760 | tf_op jit(solution)/shard_map/ppermute | solution.py:36
  75.0 76.3 %collective-permute-start.4 = (f32[6,128,256]{2,1,0:T(8,128)}, f32[6,128,256]{2,1,0:T(8,128)}, u32[]{:S(2)}, u32[]{:S(2)}) collective-permute-start(f32[6,128,256]{2,1,0:T(8,128)} %slice.32), channel_id=1, source_target_pairs={{2,0},{4,2},{6,4},{8,6},{10,8},{12,10},{14,12},{16,14},{18,16},{20... | collective-permute-start | bytes 2359304 | tf_op jit(solution)/shard_map/ppermute | solution.py:25
  80.0 11.1 %collective-permute-start.12 = (f32[257,128]{1,0:T(8,128)S(1)}, f32[257,128]{1,0:T(8,128)S(1)}, u32[]{:S(2)}, u32[]{:S(2)}) collective-permute-start(f32[257,128]{1,0:T(8,128)S(1)} %add.107), channel_id=1, source_target_pairs={{0,32},{2,34},{4,36},{6,38},{8,40},{10,42},{12,44},{14,46},{16,48}... | collective-permute-start | bytes 394760 | tf_op jit(solution)/shard_map/ppermute | solution.py:36
  91.8 23.7 %collective-permute-start.14 = (f32[257,128]{1,0:T(8,128)}, f32[257,128]{1,0:T(8,128)}, u32[]{:S(2)}, u32[]{:S(2)}) collective-permute-start(f32[257,128]{1,0:T(8,128)} %add.108), channel_id=1, source_target_pairs={{0,128},{2,130},{4,132},{6,134},{8,136},{10,138},{12,140},{14,142}... | collective-permute-start | bytes 394760 | tf_op jit(solution)/shard_map/ppermute | solution.py:36
  106.0 13.6 %collective-permute-start.13 = (f32[257,128]{1,0:T(8,128)}, f32[257,128]{1,0:T(8,128)}, u32[]{:S(2)}, u32[]{:S(2)}) collective-permute-start(f32[257,128]{1,0:T(8,128)} %add.108), channel_id=1, source_target_pairs={{0,64},{2,66},{4,68},{6,70},{8,72},{10,74},{12,76},{14,78},{16,80}... | collective-permute-start | bytes 394760 | tf_op jit(solution)/shard_map/ppermute | solution.py:36
  108.8 42.5 %collective-permute-start.5 = (bf16[6,128,256]{2,1,0:T(8,128)(2,1)}, bf16[6,128,256]{2,1,0:T(8,128)(2,1)}, u32[]{:S(2)}, u32[]{:S(2)}) collective-permute-start(bf16[6,128,256]{2,1,0:T(8,128)(2,1)} %slice.42), channel_id=1, source_target_pairs={{0,2},{2,4},{4,6},{6,8},{8,10},{10,12},{12,14},{14,16},{16,18},{18... | collective-permute-start | bytes 1179656 | tf_op jit(solution)/shard_map/ppermute | solution.py:25
  120.7 15.5 %collective-permute-start.15 = (f32[257,128]{1,0:T(8,128)S(1)}, f32[257,128]{1,0:T(8,128)S(1)}, u32[]{:S(2)}, u32[]{:S(2)}) collective-permute-start(f32[257,128]{1,0:T(8,128)S(1)} %select_add_fusion), channel_id=1, source_target_pairs={{0,4},{2,6},{4,0},{6,2},{8,12},{10,14},{12,8},{14,10},{16,20},{18,... | collective-permute-start | bytes 394760 | tf_op jit(solution)/shard_map/ppermute | solution.py:36
  136.9 11.3 %collective-permute-start.16 = (f32[257,128]{1,0:T(8,128)}, f32[257,128]{1,0:T(8,128)}, u32[]{:S(2)}, u32[]{:S(2)}) collective-permute-start(f32[257,128]{1,0:T(8,128)} %add.111), channel_id=1, source_target_pairs={{0,8},{2,10},{4,12},{6,14},{8,0},{10,2},{12,4},{14,6},{16,24},{18,... | collective-permute-start | bytes 394760 | tf_op jit(solution)/shard_map/ppermute | solution.py:36
  139.0 36.3 %copy-start.3 = (bf16[384,256]{1,0:T(8,128)(2,1)S(1)}, bf16[384,256]{1,0:T(8,128)(2,1)}, u32[]{:S(2)}) copy-start(bf16[384,256]{1,0:T(8,128)(2,1)} %copy-done.2) | copy-start | bytes 589828
  139.1 36.3 %copy-start.4 = (bf16[384,256]{1,0:T(8,128)(2,1)S(1)}, bf16[384,256]{1,0:T(8,128)(2,1)}, u32[]{:S(2)}) copy-start(bf16[384,256]{1,0:T(8,128)(2,1)} %get-tuple-element.7) | copy-start | bytes 589828
  149.2 9.8 %collective-permute-start.17 = (f32[257,128]{1,0:T(8,128)S(1)}, f32[257,128]{1,0:T(8,128)S(1)}, u32[]{:S(2)}, u32[]{:S(2)}) collective-permute-start(f32[257,128]{1,0:T(8,128)S(1)} %add.112), channel_id=1, source_target_pairs={{0,1},{1,0},{2,3},{3,2},{4,5},{5,4},{6,7},{7,6},{8,9},{9,8},{10,11... | collective-permute-start | bytes 394760 | tf_op jit(solution)/shard_map/ppermute | solution.py:71
  159.0 17.3 %collective-permute-start.18 = (f32[257,128]{1,0:T(8,128)S(1)}, f32[257,128]{1,0:T(8,128)S(1)}, u32[]{:S(2)}, u32[]{:S(2)}) collective-permute-start(f32[257,128]{1,0:T(8,128)S(1)} %add.113), channel_id=1, source_target_pairs={{0,2},{2,0},{4,6},{6,4},{8,10},{10,8},{12,14},{14,12},{16,18},{18,... | collective-permute-start | bytes 394760 | tf_op jit(solution)/shard_map/ppermute | solution.py:36
  168.9 24.0 %collective-permute-start.6 = (f32[3,128,256]{2,1,0:T(8,128)S(1)}, f32[3,128,256]{2,1,0:T(8,128)S(1)}, u32[]{:S(2)}, u32[]{:S(2)}) collective-permute-start(f32[3,128,256]{2,1,0:T(8,128)S(1)} %constant_dynamic-slice_fusion), channel_id=1, source_target_pairs={{0,1},{1,0},{2,3},{3,2},{4,5},{5,4},{6,7},{7,6},{8,9},{9,8},{10,11... | collective-permute-start | bytes 1179656 | tf_op jit(solution)/shard_map/ppermute | solution.py:77
  193.0 11.7 %collective-permute-start.7 = (bf16[3,128,256]{2,1,0:T(8,128)(2,1)S(1)}, bf16[3,128,256]{2,1,0:T(8,128)(2,1)S(1)}, u32[]{:S(2)}, u32[]{:S(2)}) collective-permute-start(bf16[3,128,256]{2,1,0:T(8,128)(2,1)S(1)} %add_convert_fusion), channel_id=1, source_target_pairs={{0,1},{1,0},{2,3},{3,2},{4,5},{5,4},{6,7},{7,6},{8,9},{9,8},{10,11... | collective-permute-start | bytes 589832 | tf_op jit(solution)/shard_map/ppermute | solution.py:77

commit v7 on v4

--- a/solution.py
+++ b/solution.py
@@ -61,7 +61,11 @@
     keep = lax.dynamic_slice_in_dim(x, core * width, width, 1)
     give = lax.dynamic_slice_in_dim(x, (1 - core) * width, width, 1)
     x = keep + moved(give, "rows", count, c_stride, c_size, lambda c: c ^ 1)
-    x = swapped_sum(x, "rows", count, x_stride, x_size, 1)
+    x_bit = (lax.axis_index("rows") // x_stride) % x_size % 2
+    height = x.shape[0] // 2
+    keep = lax.dynamic_slice_in_dim(x, x_bit * height, height, 0)
+    give = lax.dynamic_slice_in_dim(x, (1 - x_bit) * height, height, 0)
+    x = keep + moved(give, "rows", count, x_stride, x_size, lambda c: c ^ 1)
     x = swapped_sum(x, "rows", count, x_stride, x_size, 2)
     x = swapped_sum(x, "rows", count, z_stride, z_size, 1)
     x = swapped_sum(x, "rows", count, z_stride, z_size, 2)
@@ -69,6 +73,8 @@
     x = swapped_sum(x, "rows", count, y_stride, y_size, 1)
     x = swapped_sum(x, "rows", count, y_stride, y_size, 2)
     x = x + lax.ppermute(x, "rep", [(0, 1), (1, 0)])
+    other = moved(x, "rows", count, x_stride, x_size, lambda c: c ^ 1)
+    x = jnp.where(x_bit == 0, jnp.concatenate([x, other], 0), jnp.concatenate([other, x], 0))
     other = moved(x, "rows", count, c_stride, c_size, lambda c: c ^ 1)
     return jnp.where(core == 0, jnp.concatenate([x, other], 1), jnp.concatenate([other, x], 1))
 
@@ -134,7 +140,8 @@
         agg_half, grad_half, (((0,), (0,)), ((), ())), preferred_element_type=jnp.float32
     )
     bias_part = jnp.sum(grad_half.astype(jnp.float32), axis=0)
-    grad_terms = global_sum(jnp.concatenate([weight_part, bias_part[None, :]], axis=0))
+    spare_rows = jnp.zeros((15, feat_width), jnp.float32)
+    grad_terms = global_sum(jnp.concatenate([weight_part, bias_part[None, :], spare_rows], axis=0))
     weight_total = grad_terms[:feat_width]
     bias_total = grad_terms[feat_width]
     scale = 1.0 / math.sqrt(node_count)

time: 201 us -> 203 us (level)
  the two profiles are of different devices: /device:TPU:1 before, /device:TPU:49 now
where the time goes in v7:
time: 203 us; the launch traced here: 202 us
  starting transfers between devices  104 us (51%)
  waiting for transfers between devices  74.3 us (37%)
  other arithmetic  12.7 us (6%)
  matrix products  7.69 us (4%)
  local copies, waits for them, and re-layouts  2.66 us (1%)
    ppermute x11, starting transfers between devices, moved(): return lax.ppermute(x, axis, pairs)  79.5 us
    ppermute x1, waiting for transfers between devices, partner_sum(): return x + lax.ppermute(x, 'rep', [(0, 1), (1, 0)])  28.4 us
    ppermute x2, waiting for transfers between devices, partner_swap(): return lax.ppermute(x, 'rep', [(0, 1), (1, 0)])  19.9 us
    ppermute x11, waiting for transfers between devices, moved(): return lax.ppermute(x, axis, pairs)  14.9 us
    ppermute x2, starting transfers between devices, from_behind(): return lax.ppermute(x, axis, pairs)  8.21 us
    ppermute x1, waiting for transfers between devices, global_sum(): x = x + lax.ppermute(x, 'rep', [(0, 1), (1, 0)])  7.34 us
    ppermute x2, starting transfers between devices, partner_swap(): return lax.ppermute(x, 'rep', [(0, 1), (1, 0)])  6.83 us
  transfers between devices with their start and end apart: 19, of which 11 were waited for; matrix products, arithmetic and copies ran while one was open for 9% of the time, Pallas kernels for 0%

profile of v7, /device:TPU:49, one launch (start us, length us, event | category | flops | bytes accessed | tf_op | source)
XLA Modules:
  0.0 202.1 jit_solution(2547289765705395189)
XLA Ops:
  0.6 0.0 copy-start
  0.6 3.0 %collective-permute-start = (bf16[768,256]{1,0:T(8,128)(2,1)}, bf16[768,256]{1,0:T(8,128)(2,1)S(1)}, u32[]{:S(2)}, u32[]{:S(2)}) collective-permute-start(bf16[768,256]{1,0:T(8,128)(2,1)} %param.7), channel_id=1, source_target_pairs={{0,2},{2,4},{4,6},{6,8},{8,10},{10,12},{12,14},{14,16},{16,18},{18... | collective-permute-start | bytes 1179656 | tf_op jit(solution)/shard_map/ppermute | solution.py:14
  3.7 1.9 collective-permute-start.1
  5.6 0.7 broadcast_subtract_fusion
  6.3 0.7 iota_compare_fusion.1
  7.0 2.2 %convolution_convert_fusion = bf16[6,18,128,128]{3,1,2,0:T(8,128)(2,1)S(1)} fusion(bf16[6,6,128,128]{3,2,1,0:T(8,128)(2,1)S(1)} %copy-done, s32[6,6]{1,0:T(8,128)S(1)} %broadcast_subtract_fusion, pred[6,6]{1,0:T(8,128)(4,1)S(1)} %iota_compare_fusion.1), kind=kOutput, calls=%fused_computation.4 | convolution fusion | flops 23004432 | bytes 4718772 | tf_op jit(solution)/shard_map/bks,bkij->bsij/dot_general | solution.py:124
  9.3 0.0 collective-permute-done
  9.3 3.7 %collective-permute-done.1 = bf16[768,256]{1,0:T(8,128)(2,1)S(1)} collective-permute-done((bf16[768,256]{1,0:T(8,128)(2,1)}, bf16[768,256]{1,0:T(8,128)(2,1)S(1)}, u32[]{:S(2)}, u32[]{:S(2)}) %collective-permute-start.1) | collective-permute-done | bytes 393248 | tf_op jit(solution)/shard_map/ppermute | solution.py:17
  13.0 0.1 pad_maximum_fusion
  13.0 0.0 copy-start.4
  13.1 0.0 copy-start.5
  13.1 0.0 copy-start.6
  13.1 1.1 fusion.8
  14.2 4.4 %collective-permute-start.2 = (f32[384,256]{1,0:T(8,128)S(1)}, f32[384,256]{1,0:T(8,128)S(1)}, u32[]{:S(2)}, u32[]{:S(2)}) collective-permute-start(f32[384,256]{1,0:T(8,128)S(1)} %constant_dynamic-slice_fusion.2), channel_id=1, source_target_pairs={{0,1},{1,0},{2,3},{3,2},{4,5},{5,4},{6,7},{7,6},{8,9},{9,8},{10,11... | collective-permute-start | bytes 1179656 | tf_op jit(solution)/shard_map/ppermute | solution.py:83
  18.7 0.1 pad.10.clone
  18.8 13.1 %collective-permute-done.2 = f32[384,256]{1,0:T(8,128)S(1)} collective-permute-done((f32[384,256]{1,0:T(8,128)S(1)}, f32[384,256]{1,0:T(8,128)S(1)}, u32[]{:S(2)}, u32[]{:S(2)}) %collective-permute-start.2) | collective-permute-done | bytes 393248 | tf_op jit(solution)/shard_map/ppermute | solution.py:83
  31.9 0.1 add_convert_fusion.1
  32.0 0.4 convert_reduce_fusion
  32.4 0.3 fusion.18
  32.6 0.2 convolution_convert_fusion.1
  32.9 0.1 maximum_maximum_fusion
  33.0 2.5 %collective-permute-start.7 = (f32[272,128]{1,0:T(8,128)S(1)}, f32[272,128]{1,0:T(8,128)S(1)}, u32[]{:S(2)}, u32[]{:S(2)}) collective-permute-start(f32[272,128]{1,0:T(8,128)S(1)} %constant_dynamic-slice_fusion.1), channel_id=1, source_target_pairs={{0,2},{2,0},{4,6},{6,4},{8,10},{10,8},{12,14},{14,12},{16,18},{18,... | collective-permute-start | bytes 417800 | tf_op jit(solution)/shard_map/ppermute | solution.py:36
  35.5 2.4 %collective-permute-start.3 = (bf16[384,512]{1,0:T(8,128)(2,1)S(1)}, bf16[384,512]{1,0:T(8,128)(2,1)S(1)}, u32[]{:S(2)}, u32[]{:S(2)}) collective-permute-start(bf16[384,512]{1,0:T(8,128)(2,1)S(1)} %pad_maximum_fusion.1), channel_id=1, source_target_pairs={{0,1},{1,0},{2,3},{3,2},{4,5},{5,4},{6,7},{7,6},{8,9},{9,8},{10,11... | collective-permute-start | bytes 1179656 | tf_op jit(solution)/shard_map/ppermute | solution.py:83
  38.0 0.0 collective-permute-done.7
  38.1 7.3 %collective-permute-start.8 = (f32[136,128]{1,0:T(8,128)S(1)}, f32[136,128]{1,0:T(8,128)S(1)}, u32[]{:S(2)}, u32[]{:S(2)}) collective-permute-start(f32[136,128]{1,0:T(8,128)S(1)} %constant_dynamic-slice_fusion), channel_id=1, source_target_pairs={{0,192},{2,194},{4,196},{6,198},{8,200},{10,202},{12,204},{14,206}... | collective-permute-start | bytes 208904 | tf_op jit(solution)/shard_map/ppermute | solution.py:36
  45.3 6.7 %collective-permute-done.3 = bf16[384,512]{1,0:T(8,128)(2,1)S(1)} collective-permute-done((bf16[384,512]{1,0:T(8,128)(2,1)S(1)}, bf16[384,512]{1,0:T(8,128)(2,1)S(1)}, u32[]{:S(2)}, u32[]{:S(2)}) %collective-permute-start.3) | collective-permute-done | bytes 393248 | tf_op jit(solution)/shard_map/ppermute | solution.py:83
  52.1 0.7 fusion.17
  52.8 0.2 maximum_select_fusion.1
  53.0 3.5 %fusion.4 = f32[18,128,256]{2,1,0:T(8,128)S(1)} fusion(bf16[6,128,256,1]{2,1,0,3:T(8,128)(2,1)S(1)} %bitcast.30, bf16[6,18,128,128]{3,1,2,0:T(8,128)(2,1)} %copy-done.1), kind=kOutput, calls=%fused_computation.5 | convolution fusion | flops 905969664 | bytes 6291456 | tf_op jit(solution)/shard_map/bsij,bif->sjf/dot_general | solution.py:151
  56.5 1.0 slice.32
  57.4 2.7 %collective-permute-start.4 = (f32[6,128,256]{2,1,0:T(8,128)}, f32[6,128,256]{2,1,0:T(8,128)}, u32[]{:S(2)}, u32[]{:S(2)}) collective-permute-start(f32[6,128,256]{2,1,0:T(8,128)} %slice.32), channel_id=1, source_target_pairs={{2,0},{4,2},{6,4},{8,6},{10,8},{12,10},{14,12},{16,14},{18,16},{20... | collective-permute-start | bytes 2359304 | tf_op jit(solution)/shard_map/ppermute | solution.py:25
  60.2 0.0 collective-permute-done.8
  60.2 8.1 %collective-permute-start.9 = (f32[136,128]{1,0:T(8,128)S(1)}, f32[136,128]{1,0:T(8,128)S(1)}, u32[]{:S(2)}, u32[]{:S(2)}) collective-permute-start(f32[136,128]{1,0:T(8,128)S(1)} %dynamic-slice_add_fusion.1), channel_id=1, source_target_pairs={{0,384},{2,386},{4,388},{6,390},{8,392},{10,394},{12,396},{14,398}... | collective-permute-start | bytes 208904 | tf_op jit(solution)/shard_map/ppermute | solution.py:36
  68.3 1.7 collective-permute-done.9
  70.0 19.8 %collective-permute-start.10 = (f32[136,128]{1,0:T(8,128)S(1)}, f32[136,128]{1,0:T(8,128)S(1)}, u32[]{:S(2)}, u32[]{:S(2)}) collective-permute-start(f32[136,128]{1,0:T(8,128)S(1)} %add.115), channel_id=1, source_target_pairs={{0,16},{2,18},{4,20},{6,22},{8,24},{10,26},{12,28},{14,30},{16,0},... | collective-permute-start | bytes 208904 | tf_op jit(solution)/shard_map/ppermute | solution.py:36
  89.8 1.7 collective-permute-done.10
  91.5 6.0 %collective-permute-start.11 = (f32[136,128]{1,0:T(8,128)S(1)}, f32[136,128]{1,0:T(8,128)S(1)}, u32[]{:S(2)}, u32[]{:S(2)}) collective-permute-start(f32[136,128]{1,0:T(8,128)S(1)} %add.116), channel_id=1, source_target_pairs={{0,32},{2,34},{4,36},{6,38},{8,40},{10,42},{12,44},{14,46},{16,48}... | collective-permute-start | bytes 208904 | tf_op jit(solution)/shard_map/ppermute | solution.py:36
  97.5 1.7 collective-permute-done.11
  99.2 0.6 add.117
  99.8 13.6 %collective-permute-start.13 = (f32[136,128]{1,0:T(8,128)}, f32[136,128]{1,0:T(8,128)}, u32[]{:S(2)}, u32[]{:S(2)}) collective-permute-start(f32[136,128]{1,0:T(8,128)} %add.117), channel_id=1, source_target_pairs={{0,128},{2,130},{4,132},{6,134},{8,136},{10,138},{12,140},{14,142}... | collective-permute-start | bytes 208904 | tf_op jit(solution)/shard_map/ppermute | solution.py:36
  113.4 1.9 collective-permute-start.12
  115.4 0.8 slice.42
  116.2 5.5 %collective-permute-start.5 = (bf16[6,128,256]{2,1,0:T(8,128)(2,1)}, bf16[6,128,256]{2,1,0:T(8,128)(2,1)}, u32[]{:S(2)}, u32[]{:S(2)}) collective-permute-start(bf16[6,128,256]{2,1,0:T(8,128)(2,1)} %slice.42), channel_id=1, source_target_pairs={{0,2},{2,4},{4,6},{6,8},{8,10},{10,12},{12,14},{14,16},{16,18},{18... | collective-permute-start | bytes 1179656 | tf_op jit(solution)/shard_map/ppermute | solution.py:25
  121.7 1.1 collective-permute-done.12
  122.8 1.0 select_add_fusion
  123.8 2.1 %collective-permute-start.14 = (f32[136,128]{1,0:T(8,128)S(1)}, f32[136,128]{1,0:T(8,128)S(1)}, u32[]{:S(2)}, u32[]{:S(2)}) collective-permute-start(f32[136,128]{1,0:T(8,128)S(1)} %select_add_fusion), channel_id=1, source_target_pairs={{0,4},{2,6},{4,0},{6,2},{8,12},{10,14},{12,8},{14,10},{16,20},{18,... | collective-permute-start | bytes 208904 | tf_op jit(solution)/shard_map/ppermute | solution.py:36
  125.9 7.0 %collective-permute-done.14 = f32[136,128]{1,0:T(8,128)S(1)} collective-permute-done((f32[136,128]{1,0:T(8,128)S(1)}, f32[136,128]{1,0:T(8,128)S(1)}, u32[]{:S(2)}, u32[]{:S(2)}) %collective-permute-start.14) | collective-permute-done | bytes 69664 | tf_op jit(solution)/shard_map/ppermute | solution.py:36
  132.9 4.3 %collective-permute-start.15 = (f32[136,128]{1,0:T(8,128)S(1)}, f32[136,128]{1,0:T(8,128)S(1)}, u32[]{:S(2)}, u32[]{:S(2)}) collective-permute-start(f32[136,128]{1,0:T(8,128)S(1)} %add.120), channel_id=1, source_target_pairs={{0,8},{2,10},{4,12},{6,14},{8,0},{10,2},{12,4},{14,6},{16,24},{18,... | collective-permute-start | bytes 208904 | tf_op jit(solution)/shard_map/ppermute | solution.py:36
  137.3 1.7 collective-permute-done.15
  139.0 0.6 add.121
  139.6 1.9 collective-permute-start.16
  141.5 7.3 %collective-permute-done.16 = f32[136,128]{1,0:T(8,128)} collective-permute-done((f32[136,128]{1,0:T(8,128)}, f32[136,128]{1,0:T(8,128)}, u32[]{:S(2)}, u32[]{:S(2)}) %collective-permute-start.16) | collective-permute-done | bytes 69664 | tf_op jit(solution)/shard_map/ppermute | solution.py:75
  148.9 0.9 add.122
  149.8 6.0 %collective-permute-start.17 = (f32[136,128]{1,0:T(8,128)S(1)}, f32[136,128]{1,0:T(8,128)S(1)}, u32[]{:S(2)}, u32[]{:S(2)}) collective-permute-start(f32[136,128]{1,0:T(8,128)S(1)} %add.122), channel_id=1, source_target_pairs={{0,192},{2,194},{4,196},{6,198},{8,200},{10,202},{12,204},{14,206}... | collective-permute-start | bytes 208904 | tf_op jit(solution)/shard_map/ppermute | solution.py:36
  155.8 0.0 collective-permute-done.5
  155.8 0.0 collective-permute-done.4
  155.8 2.3 %fusion.11 = f32[6,128,256]{2,1,0:T(8,128)} fusion(f32[6,128,256]{2,1,0:T(8,128)} %collective-permute-done.4, f32[18,128,256]{2,1,0:T(8,128)S(1)} %fusion.4, bf16[6,128,256]{2,1,0:T(8,128)(2,1)} %collective-permute-done.5), kind=kLoop, calls=%fused_computation.13 | loop fusion | flops 589824 | bytes 2752512 | tf_op jit(solution)/shard_map/add | solution.py:158
  158.1 2.1 %collective-permute-start.6 = (f32[6,128,256]{2,1,0:T(8,128)}, f32[6,128,256]{2,1,0:T(8,128)S(1)}, u32[]{:S(2)}, u32[]{:S(2)}) collective-permute-start(f32[6,128,256]{2,1,0:T(8,128)} %fusion.11), channel_id=1, source_target_pairs={{0,1},{1,0},{2,3},{3,2},{4,5},{5,4},{6,7},{7,6},{8,9},{9,8},{10,11... | collective-permute-start | bytes 2359304 | tf_op jit(solution)/shard_map/ppermute | solution.py:93
  160.3 8.0 %collective-permute-start.18 = (f32[272,128]{1,0:T(8,128)S(1)}, f32[272,128]{1,0:T(8,128)S(1)}, u32[]{:S(2)}, u32[]{:S(2)}) collective-permute-start(f32[272,128]{1,0:T(8,128)S(1)} %maximum_select_fusion.3), channel_id=1, source_target_pairs={{0,2},{2,0},{4,6},{6,4},{8,10},{10,8},{12,14},{14,12},{16,18},{18,... | collective-permute-start | bytes 417800 | tf_op jit(solution)/shard_map/ppermute | solution.py:36
  168.3 2.1 %maximum_select_fusion = bf16[768,256]{1,0:T(8,128)(2,1)} fusion(bf16[384,256]{1,0:T(8,128)(2,1)} %get-tuple-element.7, bf16[384,256]{1,0:T(8,128)(2,1)} %copy-done.2, pred[]{:T(512)S(6)} %eq.38), kind=kLoop, calls=%fused_computation.16 | loop fusion | flops 1769472 | bytes 786433 | tf_op jit(solution)/shard_map/jit(_where)/select_n | solution.py:87
  170.4 0.6 slice_multiply_fusion.1
  171.0 0.7 slice_multiply_fusion
  171.7 28.4 %collective-permute-done.6 = f32[6,128,256]{2,1,0:T(8,128)S(1)} collective-permute-done((f32[6,128,256]{2,1,0:T(8,128)}, f32[6,128,256]{2,1,0:T(8,128)S(1)}, u32[]{:S(2)}, u32[]{:S(2)}) %collective-permute-start.6) | collective-permute-done | bytes 786464 | tf_op jit(solution)/shard_map/ppermute | solution.py:93
  200.1 2.0 add_convert_fusion
  (25 shorter events, 0.2 us)
Async XLA Ops:
  0.6 6.4 %copy-start = (bf16[6,6,128,128]{3,2,1,0:T(8,128)(2,1)S(1)}, bf16[6,6,128,128]{3,2,1,0:T(8,128)(2,1)}, u32[]{:S(2)}) copy-start(bf16[6,6,128,128]{3,2,1,0:T(8,128)(2,1)} %param.8) | copy-start | bytes 3538948
  0.6 8.6 %collective-permute-start = (bf16[768,256]{1,0:T(8,128)(2,1)}, bf16[768,256]{1,0:T(8,128)(2,1)S(1)}, u32[]{:S(2)}, u32[]{:S(2)}) collective-permute-start(bf16[768,256]{1,0:T(8,128)(2,1)} %param.7), channel_id=1, source_target_pairs={{0,2},{2,4},{4,6},{6,8},{8,10},{10,12},{12,14},{14,16},{16,18},{18... | collective-permute-start | bytes 1179656 | tf_op jit(solution)/shard_map/ppermute | solution.py:14
  3.7 9.3 %collective-permute-start.1 = (bf16[768,256]{1,0:T(8,128)(2,1)}, bf16[768,256]{1,0:T(8,128)(2,1)S(1)}, u32[]{:S(2)}, u32[]{:S(2)}) collective-permute-start(bf16[768,256]{1,0:T(8,128)(2,1)} %param.7), channel_id=1, source_target_pairs={{2,0},{4,2},{6,4},{8,6},{10,8},{12,10},{14,12},{16,14},{18,16},{20... | collective-permute-start | bytes 1179656 | tf_op jit(solution)/shard_map/ppermute | solution.py:17
  7.0 5.9 %copy-start.3 = (bf16[768,256]{1,0:T(8,128)(2,1)S(1)}, bf16[768,256]{1,0:T(8,128)(2,1)}, u32[]{:S(2)}) copy-start(bf16[768,256]{1,0:T(8,128)(2,1)} %param.7) | copy-start | bytes 1179652
  9.3 4.9 %copy-start.1 = (bf16[6,18,128,128]{3,1,2,0:T(8,128)(2,1)}, bf16[6,18,128,128]{3,1,2,0:T(8,128)(2,1)S(1)}, u32[]{:S(2)}) copy-start(bf16[6,18,128,128]{3,1,2,0:T(8,128)(2,1)S(1)} %convolution_convert_fusion) | copy-start | bytes 10616836
  13.0 18.9 %copy-start.4 = (bf16[256,256]{1,0:T(8,128)(2,1)S(1)}, bf16[256,256]{1,0:T(8,128)(2,1)}, u32[]{:S(2)}) copy-start(bf16[256,256]{1,0:T(8,128)(2,1)} %param.11) | copy-start | bytes 393220
  13.1 18.9 %copy-start.5 = (bf16[768,256]{1,0:T(8,128)(2,1)S(1)}, bf16[768,256]{1,0:T(8,128)(2,1)}, u32[]{:S(2)}) copy-start(bf16[768,256]{1,0:T(8,128)(2,1)} %param.13) | copy-start | bytes 1179652
  13.1 18.9 %copy-start.6 = (f32[256]{0:T(256)S(1)}, f32[256]{0:T(256)}, u32[]{:S(2)}) copy-start(f32[256]{0:T(256)} %param.12) | copy-start | bytes 3076
  14.2 17.7 %collective-permute-start.2 = (f32[384,256]{1,0:T(8,128)S(1)}, f32[384,256]{1,0:T(8,128)S(1)}, u32[]{:S(2)}, u32[]{:S(2)}) collective-permute-start(f32[384,256]{1,0:T(8,128)S(1)} %constant_dynamic-slice_fusion.2), channel_id=1, source_target_pairs={{0,1},{1,0},{2,3},{3,2},{4,5},{5,4},{6,7},{7,6},{8,9},{9,8},{10,11... | collective-permute-start | bytes 1179656 | tf_op jit(solution)/shard_map/ppermute | solution.py:83
  32.4 3.1 %copy-start.2 = (bf16[384,256]{1,0:T(8,128)(2,1)}, bf16[384,256]{1,0:T(8,128)(2,1)S(1)}, u32[]{:S(2)}) copy-start(bf16[384,256]{1,0:T(8,128)(2,1)S(1)} %get-tuple-element.8) | copy-start | bytes 589828
  33.0 5.0 %collective-permute-start.7 = (f32[272,128]{1,0:T(8,128)S(1)}, f32[272,128]{1,0:T(8,128)S(1)}, u32[]{:S(2)}, u32[]{:S(2)}) collective-permute-start(f32[272,128]{1,0:T(8,128)S(1)} %constant_dynamic-slice_fusion.1), channel_id=1, source_target_pairs={{0,2},{2,0},{4,6},{6,4},{8,10},{10,8},{12,14},{14,12},{16,18},{18,... | collective-permute-start | bytes 417800 | tf_op jit(solution)/shard_map/ppermute | solution.py:36
  35.5 16.5 %collective-permute-start.3 = (bf16[384,512]{1,0:T(8,128)(2,1)S(1)}, bf16[384,512]{1,0:T(8,128)(2,1)S(1)}, u32[]{:S(2)}, u32[]{:S(2)}) collective-permute-start(bf16[384,512]{1,0:T(8,128)(2,1)S(1)} %pad_maximum_fusion.1), channel_id=1, source_target_pairs={{0,1},{1,0},{2,3},{3,2},{4,5},{5,4},{6,7},{7,6},{8,9},{9,8},{10,11... | collective-permute-start | bytes 1179656 | tf_op jit(solution)/shard_map/ppermute | solution.py:83
  38.1 22.1 %collective-permute-start.8 = (f32[136,128]{1,0:T(8,128)S(1)}, f32[136,128]{1,0:T(8,128)S(1)}, u32[]{:S(2)}, u32[]{:S(2)}) collective-permute-start(f32[136,128]{1,0:T(8,128)S(1)} %constant_dynamic-slice_fusion), channel_id=1, source_target_pairs={{0,192},{2,194},{4,196},{6,198},{8,200},{10,202},{12,204},{14,206}... | collective-permute-start | bytes 208904 | tf_op jit(solution)/shard_map/ppermute | solution.py:36
  57.4 98.4 %collective-permute-start.4 = (f32[6,128,256]{2,1,0:T(8,128)}, f32[6,128,256]{2,1,0:T(8,128)}, u32[]{:S(2)}, u32[]{:S(2)}) collective-permute-start(f32[6,128,256]{2,1,0:T(8,128)} %slice.32), channel_id=1, source_target_pairs={{2,0},{4,2},{6,4},{8,6},{10,8},{12,10},{14,12},{16,14},{18,16},{20... | collective-permute-start | bytes 2359304 | tf_op jit(solution)/shard_map/ppermute | solution.py:25
  60.2 9.8 %collective-permute-start.9 = (f32[136,128]{1,0:T(8,128)S(1)}, f32[136,128]{1,0:T(8,128)S(1)}, u32[]{:S(2)}, u32[]{:S(2)}) collective-permute-start(f32[136,128]{1,0:T(8,128)S(1)} %dynamic-slice_add_fusion.1), channel_id=1, source_target_pairs={{0,384},{2,386},{4,388},{6,390},{8,392},{10,394},{12,396},{14,398}... | collective-permute-start | bytes 208904 | tf_op jit(solution)/shard_map/ppermute | solution.py:36
  70.0 21.5 %collective-permute-start.10 = (f32[136,128]{1,0:T(8,128)S(1)}, f32[136,128]{1,0:T(8,128)S(1)}, u32[]{:S(2)}, u32[]{:S(2)}) collective-permute-start(f32[136,128]{1,0:T(8,128)S(1)} %add.115), channel_id=1, source_target_pairs={{0,16},{2,18},{4,20},{6,22},{8,24},{10,26},{12,28},{14,30},{16,0},... | collective-permute-start | bytes 208904 | tf_op jit(solution)/shard_map/ppermute | solution.py:36
  91.5 7.7 %collective-permute-start.11 = (f32[136,128]{1,0:T(8,128)S(1)}, f32[136,128]{1,0:T(8,128)S(1)}, u32[]{:S(2)}, u32[]{:S(2)}) collective-permute-start(f32[136,128]{1,0:T(8,128)S(1)} %add.116), channel_id=1, source_target_pairs={{0,32},{2,34},{4,36},{6,38},{8,40},{10,42},{12,44},{14,46},{16,48}... | collective-permute-start | bytes 208904 | tf_op jit(solution)/shard_map/ppermute | solution.py:36
  99.8 21.8 %collective-permute-start.13 = (f32[136,128]{1,0:T(8,128)}, f32[136,128]{1,0:T(8,128)}, u32[]{:S(2)}, u32[]{:S(2)}) collective-permute-start(f32[136,128]{1,0:T(8,128)} %add.117), channel_id=1, source_target_pairs={{0,128},{2,130},{4,132},{6,134},{8,136},{10,138},{12,140},{14,142}... | collective-permute-start | bytes 208904 | tf_op jit(solution)/shard_map/ppermute | solution.py:36
  113.4 9.4 %collective-permute-start.12 = (f32[136,128]{1,0:T(8,128)}, f32[136,128]{1,0:T(8,128)}, u32[]{:S(2)}, u32[]{:S(2)}) collective-permute-start(f32[136,128]{1,0:T(8,128)} %add.117), channel_id=1, source_target_pairs={{0,64},{2,66},{4,68},{6,70},{8,72},{10,74},{12,76},{14,78},{16,80}... | collective-permute-start | bytes 208904 | tf_op jit(solution)/shard_map/ppermute | solution.py:36
  116.2 39.7 %collective-permute-start.5 = (bf16[6,128,256]{2,1,0:T(8,128)(2,1)}, bf16[6,128,256]{2,1,0:T(8,128)(2,1)}, u32[]{:S(2)}, u32[]{:S(2)}) collective-permute-start(bf16[6,128,256]{2,1,0:T(8,128)(2,1)} %slice.42), channel_id=1, source_target_pairs={{0,2},{2,4},{4,6},{6,8},{8,10},{10,12},{12,14},{14,16},{16,18},{18... | collective-permute-start | bytes 1179656 | tf_op jit(solution)/shard_map/ppermute | solution.py:25
  123.8 9.2 %collective-permute-start.14 = (f32[136,128]{1,0:T(8,128)S(1)}, f32[136,128]{1,0:T(8,128)S(1)}, u32[]{:S(2)}, u32[]{:S(2)}) collective-permute-start(f32[136,128]{1,0:T(8,128)S(1)} %select_add_fusion), channel_id=1, source_target_pairs={{0,4},{2,6},{4,0},{6,2},{8,12},{10,14},{12,8},{14,10},{16,20},{18,... | collective-permute-start | bytes 208904 | tf_op jit(solution)/shard_map/ppermute | solution.py:36
  132.9 6.0 %collective-permute-start.15 = (f32[136,128]{1,0:T(8,128)S(1)}, f32[136,128]{1,0:T(8,128)S(1)}, u32[]{:S(2)}, u32[]{:S(2)}) collective-permute-start(f32[136,128]{1,0:T(8,128)S(1)} %add.120), channel_id=1, source_target_pairs={{0,8},{2,10},{4,12},{6,14},{8,0},{10,2},{12,4},{14,6},{16,24},{18,... | collective-permute-start | bytes 208904 | tf_op jit(solution)/shard_map/ppermute | solution.py:36
  139.6 9.3 %collective-permute-start.16 = (f32[136,128]{1,0:T(8,128)}, f32[136,128]{1,0:T(8,128)}, u32[]{:S(2)}, u32[]{:S(2)}) collective-permute-start(f32[136,128]{1,0:T(8,128)} %add.121), channel_id=1, source_target_pairs={{0,1},{1,0},{2,3},{3,2},{4,5},{5,4},{6,7},{7,6},{8,9},{9,8},{10,11... | collective-permute-start | bytes 208904 | tf_op jit(solution)/shard_map/ppermute | solution.py:75
  149.8 10.5 %collective-permute-start.17 = (f32[136,128]{1,0:T(8,128)S(1)}, f32[136,128]{1,0:T(8,128)S(1)}, u32[]{:S(2)}, u32[]{:S(2)}) collective-permute-start(f32[136,128]{1,0:T(8,128)S(1)} %add.122), channel_id=1, source_target_pairs={{0,192},{2,194},{4,196},{6,198},{8,200},{10,202},{12,204},{14,206}... | collective-permute-start | bytes 208904 | tf_op jit(solution)/shard_map/ppermute | solution.py:36
  158.1 42.0 %collective-permute-start.6 = (f32[6,128,256]{2,1,0:T(8,128)}, f32[6,128,256]{2,1,0:T(8,128)S(1)}, u32[]{:S(2)}, u32[]{:S(2)}) collective-permute-start(f32[6,128,256]{2,1,0:T(8,128)} %fusion.11), channel_id=1, source_target_pairs={{0,1},{1,0},{2,3},{3,2},{4,5},{5,4},{6,7},{7,6},{8,9},{9,8},{10,11... | collective-permute-start | bytes 2359304 | tf_op jit(solution)/shard_map/ppermute | solution.py:93
  160.3 10.1 %collective-permute-start.18 = (f32[272,128]{1,0:T(8,128)S(1)}, f32[272,128]{1,0:T(8,128)S(1)}, u32[]{:S(2)}, u32[]{:S(2)}) collective-permute-start(f32[272,128]{1,0:T(8,128)S(1)} %maximum_select_fusion.3), channel_id=1, source_target_pairs={{0,2},{2,0},{4,6},{6,4},{8,10},{10,8},{12,14},{14,12},{16,18},{18,... | collective-permute-start | bytes 417800 | tf_op jit(solution)/shard_map/ppermute | solution.py:36

commit v8 on v4

--- a/solution.py
+++ b/solution.py
@@ -124,7 +124,8 @@
     partial_sum = partial_sum.reshape(rows_here, feat_width)
     own_part = lax.dynamic_slice_in_dim(partial_sum, partner * half_rows, half_rows, 0)
     their_part = lax.dynamic_slice_in_dim(partial_sum, (1 - partner) * half_rows, half_rows, 0)
-    agg_half = (own_part + partner_swap(their_part)).astype(jnp.bfloat16)
+    their_sent = partner_swap(their_part.astype(jnp.bfloat16))
+    agg_half = (own_part + their_sent.astype(jnp.float32)).astype(jnp.bfloat16)
     grad_in = lax.dynamic_slice_in_dim(cotangent, partner * half_rows, half_rows, 0)
     act_half, grad_half, agg_grad_half = dense_part(agg_half, grad_in, weight, bias)
     sent = partner_swap(jnp.concatenate([act_half, agg_grad_half], 1))

time: 201 us -> 193 us (0.960)
  waiting for transfers between devices: 75.4 us -> 67.7 us
    ppermute x2, waiting for transfers between devices: 24.4 us -> 15.5 us  [partner_swap(): return lax.ppermute(x, 'rep', [(0, 1), (1, 0)])]
    ppermute x10, starting transfers between devices: 56 us -> 59.3 us  [moved(): return lax.ppermute(x, axis, pairs)]
    ppermute x1, starting transfers between devices: 13 us -> 9.93 us  [global_sum(): x = x + lax.ppermute(x, 'rep', [(0, 1), (1, 0)])]
    ppermute x10, waiting for transfers between devices: 20.2 us -> 23.1 us  [moved(): return lax.ppermute(x, axis, pairs)]
  transfers between devices with their start and end apart: 18 -> 18, of which waited for: 8 -> 10; matrix products, arithmetic and copies ran while one was open for 8% -> 9% of each run, Pallas kernels for 0% -> 0%
where the time goes in v8:
time: 193 us; the launch traced here: 190 us
  starting transfers between devices  99.8 us (52%)
  waiting for transfers between devices  67.7 us (35%)
  other arithmetic  11.2 us (6%)
  matrix products  7.69 us (4%)
  local copies, waits for them, and re-layouts  2.65 us (1%)
    ppermute x10, starting transfers between devices, moved(): return lax.ppermute(x, axis, pairs)  59.3 us
    ppermute x1, waiting for transfers between devices, partner_sum(): return x + lax.ppermute(x, 'rep', [(0, 1), (1, 0)])  29 us
    ppermute x10, waiting for transfers between devices, moved(): return lax.ppermute(x, axis, pairs)  23.1 us
    ppermute x2, waiting for transfers between devices, partner_swap(): return lax.ppermute(x, 'rep', [(0, 1), (1, 0)])  15.5 us
    ppermute x2, starting transfers between devices, from_behind(): return lax.ppermute(x, axis, pairs)  10.4 us
    ppermute x1, starting transfers between devices, global_sum(): x = x + lax.ppermute(x, 'rep', [(0, 1), (1, 0)])  9.93 us
    ppermute x1, starting transfers between devices, extended(): lax.ppermute(lax.slice_in_dim(block, 0, width, axis=dim), axis, backward)  9.15 us
    ppermute x1, starting transfers between devices, extended(): lax.ppermute(lax.slice_in_dim(block, block.shape[dim] - width, None, axis...  4.73 us
  transfers between devices with their start and end apart: 18, of which 10 were waited for; matrix products, arithmetic and copies ran while one was open for 9% of the time, Pallas kernels for 0%

profile of v8, /device:TPU:1, one launch (start us, length us, event | category | flops | bytes accessed | tf_op | source)
XLA Modules:
  0.0 190.2 jit_solution(6100495627093289614)
XLA Ops:
  0.6 0.0 copy-start
  0.6 4.7 %collective-permute-start = (bf16[768,256]{1,0:T(8,128)(2,1)}, bf16[768,256]{1,0:T(8,128)(2,1)S(1)}, u32[]{:S(2)}, u32[]{:S(2)}) collective-permute-start(bf16[768,256]{1,0:T(8,128)(2,1)} %param.7), channel_id=1, source_target_pairs={{0,2},{2,4},{4,6},{6,8},{8,10},{10,12},{12,14},{14,16},{16,18},{18... | collective-permute-start | bytes 1179656 | tf_op jit(solution)/shard_map/ppermute | solution.py:14
  5.4 9.1 %collective-permute-start.1 = (bf16[768,256]{1,0:T(8,128)(2,1)}, bf16[768,256]{1,0:T(8,128)(2,1)S(1)}, u32[]{:S(2)}, u32[]{:S(2)}) collective-permute-start(bf16[768,256]{1,0:T(8,128)(2,1)} %param.7), channel_id=1, source_target_pairs={{2,0},{4,2},{6,4},{8,6},{10,8},{12,10},{14,12},{16,14},{18,16},{20... | collective-permute-start | bytes 1179656 | tf_op jit(solution)/shard_map/ppermute | solution.py:17
  14.5 0.7 broadcast_subtract_fusion
  15.2 0.7 iota_compare_fusion.1
  16.0 0.0 copy-done
  16.0 2.2 %convolution_convert_fusion = bf16[6,18,128,128]{3,1,2,0:T(8,128)(2,1)S(1)} fusion(bf16[6,6,128,128]{3,2,1,0:T(8,128)(2,1)S(1)} %copy-done, s32[6,6]{1,0:T(8,128)S(1)} %broadcast_subtract_fusion, pred[6,6]{1,0:T(8,128)(4,1)S(1)} %iota_compare_fusion.1), kind=kOutput, calls=%fused_computation.4 | convolution fusion | flops 23004432 | bytes 4718772 | tf_op jit(solution)/shard_map/bks,bkij->bsij/dot_general | solution.py:118
  18.2 0.0 copy-start.1
  18.2 0.0 collective-permute-done
  18.2 0.0 collective-permute-done.1
  18.2 0.0 copy-done.3
  18.2 0.1 pad_maximum_fusion
  18.3 0.0 copy-start.4
  18.3 0.0 copy-start.5
  18.4 0.0 copy-start.6
  18.4 1.1 fusion.8
  19.5 0.9 copy-done.1
  20.4 2.1 %collective-permute-start.2 = (bf16[384,256]{1,0:T(8,128)(2,1)S(1)}, bf16[384,256]{1,0:T(8,128)(2,1)S(1)}, u32[]{:S(2)}, u32[]{:S(2)}) collective-permute-start(bf16[384,256]{1,0:T(8,128)(2,1)S(1)} %dynamic-slice_convert_fusion), channel_id=1, source_target_pairs={{0,1},{1,0},{2,3},{3,2},{4,5},{5,4},{6,7},{7,6},{8,9},{9,8},{10,11... | collective-permute-start | bytes 589832 | tf_op jit(solution)/shard_map/ppermute | solution.py:77
  22.5 13.4 %collective-permute-done.2 = bf16[384,256]{1,0:T(8,128)(2,1)S(1)} collective-permute-done((bf16[384,256]{1,0:T(8,128)(2,1)S(1)}, bf16[384,256]{1,0:T(8,128)(2,1)S(1)}, u32[]{:S(2)}, u32[]{:S(2)}) %collective-permute-start.2) | collective-permute-done | bytes 196640 | tf_op jit(solution)/shard_map/ppermute | solution.py:77
  36.0 0.1 add_convert_fusion.1
  36.1 0.4 convert_reduce_fusion
  36.4 0.3 fusion.21
  36.7 0.2 convolution_convert_fusion.1
  37.0 2.3 %collective-permute-start.7 = (f32[257,128]{1,0:T(8,128)S(1)}, f32[257,128]{1,0:T(8,128)S(1)}, u32[]{:S(2)}, u32[]{:S(2)}) collective-permute-start(f32[257,128]{1,0:T(8,128)S(1)} %fusion.12), channel_id=1, source_target_pairs={{0,2},{2,0},{4,6},{6,4},{8,10},{10,8},{12,14},{14,12},{16,18},{18,... | collective-permute-start | bytes 394760 | tf_op jit(solution)/shard_map/ppermute | solution.py:36
  39.3 2.2 %collective-permute-start.3 = (bf16[384,512]{1,0:T(8,128)(2,1)S(1)}, bf16[384,512]{1,0:T(8,128)(2,1)S(1)}, u32[]{:S(2)}, u32[]{:S(2)}) collective-permute-start(bf16[384,512]{1,0:T(8,128)(2,1)S(1)} %pad_maximum_fusion.1), channel_id=1, source_target_pairs={{0,1},{1,0},{2,3},{3,2},{4,5},{5,4},{6,7},{7,6},{8,9},{9,8},{10,11... | collective-permute-start | bytes 1179656 | tf_op jit(solution)/shard_map/ppermute | solution.py:77
  41.6 0.0 collective-permute-done.7
  41.6 8.9 %collective-permute-start.8 = (f32[257,128]{1,0:T(8,128)S(1)}, f32[257,128]{1,0:T(8,128)S(1)}, u32[]{:S(2)}, u32[]{:S(2)}) collective-permute-start(f32[257,128]{1,0:T(8,128)S(1)} %fusion.14), channel_id=1, source_target_pairs={{0,192},{2,194},{4,196},{6,198},{8,200},{10,202},{12,204},{14,206}... | collective-permute-start | bytes 394760 | tf_op jit(solution)/shard_map/ppermute | solution.py:36
  50.5 3.7 %collective-permute-done.8 = f32[257,128]{1,0:T(8,128)S(1)} collective-permute-done((f32[257,128]{1,0:T(8,128)S(1)}, f32[257,128]{1,0:T(8,128)S(1)}, u32[]{:S(2)}, u32[]{:S(2)}) %collective-permute-start.8) | collective-permute-done | bytes 131616 | tf_op jit(solution)/shard_map/ppermute | solution.py:36
  54.2 4.6 %collective-permute-start.9 = (f32[257,128]{1,0:T(8,128)S(1)}, f32[257,128]{1,0:T(8,128)S(1)}, u32[]{:S(2)}, u32[]{:S(2)}) collective-permute-start(f32[257,128]{1,0:T(8,128)S(1)} %add.97), channel_id=1, source_target_pairs={{0,384},{2,386},{4,388},{6,390},{8,392},{10,394},{12,396},{14,398}... | collective-permute-start | bytes 394760 | tf_op jit(solution)/shard_map/ppermute | solution.py:36
  58.8 2.1 %collective-permute-done.3 = bf16[384,512]{1,0:T(8,128)(2,1)S(1)} collective-permute-done((bf16[384,512]{1,0:T(8,128)(2,1)S(1)}, bf16[384,512]{1,0:T(8,128)(2,1)S(1)}, u32[]{:S(2)}, u32[]{:S(2)}) %collective-permute-start.3) | collective-permute-done | bytes 393248 | tf_op jit(solution)/shard_map/ppermute | solution.py:77
  60.9 0.7 fusion.20
  61.6 0.2 maximum_select_fusion.1
  61.8 0.2 collective-permute-done.9
  62.0 1.9 %collective-permute-start.10 = (f32[257,128]{1,0:T(8,128)S(1)}, f32[257,128]{1,0:T(8,128)S(1)}, u32[]{:S(2)}, u32[]{:S(2)}) collective-permute-start(f32[257,128]{1,0:T(8,128)S(1)} %add.98), channel_id=1, source_target_pairs={{0,16},{2,18},{4,20},{6,22},{8,24},{10,26},{12,28},{14,30},{16,0},... | collective-permute-start | bytes 394760 | tf_op jit(solution)/shard_map/ppermute | solution.py:36
  63.9 3.5 %fusion.4 = f32[18,128,256]{2,1,0:T(8,128)S(1)} fusion(bf16[6,128,256,1]{2,1,0,3:T(8,128)(2,1)S(1)} %bitcast.30, bf16[6,18,128,128]{3,1,2,0:T(8,128)(2,1)} %copy-done.1), kind=kOutput, calls=%fused_computation.5 | convolution fusion | flops 905969664 | bytes 6291456 | tf_op jit(solution)/shard_map/bsij,bif->sjf/dot_general | solution.py:145
  67.4 1.0 slice.32
  68.4 3.6 %collective-permute-start.4 = (f32[6,128,256]{2,1,0:T(8,128)}, f32[6,128,256]{2,1,0:T(8,128)}, u32[]{:S(2)}, u32[]{:S(2)}) collective-permute-start(f32[6,128,256]{2,1,0:T(8,128)} %slice.32), channel_id=1, source_target_pairs={{2,0},{4,2},{6,4},{8,6},{10,8},{12,10},{14,12},{16,14},{18,16},{20... | collective-permute-start | bytes 2359304 | tf_op jit(solution)/shard_map/ppermute | solution.py:25
  72.0 0.0 collective-permute-done.10
  72.0 5.7 %collective-permute-start.11 = (f32[257,128]{1,0:T(8,128)S(1)}, f32[257,128]{1,0:T(8,128)S(1)}, u32[]{:S(2)}, u32[]{:S(2)}) collective-permute-start(f32[257,128]{1,0:T(8,128)S(1)} %add.99), channel_id=1, source_target_pairs={{0,32},{2,34},{4,36},{6,38},{8,40},{10,42},{12,44},{14,46},{16,48}... | collective-permute-start | bytes 394760 | tf_op jit(solution)/shard_map/ppermute | solution.py:36
  77.7 5.2 %collective-permute-done.11 = f32[257,128]{1,0:T(8,128)S(1)} collective-permute-done((f32[257,128]{1,0:T(8,128)S(1)}, f32[257,128]{1,0:T(8,128)S(1)}, u32[]{:S(2)}, u32[]{:S(2)}) %collective-permute-start.11) | collective-permute-done | bytes 131616 | tf_op jit(solution)/shard_map/ppermute | solution.py:36
  82.9 0.7 add.100
  83.6 14.0 %collective-permute-start.13 = (f32[257,128]{1,0:T(8,128)}, f32[257,128]{1,0:T(8,128)}, u32[]{:S(2)}, u32[]{:S(2)}) collective-permute-start(f32[257,128]{1,0:T(8,128)} %add.100), channel_id=1, source_target_pairs={{0,128},{2,130},{4,132},{6,134},{8,136},{10,138},{12,140},{14,142}... | collective-permute-start | bytes 394760 | tf_op jit(solution)/shard_map/ppermute | solution.py:36
  97.6 1.9 %collective-permute-start.12 = (f32[257,128]{1,0:T(8,128)}, f32[257,128]{1,0:T(8,128)}, u32[]{:S(2)}, u32[]{:S(2)}) collective-permute-start(f32[257,128]{1,0:T(8,128)} %add.100), channel_id=1, source_target_pairs={{0,64},{2,66},{4,68},{6,70},{8,72},{10,74},{12,76},{14,78},{16,80}... | collective-permute-start | bytes 394760 | tf_op jit(solution)/shard_map/ppermute | solution.py:36
  99.6 6.8 %collective-permute-start.5 = (bf16[6,128,256]{2,1,0:T(8,128)(2,1)S(1)}, bf16[6,128,256]{2,1,0:T(8,128)(2,1)S(1)}, u32[]{:S(2)}, u32[]{:S(2)}) collective-permute-start(bf16[6,128,256]{2,1,0:T(8,128)(2,1)S(1)} %slice.42), channel_id=1, source_target_pairs={{0,2},{2,4},{4,6},{6,8},{8,10},{10,12},{12,14},{14,16},{16,18},{18... | collective-permute-start | bytes 1179656 | tf_op jit(solution)/shard_map/ppermute | solution.py:25
  106.4 0.2 collective-permute-done.13
  106.7 3.0 %collective-permute-done.12 = f32[257,128]{1,0:T(8,128)} collective-permute-done((f32[257,128]{1,0:T(8,128)}, f32[257,128]{1,0:T(8,128)}, u32[]{:S(2)}, u32[]{:S(2)}) %collective-permute-start.12) | collective-permute-done | bytes 131616 | tf_op jit(solution)/shard_map/ppermute | solution.py:36
  109.7 1.1 select_add_fusion
  110.8 12.6 %collective-permute-start.14 = (f32[257,128]{1,0:T(8,128)S(1)}, f32[257,128]{1,0:T(8,128)S(1)}, u32[]{:S(2)}, u32[]{:S(2)}) collective-permute-start(f32[257,128]{1,0:T(8,128)S(1)} %select_add_fusion), channel_id=1, source_target_pairs={{0,4},{2,6},{4,0},{6,2},{8,12},{10,14},{12,8},{14,10},{16,20},{18,... | collective-permute-start | bytes 394760 | tf_op jit(solution)/shard_map/ppermute | solution.py:36
  123.4 3.2 %collective-permute-done.14 = f32[257,128]{1,0:T(8,128)S(1)} collective-permute-done((f32[257,128]{1,0:T(8,128)S(1)}, f32[257,128]{1,0:T(8,128)S(1)}, u32[]{:S(2)}, u32[]{:S(2)}) %collective-permute-start.14) | collective-permute-done | bytes 131616 | tf_op jit(solution)/shard_map/ppermute | solution.py:36
  126.6 2.5 %collective-permute-start.15 = (f32[257,128]{1,0:T(8,128)S(1)}, f32[257,128]{1,0:T(8,128)S(1)}, u32[]{:S(2)}, u32[]{:S(2)}) collective-permute-start(f32[257,128]{1,0:T(8,128)S(1)} %add.103), channel_id=1, source_target_pairs={{0,8},{2,10},{4,12},{6,14},{8,0},{10,2},{12,4},{14,6},{16,24},{18,... | collective-permute-start | bytes 394760 | tf_op jit(solution)/shard_map/ppermute | solution.py:36
  129.1 7.5 %collective-permute-done.15 = f32[257,128]{1,0:T(8,128)S(1)} collective-permute-done((f32[257,128]{1,0:T(8,128)S(1)}, f32[257,128]{1,0:T(8,128)S(1)}, u32[]{:S(2)}, u32[]{:S(2)}) %collective-permute-start.15) | collective-permute-done | bytes 131616 | tf_op jit(solution)/shard_map/ppermute | solution.py:36
  136.6 9.9 %collective-permute-start.16 = (f32[257,128]{1,0:T(8,128)S(1)}, f32[257,128]{1,0:T(8,128)S(1)}, u32[]{:S(2)}, u32[]{:S(2)}) collective-permute-start(f32[257,128]{1,0:T(8,128)S(1)} %add.104), channel_id=1, source_target_pairs={{0,1},{1,0},{2,3},{3,2},{4,5},{5,4},{6,7},{7,6},{8,9},{9,8},{10,11... | collective-permute-start | bytes 394760 | tf_op jit(solution)/shard_map/ppermute | solution.py:71
  146.6 0.0 collective-permute-done.5
  146.6 0.0 collective-permute-done.4
  146.6 2.2 %fusion.11 = f32[6,128,256]{2,1,0:T(8,128)} fusion(f32[6,128,256]{2,1,0:T(8,128)} %collective-permute-done.4, f32[18,128,256]{2,1,0:T(8,128)S(1)} %fusion.4, bf16[6,128,256]{2,1,0:T(8,128)(2,1)S(1)} %collective-permute-done.5), kind=kLoop, calls=%fused_computation.13 | loop fusion | flops 589824 | bytes 2752512 | tf_op jit(solution)/shard_map/add | solution.py:152
  148.8 1.9 %collective-permute-start.6 = (f32[6,128,256]{2,1,0:T(8,128)}, f32[6,128,256]{2,1,0:T(8,128)S(1)}, u32[]{:S(2)}, u32[]{:S(2)}) collective-permute-start(f32[6,128,256]{2,1,0:T(8,128)} %fusion.11), channel_id=1, source_target_pairs={{0,1},{1,0},{2,3},{3,2},{4,5},{5,4},{6,7},{7,6},{8,9},{9,8},{10,11... | collective-permute-start | bytes 2359304 | tf_op jit(solution)/shard_map/ppermute | solution.py:87
  150.7 0.0 collective-permute-done.16
  150.8 5.0 %collective-permute-start.17 = (f32[257,128]{1,0:T(8,128)S(1)}, f32[257,128]{1,0:T(8,128)S(1)}, u32[]{:S(2)}, u32[]{:S(2)}) collective-permute-start(f32[257,128]{1,0:T(8,128)S(1)} %add.105), channel_id=1, source_target_pairs={{0,2},{2,0},{4,6},{6,4},{8,10},{10,8},{12,14},{14,12},{16,18},{18,... | collective-permute-start | bytes 394760 | tf_op jit(solution)/shard_map/ppermute | solution.py:36
  155.8 2.1 %maximum_select_fusion = bf16[768,256]{1,0:T(8,128)(2,1)} fusion(bf16[384,256]{1,0:T(8,128)(2,1)} %get-tuple-element.7, bf16[384,256]{1,0:T(8,128)(2,1)} %copy-done.2, pred[]{:T(512)S(6)} %eq.17), kind=kLoop, calls=%fused_computation.16 | loop fusion | flops 1769472 | bytes 786433 | tf_op jit(solution)/shard_map/jit(_where)/select_n | solution.py:81
  157.8 0.0 collective-permute-done.17
  157.9 0.6 slice_multiply_fusion.1
  158.5 0.7 slice_multiply_fusion
  159.2 29.0 %collective-permute-done.6 = f32[6,128,256]{2,1,0:T(8,128)S(1)} collective-permute-done((f32[6,128,256]{2,1,0:T(8,128)}, f32[6,128,256]{2,1,0:T(8,128)S(1)}, u32[]{:S(2)}, u32[]{:S(2)}) %collective-permute-start.6) | collective-permute-done | bytes 786464 | tf_op jit(solution)/shard_map/ppermute | solution.py:87
  188.2 2.0 %add_convert_fusion = bf16[6,128,256]{2,1,0:T(8,128)(2,1)} fusion(f32[6,128,256]{2,1,0:T(8,128)} %fusion.11, f32[6,128,256]{2,1,0:T(8,128)S(1)} %collective-permute-done.6), kind=kLoop, calls=%fused_computation.14 | loop fusion | flops 393216 | bytes 1966080 | tf_op jit(solution)/shard_map/convert_element_type | solution.py:154
  (18 shorter events, 0.3 us)
Async XLA Ops:
  0.6 15.3 %copy-start = (bf16[6,6,128,128]{3,2,1,0:T(8,128)(2,1)S(1)}, bf16[6,6,128,128]{3,2,1,0:T(8,128)(2,1)}, u32[]{:S(2)}) copy-start(bf16[6,6,128,128]{3,2,1,0:T(8,128)(2,1)} %param.8) | copy-start | bytes 3538948
  0.6 17.6 %collective-permute-start = (bf16[768,256]{1,0:T(8,128)(2,1)}, bf16[768,256]{1,0:T(8,128)(2,1)S(1)}, u32[]{:S(2)}, u32[]{:S(2)}) collective-permute-start(bf16[768,256]{1,0:T(8,128)(2,1)} %param.7), channel_id=1, source_target_pairs={{0,2},{2,4},{4,6},{6,8},{8,10},{10,12},{12,14},{14,16},{16,18},{18... | collective-permute-start | bytes 1179656 | tf_op jit(solution)/shard_map/ppermute | solution.py:14
  5.4 12.8 %collective-permute-start.1 = (bf16[768,256]{1,0:T(8,128)(2,1)}, bf16[768,256]{1,0:T(8,128)(2,1)S(1)}, u32[]{:S(2)}, u32[]{:S(2)}) collective-permute-start(bf16[768,256]{1,0:T(8,128)(2,1)} %param.7), channel_id=1, source_target_pairs={{2,0},{4,2},{6,4},{8,6},{10,8},{12,10},{14,12},{16,14},{18,16},{20... | collective-permute-start | bytes 1179656 | tf_op jit(solution)/shard_map/ppermute | solution.py:17
  16.0 2.3 %copy-start.3 = (bf16[768,256]{1,0:T(8,128)(2,1)S(1)}, bf16[768,256]{1,0:T(8,128)(2,1)}, u32[]{:S(2)}) copy-start(bf16[768,256]{1,0:T(8,128)(2,1)} %param.7) | copy-start | bytes 1179652
  18.2 2.1 %copy-start.1 = (bf16[6,18,128,128]{3,1,2,0:T(8,128)(2,1)}, bf16[6,18,128,128]{3,1,2,0:T(8,128)(2,1)S(1)}, u32[]{:S(2)}) copy-start(bf16[6,18,128,128]{3,1,2,0:T(8,128)(2,1)S(1)} %convolution_convert_fusion) | copy-start | bytes 10616836
  18.3 17.7 %copy-start.4 = (bf16[256,256]{1,0:T(8,128)(2,1)S(1)}, bf16[256,256]{1,0:T(8,128)(2,1)}, u32[]{:S(2)}) copy-start(bf16[256,256]{1,0:T(8,128)(2,1)} %param.11) | copy-start | bytes 393220
  18.3 17.7 %copy-start.5 = (bf16[768,256]{1,0:T(8,128)(2,1)S(1)}, bf16[768,256]{1,0:T(8,128)(2,1)}, u32[]{:S(2)}) copy-start(bf16[768,256]{1,0:T(8,128)(2,1)} %param.13) | copy-start | bytes 1179652
  18.4 17.7 %copy-start.6 = (f32[256]{0:T(256)S(1)}, f32[256]{0:T(256)}, u32[]{:S(2)}) copy-start(f32[256]{0:T(256)} %param.12) | copy-start | bytes 3076
  20.4 15.6 %collective-permute-start.2 = (bf16[384,256]{1,0:T(8,128)(2,1)S(1)}, bf16[384,256]{1,0:T(8,128)(2,1)S(1)}, u32[]{:S(2)}, u32[]{:S(2)}) collective-permute-start(bf16[384,256]{1,0:T(8,128)(2,1)S(1)} %dynamic-slice_convert_fusion), channel_id=1, source_target_pairs={{0,1},{1,0},{2,3},{3,2},{4,5},{5,4},{6,7},{7,6},{8,9},{9,8},{10,11... | collective-permute-start | bytes 589832 | tf_op jit(solution)/shard_map/ppermute | solution.py:77
  36.4 2.9 %copy-start.2 = (bf16[384,256]{1,0:T(8,128)(2,1)}, bf16[384,256]{1,0:T(8,128)(2,1)S(1)}, u32[]{:S(2)}) copy-start(bf16[384,256]{1,0:T(8,128)(2,1)S(1)} %get-tuple-element.8) | copy-start | bytes 589828
  37.0 4.6 %collective-permute-start.7 = (f32[257,128]{1,0:T(8,128)S(1)}, f32[257,128]{1,0:T(8,128)S(1)}, u32[]{:S(2)}, u32[]{:S(2)}) collective-permute-start(f32[257,128]{1,0:T(8,128)S(1)} %fusion.12), channel_id=1, source_target_pairs={{0,2},{2,0},{4,6},{6,4},{8,10},{10,8},{12,14},{14,12},{16,18},{18,... | collective-permute-start | bytes 394760 | tf_op jit(solution)/shard_map/ppermute | solution.py:36
  39.3 21.5 %collective-permute-start.3 = (bf16[384,512]{1,0:T(8,128)(2,1)S(1)}, bf16[384,512]{1,0:T(8,128)(2,1)S(1)}, u32[]{:S(2)}, u32[]{:S(2)}) collective-permute-start(bf16[384,512]{1,0:T(8,128)(2,1)S(1)} %pad_maximum_fusion.1), channel_id=1, source_target_pairs={{0,1},{1,0},{2,3},{3,2},{4,5},{5,4},{6,7},{7,6},{8,9},{9,8},{10,11... | collective-permute-start | bytes 1179656 | tf_op jit(solution)/shard_map/ppermute | solution.py:77
  41.6 12.6 %collective-permute-start.8 = (f32[257,128]{1,0:T(8,128)S(1)}, f32[257,128]{1,0:T(8,128)S(1)}, u32[]{:S(2)}, u32[]{:S(2)}) collective-permute-start(f32[257,128]{1,0:T(8,128)S(1)} %fusion.14), channel_id=1, source_target_pairs={{0,192},{2,194},{4,196},{6,198},{8,200},{10,202},{12,204},{14,206}... | collective-permute-start | bytes 394760 | tf_op jit(solution)/shard_map/ppermute | solution.py:36
  54.2 7.7 %collective-permute-start.9 = (f32[257,128]{1,0:T(8,128)S(1)}, f32[257,128]{1,0:T(8,128)S(1)}, u32[]{:S(2)}, u32[]{:S(2)}) collective-permute-start(f32[257,128]{1,0:T(8,128)S(1)} %add.97), channel_id=1, source_target_pairs={{0,384},{2,386},{4,388},{6,390},{8,392},{10,394},{12,396},{14,398}... | collective-permute-start | bytes 394760 | tf_op jit(solution)/shard_map/ppermute | solution.py:36
  62.0 10.0 %collective-permute-start.10 = (f32[257,128]{1,0:T(8,128)S(1)}, f32[257,128]{1,0:T(8,128)S(1)}, u32[]{:S(2)}, u32[]{:S(2)}) collective-permute-start(f32[257,128]{1,0:T(8,128)S(1)} %add.98), channel_id=1, source_target_pairs={{0,16},{2,18},{4,20},{6,22},{8,24},{10,26},{12,28},{14,30},{16,0},... | collective-permute-start | bytes 394760 | tf_op jit(solution)/shard_map/ppermute | solution.py:36
  68.4 78.2 %collective-permute-start.4 = (f32[6,128,256]{2,1,0:T(8,128)}, f32[6,128,256]{2,1,0:T(8,128)}, u32[]{:S(2)}, u32[]{:S(2)}) collective-permute-start(f32[6,128,256]{2,1,0:T(8,128)} %slice.32), channel_id=1, source_target_pairs={{2,0},{4,2},{6,4},{8,6},{10,8},{12,10},{14,12},{16,14},{18,16},{20... | collective-permute-start | bytes 2359304 | tf_op jit(solution)/shard_map/ppermute | solution.py:25
  72.0 10.9 %collective-permute-start.11 = (f32[257,128]{1,0:T(8,128)S(1)}, f32[257,128]{1,0:T(8,128)S(1)}, u32[]{:S(2)}, u32[]{:S(2)}) collective-permute-start(f32[257,128]{1,0:T(8,128)S(1)} %add.99), channel_id=1, source_target_pairs={{0,32},{2,34},{4,36},{6,38},{8,40},{10,42},{12,44},{14,46},{16,48}... | collective-permute-start | bytes 394760 | tf_op jit(solution)/shard_map/ppermute | solution.py:36
  83.6 23.1 %collective-permute-start.13 = (f32[257,128]{1,0:T(8,128)}, f32[257,128]{1,0:T(8,128)}, u32[]{:S(2)}, u32[]{:S(2)}) collective-permute-start(f32[257,128]{1,0:T(8,128)} %add.100), channel_id=1, source_target_pairs={{0,128},{2,130},{4,132},{6,134},{8,136},{10,138},{12,140},{14,142}... | collective-permute-start | bytes 394760 | tf_op jit(solution)/shard_map/ppermute | solution.py:36
  97.6 12.1 %collective-permute-start.12 = (f32[257,128]{1,0:T(8,128)}, f32[257,128]{1,0:T(8,128)}, u32[]{:S(2)}, u32[]{:S(2)}) collective-permute-start(f32[257,128]{1,0:T(8,128)} %add.100), channel_id=1, source_target_pairs={{0,64},{2,66},{4,68},{6,70},{8,72},{10,74},{12,76},{14,78},{16,80}... | collective-permute-start | bytes 394760 | tf_op jit(solution)/shard_map/ppermute | solution.py:36
  99.6 47.0 %collective-permute-start.5 = (bf16[6,128,256]{2,1,0:T(8,128)(2,1)S(1)}, bf16[6,128,256]{2,1,0:T(8,128)(2,1)S(1)}, u32[]{:S(2)}, u32[]{:S(2)}) collective-permute-start(bf16[6,128,256]{2,1,0:T(8,128)(2,1)S(1)} %slice.42), channel_id=1, source_target_pairs={{0,2},{2,4},{4,6},{6,8},{8,10},{10,12},{12,14},{14,16},{16,18},{18... | collective-permute-start | bytes 1179656 | tf_op jit(solution)/shard_map/ppermute | solution.py:25
  110.8 15.8 %collective-permute-start.14 = (f32[257,128]{1,0:T(8,128)S(1)}, f32[257,128]{1,0:T(8,128)S(1)}, u32[]{:S(2)}, u32[]{:S(2)}) collective-permute-start(f32[257,128]{1,0:T(8,128)S(1)} %select_add_fusion), channel_id=1, source_target_pairs={{0,4},{2,6},{4,0},{6,2},{8,12},{10,14},{12,8},{14,10},{16,20},{18,... | collective-permute-start | bytes 394760 | tf_op jit(solution)/shard_map/ppermute | solution.py:36
  126.6 10.0 %collective-permute-start.15 = (f32[257,128]{1,0:T(8,128)S(1)}, f32[257,128]{1,0:T(8,128)S(1)}, u32[]{:S(2)}, u32[]{:S(2)}) collective-permute-start(f32[257,128]{1,0:T(8,128)S(1)} %add.103), channel_id=1, source_target_pairs={{0,8},{2,10},{4,12},{6,14},{8,0},{10,2},{12,4},{14,6},{16,24},{18,... | collective-permute-start | bytes 394760 | tf_op jit(solution)/shard_map/ppermute | solution.py:36
  136.6 14.1 %collective-permute-start.16 = (f32[257,128]{1,0:T(8,128)S(1)}, f32[257,128]{1,0:T(8,128)S(1)}, u32[]{:S(2)}, u32[]{:S(2)}) collective-permute-start(f32[257,128]{1,0:T(8,128)S(1)} %add.104), channel_id=1, source_target_pairs={{0,1},{1,0},{2,3},{3,2},{4,5},{5,4},{6,7},{7,6},{8,9},{9,8},{10,11... | collective-permute-start | bytes 394760 | tf_op jit(solution)/shard_map/ppermute | solution.py:71
  148.8 39.4 %collective-permute-start.6 = (f32[6,128,256]{2,1,0:T(8,128)}, f32[6,128,256]{2,1,0:T(8,128)S(1)}, u32[]{:S(2)}, u32[]{:S(2)}) collective-permute-start(f32[6,128,256]{2,1,0:T(8,128)} %fusion.11), channel_id=1, source_target_pairs={{0,1},{1,0},{2,3},{3,2},{4,5},{5,4},{6,7},{7,6},{8,9},{9,8},{10,11... | collective-permute-start | bytes 2359304 | tf_op jit(solution)/shard_map/ppermute | solution.py:87
  150.8 7.1 %collective-permute-start.17 = (f32[257,128]{1,0:T(8,128)S(1)}, f32[257,128]{1,0:T(8,128)S(1)}, u32[]{:S(2)}, u32[]{:S(2)}) collective-permute-start(f32[257,128]{1,0:T(8,128)S(1)} %add.105), channel_id=1, source_target_pairs={{0,2},{2,0},{4,6},{6,4},{8,10},{10,8},{12,14},{14,12},{16,18},{18,... | collective-permute-start | bytes 394760 | tf_op jit(solution)/shard_map/ppermute | solution.py:36

commit v9 on v8

--- a/solution.py
+++ b/solution.py
@@ -40,6 +40,18 @@
     return x + moved(x, axis, count, stride, size, lambda c: c ^ bit)
 
 
+def ring_sum(x, axis, count, stride, size):
+    coord = (lax.axis_index(axis) // stride) % size
+    parts = [x] + [
+        moved(x, axis, count, stride, size, lambda c, k=k: (c - k) % size) for k in range(1, size)
+    ]
+    stacked = jnp.stack(parts)
+    total = lax.dynamic_index_in_dim(stacked, (0 - coord) % size, 0, keepdims=False)
+    for position in range(1, size):
+        total = total + lax.dynamic_index_in_dim(stacked, (position - coord) % size, 0, keepdims=False)
+    return total
+
+
 def three_way_sum(x, axis, count, stride, size):
     third = size // 3
     ahead = moved(x, axis, count, stride, size, lambda c: (c + third) % size)
@@ -61,8 +73,7 @@
     keep = lax.dynamic_slice_in_dim(x, core * width, width, 1)
     give = lax.dynamic_slice_in_dim(x, (1 - core) * width, width, 1)
     x = keep + moved(give, "rows", count, c_stride, c_size, lambda c: c ^ 1)
-    x = swapped_sum(x, "rows", count, x_stride, x_size, 1)
-    x = swapped_sum(x, "rows", count, x_stride, x_size, 2)
+    x = ring_sum(x, "rows", count, x_stride, x_size)
     x = swapped_sum(x, "rows", count, z_stride, z_size, 1)
     x = swapped_sum(x, "rows", count, z_stride, z_size, 2)
     x = three_way_sum(x, "rows", count, z_stride, z_size)

time: 193 us -> 186 us (0.964); the launches traced: 190 us -> 185 us
  starting transfers between devices: 99.8 us -> 93.8 us
    ppermute x1, starting transfers between devices: 9.93 us -> 1.92 us  [global_sum(): x = x + lax.ppermute(x, 'rep', [(0, 1), (1, 0)])]
    ppermute x10 -> x11, waiting for transfers between devices: 23.1 us -> 28.6 us  [moved(): return lax.ppermute(x, axis, pairs)]
    ppermute x1, starting transfers between devices: 1.91 us -> 7.26 us  [partner_sum(): return x + lax.ppermute(x, 'rep', [(0, 1), (1, 0)])]
    ppermute x10 -> x11, starting transfers between devices: 59.3 us -> 56.6 us  [moved(): return lax.ppermute(x, axis, pairs)]
    ppermute x1, waiting for transfers between devices: 29 us -> 26.4 us  [partner_sum(): return x + lax.ppermute(x, 'rep', [(0, 1), (1, 0)])]
    ppermute x2, waiting for transfers between devices: 15.5 us -> 13.4 us  [partner_swap(): return lax.ppermute(x, 'rep', [(0, 1), (1, 0)])]
  transfers between devices with their start and end apart: 18 -> 19, of which waited for: 10 -> 8; matrix products, arithmetic and copies ran while one was open for 9% -> 9% of each run, Pallas kernels for 0% -> 0%
where the time goes in v9:
time: 186 us; the launch traced here: 185 us
  starting transfers between devices  93.8 us (50%)
  waiting for transfers between devices  68.4 us (37%)
  other arithmetic  11.3 us (6%)
  matrix products  7.69 us (4%)
  local copies, waits for them, and re-layouts  2.68 us (1%)
    ppermute x11, starting transfers between devices, moved(): return lax.ppermute(x, axis, pairs)  56.6 us
    ppermute x11, waiting for transfers between devices, moved(): return lax.ppermute(x, axis, pairs)  28.6 us
    ppermute x1, waiting for transfers between devices, partner_sum(): return x + lax.ppermute(x, 'rep', [(0, 1), (1, 0)])  26.4 us
    ppermute x2, waiting for transfers between devices, partner_swap(): return lax.ppermute(x, 'rep', [(0, 1), (1, 0)])  13.4 us
    ppermute x2, starting transfers between devices, from_behind(): return lax.ppermute(x, axis, pairs)  9.83 us
    ppermute x1, starting transfers between devices, extended(): lax.ppermute(lax.slice_in_dim(block, 0, width, axis=dim), axis, backward)  9.15 us
    ppermute x1, starting transfers between devices, partner_sum(): return x + lax.ppermute(x, 'rep', [(0, 1), (1, 0)])  7.26 us
    ppermute x1, starting transfers between devices, extended(): lax.ppermute(lax.slice_in_dim(block, block.shape[dim] - width, None, axis...  4.73 us
  transfers between devices with their start and end apart: 19, of which 8 were waited for; matrix products, arithmetic and copies ran while one was open for 9% of the time, Pallas kernels for 0%

profile of v9, /device:TPU:1, one launch (start us, length us, event | category | flops | bytes accessed | tf_op | source)
XLA Modules:
  0.0 185.2 jit_solution(8369371301080135332)
XLA Ops:
  0.6 0.0 copy-start
  0.6 4.7 %collective-permute-start = (bf16[768,256]{1,0:T(8,128)(2,1)}, bf16[768,256]{1,0:T(8,128)(2,1)S(1)}, u32[]{:S(2)}, u32[]{:S(2)}) collective-permute-start(bf16[768,256]{1,0:T(8,128)(2,1)} %param.7), channel_id=1, source_target_pairs={{0,2},{2,4},{4,6},{6,8},{8,10},{10,12},{12,14},{14,16},{16,18},{18... | collective-permute-start | bytes 1179656 | tf_op jit(solution)/shard_map/ppermute | solution.py:14
  5.4 9.1 %collective-permute-start.1 = (bf16[768,256]{1,0:T(8,128)(2,1)}, bf16[768,256]{1,0:T(8,128)(2,1)S(1)}, u32[]{:S(2)}, u32[]{:S(2)}) collective-permute-start(bf16[768,256]{1,0:T(8,128)(2,1)} %param.7), channel_id=1, source_target_pairs={{2,0},{4,2},{6,4},{8,6},{10,8},{12,10},{14,12},{16,14},{18,16},{20... | collective-permute-start | bytes 1179656 | tf_op jit(solution)/shard_map/ppermute | solution.py:17
  14.5 0.7 broadcast_subtract_fusion
  15.2 0.7 iota_compare_fusion.1
  16.0 2.2 %convolution_convert_fusion = bf16[6,18,128,128]{3,1,2,0:T(8,128)(2,1)S(1)} fusion(bf16[6,6,128,128]{3,2,1,0:T(8,128)(2,1)S(1)} %copy-done, s32[6,6]{1,0:T(8,128)S(1)} %broadcast_subtract_fusion, pred[6,6]{1,0:T(8,128)(4,1)S(1)} %iota_compare_fusion.1), kind=kOutput, calls=%fused_computation.4 | convolution fusion | flops 23004432 | bytes 4718772 | tf_op jit(solution)/shard_map/bks,bkij->bsij/dot_general | solution.py:129
  18.2 0.0 collective-permute-done
  18.2 0.0 collective-permute-done.1
  18.2 0.1 pad_maximum_fusion
  18.3 0.0 copy-start.4
  18.3 0.0 copy-start.5
  18.4 0.0 copy-start.6
  18.4 1.1 fusion.8
  19.5 0.9 copy-done.1
  20.4 2.1 %collective-permute-start.2 = (bf16[384,256]{1,0:T(8,128)(2,1)S(1)}, bf16[384,256]{1,0:T(8,128)(2,1)S(1)}, u32[]{:S(2)}, u32[]{:S(2)}) collective-permute-start(bf16[384,256]{1,0:T(8,128)(2,1)S(1)} %dynamic-slice_convert_fusion), channel_id=1, source_target_pairs={{0,1},{1,0},{2,3},{3,2},{4,5},{5,4},{6,7},{7,6},{8,9},{9,8},{10,11... | collective-permute-start | bytes 589832 | tf_op jit(solution)/shard_map/ppermute | solution.py:88
  22.5 13.4 %collective-permute-done.2 = bf16[384,256]{1,0:T(8,128)(2,1)S(1)} collective-permute-done((bf16[384,256]{1,0:T(8,128)(2,1)S(1)}, bf16[384,256]{1,0:T(8,128)(2,1)S(1)}, u32[]{:S(2)}, u32[]{:S(2)}) %collective-permute-start.2) | collective-permute-done | bytes 196640 | tf_op jit(solution)/shard_map/ppermute | solution.py:88
  36.0 0.1 add_convert_fusion.1
  36.1 0.4 convert_reduce_fusion
  36.4 0.3 fusion.21
  36.7 2.3 %collective-permute-start.7 = (f32[257,128]{1,0:T(8,128)S(1)}, f32[257,128]{1,0:T(8,128)S(1)}, u32[]{:S(2)}, u32[]{:S(2)}) collective-permute-start(f32[257,128]{1,0:T(8,128)S(1)} %fusion.12), channel_id=1, source_target_pairs={{0,2},{2,0},{4,6},{6,4},{8,10},{10,8},{12,14},{14,12},{16,18},{18,... | collective-permute-start | bytes 394760 | tf_op jit(solution)/shard_map/ppermute | solution.py:36
  39.0 0.2 convolution_convert_fusion.1
  39.3 2.3 %collective-permute-start.3 = (bf16[384,512]{1,0:T(8,128)(2,1)S(1)}, bf16[384,512]{1,0:T(8,128)(2,1)S(1)}, u32[]{:S(2)}, u32[]{:S(2)}) collective-permute-start(bf16[384,512]{1,0:T(8,128)(2,1)S(1)} %pad_maximum_fusion.2), channel_id=1, source_target_pairs={{0,1},{1,0},{2,3},{3,2},{4,5},{5,4},{6,7},{7,6},{8,9},{9,8},{10,11... | collective-permute-start | bytes 1179656 | tf_op jit(solution)/shard_map/ppermute | solution.py:88
  41.6 0.0 collective-permute-done.7
  41.6 8.8 %collective-permute-start.10 = (f32[257,128]{1,0:T(8,128)S(1)}, f32[257,128]{1,0:T(8,128)S(1)}, u32[]{:S(2)}, u32[]{:S(2)}) collective-permute-start(f32[257,128]{1,0:T(8,128)S(1)} %fusion.14), channel_id=1, source_target_pairs={{0,192},{2,194},{4,196},{6,198},{8,200},{10,202},{12,204},{14,206}... | collective-permute-start | bytes 394760 | tf_op jit(solution)/shard_map/ppermute | solution.py:36
  50.5 4.7 %collective-permute-start.9 = (f32[257,128]{1,0:T(8,128)S(1)}, f32[257,128]{1,0:T(8,128)S(1)}, u32[]{:S(2)}, u32[]{:S(2)}) collective-permute-start(f32[257,128]{1,0:T(8,128)S(1)} %fusion.14), channel_id=1, source_target_pairs={{0,384},{2,386},{4,388},{6,390},{8,392},{10,394},{12,396},{14,398}... | collective-permute-start | bytes 394760 | tf_op jit(solution)/shard_map/ppermute | solution.py:36
  55.1 2.8 %collective-permute-start.8 = (f32[257,128]{1,0:T(8,128)S(1)}, f32[257,128]{1,0:T(8,128)S(1)}, u32[]{:S(2)}, u32[]{:S(2)}) collective-permute-start(f32[257,128]{1,0:T(8,128)S(1)} %fusion.14), channel_id=1, source_target_pairs={{0,576},{2,578},{4,580},{6,582},{8,584},{10,586},{12,588},{14,590}... | collective-permute-start | bytes 394760 | tf_op jit(solution)/shard_map/ppermute | solution.py:36
  58.0 0.0 collective-permute-done.10
  58.1 1.5 collective-permute-done.9
  59.5 1.8 collective-permute-done.8
  61.3 0.1 add_bitcast_fusion
  61.4 1.9 %collective-permute-start.11 = (f32[257,128]{1,0:T(8,128)S(1)}, f32[257,128]{1,0:T(8,128)S(1)}, u32[]{:S(2)}, u32[]{:S(2)}) collective-permute-start(f32[257,128]{1,0:T(8,128)S(1)} %add_bitcast_fusion), channel_id=1, source_target_pairs={{0,16},{2,18},{4,20},{6,22},{8,24},{10,26},{12,28},{14,30},{16,0},... | collective-permute-start | bytes 394760 | tf_op jit(solution)/shard_map/ppermute | solution.py:36
  63.3 0.0 collective-permute-done.3
  63.3 0.7 fusion.20
  64.0 0.2 maximum_select_fusion.1
  64.2 3.5 %fusion.4 = f32[18,128,256]{2,1,0:T(8,128)S(1)} fusion(bf16[6,128,256,1]{2,1,0,3:T(8,128)(2,1)S(1)} %bitcast.38, bf16[6,18,128,128]{3,1,2,0:T(8,128)(2,1)} %copy-done.1), kind=kOutput, calls=%fused_computation.5 | convolution fusion | flops 905969664 | bytes 6291456 | tf_op jit(solution)/shard_map/bsij,bif->sjf/dot_general | solution.py:156
  67.7 1.0 slice.32
  68.7 3.7 %collective-permute-start.4 = (f32[6,128,256]{2,1,0:T(8,128)}, f32[6,128,256]{2,1,0:T(8,128)}, u32[]{:S(2)}, u32[]{:S(2)}) collective-permute-start(f32[6,128,256]{2,1,0:T(8,128)} %slice.32), channel_id=1, source_target_pairs={{2,0},{4,2},{6,4},{8,6},{10,8},{12,10},{14,12},{16,14},{18,16},{20... | collective-permute-start | bytes 2359304 | tf_op jit(solution)/shard_map/ppermute | solution.py:25
  72.3 0.0 collective-permute-done.11
  72.3 0.1 fusion.30
  72.4 5.7 %collective-permute-start.12 = (f32[257,128]{1,0:T(8,128)S(1)}, f32[257,128]{1,0:T(8,128)S(1)}, u32[]{:S(2)}, u32[]{:S(2)}) collective-permute-start(f32[257,128]{1,0:T(8,128)S(1)} %fusion.30), channel_id=1, source_target_pairs={{0,32},{2,34},{4,36},{6,38},{8,40},{10,42},{12,44},{14,46},{16,48}... | collective-permute-start | bytes 394760 | tf_op jit(solution)/shard_map/ppermute | solution.py:36
  78.1 5.3 %collective-permute-done.12 = f32[257,128]{1,0:T(8,128)S(1)} collective-permute-done((f32[257,128]{1,0:T(8,128)S(1)}, f32[257,128]{1,0:T(8,128)S(1)}, u32[]{:S(2)}, u32[]{:S(2)}) %collective-permute-start.12) | collective-permute-done | bytes 131616 | tf_op jit(solution)/shard_map/ppermute | solution.py:36
  83.5 0.7 add.148
  84.1 11.5 %collective-permute-start.14 = (f32[257,128]{1,0:T(8,128)}, f32[257,128]{1,0:T(8,128)}, u32[]{:S(2)}, u32[]{:S(2)}) collective-permute-start(f32[257,128]{1,0:T(8,128)} %add.148), channel_id=1, source_target_pairs={{0,128},{2,130},{4,132},{6,134},{8,136},{10,138},{12,140},{14,142}... | collective-permute-start | bytes 394760 | tf_op jit(solution)/shard_map/ppermute | solution.py:36
  95.7 1.9 %collective-permute-start.13 = (f32[257,128]{1,0:T(8,128)}, f32[257,128]{1,0:T(8,128)}, u32[]{:S(2)}, u32[]{:S(2)}) collective-permute-start(f32[257,128]{1,0:T(8,128)} %add.148), channel_id=1, source_target_pairs={{0,64},{2,66},{4,68},{6,70},{8,72},{10,74},{12,76},{14,78},{16,80}... | collective-permute-start | bytes 394760 | tf_op jit(solution)/shard_map/ppermute | solution.py:36
  97.7 6.2 %collective-permute-start.5 = (bf16[6,128,256]{2,1,0:T(8,128)(2,1)S(1)}, bf16[6,128,256]{2,1,0:T(8,128)(2,1)S(1)}, u32[]{:S(2)}, u32[]{:S(2)}) collective-permute-start(bf16[6,128,256]{2,1,0:T(8,128)(2,1)S(1)} %slice.42), channel_id=1, source_target_pairs={{0,2},{2,4},{4,6},{6,8},{8,10},{10,12},{12,14},{14,16},{16,18},{18... | collective-permute-start | bytes 1179656 | tf_op jit(solution)/shard_map/ppermute | solution.py:25
  103.9 0.0 collective-permute-done.14
  103.9 4.2 %collective-permute-done.13 = f32[257,128]{1,0:T(8,128)} collective-permute-done((f32[257,128]{1,0:T(8,128)}, f32[257,128]{1,0:T(8,128)}, u32[]{:S(2)}, u32[]{:S(2)}) %collective-permute-start.13) | collective-permute-done | bytes 131616 | tf_op jit(solution)/shard_map/ppermute | solution.py:36
  108.1 1.1 select_add_fusion
  109.2 11.5 %collective-permute-start.15 = (f32[257,128]{1,0:T(8,128)S(1)}, f32[257,128]{1,0:T(8,128)S(1)}, u32[]{:S(2)}, u32[]{:S(2)}) collective-permute-start(f32[257,128]{1,0:T(8,128)S(1)} %select_add_fusion), channel_id=1, source_target_pairs={{0,4},{2,6},{4,0},{6,2},{8,12},{10,14},{12,8},{14,10},{16,20},{18,... | collective-permute-start | bytes 394760 | tf_op jit(solution)/shard_map/ppermute | solution.py:36
  120.7 7.9 %collective-permute-done.15 = f32[257,128]{1,0:T(8,128)S(1)} collective-permute-done((f32[257,128]{1,0:T(8,128)S(1)}, f32[257,128]{1,0:T(8,128)S(1)}, u32[]{:S(2)}, u32[]{:S(2)}) %collective-permute-start.15) | collective-permute-done | bytes 131616 | tf_op jit(solution)/shard_map/ppermute | solution.py:36
  128.6 2.2 %collective-permute-start.16 = (f32[257,128]{1,0:T(8,128)S(1)}, f32[257,128]{1,0:T(8,128)S(1)}, u32[]{:S(2)}, u32[]{:S(2)}) collective-permute-start(f32[257,128]{1,0:T(8,128)S(1)} %add.151), channel_id=1, source_target_pairs={{0,8},{2,10},{4,12},{6,14},{8,0},{10,2},{12,4},{14,6},{16,24},{18,... | collective-permute-start | bytes 394760 | tf_op jit(solution)/shard_map/ppermute | solution.py:36
  130.9 7.9 %collective-permute-done.16 = f32[257,128]{1,0:T(8,128)S(1)} collective-permute-done((f32[257,128]{1,0:T(8,128)S(1)}, f32[257,128]{1,0:T(8,128)S(1)}, u32[]{:S(2)}, u32[]{:S(2)}) %collective-permute-start.16) | collective-permute-done | bytes 131616 | tf_op jit(solution)/shard_map/ppermute | solution.py:36
  138.8 1.9 %collective-permute-start.17 = (f32[257,128]{1,0:T(8,128)S(1)}, f32[257,128]{1,0:T(8,128)S(1)}, u32[]{:S(2)}, u32[]{:S(2)}) collective-permute-start(f32[257,128]{1,0:T(8,128)S(1)} %add.152), channel_id=1, source_target_pairs={{0,1},{1,0},{2,3},{3,2},{4,5},{5,4},{6,7},{7,6},{8,9},{9,8},{10,11... | collective-permute-start | bytes 394760 | tf_op jit(solution)/shard_map/ppermute | solution.py:82
  140.7 0.0 collective-permute-done.4
  140.8 2.2 %fusion.11 = f32[6,128,256]{2,1,0:T(8,128)} fusion(f32[6,128,256]{2,1,0:T(8,128)} %collective-permute-done.4, f32[18,128,256]{2,1,0:T(8,128)S(1)} %fusion.4, bf16[6,128,256]{2,1,0:T(8,128)(2,1)S(1)} %collective-permute-done.5), kind=kLoop, calls=%fused_computation.13 | loop fusion | flops 589824 | bytes 2752512 | tf_op jit(solution)/shard_map/add | solution.py:163
  143.0 7.3 %collective-permute-start.6 = (f32[6,128,256]{2,1,0:T(8,128)}, f32[6,128,256]{2,1,0:T(8,128)S(1)}, u32[]{:S(2)}, u32[]{:S(2)}) collective-permute-start(f32[6,128,256]{2,1,0:T(8,128)} %fusion.11), channel_id=1, source_target_pairs={{0,1},{1,0},{2,3},{3,2},{4,5},{5,4},{6,7},{7,6},{8,9},{9,8},{10,11... | collective-permute-start | bytes 2359304 | tf_op jit(solution)/shard_map/ppermute | solution.py:98
  150.2 0.0 collective-permute-done.17
  150.3 3.2 %collective-permute-start.18 = (f32[257,128]{1,0:T(8,128)S(1)}, f32[257,128]{1,0:T(8,128)S(1)}, u32[]{:S(2)}, u32[]{:S(2)}) collective-permute-start(f32[257,128]{1,0:T(8,128)S(1)} %add.153), channel_id=1, source_target_pairs={{0,2},{2,0},{4,6},{6,4},{8,10},{10,8},{12,14},{14,12},{16,18},{18,... | collective-permute-start | bytes 394760 | tf_op jit(solution)/shard_map/ppermute | solution.py:36
  153.5 2.1 %maximum_select_fusion = bf16[768,256]{1,0:T(8,128)(2,1)} fusion(bf16[384,256]{1,0:T(8,128)(2,1)} %get-tuple-element.7, bf16[384,256]{1,0:T(8,128)(2,1)} %copy-done.2, pred[]{:T(512)S(6)} %eq.38), kind=kLoop, calls=%fused_computation.17 | loop fusion | flops 1769472 | bytes 786433 | tf_op jit(solution)/shard_map/jit(_where)/select_n | solution.py:92
  155.5 0.0 collective-permute-done.18
  155.6 0.6 slice_multiply_fusion.1
  156.1 0.7 slice_multiply_fusion
  156.9 26.4 %collective-permute-done.6 = f32[6,128,256]{2,1,0:T(8,128)S(1)} collective-permute-done((f32[6,128,256]{2,1,0:T(8,128)}, f32[6,128,256]{2,1,0:T(8,128)S(1)}, u32[]{:S(2)}, u32[]{:S(2)}) %collective-permute-start.6) | collective-permute-done | bytes 786464 | tf_op jit(solution)/shard_map/ppermute | solution.py:98
  183.2 2.0 %add_convert_fusion = bf16[6,128,256]{2,1,0:T(8,128)(2,1)} fusion(f32[6,128,256]{2,1,0:T(8,128)} %fusion.11, f32[6,128,256]{2,1,0:T(8,128)S(1)} %collective-permute-done.6), kind=kLoop, calls=%fused_computation.14 | loop fusion | flops 393216 | bytes 1966080 | tf_op jit(solution)/shard_map/convert_element_type | solution.py:165
  (20 shorter events, 0.3 us)
Async XLA Ops:
  0.6 15.3 %copy-start = (bf16[6,6,128,128]{3,2,1,0:T(8,128)(2,1)S(1)}, bf16[6,6,128,128]{3,2,1,0:T(8,128)(2,1)}, u32[]{:S(2)}) copy-start(bf16[6,6,128,128]{3,2,1,0:T(8,128)(2,1)} %param.8) | copy-start | bytes 3538948
  0.6 17.6 %collective-permute-start = (bf16[768,256]{1,0:T(8,128)(2,1)}, bf16[768,256]{1,0:T(8,128)(2,1)S(1)}, u32[]{:S(2)}, u32[]{:S(2)}) collective-permute-start(bf16[768,256]{1,0:T(8,128)(2,1)} %param.7), channel_id=1, source_target_pairs={{0,2},{2,4},{4,6},{6,8},{8,10},{10,12},{12,14},{14,16},{16,18},{18... | collective-permute-start | bytes 1179656 | tf_op jit(solution)/shard_map/ppermute | solution.py:14
  5.4 12.8 %collective-permute-start.1 = (bf16[768,256]{1,0:T(8,128)(2,1)}, bf16[768,256]{1,0:T(8,128)(2,1)S(1)}, u32[]{:S(2)}, u32[]{:S(2)}) collective-permute-start(bf16[768,256]{1,0:T(8,128)(2,1)} %param.7), channel_id=1, source_target_pairs={{2,0},{4,2},{6,4},{8,6},{10,8},{12,10},{14,12},{16,14},{18,16},{20... | collective-permute-start | bytes 1179656 | tf_op jit(solution)/shard_map/ppermute | solution.py:17
  16.0 2.3 %copy-start.3 = (bf16[768,256]{1,0:T(8,128)(2,1)S(1)}, bf16[768,256]{1,0:T(8,128)(2,1)}, u32[]{:S(2)}) copy-start(bf16[768,256]{1,0:T(8,128)(2,1)} %param.7) | copy-start | bytes 1179652
  18.2 2.1 %copy-start.1 = (bf16[6,18,128,128]{3,1,2,0:T(8,128)(2,1)}, bf16[6,18,128,128]{3,1,2,0:T(8,128)(2,1)S(1)}, u32[]{:S(2)}) copy-start(bf16[6,18,128,128]{3,1,2,0:T(8,128)(2,1)S(1)} %convolution_convert_fusion) | copy-start | bytes 10616836
  18.3 17.7 %copy-start.4 = (bf16[256,256]{1,0:T(8,128)(2,1)S(1)}, bf16[256,256]{1,0:T(8,128)(2,1)}, u32[]{:S(2)}) copy-start(bf16[256,256]{1,0:T(8,128)(2,1)} %param.11) | copy-start | bytes 393220
  18.3 17.7 %copy-start.5 = (bf16[768,256]{1,0:T(8,128)(2,1)S(1)}, bf16[768,256]{1,0:T(8,128)(2,1)}, u32[]{:S(2)}) copy-start(bf16[768,256]{1,0:T(8,128)(2,1)} %param.13) | copy-start | bytes 1179652
  18.4 17.7 %copy-start.6 = (f32[256]{0:T(256)S(1)}, f32[256]{0:T(256)}, u32[]{:S(2)}) copy-start(f32[256]{0:T(256)} %param.12) | copy-start | bytes 3076
  20.4 15.6 %collective-permute-start.2 = (bf16[384,256]{1,0:T(8,128)(2,1)S(1)}, bf16[384,256]{1,0:T(8,128)(2,1)S(1)}, u32[]{:S(2)}, u32[]{:S(2)}) collective-permute-start(bf16[384,256]{1,0:T(8,128)(2,1)S(1)} %dynamic-slice_convert_fusion), channel_id=1, source_target_pairs={{0,1},{1,0},{2,3},{3,2},{4,5},{5,4},{6,7},{7,6},{8,9},{9,8},{10,11... | collective-permute-start | bytes 589832 | tf_op jit(solution)/shard_map/ppermute | solution.py:88
  36.4 5.2 %copy-start.2 = (bf16[384,256]{1,0:T(8,128)(2,1)}, bf16[384,256]{1,0:T(8,128)(2,1)S(1)}, u32[]{:S(2)}) copy-start(bf16[384,256]{1,0:T(8,128)(2,1)S(1)} %get-tuple-element.8) | copy-start | bytes 589828
  36.7 4.9 %collective-permute-start.7 = (f32[257,128]{1,0:T(8,128)S(1)}, f32[257,128]{1,0:T(8,128)S(1)}, u32[]{:S(2)}, u32[]{:S(2)}) collective-permute-start(f32[257,128]{1,0:T(8,128)S(1)} %fusion.12), channel_id=1, source_target_pairs={{0,2},{2,0},{4,6},{6,4},{8,10},{10,8},{12,14},{14,12},{16,18},{18,... | collective-permute-start | bytes 394760 | tf_op jit(solution)/shard_map/ppermute | solution.py:36
  39.3 24.0 %collective-permute-start.3 = (bf16[384,512]{1,0:T(8,128)(2,1)S(1)}, bf16[384,512]{1,0:T(8,128)(2,1)S(1)}, u32[]{:S(2)}, u32[]{:S(2)}) collective-permute-start(bf16[384,512]{1,0:T(8,128)(2,1)S(1)} %pad_maximum_fusion.2), channel_id=1, source_target_pairs={{0,1},{1,0},{2,3},{3,2},{4,5},{5,4},{6,7},{7,6},{8,9},{9,8},{10,11... | collective-permute-start | bytes 1179656 | tf_op jit(solution)/shard_map/ppermute | solution.py:88
  41.6 16.4 %collective-permute-start.10 = (f32[257,128]{1,0:T(8,128)S(1)}, f32[257,128]{1,0:T(8,128)S(1)}, u32[]{:S(2)}, u32[]{:S(2)}) collective-permute-start(f32[257,128]{1,0:T(8,128)S(1)} %fusion.14), channel_id=1, source_target_pairs={{0,192},{2,194},{4,196},{6,198},{8,200},{10,202},{12,204},{14,206}... | collective-permute-start | bytes 394760 | tf_op jit(solution)/shard_map/ppermute | solution.py:36
  50.5 9.0 %collective-permute-start.9 = (f32[257,128]{1,0:T(8,128)S(1)}, f32[257,128]{1,0:T(8,128)S(1)}, u32[]{:S(2)}, u32[]{:S(2)}) collective-permute-start(f32[257,128]{1,0:T(8,128)S(1)} %fusion.14), channel_id=1, source_target_pairs={{0,384},{2,386},{4,388},{6,390},{8,392},{10,394},{12,396},{14,398}... | collective-permute-start | bytes 394760 | tf_op jit(solution)/shard_map/ppermute | solution.py:36
  55.1 6.1 %collective-permute-start.8 = (f32[257,128]{1,0:T(8,128)S(1)}, f32[257,128]{1,0:T(8,128)S(1)}, u32[]{:S(2)}, u32[]{:S(2)}) collective-permute-start(f32[257,128]{1,0:T(8,128)S(1)} %fusion.14), channel_id=1, source_target_pairs={{0,576},{2,578},{4,580},{6,582},{8,584},{10,586},{12,588},{14,590}... | collective-permute-start | bytes 394760 | tf_op jit(solution)/shard_map/ppermute | solution.py:36
  61.4 10.9 %collective-permute-start.11 = (f32[257,128]{1,0:T(8,128)S(1)}, f32[257,128]{1,0:T(8,128)S(1)}, u32[]{:S(2)}, u32[]{:S(2)}) collective-permute-start(f32[257,128]{1,0:T(8,128)S(1)} %add_bitcast_fusion), channel_id=1, source_target_pairs={{0,16},{2,18},{4,20},{6,22},{8,24},{10,26},{12,28},{14,30},{16,0},... | collective-permute-start | bytes 394760 | tf_op jit(solution)/shard_map/ppermute | solution.py:36
  68.7 72.1 %collective-permute-start.4 = (f32[6,128,256]{2,1,0:T(8,128)}, f32[6,128,256]{2,1,0:T(8,128)}, u32[]{:S(2)}, u32[]{:S(2)}) collective-permute-start(f32[6,128,256]{2,1,0:T(8,128)} %slice.32), channel_id=1, source_target_pairs={{2,0},{4,2},{6,4},{8,6},{10,8},{12,10},{14,12},{16,14},{18,16},{20... | collective-permute-start | bytes 2359304 | tf_op jit(solution)/shard_map/ppermute | solution.py:25
  72.4 11.0 %collective-permute-start.12 = (f32[257,128]{1,0:T(8,128)S(1)}, f32[257,128]{1,0:T(8,128)S(1)}, u32[]{:S(2)}, u32[]{:S(2)}) collective-permute-start(f32[257,128]{1,0:T(8,128)S(1)} %fusion.30), channel_id=1, source_target_pairs={{0,32},{2,34},{4,36},{6,38},{8,40},{10,42},{12,44},{14,46},{16,48}... | collective-permute-start | bytes 394760 | tf_op jit(solution)/shard_map/ppermute | solution.py:36
  84.1 19.8 %collective-permute-start.14 = (f32[257,128]{1,0:T(8,128)}, f32[257,128]{1,0:T(8,128)}, u32[]{:S(2)}, u32[]{:S(2)}) collective-permute-start(f32[257,128]{1,0:T(8,128)} %add.148), channel_id=1, source_target_pairs={{0,128},{2,130},{4,132},{6,134},{8,136},{10,138},{12,140},{14,142}... | collective-permute-start | bytes 394760 | tf_op jit(solution)/shard_map/ppermute | solution.py:36
  95.7 12.4 %collective-permute-start.13 = (f32[257,128]{1,0:T(8,128)}, f32[257,128]{1,0:T(8,128)}, u32[]{:S(2)}, u32[]{:S(2)}) collective-permute-start(f32[257,128]{1,0:T(8,128)} %add.148), channel_id=1, source_target_pairs={{0,64},{2,66},{4,68},{6,70},{8,72},{10,74},{12,76},{14,78},{16,80}... | collective-permute-start | bytes 394760 | tf_op jit(solution)/shard_map/ppermute | solution.py:36
  97.7 43.0 %collective-permute-start.5 = (bf16[6,128,256]{2,1,0:T(8,128)(2,1)S(1)}, bf16[6,128,256]{2,1,0:T(8,128)(2,1)S(1)}, u32[]{:S(2)}, u32[]{:S(2)}) collective-permute-start(bf16[6,128,256]{2,1,0:T(8,128)(2,1)S(1)} %slice.42), channel_id=1, source_target_pairs={{0,2},{2,4},{4,6},{6,8},{8,10},{10,12},{12,14},{14,16},{16,18},{18... | collective-permute-start | bytes 1179656 | tf_op jit(solution)/shard_map/ppermute | solution.py:25
  109.2 19.4 %collective-permute-start.15 = (f32[257,128]{1,0:T(8,128)S(1)}, f32[257,128]{1,0:T(8,128)S(1)}, u32[]{:S(2)}, u32[]{:S(2)}) collective-permute-start(f32[257,128]{1,0:T(8,128)S(1)} %select_add_fusion), channel_id=1, source_target_pairs={{0,4},{2,6},{4,0},{6,2},{8,12},{10,14},{12,8},{14,10},{16,20},{18,... | collective-permute-start | bytes 394760 | tf_op jit(solution)/shard_map/ppermute | solution.py:36
  128.6 10.2 %collective-permute-start.16 = (f32[257,128]{1,0:T(8,128)S(1)}, f32[257,128]{1,0:T(8,128)S(1)}, u32[]{:S(2)}, u32[]{:S(2)}) collective-permute-start(f32[257,128]{1,0:T(8,128)S(1)} %add.151), channel_id=1, source_target_pairs={{0,8},{2,10},{4,12},{6,14},{8,0},{10,2},{12,4},{14,6},{16,24},{18,... | collective-permute-start | bytes 394760 | tf_op jit(solution)/shard_map/ppermute | solution.py:36
  138.8 11.4 %collective-permute-start.17 = (f32[257,128]{1,0:T(8,128)S(1)}, f32[257,128]{1,0:T(8,128)S(1)}, u32[]{:S(2)}, u32[]{:S(2)}) collective-permute-start(f32[257,128]{1,0:T(8,128)S(1)} %add.152), channel_id=1, source_target_pairs={{0,1},{1,0},{2,3},{3,2},{4,5},{5,4},{6,7},{7,6},{8,9},{9,8},{10,11... | collective-permute-start | bytes 394760 | tf_op jit(solution)/shard_map/ppermute | solution.py:82
  143.0 40.3 %collective-permute-start.6 = (f32[6,128,256]{2,1,0:T(8,128)}, f32[6,128,256]{2,1,0:T(8,128)S(1)}, u32[]{:S(2)}, u32[]{:S(2)}) collective-permute-start(f32[6,128,256]{2,1,0:T(8,128)} %fusion.11), channel_id=1, source_target_pairs={{0,1},{1,0},{2,3},{3,2},{4,5},{5,4},{6,7},{7,6},{8,9},{9,8},{10,11... | collective-permute-start | bytes 2359304 | tf_op jit(solution)/shard_map/ppermute | solution.py:98
  150.3 5.3 %collective-permute-start.18 = (f32[257,128]{1,0:T(8,128)S(1)}, f32[257,128]{1,0:T(8,128)S(1)}, u32[]{:S(2)}, u32[]{:S(2)}) collective-permute-start(f32[257,128]{1,0:T(8,128)S(1)} %add.153), channel_id=1, source_target_pairs={{0,2},{2,0},{4,6},{6,4},{8,10},{10,8},{12,14},{14,12},{16,18},{18,... | collective-permute-start | bytes 394760 | tf_op jit(solution)/shard_map/ppermute | solution.py:36

commit v10 on v9

--- a/solution.py
+++ b/solution.py
@@ -74,11 +74,9 @@
     give = lax.dynamic_slice_in_dim(x, (1 - core) * width, width, 1)
     x = keep + moved(give, "rows", count, c_stride, c_size, lambda c: c ^ 1)
     x = ring_sum(x, "rows", count, x_stride, x_size)
-    x = swapped_sum(x, "rows", count, z_stride, z_size, 1)
-    x = swapped_sum(x, "rows", count, z_stride, z_size, 2)
+    x = ring_sum(x, "rows", count, z_stride, z_size // 3)
     x = three_way_sum(x, "rows", count, z_stride, z_size)
-    x = swapped_sum(x, "rows", count, y_stride, y_size, 1)
-    x = swapped_sum(x, "rows", count, y_stride, y_size, 2)
+    x = ring_sum(x, "rows", count, y_stride, y_size)
     x = x + lax.ppermute(x, "rep", [(0, 1), (1, 0)])
     other = moved(x, "rows", count, c_stride, c_size, lambda c: c ^ 1)
     return jnp.where(core == 0, jnp.concatenate([x, other], 1), jnp.concatenate([other, x], 1))

time: 186 us -> 189 us (1.016)
  the two profiles are of different devices: /device:TPU:1 before, /device:TPU:200 now
where the time goes in v10:
time: 189 us; the launch traced here: 188 us
  starting transfers between devices  83.9 us (44%)
  waiting for transfers between devices  78.5 us (42%)
  other arithmetic  13.5 us (7%)
  matrix products  7.7 us (4%)
  local copies, waits for them, and re-layouts  3.33 us (2%)
    ppermute x13, starting transfers between devices, moved(): return lax.ppermute(x, axis, pairs)  48 us
    ppermute x1, waiting for transfers between devices, partner_sum(): return x + lax.ppermute(x, 'rep', [(0, 1), (1, 0)])  28.5 us
    ppermute x13, waiting for transfers between devices, moved(): return lax.ppermute(x, axis, pairs)  20 us
    ppermute x2, waiting for transfers between devices, partner_swap(): return lax.ppermute(x, 'rep', [(0, 1), (1, 0)])  18.7 us
    ppermute x2, starting transfers between devices, partner_swap(): return lax.ppermute(x, 'rep', [(0, 1), (1, 0)])  14.9 us
    ppermute x1, starting transfers between devices, global_sum(): x = x + lax.ppermute(x, 'rep', [(0, 1), (1, 0)])  9.43 us
    ppermute x1, waiting for transfers between devices, global_sum(): x = x + lax.ppermute(x, 'rep', [(0, 1), (1, 0)])  6.24 us
    ppermute x1, waiting for transfers between devices, extended(): lax.ppermute(lax.slice_in_dim(block, 0, width, axis=dim), axis, backward)  4.98 us
  transfers between devices with their start and end apart: 21, of which 10 were waited for; matrix products, arithmetic and copies ran while one was open for 11% of the time, Pallas kernels for 0%

profile of v10, /device:TPU:200, one launch (start us, length us, event | category | flops | bytes accessed | tf_op | source)
XLA Modules:
  0.0 188.4 jit_solution(419364629744979666)
XLA Ops:
  0.6 0.0 copy-start
  0.6 2.1 %collective-permute-start = (bf16[768,256]{1,0:T(8,128)(2,1)}, bf16[768,256]{1,0:T(8,128)(2,1)S(1)}, u32[]{:S(2)}, u32[]{:S(2)}) collective-permute-start(bf16[768,256]{1,0:T(8,128)(2,1)} %param.7), channel_id=1, source_target_pairs={{0,2},{2,4},{4,6},{6,8},{8,10},{10,12},{12,14},{14,16},{16,18},{18... | collective-permute-start | bytes 1179656 | tf_op jit(solution)/shard_map/ppermute | solution.py:14
  2.7 3.6 %collective-permute-start.1 = (bf16[768,256]{1,0:T(8,128)(2,1)}, bf16[768,256]{1,0:T(8,128)(2,1)S(1)}, u32[]{:S(2)}, u32[]{:S(2)}) collective-permute-start(bf16[768,256]{1,0:T(8,128)(2,1)} %param.7), channel_id=1, source_target_pairs={{2,0},{4,2},{6,4},{8,6},{10,8},{12,10},{14,12},{16,14},{18,16},{20... | collective-permute-start | bytes 1179656 | tf_op jit(solution)/shard_map/ppermute | solution.py:17
  6.4 0.7 broadcast_subtract_fusion
  7.1 0.7 iota_compare_fusion.1
  7.8 2.2 %convolution_convert_fusion = bf16[6,18,128,128]{3,1,2,0:T(8,128)(2,1)S(1)} fusion(bf16[6,6,128,128]{3,2,1,0:T(8,128)(2,1)S(1)} %copy-done, s32[6,6]{1,0:T(8,128)S(1)} %broadcast_subtract_fusion, pred[6,6]{1,0:T(8,128)(4,1)S(1)} %iota_compare_fusion.1), kind=kOutput, calls=%fused_computation.4 | convolution fusion | flops 23004432 | bytes 4718772 | tf_op jit(solution)/shard_map/bks,bkij->bsij/dot_general | solution.py:127
  10.0 0.0 collective-permute-done
  10.1 5.0 %collective-permute-done.1 = bf16[768,256]{1,0:T(8,128)(2,1)S(1)} collective-permute-done((bf16[768,256]{1,0:T(8,128)(2,1)}, bf16[768,256]{1,0:T(8,128)(2,1)S(1)}, u32[]{:S(2)}, u32[]{:S(2)}) %collective-permute-start.1) | collective-permute-done | bytes 393248 | tf_op jit(solution)/shard_map/ppermute | solution.py:17
  15.1 0.1 pad_maximum_fusion
  15.2 0.0 copy-start.5
  15.2 0.0 copy-start.6
  15.2 0.0 copy-start.7
  15.2 1.1 fusion.8
  16.3 7.7 %collective-permute-start.2 = (bf16[384,256]{1,0:T(8,128)(2,1)S(1)}, bf16[384,256]{1,0:T(8,128)(2,1)S(1)}, u32[]{:S(2)}, u32[]{:S(2)}) collective-permute-start(bf16[384,256]{1,0:T(8,128)(2,1)S(1)} %dynamic-slice_convert_fusion), channel_id=1, source_target_pairs={{0,1},{1,0},{2,3},{3,2},{4,5},{5,4},{6,7},{7,6},{8,9},{9,8},{10,11... | collective-permute-start | bytes 589832 | tf_op jit(solution)/shard_map/ppermute | solution.py:86
  24.1 10.0 %collective-permute-done.2 = bf16[384,256]{1,0:T(8,128)(2,1)S(1)} collective-permute-done((bf16[384,256]{1,0:T(8,128)(2,1)S(1)}, bf16[384,256]{1,0:T(8,128)(2,1)S(1)}, u32[]{:S(2)}, u32[]{:S(2)}) %collective-permute-start.2) | collective-permute-done | bytes 196640 | tf_op jit(solution)/shard_map/ppermute | solution.py:86
  34.1 0.1 add_convert_fusion.1
  34.1 0.4 convert_reduce_fusion
  34.5 0.3 fusion.21
  34.8 1.9 %collective-permute-start.7 = (f32[257,128]{1,0:T(8,128)S(1)}, f32[257,128]{1,0:T(8,128)S(1)}, u32[]{:S(2)}, u32[]{:S(2)}) collective-permute-start(f32[257,128]{1,0:T(8,128)S(1)} %fusion.12), channel_id=1, source_target_pairs={{0,2},{2,0},{4,6},{6,4},{8,10},{10,8},{12,14},{14,12},{16,18},{18,... | collective-permute-start | bytes 394760 | tf_op jit(solution)/shard_map/ppermute | solution.py:36
  36.8 0.2 convolution_convert_fusion.1
  37.0 1.1 collective-permute-done.7
  38.1 3.4 %collective-permute-start.10 = (f32[257,128]{1,0:T(8,128)S(1)}, f32[257,128]{1,0:T(8,128)S(1)}, u32[]{:S(2)}, u32[]{:S(2)}) collective-permute-start(f32[257,128]{1,0:T(8,128)S(1)} %fusion.14), channel_id=1, source_target_pairs={{0,192},{2,194},{4,196},{6,198},{8,200},{10,202},{12,204},{14,206}... | collective-permute-start | bytes 394760 | tf_op jit(solution)/shard_map/ppermute | solution.py:36
  41.5 4.6 %collective-permute-start.9 = (f32[257,128]{1,0:T(8,128)S(1)}, f32[257,128]{1,0:T(8,128)S(1)}, u32[]{:S(2)}, u32[]{:S(2)}) collective-permute-start(f32[257,128]{1,0:T(8,128)S(1)} %fusion.14), channel_id=1, source_target_pairs={{0,384},{2,386},{4,388},{6,390},{8,392},{10,394},{12,396},{14,398}... | collective-permute-start | bytes 394760 | tf_op jit(solution)/shard_map/ppermute | solution.py:36
  46.2 3.3 %collective-permute-start.8 = (f32[257,128]{1,0:T(8,128)S(1)}, f32[257,128]{1,0:T(8,128)S(1)}, u32[]{:S(2)}, u32[]{:S(2)}) collective-permute-start(f32[257,128]{1,0:T(8,128)S(1)} %fusion.14), channel_id=1, source_target_pairs={{0,576},{2,578},{4,580},{6,582},{8,584},{10,586},{12,588},{14,590}... | collective-permute-start | bytes 394760 | tf_op jit(solution)/shard_map/ppermute | solution.py:36
  49.5 7.2 %collective-permute-start.3 = (bf16[384,512]{1,0:T(8,128)(2,1)S(1)}, bf16[384,512]{1,0:T(8,128)(2,1)S(1)}, u32[]{:S(2)}, u32[]{:S(2)}) collective-permute-start(bf16[384,512]{1,0:T(8,128)(2,1)S(1)} %pad_maximum_fusion.4), channel_id=1, source_target_pairs={{0,1},{1,0},{2,3},{3,2},{4,5},{5,4},{6,7},{7,6},{8,9},{9,8},{10,11... | collective-permute-start | bytes 1179656 | tf_op jit(solution)/shard_map/ppermute | solution.py:86
  56.9 0.0 collective-permute-done.10
  57.0 0.1 fusion.31
  57.1 1.9 %collective-permute-start.13 = (f32[257,128]{1,0:T(8,128)S(1)}, f32[257,128]{1,0:T(8,128)S(1)}, u32[]{:S(2)}, u32[]{:S(2)}) collective-permute-start(f32[257,128]{1,0:T(8,128)S(1)} %fusion.31), channel_id=1, source_target_pairs={{0,16},{2,18},{4,20},{6,22},{8,24},{10,26},{12,28},{14,30},{16,32}... | collective-permute-start | bytes 394760 | tf_op jit(solution)/shard_map/ppermute | solution.py:36
  59.0 3.1 %collective-permute-start.12 = (f32[257,128]{1,0:T(8,128)S(1)}, f32[257,128]{1,0:T(8,128)S(1)}, u32[]{:S(2)}, u32[]{:S(2)}) collective-permute-start(f32[257,128]{1,0:T(8,128)S(1)} %fusion.31), channel_id=1, source_target_pairs={{0,32},{2,34},{4,36},{6,38},{8,40},{10,42},{12,44},{14,46},{16,48}... | collective-permute-start | bytes 394760 | tf_op jit(solution)/shard_map/ppermute | solution.py:36
  62.1 2.7 %collective-permute-start.11 = (f32[257,128]{1,0:T(8,128)S(1)}, f32[257,128]{1,0:T(8,128)S(1)}, u32[]{:S(2)}, u32[]{:S(2)}) collective-permute-start(f32[257,128]{1,0:T(8,128)S(1)} %fusion.31), channel_id=1, source_target_pairs={{0,48},{2,50},{4,52},{6,54},{8,56},{10,58},{12,60},{14,62},{16,0},... | collective-permute-start | bytes 394760 | tf_op jit(solution)/shard_map/ppermute | solution.py:36
  64.9 0.1 dynamic-slice_add_fusion
  64.9 8.7 %collective-permute-done.3 = bf16[384,512]{1,0:T(8,128)(2,1)S(1)} collective-permute-done((bf16[384,512]{1,0:T(8,128)(2,1)S(1)}, bf16[384,512]{1,0:T(8,128)(2,1)S(1)}, u32[]{:S(2)}, u32[]{:S(2)}) %collective-permute-start.3) | collective-permute-done | bytes 393248 | tf_op jit(solution)/shard_map/ppermute | solution.py:86
  73.6 0.7 fusion.20
  74.3 0.2 maximum_select_fusion.1
  74.5 3.5 %fusion.4 = f32[18,128,256]{2,1,0:T(8,128)S(1)} fusion(bf16[6,128,256,1]{2,1,0,3:T(8,128)(2,1)S(1)} %bitcast.51, bf16[6,18,128,128]{3,1,2,0:T(8,128)(2,1)} %copy-done.1), kind=kOutput, calls=%fused_computation.5 | convolution fusion | flops 905969664 | bytes 6291456 | tf_op jit(solution)/shard_map/bsij,bif->sjf/dot_general | solution.py:154
  78.0 1.0 slice.32
  79.0 1.9 %collective-permute-start.4 = (f32[6,128,256]{2,1,0:T(8,128)}, f32[6,128,256]{2,1,0:T(8,128)}, u32[]{:S(2)}, u32[]{:S(2)}) collective-permute-start(f32[6,128,256]{2,1,0:T(8,128)} %slice.32), channel_id=1, source_target_pairs={{2,0},{4,2},{6,4},{8,6},{10,8},{12,10},{14,12},{16,14},{18,16},{20... | collective-permute-start | bytes 2359304 | tf_op jit(solution)/shard_map/ppermute | solution.py:25
  81.0 0.8 copy-done.2
  81.8 0.7 add_bitcast_fusion.1
  82.5 12.5 %collective-permute-start.15 = (f32[257,128]{1,0:T(8,128)}, f32[257,128]{1,0:T(8,128)}, u32[]{:S(2)}, u32[]{:S(2)}) collective-permute-start(f32[257,128]{1,0:T(8,128)} %add_bitcast_fusion.1), channel_id=1, source_target_pairs={{0,128},{2,130},{4,132},{6,134},{8,136},{10,138},{12,140},{14,142}... | collective-permute-start | bytes 394760 | tf_op jit(solution)/shard_map/ppermute | solution.py:36
  95.0 1.9 %collective-permute-start.14 = (f32[257,128]{1,0:T(8,128)}, f32[257,128]{1,0:T(8,128)}, u32[]{:S(2)}, u32[]{:S(2)}) collective-permute-start(f32[257,128]{1,0:T(8,128)} %add_bitcast_fusion.1), channel_id=1, source_target_pairs={{0,64},{2,66},{4,68},{6,70},{8,72},{10,74},{12,76},{14,78},{16,80}... | collective-permute-start | bytes 394760 | tf_op jit(solution)/shard_map/ppermute | solution.py:36
  97.0 0.8 slice.42
  97.8 2.1 %collective-permute-start.5 = (bf16[6,128,256]{2,1,0:T(8,128)(2,1)}, bf16[6,128,256]{2,1,0:T(8,128)(2,1)}, u32[]{:S(2)}, u32[]{:S(2)}) collective-permute-start(bf16[6,128,256]{2,1,0:T(8,128)(2,1)} %slice.42), channel_id=1, source_target_pairs={{0,2},{2,4},{4,6},{6,8},{8,10},{10,12},{12,14},{14,16},{16,18},{18... | collective-permute-start | bytes 1179656 | tf_op jit(solution)/shard_map/ppermute | solution.py:25
  99.9 3.4 %collective-permute-done.15 = f32[257,128]{1,0:T(8,128)} collective-permute-done((f32[257,128]{1,0:T(8,128)}, f32[257,128]{1,0:T(8,128)}, u32[]{:S(2)}, u32[]{:S(2)}) %collective-permute-start.15) | collective-permute-done | bytes 131616 | tf_op jit(solution)/shard_map/ppermute | solution.py:36
  103.3 9.0 %collective-permute-done.14 = f32[257,128]{1,0:T(8,128)} collective-permute-done((f32[257,128]{1,0:T(8,128)}, f32[257,128]{1,0:T(8,128)}, u32[]{:S(2)}, u32[]{:S(2)}) %collective-permute-start.14) | collective-permute-done | bytes 131616 | tf_op jit(solution)/shard_map/ppermute | solution.py:36
  112.2 1.9 %select_add_fusion = f32[257,128]{1,0:T(8,128)} fusion(f32[257,128]{1,0:T(8,128)} %collective-permute-done.14, f32[257,128]{1,0:T(8,128)} %collective-permute-done.15, pred[]{:T(512)S(6)} %eq.54, pred[]{:T(512)S(6)} %eq.53, f32[4,257,128]{2,1,0:T(8,128)} %copy-done.2, s32[]{:T(128)S(6)} %select_n.222, s32[]{:T(128)S(6)} %select_n.220, s32[]{:T(128)S(6)} %select_n.218, ...), kind=kLoop, calls=%fused_computation.37 | loop fusion | flops 361856 | bytes 921106 | tf_op jit(solution)/shard_map/add | solution.py:63
  114.1 5.3 %collective-permute-start.18 = (f32[257,128]{1,0:T(8,128)}, f32[257,128]{1,0:T(8,128)}, u32[]{:S(2)}, u32[]{:S(2)}) collective-permute-start(f32[257,128]{1,0:T(8,128)} %select_add_fusion), channel_id=1, source_target_pairs={{0,4},{2,6},{4,8},{6,10},{8,12},{10,14},{12,0},{14,2},{16,20},{18,... | collective-permute-start | bytes 394760 | tf_op jit(solution)/shard_map/ppermute | solution.py:36
  119.4 1.9 %collective-permute-start.17 = (f32[257,128]{1,0:T(8,128)}, f32[257,128]{1,0:T(8,128)}, u32[]{:S(2)}, u32[]{:S(2)}) collective-permute-start(f32[257,128]{1,0:T(8,128)} %select_add_fusion), channel_id=1, source_target_pairs={{0,8},{2,10},{4,12},{6,14},{8,0},{10,2},{12,4},{14,6},{16,24},{18,... | collective-permute-start | bytes 394760 | tf_op jit(solution)/shard_map/ppermute | solution.py:36
  121.4 3.4 %collective-permute-start.16 = (f32[257,128]{1,0:T(8,128)}, f32[257,128]{1,0:T(8,128)}, u32[]{:S(2)}, u32[]{:S(2)}) collective-permute-start(f32[257,128]{1,0:T(8,128)} %select_add_fusion), channel_id=1, source_target_pairs={{0,12},{2,14},{4,0},{6,2},{8,4},{10,6},{12,8},{14,10},{16,28},{18,... | collective-permute-start | bytes 394760 | tf_op jit(solution)/shard_map/ppermute | solution.py:36
  124.9 1.7 collective-permute-done.18
  126.6 4.9 %collective-permute-done.17 = f32[257,128]{1,0:T(8,128)} collective-permute-done((f32[257,128]{1,0:T(8,128)}, f32[257,128]{1,0:T(8,128)}, u32[]{:S(2)}, u32[]{:S(2)}) %collective-permute-start.17) | collective-permute-done | bytes 131616 | tf_op jit(solution)/shard_map/ppermute | solution.py:36
  131.4 1.1 pad_maximum_fusion.3
  132.6 0.1 add_bitcast_fusion
  132.6 9.4 %collective-permute-start.19 = (f32[257,128]{1,0:T(8,128)S(1)}, f32[257,128]{1,0:T(8,128)S(1)}, u32[]{:S(2)}, u32[]{:S(2)}) collective-permute-start(f32[257,128]{1,0:T(8,128)S(1)} %add_bitcast_fusion), channel_id=1, source_target_pairs={{0,1},{1,0},{2,3},{3,2},{4,5},{5,4},{6,7},{7,6},{8,9},{9,8},{10,11... | collective-permute-start | bytes 394760 | tf_op jit(solution)/shard_map/ppermute | solution.py:80
  142.1 2.3 %fusion.11 = f32[6,128,256]{2,1,0:T(8,128)} fusion(f32[6,128,256]{2,1,0:T(8,128)} %collective-permute-done.4, f32[18,128,256]{2,1,0:T(8,128)S(1)} %fusion.4, bf16[6,128,256]{2,1,0:T(8,128)(2,1)} %collective-permute-done.5), kind=kLoop, calls=%fused_computation.13 | loop fusion | flops 589824 | bytes 2752512 | tf_op jit(solution)/shard_map/add | solution.py:161
  144.4 1.9 %collective-permute-start.6 = (f32[6,128,256]{2,1,0:T(8,128)}, f32[6,128,256]{2,1,0:T(8,128)S(1)}, u32[]{:S(2)}, u32[]{:S(2)}) collective-permute-start(f32[6,128,256]{2,1,0:T(8,128)} %fusion.11), channel_id=1, source_target_pairs={{0,1},{1,0},{2,3},{3,2},{4,5},{5,4},{6,7},{7,6},{8,9},{9,8},{10,11... | collective-permute-start | bytes 2359304 | tf_op jit(solution)/shard_map/ppermute | solution.py:96
  146.3 6.2 %collective-permute-done.19 = f32[257,128]{1,0:T(8,128)S(1)} collective-permute-done((f32[257,128]{1,0:T(8,128)S(1)}, f32[257,128]{1,0:T(8,128)S(1)}, u32[]{:S(2)}, u32[]{:S(2)}) %collective-permute-start.19) | collective-permute-done | bytes 131616 | tf_op jit(solution)/shard_map/ppermute | solution.py:80
  152.5 0.1 fusion.30
  152.6 1.9 %collective-permute-start.20 = (f32[257,128]{1,0:T(8,128)S(1)}, f32[257,128]{1,0:T(8,128)S(1)}, u32[]{:S(2)}, u32[]{:S(2)}) collective-permute-start(f32[257,128]{1,0:T(8,128)S(1)} %fusion.30), channel_id=1, source_target_pairs={{0,2},{2,0},{4,6},{6,4},{8,10},{10,8},{12,14},{14,12},{16,18},{18,... | collective-permute-start | bytes 394760 | tf_op jit(solution)/shard_map/ppermute | solution.py:36
  154.5 2.1 %maximum_select_fusion = bf16[768,256]{1,0:T(8,128)(2,1)} fusion(bf16[384,256]{1,0:T(8,128)(2,1)} %get-tuple-element.7, bf16[384,256]{1,0:T(8,128)(2,1)} %copy-done.3, pred[]{:T(512)S(6)} %eq.48), kind=kLoop, calls=%fused_computation.19 | loop fusion | flops 1769472 | bytes 786433 | tf_op jit(solution)/shard_map/jit(_where)/select_n | solution.py:90
  156.6 0.6 slice_multiply_fusion.1
  157.2 0.7 slice_multiply_fusion
  157.9 28.5 %collective-permute-done.6 = f32[6,128,256]{2,1,0:T(8,128)S(1)} collective-permute-done((f32[6,128,256]{2,1,0:T(8,128)}, f32[6,128,256]{2,1,0:T(8,128)S(1)}, u32[]{:S(2)}, u32[]{:S(2)}) %collective-permute-start.6) | collective-permute-done | bytes 786464 | tf_op jit(solution)/shard_map/ppermute | solution.py:96
  186.4 2.0 %add_convert_fusion = bf16[6,128,256]{2,1,0:T(8,128)(2,1)} fusion(f32[6,128,256]{2,1,0:T(8,128)} %fusion.11, f32[6,128,256]{2,1,0:T(8,128)S(1)} %collective-permute-done.6), kind=kLoop, calls=%fused_computation.14 | loop fusion | flops 393216 | bytes 1966080 | tf_op jit(solution)/shard_map/convert_element_type | solution.py:163
  (27 shorter events, 0.3 us)
Async XLA Ops:
  0.6 7.2 %copy-start = (bf16[6,6,128,128]{3,2,1,0:T(8,128)(2,1)S(1)}, bf16[6,6,128,128]{3,2,1,0:T(8,128)(2,1)}, u32[]{:S(2)}) copy-start(bf16[6,6,128,128]{3,2,1,0:T(8,128)(2,1)} %param.8) | copy-start | bytes 3538948
  0.6 9.4 %collective-permute-start = (bf16[768,256]{1,0:T(8,128)(2,1)}, bf16[768,256]{1,0:T(8,128)(2,1)S(1)}, u32[]{:S(2)}, u32[]{:S(2)}) collective-permute-start(bf16[768,256]{1,0:T(8,128)(2,1)} %param.7), channel_id=1, source_target_pairs={{0,2},{2,4},{4,6},{6,8},{8,10},{10,12},{12,14},{14,16},{16,18},{18... | collective-permute-start | bytes 1179656 | tf_op jit(solution)/shard_map/ppermute | solution.py:14
  2.7 12.4 %collective-permute-start.1 = (bf16[768,256]{1,0:T(8,128)(2,1)}, bf16[768,256]{1,0:T(8,128)(2,1)S(1)}, u32[]{:S(2)}, u32[]{:S(2)}) collective-permute-start(bf16[768,256]{1,0:T(8,128)(2,1)} %param.7), channel_id=1, source_target_pairs={{2,0},{4,2},{6,4},{8,6},{10,8},{12,10},{14,12},{16,14},{18,16},{20... | collective-permute-start | bytes 1179656 | tf_op jit(solution)/shard_map/ppermute | solution.py:17
  7.8 7.3 %copy-start.4 = (bf16[768,256]{1,0:T(8,128)(2,1)S(1)}, bf16[768,256]{1,0:T(8,128)(2,1)}, u32[]{:S(2)}) copy-start(bf16[768,256]{1,0:T(8,128)(2,1)} %param.7) | copy-start | bytes 1179652
  10.0 6.3 %copy-start.1 = (bf16[6,18,128,128]{3,1,2,0:T(8,128)(2,1)}, bf16[6,18,128,128]{3,1,2,0:T(8,128)(2,1)S(1)}, u32[]{:S(2)}) copy-start(bf16[6,18,128,128]{3,1,2,0:T(8,128)(2,1)S(1)} %convolution_convert_fusion) | copy-start | bytes 10616836
  15.2 19.0 %copy-start.5 = (bf16[256,256]{1,0:T(8,128)(2,1)S(1)}, bf16[256,256]{1,0:T(8,128)(2,1)}, u32[]{:S(2)}) copy-start(bf16[256,256]{1,0:T(8,128)(2,1)} %param.11) | copy-start | bytes 393220
  15.2 19.0 %copy-start.6 = (bf16[768,256]{1,0:T(8,128)(2,1)S(1)}, bf16[768,256]{1,0:T(8,128)(2,1)}, u32[]{:S(2)}) copy-start(bf16[768,256]{1,0:T(8,128)(2,1)} %param.13) | copy-start | bytes 1179652
  15.2 19.0 %copy-start.7 = (f32[256]{0:T(256)S(1)}, f32[256]{0:T(256)}, u32[]{:S(2)}) copy-start(f32[256]{0:T(256)} %param.12) | copy-start | bytes 3076
  16.3 17.7 %collective-permute-start.2 = (bf16[384,256]{1,0:T(8,128)(2,1)S(1)}, bf16[384,256]{1,0:T(8,128)(2,1)S(1)}, u32[]{:S(2)}, u32[]{:S(2)}) collective-permute-start(bf16[384,256]{1,0:T(8,128)(2,1)S(1)} %dynamic-slice_convert_fusion), channel_id=1, source_target_pairs={{0,1},{1,0},{2,3},{3,2},{4,5},{5,4},{6,7},{7,6},{8,9},{9,8},{10,11... | collective-permute-start | bytes 589832 | tf_op jit(solution)/shard_map/ppermute | solution.py:86
  34.5 15.0 %copy-start.3 = (bf16[384,256]{1,0:T(8,128)(2,1)}, bf16[384,256]{1,0:T(8,128)(2,1)S(1)}, u32[]{:S(2)}) copy-start(bf16[384,256]{1,0:T(8,128)(2,1)S(1)} %get-tuple-element.8) | copy-start | bytes 589828
  34.8 3.2 %collective-permute-start.7 = (f32[257,128]{1,0:T(8,128)S(1)}, f32[257,128]{1,0:T(8,128)S(1)}, u32[]{:S(2)}, u32[]{:S(2)}) collective-permute-start(f32[257,128]{1,0:T(8,128)S(1)} %fusion.12), channel_id=1, source_target_pairs={{0,2},{2,0},{4,6},{6,4},{8,10},{10,8},{12,14},{14,12},{16,18},{18,... | collective-permute-start | bytes 394760 | tf_op jit(solution)/shard_map/ppermute | solution.py:36
  38.1 18.8 %collective-permute-start.10 = (f32[257,128]{1,0:T(8,128)S(1)}, f32[257,128]{1,0:T(8,128)S(1)}, u32[]{:S(2)}, u32[]{:S(2)}) collective-permute-start(f32[257,128]{1,0:T(8,128)S(1)} %fusion.14), channel_id=1, source_target_pairs={{0,192},{2,194},{4,196},{6,198},{8,200},{10,202},{12,204},{14,206}... | collective-permute-start | bytes 394760 | tf_op jit(solution)/shard_map/ppermute | solution.py:36
  41.5 15.4 %collective-permute-start.9 = (f32[257,128]{1,0:T(8,128)S(1)}, f32[257,128]{1,0:T(8,128)S(1)}, u32[]{:S(2)}, u32[]{:S(2)}) collective-permute-start(f32[257,128]{1,0:T(8,128)S(1)} %fusion.14), channel_id=1, source_target_pairs={{0,384},{2,386},{4,388},{6,390},{8,392},{10,394},{12,396},{14,398}... | collective-permute-start | bytes 394760 | tf_op jit(solution)/shard_map/ppermute | solution.py:36
  46.2 10.8 %collective-permute-start.8 = (f32[257,128]{1,0:T(8,128)S(1)}, f32[257,128]{1,0:T(8,128)S(1)}, u32[]{:S(2)}, u32[]{:S(2)}) collective-permute-start(f32[257,128]{1,0:T(8,128)S(1)} %fusion.14), channel_id=1, source_target_pairs={{0,576},{2,578},{4,580},{6,582},{8,584},{10,586},{12,588},{14,590}... | collective-permute-start | bytes 394760 | tf_op jit(solution)/shard_map/ppermute | solution.py:36
  49.5 24.1 %collective-permute-start.3 = (bf16[384,512]{1,0:T(8,128)(2,1)S(1)}, bf16[384,512]{1,0:T(8,128)(2,1)S(1)}, u32[]{:S(2)}, u32[]{:S(2)}) collective-permute-start(bf16[384,512]{1,0:T(8,128)(2,1)S(1)} %pad_maximum_fusion.4), channel_id=1, source_target_pairs={{0,1},{1,0},{2,3},{3,2},{4,5},{5,4},{6,7},{7,6},{8,9},{9,8},{10,11... | collective-permute-start | bytes 1179656 | tf_op jit(solution)/shard_map/ppermute | solution.py:86
  57.1 23.8 %collective-permute-start.13 = (f32[257,128]{1,0:T(8,128)S(1)}, f32[257,128]{1,0:T(8,128)S(1)}, u32[]{:S(2)}, u32[]{:S(2)}) collective-permute-start(f32[257,128]{1,0:T(8,128)S(1)} %fusion.31), channel_id=1, source_target_pairs={{0,16},{2,18},{4,20},{6,22},{8,24},{10,26},{12,28},{14,30},{16,32}... | collective-permute-start | bytes 394760 | tf_op jit(solution)/shard_map/ppermute | solution.py:36
  59.0 21.9 %collective-permute-start.12 = (f32[257,128]{1,0:T(8,128)S(1)}, f32[257,128]{1,0:T(8,128)S(1)}, u32[]{:S(2)}, u32[]{:S(2)}) collective-permute-start(f32[257,128]{1,0:T(8,128)S(1)} %fusion.31), channel_id=1, source_target_pairs={{0,32},{2,34},{4,36},{6,38},{8,40},{10,42},{12,44},{14,46},{16,48}... | collective-permute-start | bytes 394760 | tf_op jit(solution)/shard_map/ppermute | solution.py:36
  62.1 18.8 %collective-permute-start.11 = (f32[257,128]{1,0:T(8,128)S(1)}, f32[257,128]{1,0:T(8,128)S(1)}, u32[]{:S(2)}, u32[]{:S(2)}) collective-permute-start(f32[257,128]{1,0:T(8,128)S(1)} %fusion.31), channel_id=1, source_target_pairs={{0,48},{2,50},{4,52},{6,54},{8,56},{10,58},{12,60},{14,62},{16,0},... | collective-permute-start | bytes 394760 | tf_op jit(solution)/shard_map/ppermute | solution.py:36
  79.0 63.1 %collective-permute-start.4 = (f32[6,128,256]{2,1,0:T(8,128)}, f32[6,128,256]{2,1,0:T(8,128)}, u32[]{:S(2)}, u32[]{:S(2)}) collective-permute-start(f32[6,128,256]{2,1,0:T(8,128)} %slice.32), channel_id=1, source_target_pairs={{2,0},{4,2},{6,4},{8,6},{10,8},{12,10},{14,12},{16,14},{18,16},{20... | collective-permute-start | bytes 2359304 | tf_op jit(solution)/shard_map/ppermute | solution.py:25
  81.0 0.8 copy-start.2
  82.5 20.8 %collective-permute-start.15 = (f32[257,128]{1,0:T(8,128)}, f32[257,128]{1,0:T(8,128)}, u32[]{:S(2)}, u32[]{:S(2)}) collective-permute-start(f32[257,128]{1,0:T(8,128)} %add_bitcast_fusion.1), channel_id=1, source_target_pairs={{0,128},{2,130},{4,132},{6,134},{8,136},{10,138},{12,140},{14,142}... | collective-permute-start | bytes 394760 | tf_op jit(solution)/shard_map/ppermute | solution.py:36
  95.0 17.2 %collective-permute-start.14 = (f32[257,128]{1,0:T(8,128)}, f32[257,128]{1,0:T(8,128)}, u32[]{:S(2)}, u32[]{:S(2)}) collective-permute-start(f32[257,128]{1,0:T(8,128)} %add_bitcast_fusion.1), channel_id=1, source_target_pairs={{0,64},{2,66},{4,68},{6,70},{8,72},{10,74},{12,76},{14,78},{16,80}... | collective-permute-start | bytes 394760 | tf_op jit(solution)/shard_map/ppermute | solution.py:36
  97.8 44.3 %collective-permute-start.5 = (bf16[6,128,256]{2,1,0:T(8,128)(2,1)}, bf16[6,128,256]{2,1,0:T(8,128)(2,1)}, u32[]{:S(2)}, u32[]{:S(2)}) collective-permute-start(bf16[6,128,256]{2,1,0:T(8,128)(2,1)} %slice.42), channel_id=1, source_target_pairs={{0,2},{2,4},{4,6},{6,8},{8,10},{10,12},{12,14},{14,16},{16,18},{18... | collective-permute-start | bytes 1179656 | tf_op jit(solution)/shard_map/ppermute | solution.py:25
  114.1 12.4 %collective-permute-start.18 = (f32[257,128]{1,0:T(8,128)}, f32[257,128]{1,0:T(8,128)}, u32[]{:S(2)}, u32[]{:S(2)}) collective-permute-start(f32[257,128]{1,0:T(8,128)} %select_add_fusion), channel_id=1, source_target_pairs={{0,4},{2,6},{4,8},{6,10},{8,12},{10,14},{12,0},{14,2},{16,20},{18,... | collective-permute-start | bytes 394760 | tf_op jit(solution)/shard_map/ppermute | solution.py:36
  119.4 12.0 %collective-permute-start.17 = (f32[257,128]{1,0:T(8,128)}, f32[257,128]{1,0:T(8,128)}, u32[]{:S(2)}, u32[]{:S(2)}) collective-permute-start(f32[257,128]{1,0:T(8,128)} %select_add_fusion), channel_id=1, source_target_pairs={{0,8},{2,10},{4,12},{6,14},{8,0},{10,2},{12,4},{14,6},{16,24},{18,... | collective-permute-start | bytes 394760 | tf_op jit(solution)/shard_map/ppermute | solution.py:36
  121.4 10.1 %collective-permute-start.16 = (f32[257,128]{1,0:T(8,128)}, f32[257,128]{1,0:T(8,128)}, u32[]{:S(2)}, u32[]{:S(2)}) collective-permute-start(f32[257,128]{1,0:T(8,128)} %select_add_fusion), channel_id=1, source_target_pairs={{0,12},{2,14},{4,0},{6,2},{8,4},{10,6},{12,8},{14,10},{16,28},{18,... | collective-permute-start | bytes 394760 | tf_op jit(solution)/shard_map/ppermute | solution.py:36
  132.6 19.9 %collective-permute-start.19 = (f32[257,128]{1,0:T(8,128)S(1)}, f32[257,128]{1,0:T(8,128)S(1)}, u32[]{:S(2)}, u32[]{:S(2)}) collective-permute-start(f32[257,128]{1,0:T(8,128)S(1)} %add_bitcast_fusion), channel_id=1, source_target_pairs={{0,1},{1,0},{2,3},{3,2},{4,5},{5,4},{6,7},{7,6},{8,9},{9,8},{10,11... | collective-permute-start | bytes 394760 | tf_op jit(solution)/shard_map/ppermute | solution.py:80
  144.4 42.0 %collective-permute-start.6 = (f32[6,128,256]{2,1,0:T(8,128)}, f32[6,128,256]{2,1,0:T(8,128)S(1)}, u32[]{:S(2)}, u32[]{:S(2)}) collective-permute-start(f32[6,128,256]{2,1,0:T(8,128)} %fusion.11), channel_id=1, source_target_pairs={{0,1},{1,0},{2,3},{3,2},{4,5},{5,4},{6,7},{7,6},{8,9},{9,8},{10,11... | collective-permute-start | bytes 2359304 | tf_op jit(solution)/shard_map/ppermute | solution.py:96
  152.6 4.0 %collective-permute-start.20 = (f32[257,128]{1,0:T(8,128)S(1)}, f32[257,128]{1,0:T(8,128)S(1)}, u32[]{:S(2)}, u32[]{:S(2)}) collective-permute-start(f32[257,128]{1,0:T(8,128)S(1)} %fusion.30), channel_id=1, source_target_pairs={{0,2},{2,0},{4,6},{6,4},{8,10},{10,8},{12,14},{14,12},{16,18},{18,... | collective-permute-start | bytes 394760 | tf_op jit(solution)/shard_map/ppermute | solution.py:36

commit v11 on v10

--- a/solution.py
+++ b/solution.py
@@ -76,7 +76,8 @@
     x = ring_sum(x, "rows", count, x_stride, x_size)
     x = ring_sum(x, "rows", count, z_stride, z_size // 3)
     x = three_way_sum(x, "rows", count, z_stride, z_size)
-    x = ring_sum(x, "rows", count, y_stride, y_size)
+    x = swapped_sum(x, "rows", count, y_stride, y_size, 1)
+    x = swapped_sum(x, "rows", count, y_stride, y_size, 2)
     x = x + lax.ppermute(x, "rep", [(0, 1), (1, 0)])
     other = moved(x, "rows", count, c_stride, c_size, lambda c: c ^ 1)
     return jnp.where(core == 0, jnp.concatenate([x, other], 1), jnp.concatenate([other, x], 1))

time: 189 us -> 187 us (0.989)
  the two profiles are of different devices: /device:TPU:200 before, /device:TPU:1 now
where the time goes in v11:
time: 187 us; the launch traced here: 183 us
  starting transfers between devices  100 us (53%)
  waiting for transfers between devices  59.1 us (32%)
  other arithmetic  11.6 us (6%)
  matrix products  7.69 us (4%)
  local copies, waits for them, and re-layouts  3.45 us (2%)
    ppermute x12, starting transfers between devices, moved(): return lax.ppermute(x, axis, pairs)  62.9 us
    ppermute x12, waiting for transfers between devices, moved(): return lax.ppermute(x, axis, pairs)  21.1 us
    ppermute x1, waiting for transfers between devices, partner_sum(): return x + lax.ppermute(x, 'rep', [(0, 1), (1, 0)])  19.7 us
    ppermute x2, waiting for transfers between devices, partner_swap(): return lax.ppermute(x, 'rep', [(0, 1), (1, 0)])  18.3 us
    ppermute x1, starting transfers between devices, global_sum(): x = x + lax.ppermute(x, 'rep', [(0, 1), (1, 0)])  10.1 us
    ppermute x1, starting transfers between devices, extended(): lax.ppermute(lax.slice_in_dim(block, 0, width, axis=dim), axis, backward)  9.15 us
    ppermute x2, starting transfers between devices, partner_swap(): return lax.ppermute(x, 'rep', [(0, 1), (1, 0)])  6.89 us
    ppermute x1, starting transfers between devices, extended(): lax.ppermute(lax.slice_in_dim(block, block.shape[dim] - width, None, axis...  4.73 us
  transfers between devices with their start and end apart: 20, of which 8 were waited for; matrix products, arithmetic and copies ran while one was open for 9% of the time, Pallas kernels for 0%

profile of v11, /device:TPU:1, one launch (start us, length us, event | category | flops | bytes accessed | tf_op | source)
XLA Modules:
  0.0 183.2 jit_solution(16464029446120432896)
XLA Ops:
  0.6 0.0 copy-start
  0.6 4.7 %collective-permute-start = (bf16[768,256]{1,0:T(8,128)(2,1)}, bf16[768,256]{1,0:T(8,128)(2,1)S(1)}, u32[]{:S(2)}, u32[]{:S(2)}) collective-permute-start(bf16[768,256]{1,0:T(8,128)(2,1)} %param.7), channel_id=1, source_target_pairs={{0,2},{2,4},{4,6},{6,8},{8,10},{10,12},{12,14},{14,16},{16,18},{18... | collective-permute-start | bytes 1179656 | tf_op jit(solution)/shard_map/ppermute | solution.py:14
  5.4 9.1 %collective-permute-start.1 = (bf16[768,256]{1,0:T(8,128)(2,1)}, bf16[768,256]{1,0:T(8,128)(2,1)S(1)}, u32[]{:S(2)}, u32[]{:S(2)}) collective-permute-start(bf16[768,256]{1,0:T(8,128)(2,1)} %param.7), channel_id=1, source_target_pairs={{2,0},{4,2},{6,4},{8,6},{10,8},{12,10},{14,12},{16,14},{18,16},{20... | collective-permute-start | bytes 1179656 | tf_op jit(solution)/shard_map/ppermute | solution.py:17
  14.5 0.7 broadcast_subtract_fusion
  15.2 0.7 iota_compare_fusion.1
  16.0 2.2 %convolution_convert_fusion = bf16[6,18,128,128]{3,1,2,0:T(8,128)(2,1)S(1)} fusion(bf16[6,6,128,128]{3,2,1,0:T(8,128)(2,1)S(1)} %copy-done, s32[6,6]{1,0:T(8,128)S(1)} %broadcast_subtract_fusion, pred[6,6]{1,0:T(8,128)(4,1)S(1)} %iota_compare_fusion.1), kind=kOutput, calls=%fused_computation.4 | convolution fusion | flops 23004432 | bytes 4718772 | tf_op jit(solution)/shard_map/bks,bkij->bsij/dot_general | solution.py:128
  18.2 0.0 collective-permute-done
  18.2 0.0 collective-permute-done.1
  18.2 0.1 pad_maximum_fusion
  18.3 0.0 copy-start.5
  18.3 0.0 copy-start.6
  18.4 0.0 copy-start.7
  18.4 1.1 fusion.8
  19.5 0.9 copy-done.1
  20.4 2.1 %collective-permute-start.2 = (bf16[384,256]{1,0:T(8,128)(2,1)S(1)}, bf16[384,256]{1,0:T(8,128)(2,1)S(1)}, u32[]{:S(2)}, u32[]{:S(2)}) collective-permute-start(bf16[384,256]{1,0:T(8,128)(2,1)S(1)} %dynamic-slice_convert_fusion), channel_id=1, source_target_pairs={{0,1},{1,0},{2,3},{3,2},{4,5},{5,4},{6,7},{7,6},{8,9},{9,8},{10,11... | collective-permute-start | bytes 589832 | tf_op jit(solution)/shard_map/ppermute | solution.py:87
  22.5 13.4 %collective-permute-done.2 = bf16[384,256]{1,0:T(8,128)(2,1)S(1)} collective-permute-done((bf16[384,256]{1,0:T(8,128)(2,1)S(1)}, bf16[384,256]{1,0:T(8,128)(2,1)S(1)}, u32[]{:S(2)}, u32[]{:S(2)}) %collective-permute-start.2) | collective-permute-done | bytes 196640 | tf_op jit(solution)/shard_map/ppermute | solution.py:87
  36.0 0.1 add_convert_fusion.1
  36.1 0.4 convert_reduce_fusion
  36.4 0.3 fusion.21
  36.7 2.3 %collective-permute-start.7 = (f32[257,128]{1,0:T(8,128)S(1)}, f32[257,128]{1,0:T(8,128)S(1)}, u32[]{:S(2)}, u32[]{:S(2)}) collective-permute-start(f32[257,128]{1,0:T(8,128)S(1)} %fusion.12), channel_id=1, source_target_pairs={{0,2},{2,0},{4,6},{6,4},{8,10},{10,8},{12,14},{14,12},{16,18},{18,... | collective-permute-start | bytes 394760 | tf_op jit(solution)/shard_map/ppermute | solution.py:36
  39.0 0.2 convolution_convert_fusion.1
  39.3 0.7 collective-permute-done.7
  40.0 6.3 %collective-permute-start.10 = (f32[257,128]{1,0:T(8,128)S(1)}, f32[257,128]{1,0:T(8,128)S(1)}, u32[]{:S(2)}, u32[]{:S(2)}) collective-permute-start(f32[257,128]{1,0:T(8,128)S(1)} %fusion.14), channel_id=1, source_target_pairs={{0,192},{2,194},{4,196},{6,198},{8,200},{10,202},{12,204},{14,206}... | collective-permute-start | bytes 394760 | tf_op jit(solution)/shard_map/ppermute | solution.py:36
  46.4 4.7 %collective-permute-start.9 = (f32[257,128]{1,0:T(8,128)S(1)}, f32[257,128]{1,0:T(8,128)S(1)}, u32[]{:S(2)}, u32[]{:S(2)}) collective-permute-start(f32[257,128]{1,0:T(8,128)S(1)} %fusion.14), channel_id=1, source_target_pairs={{0,384},{2,386},{4,388},{6,390},{8,392},{10,394},{12,396},{14,398}... | collective-permute-start | bytes 394760 | tf_op jit(solution)/shard_map/ppermute | solution.py:36
  51.0 2.8 %collective-permute-start.8 = (f32[257,128]{1,0:T(8,128)S(1)}, f32[257,128]{1,0:T(8,128)S(1)}, u32[]{:S(2)}, u32[]{:S(2)}) collective-permute-start(f32[257,128]{1,0:T(8,128)S(1)} %fusion.14), channel_id=1, source_target_pairs={{0,576},{2,578},{4,580},{6,582},{8,584},{10,586},{12,588},{14,590}... | collective-permute-start | bytes 394760 | tf_op jit(solution)/shard_map/ppermute | solution.py:36
  53.9 4.8 %collective-permute-start.3 = (bf16[384,512]{1,0:T(8,128)(2,1)S(1)}, bf16[384,512]{1,0:T(8,128)(2,1)S(1)}, u32[]{:S(2)}, u32[]{:S(2)}) collective-permute-start(bf16[384,512]{1,0:T(8,128)(2,1)S(1)} %pad_maximum_fusion.3), channel_id=1, source_target_pairs={{0,1},{1,0},{2,3},{3,2},{4,5},{5,4},{6,7},{7,6},{8,9},{9,8},{10,11... | collective-permute-start | bytes 1179656 | tf_op jit(solution)/shard_map/ppermute | solution.py:87
  58.9 0.0 collective-permute-done.10
  58.9 0.0 collective-permute-done.8
  58.9 0.1 fusion.30
  59.0 1.9 %collective-permute-start.13 = (f32[257,128]{1,0:T(8,128)S(1)}, f32[257,128]{1,0:T(8,128)S(1)}, u32[]{:S(2)}, u32[]{:S(2)}) collective-permute-start(f32[257,128]{1,0:T(8,128)S(1)} %fusion.30), channel_id=1, source_target_pairs={{0,16},{2,18},{4,20},{6,22},{8,24},{10,26},{12,28},{14,30},{16,32}... | collective-permute-start | bytes 394760 | tf_op jit(solution)/shard_map/ppermute | solution.py:36
  60.9 5.7 %collective-permute-start.12 = (f32[257,128]{1,0:T(8,128)S(1)}, f32[257,128]{1,0:T(8,128)S(1)}, u32[]{:S(2)}, u32[]{:S(2)}) collective-permute-start(f32[257,128]{1,0:T(8,128)S(1)} %fusion.30), channel_id=1, source_target_pairs={{0,32},{2,34},{4,36},{6,38},{8,40},{10,42},{12,44},{14,46},{16,48}... | collective-permute-start | bytes 394760 | tf_op jit(solution)/shard_map/ppermute | solution.py:36
  66.6 1.9 %collective-permute-start.11 = (f32[257,128]{1,0:T(8,128)S(1)}, f32[257,128]{1,0:T(8,128)S(1)}, u32[]{:S(2)}, u32[]{:S(2)}) collective-permute-start(f32[257,128]{1,0:T(8,128)S(1)} %fusion.30), channel_id=1, source_target_pairs={{0,48},{2,50},{4,52},{6,54},{8,56},{10,58},{12,60},{14,62},{16,0},... | collective-permute-start | bytes 394760 | tf_op jit(solution)/shard_map/ppermute | solution.py:36
  68.6 0.1 dynamic-slice_add_fusion
  68.6 4.9 %collective-permute-done.3 = bf16[384,512]{1,0:T(8,128)(2,1)S(1)} collective-permute-done((bf16[384,512]{1,0:T(8,128)(2,1)S(1)}, bf16[384,512]{1,0:T(8,128)(2,1)S(1)}, u32[]{:S(2)}, u32[]{:S(2)}) %collective-permute-start.3) | collective-permute-done | bytes 393248 | tf_op jit(solution)/shard_map/ppermute | solution.py:87
  73.5 0.7 fusion.20
  74.2 0.2 maximum_select_fusion.1
  74.4 3.5 %fusion.4 = f32[18,128,256]{2,1,0:T(8,128)S(1)} fusion(bf16[6,128,256,1]{2,1,0,3:T(8,128)(2,1)S(1)} %bitcast.43, bf16[6,18,128,128]{3,1,2,0:T(8,128)(2,1)} %copy-done.1), kind=kOutput, calls=%fused_computation.5 | convolution fusion | flops 905969664 | bytes 6291456 | tf_op jit(solution)/shard_map/bsij,bif->sjf/dot_general | solution.py:155
  77.9 1.0 slice.32
  78.9 2.4 %collective-permute-start.4 = (f32[6,128,256]{2,1,0:T(8,128)}, f32[6,128,256]{2,1,0:T(8,128)}, u32[]{:S(2)}, u32[]{:S(2)}) collective-permute-start(f32[6,128,256]{2,1,0:T(8,128)} %slice.32), channel_id=1, source_target_pairs={{2,0},{4,2},{6,4},{8,6},{10,8},{12,10},{14,12},{16,14},{18,16},{20... | collective-permute-start | bytes 2359304 | tf_op jit(solution)/shard_map/ppermute | solution.py:25
  81.3 0.0 collective-permute-done.12
  81.3 0.0 collective-permute-done.11
  81.4 0.8 copy-done.2
  82.1 0.7 add_bitcast_fusion
  82.8 15.3 %collective-permute-start.15 = (f32[257,128]{1,0:T(8,128)}, f32[257,128]{1,0:T(8,128)}, u32[]{:S(2)}, u32[]{:S(2)}) collective-permute-start(f32[257,128]{1,0:T(8,128)} %add_bitcast_fusion), channel_id=1, source_target_pairs={{0,128},{2,130},{4,132},{6,134},{8,136},{10,138},{12,140},{14,142}... | collective-permute-start | bytes 394760 | tf_op jit(solution)/shard_map/ppermute | solution.py:36
  98.2 1.9 %collective-permute-start.14 = (f32[257,128]{1,0:T(8,128)}, f32[257,128]{1,0:T(8,128)}, u32[]{:S(2)}, u32[]{:S(2)}) collective-permute-start(f32[257,128]{1,0:T(8,128)} %add_bitcast_fusion), channel_id=1, source_target_pairs={{0,64},{2,66},{4,68},{6,70},{8,72},{10,74},{12,76},{14,78},{16,80}... | collective-permute-start | bytes 394760 | tf_op jit(solution)/shard_map/ppermute | solution.py:36
  100.2 1.9 %collective-permute-start.5 = (bf16[6,128,256]{2,1,0:T(8,128)(2,1)S(1)}, bf16[6,128,256]{2,1,0:T(8,128)(2,1)S(1)}, u32[]{:S(2)}, u32[]{:S(2)}) collective-permute-start(bf16[6,128,256]{2,1,0:T(8,128)(2,1)S(1)} %slice.42), channel_id=1, source_target_pairs={{0,2},{2,4},{4,6},{6,8},{8,10},{10,12},{12,14},{14,16},{16,18},{18... | collective-permute-start | bytes 1179656 | tf_op jit(solution)/shard_map/ppermute | solution.py:25
  102.1 4.5 %collective-permute-done.15 = f32[257,128]{1,0:T(8,128)} collective-permute-done((f32[257,128]{1,0:T(8,128)}, f32[257,128]{1,0:T(8,128)}, u32[]{:S(2)}, u32[]{:S(2)}) %collective-permute-start.15) | collective-permute-done | bytes 131616 | tf_op jit(solution)/shard_map/ppermute | solution.py:36
  106.6 4.3 %collective-permute-done.14 = f32[257,128]{1,0:T(8,128)} collective-permute-done((f32[257,128]{1,0:T(8,128)}, f32[257,128]{1,0:T(8,128)}, u32[]{:S(2)}, u32[]{:S(2)}) %collective-permute-start.14) | collective-permute-done | bytes 131616 | tf_op jit(solution)/shard_map/ppermute | solution.py:36
  110.9 1.3 select_add_fusion
  112.2 1.9 %collective-permute-start.16 = (f32[257,128]{1,0:T(8,128)S(1)}, f32[257,128]{1,0:T(8,128)S(1)}, u32[]{:S(2)}, u32[]{:S(2)}) collective-permute-start(f32[257,128]{1,0:T(8,128)S(1)} %select_add_fusion), channel_id=1, source_target_pairs={{0,4},{2,6},{4,0},{6,2},{8,12},{10,14},{12,8},{14,10},{16,20},{18,... | collective-permute-start | bytes 394760 | tf_op jit(solution)/shard_map/ppermute | solution.py:36
  114.1 6.4 %collective-permute-done.16 = f32[257,128]{1,0:T(8,128)S(1)} collective-permute-done((f32[257,128]{1,0:T(8,128)S(1)}, f32[257,128]{1,0:T(8,128)S(1)}, u32[]{:S(2)}, u32[]{:S(2)}) %collective-permute-start.16) | collective-permute-done | bytes 131616 | tf_op jit(solution)/shard_map/ppermute | solution.py:36
  120.6 2.0 %collective-permute-start.17 = (f32[257,128]{1,0:T(8,128)S(1)}, f32[257,128]{1,0:T(8,128)S(1)}, u32[]{:S(2)}, u32[]{:S(2)}) collective-permute-start(f32[257,128]{1,0:T(8,128)S(1)} %add.200), channel_id=1, source_target_pairs={{0,8},{2,10},{4,12},{6,14},{8,0},{10,2},{12,4},{14,6},{16,24},{18,... | collective-permute-start | bytes 394760 | tf_op jit(solution)/shard_map/ppermute | solution.py:36
  122.6 5.1 %collective-permute-done.17 = f32[257,128]{1,0:T(8,128)S(1)} collective-permute-done((f32[257,128]{1,0:T(8,128)S(1)}, f32[257,128]{1,0:T(8,128)S(1)}, u32[]{:S(2)}, u32[]{:S(2)}) %collective-permute-start.17) | collective-permute-done | bytes 131616 | tf_op jit(solution)/shard_map/ppermute | solution.py:36
  127.7 10.1 %collective-permute-start.18 = (f32[257,128]{1,0:T(8,128)S(1)}, f32[257,128]{1,0:T(8,128)S(1)}, u32[]{:S(2)}, u32[]{:S(2)}) collective-permute-start(f32[257,128]{1,0:T(8,128)S(1)} %add.201), channel_id=1, source_target_pairs={{0,1},{1,0},{2,3},{3,2},{4,5},{5,4},{6,7},{7,6},{8,9},{9,8},{10,11... | collective-permute-start | bytes 394760 | tf_op jit(solution)/shard_map/ppermute | solution.py:81
  137.8 0.0 collective-permute-done.4
  137.8 2.2 %fusion.11 = f32[6,128,256]{2,1,0:T(8,128)} fusion(f32[6,128,256]{2,1,0:T(8,128)} %collective-permute-done.4, f32[18,128,256]{2,1,0:T(8,128)S(1)} %fusion.4, bf16[6,128,256]{2,1,0:T(8,128)(2,1)S(1)} %collective-permute-done.5), kind=kLoop, calls=%fused_computation.13 | loop fusion | flops 589824 | bytes 2752512 | tf_op jit(solution)/shard_map/add | solution.py:162
  140.0 1.9 %collective-permute-start.6 = (f32[6,128,256]{2,1,0:T(8,128)}, f32[6,128,256]{2,1,0:T(8,128)S(1)}, u32[]{:S(2)}, u32[]{:S(2)}) collective-permute-start(f32[6,128,256]{2,1,0:T(8,128)} %fusion.11), channel_id=1, source_target_pairs={{0,1},{1,0},{2,3},{3,2},{4,5},{5,4},{6,7},{7,6},{8,9},{9,8},{10,11... | collective-permute-start | bytes 2359304 | tf_op jit(solution)/shard_map/ppermute | solution.py:97
  141.9 0.0 collective-permute-done.18
  142.0 16.2 %collective-permute-start.19 = (f32[257,128]{1,0:T(8,128)S(1)}, f32[257,128]{1,0:T(8,128)S(1)}, u32[]{:S(2)}, u32[]{:S(2)}) collective-permute-start(f32[257,128]{1,0:T(8,128)S(1)} %add.202), channel_id=1, source_target_pairs={{0,2},{2,0},{4,6},{6,4},{8,10},{10,8},{12,14},{14,12},{16,18},{18,... | collective-permute-start | bytes 394760 | tf_op jit(solution)/shard_map/ppermute | solution.py:36
  158.2 2.1 %maximum_select_fusion = bf16[768,256]{1,0:T(8,128)(2,1)} fusion(bf16[384,256]{1,0:T(8,128)(2,1)} %get-tuple-element.7, bf16[384,256]{1,0:T(8,128)(2,1)} %copy-done.3, pred[]{:T(512)S(6)} %eq.43), kind=kLoop, calls=%fused_computation.18 | loop fusion | flops 1769472 | bytes 786433 | tf_op jit(solution)/shard_map/jit(_where)/select_n | solution.py:91
  160.3 0.6 slice_multiply_fusion.1
  160.8 0.7 slice_multiply_fusion
  161.6 19.7 %collective-permute-done.6 = f32[6,128,256]{2,1,0:T(8,128)S(1)} collective-permute-done((f32[6,128,256]{2,1,0:T(8,128)}, f32[6,128,256]{2,1,0:T(8,128)S(1)}, u32[]{:S(2)}, u32[]{:S(2)}) %collective-permute-start.6) | collective-permute-done | bytes 786464 | tf_op jit(solution)/shard_map/ppermute | solution.py:97
  181.2 2.0 %add_convert_fusion = bf16[6,128,256]{2,1,0:T(8,128)(2,1)} fusion(f32[6,128,256]{2,1,0:T(8,128)} %fusion.11, f32[6,128,256]{2,1,0:T(8,128)S(1)} %collective-permute-done.6), kind=kLoop, calls=%fused_computation.14 | loop fusion | flops 393216 | bytes 1966080 | tf_op jit(solution)/shard_map/convert_element_type | solution.py:164
  (25 shorter events, 0.3 us)
Async XLA Ops:
  0.6 15.3 %copy-start = (bf16[6,6,128,128]{3,2,1,0:T(8,128)(2,1)S(1)}, bf16[6,6,128,128]{3,2,1,0:T(8,128)(2,1)}, u32[]{:S(2)}) copy-start(bf16[6,6,128,128]{3,2,1,0:T(8,128)(2,1)} %param.8) | copy-start | bytes 3538948
  0.6 17.6 %collective-permute-start = (bf16[768,256]{1,0:T(8,128)(2,1)}, bf16[768,256]{1,0:T(8,128)(2,1)S(1)}, u32[]{:S(2)}, u32[]{:S(2)}) collective-permute-start(bf16[768,256]{1,0:T(8,128)(2,1)} %param.7), channel_id=1, source_target_pairs={{0,2},{2,4},{4,6},{6,8},{8,10},{10,12},{12,14},{14,16},{16,18},{18... | collective-permute-start | bytes 1179656 | tf_op jit(solution)/shard_map/ppermute | solution.py:14
  5.4 12.8 %collective-permute-start.1 = (bf16[768,256]{1,0:T(8,128)(2,1)}, bf16[768,256]{1,0:T(8,128)(2,1)S(1)}, u32[]{:S(2)}, u32[]{:S(2)}) collective-permute-start(bf16[768,256]{1,0:T(8,128)(2,1)} %param.7), channel_id=1, source_target_pairs={{2,0},{4,2},{6,4},{8,6},{10,8},{12,10},{14,12},{16,14},{18,16},{20... | collective-permute-start | bytes 1179656 | tf_op jit(solution)/shard_map/ppermute | solution.py:17
  16.0 2.3 %copy-start.4 = (bf16[768,256]{1,0:T(8,128)(2,1)S(1)}, bf16[768,256]{1,0:T(8,128)(2,1)}, u32[]{:S(2)}) copy-start(bf16[768,256]{1,0:T(8,128)(2,1)} %param.7) | copy-start | bytes 1179652
  18.2 2.1 %copy-start.1 = (bf16[6,18,128,128]{3,1,2,0:T(8,128)(2,1)}, bf16[6,18,128,128]{3,1,2,0:T(8,128)(2,1)S(1)}, u32[]{:S(2)}) copy-start(bf16[6,18,128,128]{3,1,2,0:T(8,128)(2,1)S(1)} %convolution_convert_fusion) | copy-start | bytes 10616836
  18.3 17.7 %copy-start.5 = (bf16[256,256]{1,0:T(8,128)(2,1)S(1)}, bf16[256,256]{1,0:T(8,128)(2,1)}, u32[]{:S(2)}) copy-start(bf16[256,256]{1,0:T(8,128)(2,1)} %param.11) | copy-start | bytes 393220
  18.3 17.7 %copy-start.6 = (bf16[768,256]{1,0:T(8,128)(2,1)S(1)}, bf16[768,256]{1,0:T(8,128)(2,1)}, u32[]{:S(2)}) copy-start(bf16[768,256]{1,0:T(8,128)(2,1)} %param.13) | copy-start | bytes 1179652
  18.4 17.7 %copy-start.7 = (f32[256]{0:T(256)S(1)}, f32[256]{0:T(256)}, u32[]{:S(2)}) copy-start(f32[256]{0:T(256)} %param.12) | copy-start | bytes 3076
  20.4 15.6 %collective-permute-start.2 = (bf16[384,256]{1,0:T(8,128)(2,1)S(1)}, bf16[384,256]{1,0:T(8,128)(2,1)S(1)}, u32[]{:S(2)}, u32[]{:S(2)}) collective-permute-start(bf16[384,256]{1,0:T(8,128)(2,1)S(1)} %dynamic-slice_convert_fusion), channel_id=1, source_target_pairs={{0,1},{1,0},{2,3},{3,2},{4,5},{5,4},{6,7},{7,6},{8,9},{9,8},{10,11... | collective-permute-start | bytes 589832 | tf_op jit(solution)/shard_map/ppermute | solution.py:87
  36.4 17.4 %copy-start.3 = (bf16[384,256]{1,0:T(8,128)(2,1)}, bf16[384,256]{1,0:T(8,128)(2,1)S(1)}, u32[]{:S(2)}) copy-start(bf16[384,256]{1,0:T(8,128)(2,1)S(1)} %get-tuple-element.8) | copy-start | bytes 589828
  36.7 3.3 %collective-permute-start.7 = (f32[257,128]{1,0:T(8,128)S(1)}, f32[257,128]{1,0:T(8,128)S(1)}, u32[]{:S(2)}, u32[]{:S(2)}) collective-permute-start(f32[257,128]{1,0:T(8,128)S(1)} %fusion.12), channel_id=1, source_target_pairs={{0,2},{2,0},{4,6},{6,4},{8,10},{10,8},{12,14},{14,12},{16,18},{18,... | collective-permute-start | bytes 394760 | tf_op jit(solution)/shard_map/ppermute | solution.py:36
  40.0 18.8 %collective-permute-start.10 = (f32[257,128]{1,0:T(8,128)S(1)}, f32[257,128]{1,0:T(8,128)S(1)}, u32[]{:S(2)}, u32[]{:S(2)}) collective-permute-start(f32[257,128]{1,0:T(8,128)S(1)} %fusion.14), channel_id=1, source_target_pairs={{0,192},{2,194},{4,196},{6,198},{8,200},{10,202},{12,204},{14,206}... | collective-permute-start | bytes 394760 | tf_op jit(solution)/shard_map/ppermute | solution.py:36
  46.4 12.5 %collective-permute-start.9 = (f32[257,128]{1,0:T(8,128)S(1)}, f32[257,128]{1,0:T(8,128)S(1)}, u32[]{:S(2)}, u32[]{:S(2)}) collective-permute-start(f32[257,128]{1,0:T(8,128)S(1)} %fusion.14), channel_id=1, source_target_pairs={{0,384},{2,386},{4,388},{6,390},{8,392},{10,394},{12,396},{14,398}... | collective-permute-start | bytes 394760 | tf_op jit(solution)/shard_map/ppermute | solution.py:36
  51.0 7.8 %collective-permute-start.8 = (f32[257,128]{1,0:T(8,128)S(1)}, f32[257,128]{1,0:T(8,128)S(1)}, u32[]{:S(2)}, u32[]{:S(2)}) collective-permute-start(f32[257,128]{1,0:T(8,128)S(1)} %fusion.14), channel_id=1, source_target_pairs={{0,576},{2,578},{4,580},{6,582},{8,584},{10,586},{12,588},{14,590}... | collective-permute-start | bytes 394760 | tf_op jit(solution)/shard_map/ppermute | solution.py:36
  53.9 19.7 %collective-permute-start.3 = (bf16[384,512]{1,0:T(8,128)(2,1)S(1)}, bf16[384,512]{1,0:T(8,128)(2,1)S(1)}, u32[]{:S(2)}, u32[]{:S(2)}) collective-permute-start(bf16[384,512]{1,0:T(8,128)(2,1)S(1)} %pad_maximum_fusion.3), channel_id=1, source_target_pairs={{0,1},{1,0},{2,3},{3,2},{4,5},{5,4},{6,7},{7,6},{8,9},{9,8},{10,11... | collective-permute-start | bytes 1179656 | tf_op jit(solution)/shard_map/ppermute | solution.py:87
  59.0 22.3 %collective-permute-start.13 = (f32[257,128]{1,0:T(8,128)S(1)}, f32[257,128]{1,0:T(8,128)S(1)}, u32[]{:S(2)}, u32[]{:S(2)}) collective-permute-start(f32[257,128]{1,0:T(8,128)S(1)} %fusion.30), channel_id=1, source_target_pairs={{0,16},{2,18},{4,20},{6,22},{8,24},{10,26},{12,28},{14,30},{16,32}... | collective-permute-start | bytes 394760 | tf_op jit(solution)/shard_map/ppermute | solution.py:36
  60.9 20.4 %collective-permute-start.12 = (f32[257,128]{1,0:T(8,128)S(1)}, f32[257,128]{1,0:T(8,128)S(1)}, u32[]{:S(2)}, u32[]{:S(2)}) collective-permute-start(f32[257,128]{1,0:T(8,128)S(1)} %fusion.30), channel_id=1, source_target_pairs={{0,32},{2,34},{4,36},{6,38},{8,40},{10,42},{12,44},{14,46},{16,48}... | collective-permute-start | bytes 394760 | tf_op jit(solution)/shard_map/ppermute | solution.py:36
  66.6 14.7 %collective-permute-start.11 = (f32[257,128]{1,0:T(8,128)S(1)}, f32[257,128]{1,0:T(8,128)S(1)}, u32[]{:S(2)}, u32[]{:S(2)}) collective-permute-start(f32[257,128]{1,0:T(8,128)S(1)} %fusion.30), channel_id=1, source_target_pairs={{0,48},{2,50},{4,52},{6,54},{8,56},{10,58},{12,60},{14,62},{16,0},... | collective-permute-start | bytes 394760 | tf_op jit(solution)/shard_map/ppermute | solution.py:36
  78.9 59.0 %collective-permute-start.4 = (f32[6,128,256]{2,1,0:T(8,128)}, f32[6,128,256]{2,1,0:T(8,128)}, u32[]{:S(2)}, u32[]{:S(2)}) collective-permute-start(f32[6,128,256]{2,1,0:T(8,128)} %slice.32), channel_id=1, source_target_pairs={{2,0},{4,2},{6,4},{8,6},{10,8},{12,10},{14,12},{16,14},{18,16},{20... | collective-permute-start | bytes 2359304 | tf_op jit(solution)/shard_map/ppermute | solution.py:25
  81.3 0.8 copy-start.2
  82.8 23.8 %collective-permute-start.15 = (f32[257,128]{1,0:T(8,128)}, f32[257,128]{1,0:T(8,128)}, u32[]{:S(2)}, u32[]{:S(2)}) collective-permute-start(f32[257,128]{1,0:T(8,128)} %add_bitcast_fusion), channel_id=1, source_target_pairs={{0,128},{2,130},{4,132},{6,134},{8,136},{10,138},{12,140},{14,142}... | collective-permute-start | bytes 394760 | tf_op jit(solution)/shard_map/ppermute | solution.py:36
  98.2 12.8 %collective-permute-start.14 = (f32[257,128]{1,0:T(8,128)}, f32[257,128]{1,0:T(8,128)}, u32[]{:S(2)}, u32[]{:S(2)}) collective-permute-start(f32[257,128]{1,0:T(8,128)} %add_bitcast_fusion), channel_id=1, source_target_pairs={{0,64},{2,66},{4,68},{6,70},{8,72},{10,74},{12,76},{14,78},{16,80}... | collective-permute-start | bytes 394760 | tf_op jit(solution)/shard_map/ppermute | solution.py:36
  100.2 37.6 %collective-permute-start.5 = (bf16[6,128,256]{2,1,0:T(8,128)(2,1)S(1)}, bf16[6,128,256]{2,1,0:T(8,128)(2,1)S(1)}, u32[]{:S(2)}, u32[]{:S(2)}) collective-permute-start(bf16[6,128,256]{2,1,0:T(8,128)(2,1)S(1)} %slice.42), channel_id=1, source_target_pairs={{0,2},{2,4},{4,6},{6,8},{8,10},{10,12},{12,14},{14,16},{16,18},{18... | collective-permute-start | bytes 1179656 | tf_op jit(solution)/shard_map/ppermute | solution.py:25
  112.2 8.3 %collective-permute-start.16 = (f32[257,128]{1,0:T(8,128)S(1)}, f32[257,128]{1,0:T(8,128)S(1)}, u32[]{:S(2)}, u32[]{:S(2)}) collective-permute-start(f32[257,128]{1,0:T(8,128)S(1)} %select_add_fusion), channel_id=1, source_target_pairs={{0,4},{2,6},{4,0},{6,2},{8,12},{10,14},{12,8},{14,10},{16,20},{18,... | collective-permute-start | bytes 394760 | tf_op jit(solution)/shard_map/ppermute | solution.py:36
  120.6 7.1 %collective-permute-start.17 = (f32[257,128]{1,0:T(8,128)S(1)}, f32[257,128]{1,0:T(8,128)S(1)}, u32[]{:S(2)}, u32[]{:S(2)}) collective-permute-start(f32[257,128]{1,0:T(8,128)S(1)} %add.200), channel_id=1, source_target_pairs={{0,8},{2,10},{4,12},{6,14},{8,0},{10,2},{12,4},{14,6},{16,24},{18,... | collective-permute-start | bytes 394760 | tf_op jit(solution)/shard_map/ppermute | solution.py:36
  127.7 14.3 %collective-permute-start.18 = (f32[257,128]{1,0:T(8,128)S(1)}, f32[257,128]{1,0:T(8,128)S(1)}, u32[]{:S(2)}, u32[]{:S(2)}) collective-permute-start(f32[257,128]{1,0:T(8,128)S(1)} %add.201), channel_id=1, source_target_pairs={{0,1},{1,0},{2,3},{3,2},{4,5},{5,4},{6,7},{7,6},{8,9},{9,8},{10,11... | collective-permute-start | bytes 394760 | tf_op jit(solution)/shard_map/ppermute | solution.py:81
  140.0 41.2 %collective-permute-start.6 = (f32[6,128,256]{2,1,0:T(8,128)}, f32[6,128,256]{2,1,0:T(8,128)S(1)}, u32[]{:S(2)}, u32[]{:S(2)}) collective-permute-start(f32[6,128,256]{2,1,0:T(8,128)} %fusion.11), channel_id=1, source_target_pairs={{0,1},{1,0},{2,3},{3,2},{4,5},{5,4},{6,7},{7,6},{8,9},{9,8},{10,11... | collective-permute-start | bytes 2359304 | tf_op jit(solution)/shard_map/ppermute | solution.py:97
  142.0 18.2 %collective-permute-start.19 = (f32[257,128]{1,0:T(8,128)S(1)}, f32[257,128]{1,0:T(8,128)S(1)}, u32[]{:S(2)}, u32[]{:S(2)}) collective-permute-start(f32[257,128]{1,0:T(8,128)S(1)} %add.202), channel_id=1, source_target_pairs={{0,2},{2,0},{4,6},{6,4},{8,10},{10,8},{12,14},{14,12},{16,18},{18,... | collective-permute-start | bytes 394760 | tf_op jit(solution)/shard_map/ppermute | solution.py:36

commit v12 on v11

--- a/solution.py
+++ b/solution.py
@@ -74,11 +74,12 @@
     give = lax.dynamic_slice_in_dim(x, (1 - core) * width, width, 1)
     x = keep + moved(give, "rows", count, c_stride, c_size, lambda c: c ^ 1)
     x = ring_sum(x, "rows", count, x_stride, x_size)
-    x = ring_sum(x, "rows", count, z_stride, z_size // 3)
-    x = three_way_sum(x, "rows", count, z_stride, z_size)
     x = swapped_sum(x, "rows", count, y_stride, y_size, 1)
     x = swapped_sum(x, "rows", count, y_stride, y_size, 2)
     x = x + lax.ppermute(x, "rep", [(0, 1), (1, 0)])
+    x = swapped_sum(x, "rows", count, z_stride, z_size, 1)
+    x = swapped_sum(x, "rows", count, z_stride, z_size, 2)
+    x = three_way_sum(x, "rows", count, z_stride, z_size)
     other = moved(x, "rows", count, c_stride, c_size, lambda c: c ^ 1)
     return jnp.where(core == 0, jnp.concatenate([x, other], 1), jnp.concatenate([other, x], 1))
 

time: 187 us -> 181 us (0.968)
  the two profiles are of different devices: /device:TPU:1 before, /device:TPU:56 now
where the time goes in v12:
time: 181 us; the launch traced here: 180 us
  starting transfers between devices  87.7 us (48%)
  waiting for transfers between devices  69.9 us (39%)
  other arithmetic  11.3 us (6%)
  matrix products  7.69 us (4%)
  local copies, waits for them, and re-layouts  2.54 us (1%)
    ppermute x11, starting transfers between devices, moved(): return lax.ppermute(x, axis, pairs)  57 us
    ppermute x11, waiting for transfers between devices, moved(): return lax.ppermute(x, axis, pairs)  29.2 us
    ppermute x1, waiting for transfers between devices, partner_sum(): return x + lax.ppermute(x, 'rep', [(0, 1), (1, 0)])  20.7 us
    ppermute x2, waiting for transfers between devices, partner_swap(): return lax.ppermute(x, 'rep', [(0, 1), (1, 0)])  11.9 us
    ppermute x2, starting transfers between devices, partner_swap(): return lax.ppermute(x, 'rep', [(0, 1), (1, 0)])  8.47 us
    ppermute x1, starting transfers between devices, partner_sum(): return x + lax.ppermute(x, 'rep', [(0, 1), (1, 0)])  7.99 us
    ppermute x1, waiting for transfers between devices, global_sum(): x = x + lax.ppermute(x, 'rep', [(0, 1), (1, 0)])  6.29 us
    ppermute x1, starting transfers between devices, global_sum(): x = x + lax.ppermute(x, 'rep', [(0, 1), (1, 0)])  4.73 us
  transfers between devices with their start and end apart: 19, of which 11 were waited for; matrix products, arithmetic and copies ran while one was open for 10% of the time, Pallas kernels for 0%

profile of v12, /device:TPU:56, one launch (start us, length us, event | category | flops | bytes accessed | tf_op | source)
XLA Modules:
  0.0 180.5 jit_solution(10166548981698982179)
XLA Ops:
  0.6 0.0 copy-start
  0.6 2.1 %collective-permute-start = (bf16[768,256]{1,0:T(8,128)(2,1)}, bf16[768,256]{1,0:T(8,128)(2,1)S(1)}, u32[]{:S(2)}, u32[]{:S(2)}) collective-permute-start(bf16[768,256]{1,0:T(8,128)(2,1)} %param.7), channel_id=1, source_target_pairs={{0,2},{2,4},{4,6},{6,8},{8,10},{10,12},{12,14},{14,16},{16,18},{18... | collective-permute-start | bytes 1179656 | tf_op jit(solution)/shard_map/ppermute | solution.py:14
  2.7 3.6 %collective-permute-start.1 = (bf16[768,256]{1,0:T(8,128)(2,1)}, bf16[768,256]{1,0:T(8,128)(2,1)S(1)}, u32[]{:S(2)}, u32[]{:S(2)}) collective-permute-start(bf16[768,256]{1,0:T(8,128)(2,1)} %param.7), channel_id=1, source_target_pairs={{2,0},{4,2},{6,4},{8,6},{10,8},{12,10},{14,12},{16,14},{18,16},{20... | collective-permute-start | bytes 1179656 | tf_op jit(solution)/shard_map/ppermute | solution.py:17
  6.4 0.7 broadcast_subtract_fusion
  7.1 0.7 iota_compare_fusion.1
  7.8 2.2 %convolution_convert_fusion = bf16[6,18,128,128]{3,1,2,0:T(8,128)(2,1)S(1)} fusion(bf16[6,6,128,128]{3,2,1,0:T(8,128)(2,1)S(1)} %copy-done, s32[6,6]{1,0:T(8,128)S(1)} %broadcast_subtract_fusion, pred[6,6]{1,0:T(8,128)(4,1)S(1)} %iota_compare_fusion.1), kind=kOutput, calls=%fused_computation.4 | convolution fusion | flops 23004432 | bytes 4718772 | tf_op jit(solution)/shard_map/bks,bkij->bsij/dot_general | solution.py:129
  10.0 0.0 collective-permute-done
  10.1 1.9 %collective-permute-done.1 = bf16[768,256]{1,0:T(8,128)(2,1)S(1)} collective-permute-done((bf16[768,256]{1,0:T(8,128)(2,1)}, bf16[768,256]{1,0:T(8,128)(2,1)S(1)}, u32[]{:S(2)}, u32[]{:S(2)}) %collective-permute-start.1) | collective-permute-done | bytes 393248 | tf_op jit(solution)/shard_map/ppermute | solution.py:17
  12.0 0.1 pad_maximum_fusion
  12.0 0.0 copy-start.4
  12.0 0.0 copy-start.5
  12.1 0.0 copy-start.6
  12.1 1.1 fusion.8
  13.2 4.7 %collective-permute-start.2 = (bf16[384,256]{1,0:T(8,128)(2,1)S(1)}, bf16[384,256]{1,0:T(8,128)(2,1)S(1)}, u32[]{:S(2)}, u32[]{:S(2)}) collective-permute-start(bf16[384,256]{1,0:T(8,128)(2,1)S(1)} %dynamic-slice_convert_fusion), channel_id=1, source_target_pairs={{0,1},{1,0},{2,3},{3,2},{4,5},{5,4},{6,7},{7,6},{8,9},{9,8},{10,11... | collective-permute-start | bytes 589832 | tf_op jit(solution)/shard_map/ppermute | solution.py:88
  18.0 7.0 %collective-permute-done.2 = bf16[384,256]{1,0:T(8,128)(2,1)S(1)} collective-permute-done((bf16[384,256]{1,0:T(8,128)(2,1)S(1)}, bf16[384,256]{1,0:T(8,128)(2,1)S(1)}, u32[]{:S(2)}, u32[]{:S(2)}) %collective-permute-start.2) | collective-permute-done | bytes 196640 | tf_op jit(solution)/shard_map/ppermute | solution.py:88
  24.9 0.1 add_convert_fusion.1
  25.0 0.4 convert_reduce_fusion
  25.4 0.3 fusion.21
  25.7 10.7 %collective-permute-start.7 = (f32[257,128]{1,0:T(8,128)S(1)}, f32[257,128]{1,0:T(8,128)S(1)}, u32[]{:S(2)}, u32[]{:S(2)}) collective-permute-start(f32[257,128]{1,0:T(8,128)S(1)} %fusion.12), channel_id=1, source_target_pairs={{0,2},{2,0},{4,6},{6,4},{8,10},{10,8},{12,14},{14,12},{16,18},{18,... | collective-permute-start | bytes 394760 | tf_op jit(solution)/shard_map/ppermute | solution.py:36
  36.4 0.2 convolution_convert_fusion.1
  36.7 3.8 %collective-permute-start.3 = (bf16[384,512]{1,0:T(8,128)(2,1)S(1)}, bf16[384,512]{1,0:T(8,128)(2,1)S(1)}, u32[]{:S(2)}, u32[]{:S(2)}) collective-permute-start(bf16[384,512]{1,0:T(8,128)(2,1)S(1)} %pad_maximum_fusion.2), channel_id=1, source_target_pairs={{0,1},{1,0},{2,3},{3,2},{4,5},{5,4},{6,7},{7,6},{8,9},{9,8},{10,11... | collective-permute-start | bytes 1179656 | tf_op jit(solution)/shard_map/ppermute | solution.py:88
  40.4 0.0 collective-permute-done.7
  40.5 3.4 %collective-permute-start.10 = (f32[257,128]{1,0:T(8,128)S(1)}, f32[257,128]{1,0:T(8,128)S(1)}, u32[]{:S(2)}, u32[]{:S(2)}) collective-permute-start(f32[257,128]{1,0:T(8,128)S(1)} %fusion.14), channel_id=1, source_target_pairs={{0,192},{2,194},{4,196},{6,198},{8,200},{10,202},{12,204},{14,206}... | collective-permute-start | bytes 394760 | tf_op jit(solution)/shard_map/ppermute | solution.py:36
  43.9 3.5 %collective-permute-start.9 = (f32[257,128]{1,0:T(8,128)S(1)}, f32[257,128]{1,0:T(8,128)S(1)}, u32[]{:S(2)}, u32[]{:S(2)}) collective-permute-start(f32[257,128]{1,0:T(8,128)S(1)} %fusion.14), channel_id=1, source_target_pairs={{0,384},{2,386},{4,388},{6,390},{8,392},{10,394},{12,396},{14,398}... | collective-permute-start | bytes 394760 | tf_op jit(solution)/shard_map/ppermute | solution.py:36
  47.3 4.5 %collective-permute-start.8 = (f32[257,128]{1,0:T(8,128)S(1)}, f32[257,128]{1,0:T(8,128)S(1)}, u32[]{:S(2)}, u32[]{:S(2)}) collective-permute-start(f32[257,128]{1,0:T(8,128)S(1)} %fusion.14), channel_id=1, source_target_pairs={{0,576},{2,578},{4,580},{6,582},{8,584},{10,586},{12,588},{14,590}... | collective-permute-start | bytes 394760 | tf_op jit(solution)/shard_map/ppermute | solution.py:36
  52.0 0.0 collective-permute-done.10
  52.0 0.3 collective-permute-done.9
  52.3 2.1 %collective-permute-done.8 = f32[257,128]{1,0:T(8,128)S(1)} collective-permute-done((f32[257,128]{1,0:T(8,128)S(1)}, f32[257,128]{1,0:T(8,128)S(1)}, u32[]{:S(2)}, u32[]{:S(2)}) %collective-permute-start.8) | collective-permute-done | bytes 131616 | tf_op jit(solution)/shard_map/ppermute | solution.py:36
  54.5 0.1 add_bitcast_fusion
  54.5 1.9 %collective-permute-start.11 = (f32[257,128]{1,0:T(8,128)S(1)}, f32[257,128]{1,0:T(8,128)S(1)}, u32[]{:S(2)}, u32[]{:S(2)}) collective-permute-start(f32[257,128]{1,0:T(8,128)S(1)} %add_bitcast_fusion), channel_id=1, source_target_pairs={{0,4},{2,6},{4,0},{6,2},{8,12},{10,14},{12,8},{14,10},{16,20},{18,... | collective-permute-start | bytes 394760 | tf_op jit(solution)/shard_map/ppermute | solution.py:36
  56.4 4.9 %collective-permute-done.3 = bf16[384,512]{1,0:T(8,128)(2,1)S(1)} collective-permute-done((bf16[384,512]{1,0:T(8,128)(2,1)S(1)}, bf16[384,512]{1,0:T(8,128)(2,1)S(1)}, u32[]{:S(2)}, u32[]{:S(2)}) %collective-permute-start.3) | collective-permute-done | bytes 393248 | tf_op jit(solution)/shard_map/ppermute | solution.py:88
  61.3 0.7 fusion.20
  62.0 0.2 maximum_select_fusion.1
  62.2 3.5 %fusion.4 = f32[18,128,256]{2,1,0:T(8,128)S(1)} fusion(bf16[6,128,256,1]{2,1,0,3:T(8,128)(2,1)S(1)} %bitcast.38, bf16[6,18,128,128]{3,1,2,0:T(8,128)(2,1)} %copy-done.1), kind=kOutput, calls=%fused_computation.5 | convolution fusion | flops 905969664 | bytes 6291456 | tf_op jit(solution)/shard_map/bsij,bif->sjf/dot_general | solution.py:156
  65.7 1.0 slice.32
  66.7 1.9 %collective-permute-start.4 = (f32[6,128,256]{2,1,0:T(8,128)}, f32[6,128,256]{2,1,0:T(8,128)}, u32[]{:S(2)}, u32[]{:S(2)}) collective-permute-start(f32[6,128,256]{2,1,0:T(8,128)} %slice.32), channel_id=1, source_target_pairs={{2,0},{4,2},{6,4},{8,6},{10,8},{12,10},{14,12},{16,14},{18,16},{20... | collective-permute-start | bytes 2359304 | tf_op jit(solution)/shard_map/ppermute | solution.py:25
  68.6 0.0 collective-permute-done.11
  68.6 0.1 fusion.30
  68.7 4.6 %collective-permute-start.12 = (f32[257,128]{1,0:T(8,128)S(1)}, f32[257,128]{1,0:T(8,128)S(1)}, u32[]{:S(2)}, u32[]{:S(2)}) collective-permute-start(f32[257,128]{1,0:T(8,128)S(1)} %fusion.30), channel_id=1, source_target_pairs={{0,8},{2,10},{4,12},{6,14},{8,0},{10,2},{12,4},{14,6},{16,24},{18,... | collective-permute-start | bytes 394760 | tf_op jit(solution)/shard_map/ppermute | solution.py:36
  73.3 15.0 %collective-permute-done.12 = f32[257,128]{1,0:T(8,128)S(1)} collective-permute-done((f32[257,128]{1,0:T(8,128)S(1)}, f32[257,128]{1,0:T(8,128)S(1)}, u32[]{:S(2)}, u32[]{:S(2)}) %collective-permute-start.12) | collective-permute-done | bytes 131616 | tf_op jit(solution)/shard_map/ppermute | solution.py:36
  88.3 4.7 %collective-permute-start.13 = (f32[257,128]{1,0:T(8,128)S(1)}, f32[257,128]{1,0:T(8,128)S(1)}, u32[]{:S(2)}, u32[]{:S(2)}) collective-permute-start(f32[257,128]{1,0:T(8,128)S(1)} %add.148), channel_id=1, source_target_pairs={{0,1},{1,0},{2,3},{3,2},{4,5},{5,4},{6,7},{7,6},{8,9},{9,8},{10,11... | collective-permute-start | bytes 394760 | tf_op jit(solution)/shard_map/ppermute | solution.py:79
  93.0 0.8 slice.42
  93.8 1.9 %collective-permute-start.5 = (bf16[6,128,256]{2,1,0:T(8,128)(2,1)}, bf16[6,128,256]{2,1,0:T(8,128)(2,1)}, u32[]{:S(2)}, u32[]{:S(2)}) collective-permute-start(bf16[6,128,256]{2,1,0:T(8,128)(2,1)} %slice.42), channel_id=1, source_target_pairs={{0,2},{2,4},{4,6},{6,8},{8,10},{10,12},{12,14},{14,16},{16,18},{18... | collective-permute-start | bytes 1179656 | tf_op jit(solution)/shard_map/ppermute | solution.py:25
  95.8 6.3 %collective-permute-done.13 = f32[257,128]{1,0:T(8,128)S(1)} collective-permute-done((f32[257,128]{1,0:T(8,128)S(1)}, f32[257,128]{1,0:T(8,128)S(1)}, u32[]{:S(2)}, u32[]{:S(2)}) %collective-permute-start.13) | collective-permute-done | bytes 131616 | tf_op jit(solution)/shard_map/ppermute | solution.py:79
  102.1 5.4 %collective-permute-start.14 = (f32[257,128]{1,0:T(8,128)S(1)}, f32[257,128]{1,0:T(8,128)S(1)}, u32[]{:S(2)}, u32[]{:S(2)}) collective-permute-start(f32[257,128]{1,0:T(8,128)S(1)} %add.149), channel_id=1, source_target_pairs={{0,16},{2,18},{4,20},{6,22},{8,24},{10,26},{12,28},{14,30},{16,0},... | collective-permute-start | bytes 394760 | tf_op jit(solution)/shard_map/ppermute | solution.py:36
  107.5 3.0 %collective-permute-done.14 = f32[257,128]{1,0:T(8,128)S(1)} collective-permute-done((f32[257,128]{1,0:T(8,128)S(1)}, f32[257,128]{1,0:T(8,128)S(1)}, u32[]{:S(2)}, u32[]{:S(2)}) %collective-permute-start.14) | collective-permute-done | bytes 131616 | tf_op jit(solution)/shard_map/ppermute | solution.py:36
  110.5 0.7 add.150
  111.1 5.6 %collective-permute-start.15 = (f32[257,128]{1,0:T(8,128)}, f32[257,128]{1,0:T(8,128)}, u32[]{:S(2)}, u32[]{:S(2)}) collective-permute-start(f32[257,128]{1,0:T(8,128)} %add.150), channel_id=1, source_target_pairs={{0,32},{2,34},{4,36},{6,38},{8,40},{10,42},{12,44},{14,46},{16,48}... | collective-permute-start | bytes 394760 | tf_op jit(solution)/shard_map/ppermute | solution.py:36
  116.8 4.8 %collective-permute-done.15 = f32[257,128]{1,0:T(8,128)} collective-permute-done((f32[257,128]{1,0:T(8,128)}, f32[257,128]{1,0:T(8,128)}, u32[]{:S(2)}, u32[]{:S(2)}) %collective-permute-start.15) | collective-permute-done | bytes 131616 | tf_op jit(solution)/shard_map/ppermute | solution.py:36
  121.6 1.0 add.151
  122.6 13.6 %collective-permute-start.17 = (f32[257,128]{1,0:T(8,128)S(1)}, f32[257,128]{1,0:T(8,128)S(1)}, u32[]{:S(2)}, u32[]{:S(2)}) collective-permute-start(f32[257,128]{1,0:T(8,128)S(1)} %add.151), channel_id=1, source_target_pairs={{0,128},{2,130},{4,132},{6,134},{8,136},{10,138},{12,140},{14,142}... | collective-permute-start | bytes 394760 | tf_op jit(solution)/shard_map/ppermute | solution.py:36
  136.2 1.9 %collective-permute-start.16 = (f32[257,128]{1,0:T(8,128)S(1)}, f32[257,128]{1,0:T(8,128)S(1)}, u32[]{:S(2)}, u32[]{:S(2)}) collective-permute-start(f32[257,128]{1,0:T(8,128)S(1)} %add.151), channel_id=1, source_target_pairs={{0,64},{2,66},{4,68},{6,70},{8,72},{10,74},{12,76},{14,78},{16,80}... | collective-permute-start | bytes 394760 | tf_op jit(solution)/shard_map/ppermute | solution.py:36
  138.1 0.0 collective-permute-done.5
  138.1 0.0 collective-permute-done.4
  138.1 2.3 %fusion.11 = f32[6,128,256]{2,1,0:T(8,128)} fusion(f32[6,128,256]{2,1,0:T(8,128)} %collective-permute-done.4, f32[18,128,256]{2,1,0:T(8,128)S(1)} %fusion.4, bf16[6,128,256]{2,1,0:T(8,128)(2,1)} %collective-permute-done.5), kind=kLoop, calls=%fused_computation.13 | loop fusion | flops 589824 | bytes 2752512 | tf_op jit(solution)/shard_map/add | solution.py:163
  140.4 8.0 %collective-permute-start.6 = (f32[6,128,256]{2,1,0:T(8,128)}, f32[6,128,256]{2,1,0:T(8,128)S(1)}, u32[]{:S(2)}, u32[]{:S(2)}) collective-permute-start(f32[6,128,256]{2,1,0:T(8,128)} %fusion.11), channel_id=1, source_target_pairs={{0,1},{1,0},{2,3},{3,2},{4,5},{5,4},{6,7},{7,6},{8,9},{9,8},{10,11... | collective-permute-start | bytes 2359304 | tf_op jit(solution)/shard_map/ppermute | solution.py:98
  148.4 4.0 %collective-permute-done.16 = f32[257,128]{1,0:T(8,128)S(1)} collective-permute-done((f32[257,128]{1,0:T(8,128)S(1)}, f32[257,128]{1,0:T(8,128)S(1)}, u32[]{:S(2)}, u32[]{:S(2)}) %collective-permute-start.16) | collective-permute-done | bytes 131616 | tf_op jit(solution)/shard_map/ppermute | solution.py:36
  152.5 1.9 %collective-permute-start.18 = (f32[257,128]{1,0:T(8,128)S(1)}, f32[257,128]{1,0:T(8,128)S(1)}, u32[]{:S(2)}, u32[]{:S(2)}) collective-permute-start(f32[257,128]{1,0:T(8,128)S(1)} %select_add_fusion), channel_id=1, source_target_pairs={{0,2},{2,0},{4,6},{6,4},{8,10},{10,8},{12,14},{14,12},{16,18},{18,... | collective-permute-start | bytes 394760 | tf_op jit(solution)/shard_map/ppermute | solution.py:36
  154.4 2.1 %maximum_select_fusion = bf16[768,256]{1,0:T(8,128)(2,1)} fusion(bf16[384,256]{1,0:T(8,128)(2,1)} %get-tuple-element.7, bf16[384,256]{1,0:T(8,128)(2,1)} %copy-done.2, pred[]{:T(512)S(6)} %eq.38), kind=kLoop, calls=%fused_computation.17 | loop fusion | flops 1769472 | bytes 786433 | tf_op jit(solution)/shard_map/jit(_where)/select_n | solution.py:92
  156.5 0.0 collective-permute-done.18
  156.5 0.6 slice_multiply_fusion.1
  157.1 0.7 slice_multiply_fusion
  157.8 20.7 %collective-permute-done.6 = f32[6,128,256]{2,1,0:T(8,128)S(1)} collective-permute-done((f32[6,128,256]{2,1,0:T(8,128)}, f32[6,128,256]{2,1,0:T(8,128)S(1)}, u32[]{:S(2)}, u32[]{:S(2)}) %collective-permute-start.6) | collective-permute-done | bytes 786464 | tf_op jit(solution)/shard_map/ppermute | solution.py:98
  178.5 2.0 %add_convert_fusion = bf16[6,128,256]{2,1,0:T(8,128)(2,1)} fusion(f32[6,128,256]{2,1,0:T(8,128)} %fusion.11, f32[6,128,256]{2,1,0:T(8,128)S(1)} %collective-permute-done.6), kind=kLoop, calls=%fused_computation.14 | loop fusion | flops 393216 | bytes 1966080 | tf_op jit(solution)/shard_map/convert_element_type | solution.py:165
  (20 shorter events, 0.3 us)
Async XLA Ops:
  0.6 7.2 %copy-start = (bf16[6,6,128,128]{3,2,1,0:T(8,128)(2,1)S(1)}, bf16[6,6,128,128]{3,2,1,0:T(8,128)(2,1)}, u32[]{:S(2)}) copy-start(bf16[6,6,128,128]{3,2,1,0:T(8,128)(2,1)} %param.8) | copy-start | bytes 3538948
  0.6 9.4 %collective-permute-start = (bf16[768,256]{1,0:T(8,128)(2,1)}, bf16[768,256]{1,0:T(8,128)(2,1)S(1)}, u32[]{:S(2)}, u32[]{:S(2)}) collective-permute-start(bf16[768,256]{1,0:T(8,128)(2,1)} %param.7), channel_id=1, source_target_pairs={{0,2},{2,4},{4,6},{6,8},{8,10},{10,12},{12,14},{14,16},{16,18},{18... | collective-permute-start | bytes 1179656 | tf_op jit(solution)/shard_map/ppermute | solution.py:14
  2.7 9.2 %collective-permute-start.1 = (bf16[768,256]{1,0:T(8,128)(2,1)}, bf16[768,256]{1,0:T(8,128)(2,1)S(1)}, u32[]{:S(2)}, u32[]{:S(2)}) collective-permute-start(bf16[768,256]{1,0:T(8,128)(2,1)} %param.7), channel_id=1, source_target_pairs={{2,0},{4,2},{6,4},{8,6},{10,8},{12,10},{14,12},{16,14},{18,16},{20... | collective-permute-start | bytes 1179656 | tf_op jit(solution)/shard_map/ppermute | solution.py:17
  7.8 4.2 %copy-start.3 = (bf16[768,256]{1,0:T(8,128)(2,1)S(1)}, bf16[768,256]{1,0:T(8,128)(2,1)}, u32[]{:S(2)}) copy-start(bf16[768,256]{1,0:T(8,128)(2,1)} %param.7) | copy-start | bytes 1179652
  10.0 3.1 %copy-start.1 = (bf16[6,18,128,128]{3,1,2,0:T(8,128)(2,1)}, bf16[6,18,128,128]{3,1,2,0:T(8,128)(2,1)S(1)}, u32[]{:S(2)}) copy-start(bf16[6,18,128,128]{3,1,2,0:T(8,128)(2,1)S(1)} %convolution_convert_fusion) | copy-start | bytes 10616836
  12.0 12.9 %copy-start.4 = (bf16[256,256]{1,0:T(8,128)(2,1)S(1)}, bf16[256,256]{1,0:T(8,128)(2,1)}, u32[]{:S(2)}) copy-start(bf16[256,256]{1,0:T(8,128)(2,1)} %param.11) | copy-start | bytes 393220
  12.0 12.9 %copy-start.5 = (bf16[768,256]{1,0:T(8,128)(2,1)S(1)}, bf16[768,256]{1,0:T(8,128)(2,1)}, u32[]{:S(2)}) copy-start(bf16[768,256]{1,0:T(8,128)(2,1)} %param.13) | copy-start | bytes 1179652
  12.1 12.9 %copy-start.6 = (f32[256]{0:T(256)S(1)}, f32[256]{0:T(256)}, u32[]{:S(2)}) copy-start(f32[256]{0:T(256)} %param.12) | copy-start | bytes 3076
  13.2 11.7 %collective-permute-start.2 = (bf16[384,256]{1,0:T(8,128)(2,1)S(1)}, bf16[384,256]{1,0:T(8,128)(2,1)S(1)}, u32[]{:S(2)}, u32[]{:S(2)}) collective-permute-start(bf16[384,256]{1,0:T(8,128)(2,1)S(1)} %dynamic-slice_convert_fusion), channel_id=1, source_target_pairs={{0,1},{1,0},{2,3},{3,2},{4,5},{5,4},{6,7},{7,6},{8,9},{9,8},{10,11... | collective-permute-start | bytes 589832 | tf_op jit(solution)/shard_map/ppermute | solution.py:88
  25.4 15.1 %copy-start.2 = (bf16[384,256]{1,0:T(8,128)(2,1)}, bf16[384,256]{1,0:T(8,128)(2,1)S(1)}, u32[]{:S(2)}) copy-start(bf16[384,256]{1,0:T(8,128)(2,1)S(1)} %get-tuple-element.8) | copy-start | bytes 589828
  25.7 14.7 %collective-permute-start.7 = (f32[257,128]{1,0:T(8,128)S(1)}, f32[257,128]{1,0:T(8,128)S(1)}, u32[]{:S(2)}, u32[]{:S(2)}) collective-permute-start(f32[257,128]{1,0:T(8,128)S(1)} %fusion.12), channel_id=1, source_target_pairs={{0,2},{2,0},{4,6},{6,4},{8,10},{10,8},{12,14},{14,12},{16,18},{18,... | collective-permute-start | bytes 394760 | tf_op jit(solution)/shard_map/ppermute | solution.py:36
  36.7 24.7 %collective-permute-start.3 = (bf16[384,512]{1,0:T(8,128)(2,1)S(1)}, bf16[384,512]{1,0:T(8,128)(2,1)S(1)}, u32[]{:S(2)}, u32[]{:S(2)}) collective-permute-start(bf16[384,512]{1,0:T(8,128)(2,1)S(1)} %pad_maximum_fusion.2), channel_id=1, source_target_pairs={{0,1},{1,0},{2,3},{3,2},{4,5},{5,4},{6,7},{7,6},{8,9},{9,8},{10,11... | collective-permute-start | bytes 1179656 | tf_op jit(solution)/shard_map/ppermute | solution.py:88
  40.5 11.5 %collective-permute-start.10 = (f32[257,128]{1,0:T(8,128)S(1)}, f32[257,128]{1,0:T(8,128)S(1)}, u32[]{:S(2)}, u32[]{:S(2)}) collective-permute-start(f32[257,128]{1,0:T(8,128)S(1)} %fusion.14), channel_id=1, source_target_pairs={{0,192},{2,194},{4,196},{6,198},{8,200},{10,202},{12,204},{14,206}... | collective-permute-start | bytes 394760 | tf_op jit(solution)/shard_map/ppermute | solution.py:36
  43.9 8.4 %collective-permute-start.9 = (f32[257,128]{1,0:T(8,128)S(1)}, f32[257,128]{1,0:T(8,128)S(1)}, u32[]{:S(2)}, u32[]{:S(2)}) collective-permute-start(f32[257,128]{1,0:T(8,128)S(1)} %fusion.14), channel_id=1, source_target_pairs={{0,384},{2,386},{4,388},{6,390},{8,392},{10,394},{12,396},{14,398}... | collective-permute-start | bytes 394760 | tf_op jit(solution)/shard_map/ppermute | solution.py:36
  47.3 7.1 %collective-permute-start.8 = (f32[257,128]{1,0:T(8,128)S(1)}, f32[257,128]{1,0:T(8,128)S(1)}, u32[]{:S(2)}, u32[]{:S(2)}) collective-permute-start(f32[257,128]{1,0:T(8,128)S(1)} %fusion.14), channel_id=1, source_target_pairs={{0,576},{2,578},{4,580},{6,582},{8,584},{10,586},{12,588},{14,590}... | collective-permute-start | bytes 394760 | tf_op jit(solution)/shard_map/ppermute | solution.py:36
  54.5 14.1 %collective-permute-start.11 = (f32[257,128]{1,0:T(8,128)S(1)}, f32[257,128]{1,0:T(8,128)S(1)}, u32[]{:S(2)}, u32[]{:S(2)}) collective-permute-start(f32[257,128]{1,0:T(8,128)S(1)} %add_bitcast_fusion), channel_id=1, source_target_pairs={{0,4},{2,6},{4,0},{6,2},{8,12},{10,14},{12,8},{14,10},{16,20},{18,... | collective-permute-start | bytes 394760 | tf_op jit(solution)/shard_map/ppermute | solution.py:36
  66.7 71.4 %collective-permute-start.4 = (f32[6,128,256]{2,1,0:T(8,128)}, f32[6,128,256]{2,1,0:T(8,128)}, u32[]{:S(2)}, u32[]{:S(2)}) collective-permute-start(f32[6,128,256]{2,1,0:T(8,128)} %slice.32), channel_id=1, source_target_pairs={{2,0},{4,2},{6,4},{8,6},{10,8},{12,10},{14,12},{16,14},{18,16},{20... | collective-permute-start | bytes 2359304 | tf_op jit(solution)/shard_map/ppermute | solution.py:25
  68.7 19.6 %collective-permute-start.12 = (f32[257,128]{1,0:T(8,128)S(1)}, f32[257,128]{1,0:T(8,128)S(1)}, u32[]{:S(2)}, u32[]{:S(2)}) collective-permute-start(f32[257,128]{1,0:T(8,128)S(1)} %fusion.30), channel_id=1, source_target_pairs={{0,8},{2,10},{4,12},{6,14},{8,0},{10,2},{12,4},{14,6},{16,24},{18,... | collective-permute-start | bytes 394760 | tf_op jit(solution)/shard_map/ppermute | solution.py:36
  88.3 13.7 %collective-permute-start.13 = (f32[257,128]{1,0:T(8,128)S(1)}, f32[257,128]{1,0:T(8,128)S(1)}, u32[]{:S(2)}, u32[]{:S(2)}) collective-permute-start(f32[257,128]{1,0:T(8,128)S(1)} %add.148), channel_id=1, source_target_pairs={{0,1},{1,0},{2,3},{3,2},{4,5},{5,4},{6,7},{7,6},{8,9},{9,8},{10,11... | collective-permute-start | bytes 394760 | tf_op jit(solution)/shard_map/ppermute | solution.py:79
  93.8 44.3 %collective-permute-start.5 = (bf16[6,128,256]{2,1,0:T(8,128)(2,1)}, bf16[6,128,256]{2,1,0:T(8,128)(2,1)}, u32[]{:S(2)}, u32[]{:S(2)}) collective-permute-start(bf16[6,128,256]{2,1,0:T(8,128)(2,1)} %slice.42), channel_id=1, source_target_pairs={{0,2},{2,4},{4,6},{6,8},{8,10},{10,12},{12,14},{14,16},{16,18},{18... | collective-permute-start | bytes 1179656 | tf_op jit(solution)/shard_map/ppermute | solution.py:25
  102.1 8.4 %collective-permute-start.14 = (f32[257,128]{1,0:T(8,128)S(1)}, f32[257,128]{1,0:T(8,128)S(1)}, u32[]{:S(2)}, u32[]{:S(2)}) collective-permute-start(f32[257,128]{1,0:T(8,128)S(1)} %add.149), channel_id=1, source_target_pairs={{0,16},{2,18},{4,20},{6,22},{8,24},{10,26},{12,28},{14,30},{16,0},... | collective-permute-start | bytes 394760 | tf_op jit(solution)/shard_map/ppermute | solution.py:36
  111.1 10.4 %collective-permute-start.15 = (f32[257,128]{1,0:T(8,128)}, f32[257,128]{1,0:T(8,128)}, u32[]{:S(2)}, u32[]{:S(2)}) collective-permute-start(f32[257,128]{1,0:T(8,128)} %add.150), channel_id=1, source_target_pairs={{0,32},{2,34},{4,36},{6,38},{8,40},{10,42},{12,44},{14,46},{16,48}... | collective-permute-start | bytes 394760 | tf_op jit(solution)/shard_map/ppermute | solution.py:36
  122.6 25.8 %collective-permute-start.17 = (f32[257,128]{1,0:T(8,128)S(1)}, f32[257,128]{1,0:T(8,128)S(1)}, u32[]{:S(2)}, u32[]{:S(2)}) collective-permute-start(f32[257,128]{1,0:T(8,128)S(1)} %add.151), channel_id=1, source_target_pairs={{0,128},{2,130},{4,132},{6,134},{8,136},{10,138},{12,140},{14,142}... | collective-permute-start | bytes 394760 | tf_op jit(solution)/shard_map/ppermute | solution.py:36
  136.2 16.2 %collective-permute-start.16 = (f32[257,128]{1,0:T(8,128)S(1)}, f32[257,128]{1,0:T(8,128)S(1)}, u32[]{:S(2)}, u32[]{:S(2)}) collective-permute-start(f32[257,128]{1,0:T(8,128)S(1)} %add.151), channel_id=1, source_target_pairs={{0,64},{2,66},{4,68},{6,70},{8,72},{10,74},{12,76},{14,78},{16,80}... | collective-permute-start | bytes 394760 | tf_op jit(solution)/shard_map/ppermute | solution.py:36
  140.4 38.1 %collective-permute-start.6 = (f32[6,128,256]{2,1,0:T(8,128)}, f32[6,128,256]{2,1,0:T(8,128)S(1)}, u32[]{:S(2)}, u32[]{:S(2)}) collective-permute-start(f32[6,128,256]{2,1,0:T(8,128)} %fusion.11), channel_id=1, source_target_pairs={{0,1},{1,0},{2,3},{3,2},{4,5},{5,4},{6,7},{7,6},{8,9},{9,8},{10,11... | collective-permute-start | bytes 2359304 | tf_op jit(solution)/shard_map/ppermute | solution.py:98
  152.5 4.0 %collective-permute-start.18 = (f32[257,128]{1,0:T(8,128)S(1)}, f32[257,128]{1,0:T(8,128)S(1)}, u32[]{:S(2)}, u32[]{:S(2)}) collective-permute-start(f32[257,128]{1,0:T(8,128)S(1)} %select_add_fusion), channel_id=1, source_target_pairs={{0,2},{2,0},{4,6},{6,4},{8,10},{10,8},{12,14},{14,12},{16,18},{18,... | collective-permute-start | bytes 394760 | tf_op jit(solution)/shard_map/ppermute | solution.py:36

commit v13 on v12

--- a/solution.py
+++ b/solution.py
@@ -63,10 +63,10 @@
     return (first + second) + third_part
 
 
-def global_sum(x):
+def global_sum(x, tie):
     count = lax.axis_size("rows")
     if count not in ROW_AXES or lax.axis_size("rep") != 2:
-        return lax.psum(x, ("rows", "rep"))
+        return lax.psum(x, ("rows", "rep")), tie
     (x_stride, x_size), (z_stride, z_size), (y_stride, y_size), (c_stride, c_size) = ROW_AXES[count]
     core = (lax.axis_index("rows") // c_stride) % c_size
     width = x.shape[1] // 2
@@ -77,11 +77,13 @@
     x = swapped_sum(x, "rows", count, y_stride, y_size, 1)
     x = swapped_sum(x, "rows", count, y_stride, y_size, 2)
     x = x + lax.ppermute(x, "rep", [(0, 1), (1, 0)])
+    x, tie = lax.optimization_barrier((x, tie))
     x = swapped_sum(x, "rows", count, z_stride, z_size, 1)
     x = swapped_sum(x, "rows", count, z_stride, z_size, 2)
     x = three_way_sum(x, "rows", count, z_stride, z_size)
     other = moved(x, "rows", count, c_stride, c_size, lambda c: c ^ 1)
-    return jnp.where(core == 0, jnp.concatenate([x, other], 1), jnp.concatenate([other, x], 1))
+    joined = jnp.where(core == 0, jnp.concatenate([x, other], 1), jnp.concatenate([other, x], 1))
+    return joined, tie
 
 
 def partner_swap(x):
@@ -146,12 +148,6 @@
         agg_half, grad_half, (((0,), (0,)), ((), ())), preferred_element_type=jnp.float32
     )
     bias_part = jnp.sum(grad_half.astype(jnp.float32), axis=0)
-    grad_terms = global_sum(jnp.concatenate([weight_part, bias_part[None, :]], axis=0))
-    weight_total = grad_terms[:feat_width]
-    bias_total = grad_terms[feat_width]
-    scale = 1.0 / math.sqrt(node_count)
-    weight_grad = weight_total * scale
-    bias_grad = bias_total * scale
     grad_blocks = agg_grad.reshape(num_blocks, tile_size, feat_width)
     spread = jnp.einsum(
         "bsij,bif->sjf", band_tiles, grad_blocks, preferred_element_type=jnp.float32
@@ -161,6 +157,14 @@
         jnp.float32
     )
     own_terms = spread[num_blocks : 2 * num_blocks] + from_above + from_below
+    grad_terms, own_terms = global_sum(
+        jnp.concatenate([weight_part, bias_part[None, :]], axis=0), own_terms
+    )
+    weight_total = grad_terms[:feat_width]
+    bias_total = grad_terms[feat_width]
+    scale = 1.0 / math.sqrt(node_count)
+    weight_grad = weight_total * scale
+    bias_grad = bias_total * scale
     own_total = partner_sum(own_terms)
     feature_grad = own_total.reshape(rows_here, feat_width).astype(jnp.bfloat16)
     return (activations, feature_grad, weight_grad, bias_grad)

time: 181 us -> 173 us (0.956)
  the two profiles are of different devices: /device:TPU:56 before, /device:TPU:68 now
where the time goes in v13:
time: 173 us; the launch traced here: 172 us
  starting transfers between devices  104 us (60%)
  waiting for transfers between devices  53.3 us (31%)
  matrix products  7.71 us (4%)
  other arithmetic  6.19 us (4%)
    ppermute x11, starting transfers between devices, moved(): return lax.ppermute(x, axis, pairs)  60.8 us
    ppermute x11, waiting for transfers between devices, moved(): return lax.ppermute(x, axis, pairs)  34.5 us
    ppermute x2, starting transfers between devices, partner_swap(): return lax.ppermute(x, 'rep', [(0, 1), (1, 0)])  15.7 us
    ppermute x1, waiting for transfers between devices, partner_sum(): return x + lax.ppermute(x, 'rep', [(0, 1), (1, 0)])  8.45 us
    ppermute x2, starting transfers between devices, from_behind(): return lax.ppermute(x, axis, pairs)  7.47 us
    ppermute x1, starting transfers between devices, global_sum(): x = x + lax.ppermute(x, 'rep', [(0, 1), (1, 0)])  7.29 us
    ppermute x1, starting transfers between devices, extended(): lax.ppermute(lax.slice_in_dim(block, 0, width, axis=dim), axis, backward)  6.34 us
    ppermute x2, waiting for transfers between devices, partner_swap(): return lax.ppermute(x, 'rep', [(0, 1), (1, 0)])  4.49 us
  transfers between devices with their start and end apart: 19, of which 12 were waited for; matrix products, arithmetic and copies ran while one was open for 6% of the time, Pallas kernels for 0%

profile of v13, /device:TPU:68, one launch (start us, length us, event | category | flops | bytes accessed | tf_op | source)
XLA Modules:
  0.0 172.4 jit_solution(15800932410990377366)
XLA Ops:
  0.6 0.0 copy-start
  0.6 2.1 %collective-permute-start = (bf16[768,256]{1,0:T(8,128)(2,1)}, bf16[768,256]{1,0:T(8,128)(2,1)S(1)}, u32[]{:S(2)}, u32[]{:S(2)}) collective-permute-start(bf16[768,256]{1,0:T(8,128)(2,1)} %param.7), channel_id=1, source_target_pairs={{0,2},{2,4},{4,6},{6,8},{8,10},{10,12},{12,14},{14,16},{16,18},{18... | collective-permute-start | bytes 1179656 | tf_op jit(solution)/shard_map/ppermute | solution.py:14
  2.7 6.3 %collective-permute-start.1 = (bf16[768,256]{1,0:T(8,128)(2,1)}, bf16[768,256]{1,0:T(8,128)(2,1)S(1)}, u32[]{:S(2)}, u32[]{:S(2)}) collective-permute-start(bf16[768,256]{1,0:T(8,128)(2,1)} %param.7), channel_id=1, source_target_pairs={{2,0},{4,2},{6,4},{8,6},{10,8},{12,10},{14,12},{16,14},{18,16},{20... | collective-permute-start | bytes 1179656 | tf_op jit(solution)/shard_map/ppermute | solution.py:17
  9.1 0.7 broadcast_subtract_fusion
  9.8 0.7 iota_compare_fusion.1
  10.5 2.2 %convolution_convert_fusion = bf16[6,18,128,128]{3,1,2,0:T(8,128)(2,1)S(1)} fusion(bf16[6,6,128,128]{3,2,1,0:T(8,128)(2,1)S(1)} %copy-done, s32[6,6]{1,0:T(8,128)S(1)} %broadcast_subtract_fusion, pred[6,6]{1,0:T(8,128)(4,1)S(1)} %iota_compare_fusion.1), kind=kOutput, calls=%fused_computation.4 | convolution fusion | flops 23004432 | bytes 4718772 | tf_op jit(solution)/shard_map/bks,bkij->bsij/dot_general | solution.py:131
  12.7 0.3 collective-permute-done
  13.0 1.6 collective-permute-done.1
  14.6 0.0 copy-done.2
  14.6 0.1 pad_maximum_fusion
  14.7 0.0 copy-start.3
  14.7 0.0 copy-start.4
  14.8 0.0 copy-start.5
  14.8 1.1 fusion.8
  15.9 0.0 copy-done.1
  15.9 7.7 %collective-permute-start.2 = (bf16[384,256]{1,0:T(8,128)(2,1)S(1)}, bf16[384,256]{1,0:T(8,128)(2,1)S(1)}, u32[]{:S(2)}, u32[]{:S(2)}) collective-permute-start(bf16[384,256]{1,0:T(8,128)(2,1)S(1)} %dynamic-slice_convert_fusion), channel_id=1, source_target_pairs={{0,1},{1,0},{2,3},{3,2},{4,5},{5,4},{6,7},{7,6},{8,9},{9,8},{10,11... | collective-permute-start | bytes 589832 | tf_op jit(solution)/shard_map/ppermute | solution.py:90
  23.7 4.5 %collective-permute-done.2 = bf16[384,256]{1,0:T(8,128)(2,1)S(1)} collective-permute-done((bf16[384,256]{1,0:T(8,128)(2,1)S(1)}, bf16[384,256]{1,0:T(8,128)(2,1)S(1)}, u32[]{:S(2)}, u32[]{:S(2)}) %collective-permute-start.2) | collective-permute-done | bytes 196640 | tf_op jit(solution)/shard_map/ppermute | solution.py:90
  28.1 0.1 add_convert_fusion.1
  28.2 0.4 convert_reduce_fusion
  28.6 0.3 fusion.21
  28.9 0.2 convolution_convert_fusion.1
  29.2 7.9 %collective-permute-start.3 = (bf16[384,512]{1,0:T(8,128)(2,1)S(1)}, bf16[384,512]{1,0:T(8,128)(2,1)S(1)}, u32[]{:S(2)}, u32[]{:S(2)}) collective-permute-start(bf16[384,512]{1,0:T(8,128)(2,1)S(1)} %pad_maximum_fusion.2), channel_id=1, source_target_pairs={{0,1},{1,0},{2,3},{3,2},{4,5},{5,4},{6,7},{7,6},{8,9},{9,8},{10,11... | collective-permute-start | bytes 1179656 | tf_op jit(solution)/shard_map/ppermute | solution.py:90
  37.1 6.3 %collective-permute-start.4 = (f32[257,128]{1,0:T(8,128)S(1)}, f32[257,128]{1,0:T(8,128)S(1)}, u32[]{:S(2)}, u32[]{:S(2)}) collective-permute-start(f32[257,128]{1,0:T(8,128)S(1)} %fusion.12), channel_id=1, source_target_pairs={{0,2},{2,0},{4,6},{6,4},{8,10},{10,8},{12,14},{14,12},{16,18},{18,... | collective-permute-start | bytes 394760 | tf_op jit(solution)/shard_map/ppermute | solution.py:36
  43.6 0.8 collective-permute-done.4
  44.5 3.1 %collective-permute-start.7 = (f32[257,128]{1,0:T(8,128)S(1)}, f32[257,128]{1,0:T(8,128)S(1)}, u32[]{:S(2)}, u32[]{:S(2)}) collective-permute-start(f32[257,128]{1,0:T(8,128)S(1)} %fusion.14), channel_id=1, source_target_pairs={{0,192},{2,194},{4,196},{6,198},{8,200},{10,202},{12,204},{14,206}... | collective-permute-start | bytes 394760 | tf_op jit(solution)/shard_map/ppermute | solution.py:36
  47.6 2.7 %collective-permute-start.6 = (f32[257,128]{1,0:T(8,128)S(1)}, f32[257,128]{1,0:T(8,128)S(1)}, u32[]{:S(2)}, u32[]{:S(2)}) collective-permute-start(f32[257,128]{1,0:T(8,128)S(1)} %fusion.14), channel_id=1, source_target_pairs={{0,384},{2,386},{4,388},{6,390},{8,392},{10,394},{12,396},{14,398}... | collective-permute-start | bytes 394760 | tf_op jit(solution)/shard_map/ppermute | solution.py:36
  50.3 3.0 %collective-permute-start.5 = (f32[257,128]{1,0:T(8,128)S(1)}, f32[257,128]{1,0:T(8,128)S(1)}, u32[]{:S(2)}, u32[]{:S(2)}) collective-permute-start(f32[257,128]{1,0:T(8,128)S(1)} %fusion.14), channel_id=1, source_target_pairs={{0,576},{2,578},{4,580},{6,582},{8,584},{10,586},{12,588},{14,590}... | collective-permute-start | bytes 394760 | tf_op jit(solution)/shard_map/ppermute | solution.py:36
  53.4 0.0 collective-permute-done.3
  53.4 0.2 maximum_select_fusion.1
  53.6 3.5 %fusion.4 = f32[18,128,256]{2,1,0:T(8,128)S(1)} fusion(bf16[6,128,256,1]{2,1,0,3:T(8,128)(2,1)S(1)} %bitcast.38, bf16[6,18,128,128]{3,1,2,0:T(8,128)(2,1)} %copy-done.1), kind=kOutput, calls=%fused_computation.5 | convolution fusion | flops 905969664 | bytes 6291456 | tf_op jit(solution)/shard_map/bsij,bif->sjf/dot_general | solution.py:152
  57.1 0.1 slice.32
  57.2 5.3 %collective-permute-start.11 = (f32[6,128,256]{2,1,0:T(8,128)S(1)}, f32[6,128,256]{2,1,0:T(8,128)S(1)}, u32[]{:S(2)}, u32[]{:S(2)}) collective-permute-start(f32[6,128,256]{2,1,0:T(8,128)S(1)} %slice.32), channel_id=1, source_target_pairs={{2,0},{4,2},{6,4},{8,6},{10,8},{12,10},{14,12},{16,14},{18,16},{20... | collective-permute-start | bytes 2359304 | tf_op jit(solution)/shard_map/ppermute | solution.py:25
  62.5 0.0 collective-permute-done.7
  62.5 0.0 collective-permute-done.6
  62.5 0.0 collective-permute-done.5
  62.6 0.1 add_bitcast_fusion
  62.6 2.9 %collective-permute-start.8 = (f32[257,128]{1,0:T(8,128)S(1)}, f32[257,128]{1,0:T(8,128)S(1)}, u32[]{:S(2)}, u32[]{:S(2)}) collective-permute-start(f32[257,128]{1,0:T(8,128)S(1)} %add_bitcast_fusion), channel_id=1, source_target_pairs={{0,4},{2,6},{4,0},{6,2},{8,12},{10,14},{12,8},{14,10},{16,20},{18,... | collective-permute-start | bytes 394760 | tf_op jit(solution)/shard_map/ppermute | solution.py:36
  65.6 2.1 %collective-permute-start.12 = (bf16[6,128,256]{2,1,0:T(8,128)(2,1)S(1)}, bf16[6,128,256]{2,1,0:T(8,128)(2,1)S(1)}, u32[]{:S(2)}, u32[]{:S(2)}) collective-permute-start(bf16[6,128,256]{2,1,0:T(8,128)(2,1)S(1)} %slice.42), channel_id=1, source_target_pairs={{0,2},{2,4},{4,6},{6,8},{8,10},{10,12},{12,14},{14,16},{16,18},{18... | collective-permute-start | bytes 1179656 | tf_op jit(solution)/shard_map/ppermute | solution.py:25
  67.7 12.8 %collective-permute-done.8 = f32[257,128]{1,0:T(8,128)S(1)} collective-permute-done((f32[257,128]{1,0:T(8,128)S(1)}, f32[257,128]{1,0:T(8,128)S(1)}, u32[]{:S(2)}, u32[]{:S(2)}) %collective-permute-start.8) | collective-permute-done | bytes 131616 | tf_op jit(solution)/shard_map/ppermute | solution.py:36
  80.5 0.1 fusion.30
  80.6 3.6 %collective-permute-start.9 = (f32[257,128]{1,0:T(8,128)S(1)}, f32[257,128]{1,0:T(8,128)S(1)}, u32[]{:S(2)}, u32[]{:S(2)}) collective-permute-start(f32[257,128]{1,0:T(8,128)S(1)} %fusion.30), channel_id=1, source_target_pairs={{0,8},{2,10},{4,12},{6,14},{8,0},{10,2},{12,4},{14,6},{16,24},{18,... | collective-permute-start | bytes 394760 | tf_op jit(solution)/shard_map/ppermute | solution.py:36
  84.2 4.6 %collective-permute-done.9 = f32[257,128]{1,0:T(8,128)S(1)} collective-permute-done((f32[257,128]{1,0:T(8,128)S(1)}, f32[257,128]{1,0:T(8,128)S(1)}, u32[]{:S(2)}, u32[]{:S(2)}) %collective-permute-start.9) | collective-permute-done | bytes 131616 | tf_op jit(solution)/shard_map/ppermute | solution.py:36
  88.9 7.3 %collective-permute-start.10 = (f32[257,128]{1,0:T(8,128)S(1)}, f32[257,128]{1,0:T(8,128)S(1)}, u32[]{:S(2)}, u32[]{:S(2)}) collective-permute-start(f32[257,128]{1,0:T(8,128)S(1)} %add.144), channel_id=1, source_target_pairs={{0,1},{1,0},{2,3},{3,2},{4,5},{5,4},{6,7},{7,6},{8,9},{9,8},{10,11... | collective-permute-start | bytes 394760 | tf_op jit(solution)/shard_map/ppermute | solution.py:79
  96.2 4.0 %collective-permute-done.10 = f32[257,128]{1,0:T(8,128)S(1)} collective-permute-done((f32[257,128]{1,0:T(8,128)S(1)}, f32[257,128]{1,0:T(8,128)S(1)}, u32[]{:S(2)}, u32[]{:S(2)}) %collective-permute-start.10) | collective-permute-done | bytes 131616 | tf_op jit(solution)/shard_map/ppermute | solution.py:79
  100.2 0.0 collective-permute-done.12
  100.2 0.0 collective-permute-done.11
  100.2 0.2 fusion.11
  100.4 10.9 %collective-permute-start.14 = (f32[257,128]{1,0:T(8,128)S(1)}, f32[257,128]{1,0:T(8,128)S(1)}, u32[]{:S(2)}, u32[]{:S(2)}) collective-permute-start(f32[257,128]{1,0:T(8,128)S(1)} %add.145), channel_id=1, source_target_pairs={{0,16},{2,18},{4,20},{6,22},{8,24},{10,26},{12,28},{14,30},{16,0},... | collective-permute-start | bytes 394760 | tf_op jit(solution)/shard_map/ppermute | solution.py:36
  111.3 3.4 %collective-permute-done.14 = f32[257,128]{1,0:T(8,128)S(1)} collective-permute-done((f32[257,128]{1,0:T(8,128)S(1)}, f32[257,128]{1,0:T(8,128)S(1)}, u32[]{:S(2)}, u32[]{:S(2)}) %collective-permute-start.14) | collective-permute-done | bytes 131616 | tf_op jit(solution)/shard_map/ppermute | solution.py:36
  114.7 3.7 %collective-permute-start.15 = (f32[257,128]{1,0:T(8,128)S(1)}, f32[257,128]{1,0:T(8,128)S(1)}, u32[]{:S(2)}, u32[]{:S(2)}) collective-permute-start(f32[257,128]{1,0:T(8,128)S(1)} %add.150), channel_id=1, source_target_pairs={{0,32},{2,34},{4,36},{6,38},{8,40},{10,42},{12,44},{14,46},{16,48}... | collective-permute-start | bytes 394760 | tf_op jit(solution)/shard_map/ppermute | solution.py:36
  118.4 4.1 %collective-permute-done.15 = f32[257,128]{1,0:T(8,128)S(1)} collective-permute-done((f32[257,128]{1,0:T(8,128)S(1)}, f32[257,128]{1,0:T(8,128)S(1)}, u32[]{:S(2)}, u32[]{:S(2)}) %collective-permute-start.15) | collective-permute-done | bytes 131616 | tf_op jit(solution)/shard_map/ppermute | solution.py:36
  122.6 20.7 %collective-permute-start.17 = (f32[257,128]{1,0:T(8,128)S(1)}, f32[257,128]{1,0:T(8,128)S(1)}, u32[]{:S(2)}, u32[]{:S(2)}) collective-permute-start(f32[257,128]{1,0:T(8,128)S(1)} %add.151), channel_id=1, source_target_pairs={{0,128},{2,130},{4,132},{6,134},{8,136},{10,138},{12,140},{14,142}... | collective-permute-start | bytes 394760 | tf_op jit(solution)/shard_map/ppermute | solution.py:36
  143.3 1.9 %collective-permute-start.16 = (f32[257,128]{1,0:T(8,128)S(1)}, f32[257,128]{1,0:T(8,128)}, u32[]{:S(2)}, u32[]{:S(2)}) collective-permute-start(f32[257,128]{1,0:T(8,128)S(1)} %add.151), channel_id=1, source_target_pairs={{0,64},{2,66},{4,68},{6,70},{8,72},{10,74},{12,76},{14,78},{16,80}... | collective-permute-start | bytes 394760 | tf_op jit(solution)/shard_map/ppermute | solution.py:36
  145.3 4.1 %collective-permute-start.13 = (f32[6,128,256]{2,1,0:T(8,128)S(1)}, f32[6,128,256]{2,1,0:T(8,128)S(1)}, u32[]{:S(2)}, u32[]{:S(2)}) collective-permute-start(f32[6,128,256]{2,1,0:T(8,128)S(1)} %fusion.11), channel_id=1, source_target_pairs={{0,1},{1,0},{2,3},{3,2},{4,5},{5,4},{6,7},{7,6},{8,9},{9,8},{10,11... | collective-permute-start | bytes 2359304 | tf_op jit(solution)/shard_map/ppermute | solution.py:100
  149.4 0.0 collective-permute-done.17
  149.4 8.2 %collective-permute-done.16 = f32[257,128]{1,0:T(8,128)} collective-permute-done((f32[257,128]{1,0:T(8,128)S(1)}, f32[257,128]{1,0:T(8,128)}, u32[]{:S(2)}, u32[]{:S(2)}) %collective-permute-start.16) | collective-permute-done | bytes 131616 | tf_op jit(solution)/shard_map/ppermute | solution.py:36
  157.6 0.9 select_add_fusion
  158.5 1.9 %collective-permute-start.18 = (f32[257,128]{1,0:T(8,128)S(1)}, f32[257,128]{1,0:T(8,128)S(1)}, u32[]{:S(2)}, u32[]{:S(2)}) collective-permute-start(f32[257,128]{1,0:T(8,128)S(1)} %select_add_fusion), channel_id=1, source_target_pairs={{0,2},{2,0},{4,6},{6,4},{8,10},{10,8},{12,14},{14,12},{16,18},{18,... | collective-permute-start | bytes 394760 | tf_op jit(solution)/shard_map/ppermute | solution.py:36
  160.5 0.9 maximum_select_fusion
  161.4 0.4 collective-permute-done.18
  161.8 0.6 slice_multiply_fusion.1
  162.4 0.7 slice_multiply_fusion
  163.1 8.4 %collective-permute-done.13 = f32[6,128,256]{2,1,0:T(8,128)S(1)} collective-permute-done((f32[6,128,256]{2,1,0:T(8,128)S(1)}, f32[6,128,256]{2,1,0:T(8,128)S(1)}, u32[]{:S(2)}, u32[]{:S(2)}) %collective-permute-start.13) | collective-permute-done | bytes 786464 | tf_op jit(solution)/shard_map/ppermute | solution.py:100
  171.6 0.8 add_convert_fusion
  (18 shorter events, 0.3 us)
Async XLA Ops:
  0.6 9.9 %copy-start = (bf16[6,6,128,128]{3,2,1,0:T(8,128)(2,1)S(1)}, bf16[6,6,128,128]{3,2,1,0:T(8,128)(2,1)}, u32[]{:S(2)}) copy-start(bf16[6,6,128,128]{3,2,1,0:T(8,128)(2,1)} %param.8) | copy-start | bytes 3538948
  0.6 12.4 %collective-permute-start = (bf16[768,256]{1,0:T(8,128)(2,1)}, bf16[768,256]{1,0:T(8,128)(2,1)S(1)}, u32[]{:S(2)}, u32[]{:S(2)}) collective-permute-start(bf16[768,256]{1,0:T(8,128)(2,1)} %param.7), channel_id=1, source_target_pairs={{0,2},{2,4},{4,6},{6,8},{8,10},{10,12},{12,14},{14,16},{16,18},{18... | collective-permute-start | bytes 1179656 | tf_op jit(solution)/shard_map/ppermute | solution.py:14
  2.7 11.9 %collective-permute-start.1 = (bf16[768,256]{1,0:T(8,128)(2,1)}, bf16[768,256]{1,0:T(8,128)(2,1)S(1)}, u32[]{:S(2)}, u32[]{:S(2)}) collective-permute-start(bf16[768,256]{1,0:T(8,128)(2,1)} %param.7), channel_id=1, source_target_pairs={{2,0},{4,2},{6,4},{8,6},{10,8},{12,10},{14,12},{16,14},{18,16},{20... | collective-permute-start | bytes 1179656 | tf_op jit(solution)/shard_map/ppermute | solution.py:17
  10.5 4.2 %copy-start.2 = (bf16[768,256]{1,0:T(8,128)(2,1)S(1)}, bf16[768,256]{1,0:T(8,128)(2,1)}, u32[]{:S(2)}) copy-start(bf16[768,256]{1,0:T(8,128)(2,1)} %param.7) | copy-start | bytes 1179652
  12.7 3.1 %copy-start.1 = (bf16[6,18,128,128]{3,1,2,0:T(8,128)(2,1)}, bf16[6,18,128,128]{3,1,2,0:T(8,128)(2,1)S(1)}, u32[]{:S(2)}) copy-start(bf16[6,18,128,128]{3,1,2,0:T(8,128)(2,1)S(1)} %convolution_convert_fusion) | copy-start | bytes 10616836
  14.7 13.5 %copy-start.3 = (bf16[256,256]{1,0:T(8,128)(2,1)S(1)}, bf16[256,256]{1,0:T(8,128)(2,1)}, u32[]{:S(2)}) copy-start(bf16[256,256]{1,0:T(8,128)(2,1)} %param.11) | copy-start | bytes 393220
  14.7 13.5 %copy-start.4 = (bf16[768,256]{1,0:T(8,128)(2,1)S(1)}, bf16[768,256]{1,0:T(8,128)(2,1)}, u32[]{:S(2)}) copy-start(bf16[768,256]{1,0:T(8,128)(2,1)} %param.13) | copy-start | bytes 1179652
  14.8 13.5 %copy-start.5 = (f32[256]{0:T(256)S(1)}, f32[256]{0:T(256)}, u32[]{:S(2)}) copy-start(f32[256]{0:T(256)} %param.12) | copy-start | bytes 3076
  15.9 12.2 %collective-permute-start.2 = (bf16[384,256]{1,0:T(8,128)(2,1)S(1)}, bf16[384,256]{1,0:T(8,128)(2,1)S(1)}, u32[]{:S(2)}, u32[]{:S(2)}) collective-permute-start(bf16[384,256]{1,0:T(8,128)(2,1)S(1)} %dynamic-slice_convert_fusion), channel_id=1, source_target_pairs={{0,1},{1,0},{2,3},{3,2},{4,5},{5,4},{6,7},{7,6},{8,9},{9,8},{10,11... | collective-permute-start | bytes 589832 | tf_op jit(solution)/shard_map/ppermute | solution.py:90
  29.2 24.2 %collective-permute-start.3 = (bf16[384,512]{1,0:T(8,128)(2,1)S(1)}, bf16[384,512]{1,0:T(8,128)(2,1)S(1)}, u32[]{:S(2)}, u32[]{:S(2)}) collective-permute-start(bf16[384,512]{1,0:T(8,128)(2,1)S(1)} %pad_maximum_fusion.2), channel_id=1, source_target_pairs={{0,1},{1,0},{2,3},{3,2},{4,5},{5,4},{6,7},{7,6},{8,9},{9,8},{10,11... | collective-permute-start | bytes 1179656 | tf_op jit(solution)/shard_map/ppermute | solution.py:90
  37.1 7.3 %collective-permute-start.4 = (f32[257,128]{1,0:T(8,128)S(1)}, f32[257,128]{1,0:T(8,128)S(1)}, u32[]{:S(2)}, u32[]{:S(2)}) collective-permute-start(f32[257,128]{1,0:T(8,128)S(1)} %fusion.12), channel_id=1, source_target_pairs={{0,2},{2,0},{4,6},{6,4},{8,10},{10,8},{12,14},{14,12},{16,18},{18,... | collective-permute-start | bytes 394760 | tf_op jit(solution)/shard_map/ppermute | solution.py:36
  44.5 18.1 %collective-permute-start.7 = (f32[257,128]{1,0:T(8,128)S(1)}, f32[257,128]{1,0:T(8,128)S(1)}, u32[]{:S(2)}, u32[]{:S(2)}) collective-permute-start(f32[257,128]{1,0:T(8,128)S(1)} %fusion.14), channel_id=1, source_target_pairs={{0,192},{2,194},{4,196},{6,198},{8,200},{10,202},{12,204},{14,206}... | collective-permute-start | bytes 394760 | tf_op jit(solution)/shard_map/ppermute | solution.py:36
  47.6 14.9 %collective-permute-start.6 = (f32[257,128]{1,0:T(8,128)S(1)}, f32[257,128]{1,0:T(8,128)S(1)}, u32[]{:S(2)}, u32[]{:S(2)}) collective-permute-start(f32[257,128]{1,0:T(8,128)S(1)} %fusion.14), channel_id=1, source_target_pairs={{0,384},{2,386},{4,388},{6,390},{8,392},{10,394},{12,396},{14,398}... | collective-permute-start | bytes 394760 | tf_op jit(solution)/shard_map/ppermute | solution.py:36
  50.3 12.2 %collective-permute-start.5 = (f32[257,128]{1,0:T(8,128)S(1)}, f32[257,128]{1,0:T(8,128)S(1)}, u32[]{:S(2)}, u32[]{:S(2)}) collective-permute-start(f32[257,128]{1,0:T(8,128)S(1)} %fusion.14), channel_id=1, source_target_pairs={{0,576},{2,578},{4,580},{6,582},{8,584},{10,586},{12,588},{14,590}... | collective-permute-start | bytes 394760 | tf_op jit(solution)/shard_map/ppermute | solution.py:36
  57.2 43.0 %collective-permute-start.11 = (f32[6,128,256]{2,1,0:T(8,128)S(1)}, f32[6,128,256]{2,1,0:T(8,128)S(1)}, u32[]{:S(2)}, u32[]{:S(2)}) collective-permute-start(f32[6,128,256]{2,1,0:T(8,128)S(1)} %slice.32), channel_id=1, source_target_pairs={{2,0},{4,2},{6,4},{8,6},{10,8},{12,10},{14,12},{16,14},{18,16},{20... | collective-permute-start | bytes 2359304 | tf_op jit(solution)/shard_map/ppermute | solution.py:25
  62.6 17.9 %collective-permute-start.8 = (f32[257,128]{1,0:T(8,128)S(1)}, f32[257,128]{1,0:T(8,128)S(1)}, u32[]{:S(2)}, u32[]{:S(2)}) collective-permute-start(f32[257,128]{1,0:T(8,128)S(1)} %add_bitcast_fusion), channel_id=1, source_target_pairs={{0,4},{2,6},{4,0},{6,2},{8,12},{10,14},{12,8},{14,10},{16,20},{18,... | collective-permute-start | bytes 394760 | tf_op jit(solution)/shard_map/ppermute | solution.py:36
  65.6 34.6 %collective-permute-start.12 = (bf16[6,128,256]{2,1,0:T(8,128)(2,1)S(1)}, bf16[6,128,256]{2,1,0:T(8,128)(2,1)S(1)}, u32[]{:S(2)}, u32[]{:S(2)}) collective-permute-start(bf16[6,128,256]{2,1,0:T(8,128)(2,1)S(1)} %slice.42), channel_id=1, source_target_pairs={{0,2},{2,4},{4,6},{6,8},{8,10},{10,12},{12,14},{14,16},{16,18},{18... | collective-permute-start | bytes 1179656 | tf_op jit(solution)/shard_map/ppermute | solution.py:25
  80.6 8.2 %collective-permute-start.9 = (f32[257,128]{1,0:T(8,128)S(1)}, f32[257,128]{1,0:T(8,128)S(1)}, u32[]{:S(2)}, u32[]{:S(2)}) collective-permute-start(f32[257,128]{1,0:T(8,128)S(1)} %fusion.30), channel_id=1, source_target_pairs={{0,8},{2,10},{4,12},{6,14},{8,0},{10,2},{12,4},{14,6},{16,24},{18,... | collective-permute-start | bytes 394760 | tf_op jit(solution)/shard_map/ppermute | solution.py:36
  88.9 11.3 %collective-permute-start.10 = (f32[257,128]{1,0:T(8,128)S(1)}, f32[257,128]{1,0:T(8,128)S(1)}, u32[]{:S(2)}, u32[]{:S(2)}) collective-permute-start(f32[257,128]{1,0:T(8,128)S(1)} %add.144), channel_id=1, source_target_pairs={{0,1},{1,0},{2,3},{3,2},{4,5},{5,4},{6,7},{7,6},{8,9},{9,8},{10,11... | collective-permute-start | bytes 394760 | tf_op jit(solution)/shard_map/ppermute | solution.py:79
  100.4 14.3 %collective-permute-start.14 = (f32[257,128]{1,0:T(8,128)S(1)}, f32[257,128]{1,0:T(8,128)S(1)}, u32[]{:S(2)}, u32[]{:S(2)}) collective-permute-start(f32[257,128]{1,0:T(8,128)S(1)} %add.145), channel_id=1, source_target_pairs={{0,16},{2,18},{4,20},{6,22},{8,24},{10,26},{12,28},{14,30},{16,0},... | collective-permute-start | bytes 394760 | tf_op jit(solution)/shard_map/ppermute | solution.py:36
  114.7 7.8 %collective-permute-start.15 = (f32[257,128]{1,0:T(8,128)S(1)}, f32[257,128]{1,0:T(8,128)S(1)}, u32[]{:S(2)}, u32[]{:S(2)}) collective-permute-start(f32[257,128]{1,0:T(8,128)S(1)} %add.150), channel_id=1, source_target_pairs={{0,32},{2,34},{4,36},{6,38},{8,40},{10,42},{12,44},{14,46},{16,48}... | collective-permute-start | bytes 394760 | tf_op jit(solution)/shard_map/ppermute | solution.py:36
  122.6 26.8 %collective-permute-start.17 = (f32[257,128]{1,0:T(8,128)S(1)}, f32[257,128]{1,0:T(8,128)S(1)}, u32[]{:S(2)}, u32[]{:S(2)}) collective-permute-start(f32[257,128]{1,0:T(8,128)S(1)} %add.151), channel_id=1, source_target_pairs={{0,128},{2,130},{4,132},{6,134},{8,136},{10,138},{12,140},{14,142}... | collective-permute-start | bytes 394760 | tf_op jit(solution)/shard_map/ppermute | solution.py:36
  143.3 14.3 %collective-permute-start.16 = (f32[257,128]{1,0:T(8,128)S(1)}, f32[257,128]{1,0:T(8,128)}, u32[]{:S(2)}, u32[]{:S(2)}) collective-permute-start(f32[257,128]{1,0:T(8,128)S(1)} %add.151), channel_id=1, source_target_pairs={{0,64},{2,66},{4,68},{6,70},{8,72},{10,74},{12,76},{14,78},{16,80}... | collective-permute-start | bytes 394760 | tf_op jit(solution)/shard_map/ppermute | solution.py:36
  145.3 26.3 %collective-permute-start.13 = (f32[6,128,256]{2,1,0:T(8,128)S(1)}, f32[6,128,256]{2,1,0:T(8,128)S(1)}, u32[]{:S(2)}, u32[]{:S(2)}) collective-permute-start(f32[6,128,256]{2,1,0:T(8,128)S(1)} %fusion.11), channel_id=1, source_target_pairs={{0,1},{1,0},{2,3},{3,2},{4,5},{5,4},{6,7},{7,6},{8,9},{9,8},{10,11... | collective-permute-start | bytes 2359304 | tf_op jit(solution)/shard_map/ppermute | solution.py:100
  158.5 3.2 %collective-permute-start.18 = (f32[257,128]{1,0:T(8,128)S(1)}, f32[257,128]{1,0:T(8,128)S(1)}, u32[]{:S(2)}, u32[]{:S(2)}) collective-permute-start(f32[257,128]{1,0:T(8,128)S(1)} %select_add_fusion), channel_id=1, source_target_pairs={{0,2},{2,0},{4,6},{6,4},{8,10},{10,8},{12,14},{14,12},{16,18},{18,... | collective-permute-start | bytes 394760 | tf_op jit(solution)/shard_map/ppermute | solution.py:36

commit v14 on v13

--- a/solution.py
+++ b/solution.py
@@ -66,7 +66,7 @@
 def global_sum(x, tie):
     count = lax.axis_size("rows")
     if count not in ROW_AXES or lax.axis_size("rep") != 2:
-        return lax.psum(x, ("rows", "rep")), tie
+        return x, tie
     (x_stride, x_size), (z_stride, z_size), (y_stride, y_size), (c_stride, c_size) = ROW_AXES[count]
     core = (lax.axis_index("rows") // c_stride) % c_size
     width = x.shape[1] // 2
@@ -80,6 +80,16 @@
     x, tie = lax.optimization_barrier((x, tie))
     x = swapped_sum(x, "rows", count, z_stride, z_size, 1)
     x = swapped_sum(x, "rows", count, z_stride, z_size, 2)
+    return x, tie
+
+
+def global_sum_end(x, tie):
+    count = lax.axis_size("rows")
+    if count not in ROW_AXES or lax.axis_size("rep") != 2:
+        return lax.psum(x, ("rows", "rep")), tie
+    (x_stride, x_size), (z_stride, z_size), (y_stride, y_size), (c_stride, c_size) = ROW_AXES[count]
+    core = (lax.axis_index("rows") // c_stride) % c_size
+    x, tie = lax.optimization_barrier((x, tie))
     x = three_way_sum(x, "rows", count, z_stride, z_size)
     other = moved(x, "rows", count, c_stride, c_size, lambda c: c ^ 1)
     joined = jnp.where(core == 0, jnp.concatenate([x, other], 1), jnp.concatenate([other, x], 1))
@@ -157,15 +167,15 @@
         jnp.float32
     )
     own_terms = spread[num_blocks : 2 * num_blocks] + from_above + from_below
-    grad_terms, own_terms = global_sum(
+    chain, own_terms = global_sum(
         jnp.concatenate([weight_part, bias_part[None, :]], axis=0), own_terms
     )
+    grad_terms, own_total = global_sum_end(chain, partner_sum(own_terms))
     weight_total = grad_terms[:feat_width]
     bias_total = grad_terms[feat_width]
     scale = 1.0 / math.sqrt(node_count)
     weight_grad = weight_total * scale
     bias_grad = bias_total * scale
-    own_total = partner_sum(own_terms)
     feature_grad = own_total.reshape(rows_here, feat_width).astype(jnp.bfloat16)
     return (activations, feature_grad, weight_grad, bias_grad)
 

time: 173 us -> 177 us (1.023)
  the two profiles are of different devices: /device:TPU:68 before, /device:TPU:1 now
where the time goes in v14:
time: 177 us; the launch traced here: 176 us
  starting transfers between devices  115 us (65%)
  waiting for transfers between devices  45.9 us (26%)
  matrix products  7.72 us (4%)
  other arithmetic  5.28 us (3%)
    ppermute x11, starting transfers between devices, moved(): return lax.ppermute(x, axis, pairs)  80.6 us
    ppermute x11, waiting for transfers between devices, moved(): return lax.ppermute(x, axis, pairs)  27.5 us
    ppermute x2, waiting for transfers between devices, partner_swap(): return lax.ppermute(x, 'rep', [(0, 1), (1, 0)])  13.4 us
    ppermute x1, starting transfers between devices, extended(): lax.ppermute(lax.slice_in_dim(block, 0, width, axis=dim), axis, backward)  9.15 us
    ppermute x2, starting transfers between devices, from_behind(): return lax.ppermute(x, axis, pairs)  6.02 us
    ppermute x1, waiting for transfers between devices, global_sum(): x = x + lax.ppermute(x, 'rep', [(0, 1), (1, 0)])  4.96 us
    ppermute x1, starting transfers between devices, partner_sum(): return x + lax.ppermute(x, 'rep', [(0, 1), (1, 0)])  4.79 us
    ppermute x1, starting transfers between devices, global_sum(): x = x + lax.ppermute(x, 'rep', [(0, 1), (1, 0)])  4.79 us
  transfers between devices with their start and end apart: 19, of which 10 were waited for; matrix products, arithmetic and copies ran while one was open for 5% of the time, Pallas kernels for 0%

profile of v14, /device:TPU:1, one launch (start us, length us, event | category | flops | bytes accessed | tf_op | source)
XLA Modules:
  0.0 176.0 jit_solution(12147310674798133266)
XLA Ops:
  0.6 0.0 copy-start
  0.6 4.7 %collective-permute-start = (bf16[768,256]{1,0:T(8,128)(2,1)}, bf16[768,256]{1,0:T(8,128)(2,1)S(1)}, u32[]{:S(2)}, u32[]{:S(2)}) collective-permute-start(bf16[768,256]{1,0:T(8,128)(2,1)} %param.7), channel_id=1, source_target_pairs={{0,2},{2,4},{4,6},{6,8},{8,10},{10,12},{12,14},{14,16},{16,18},{18... | collective-permute-start | bytes 1179656 | tf_op jit(solution)/shard_map/ppermute | solution.py:14
  5.4 9.1 %collective-permute-start.1 = (bf16[768,256]{1,0:T(8,128)(2,1)}, bf16[768,256]{1,0:T(8,128)(2,1)S(1)}, u32[]{:S(2)}, u32[]{:S(2)}) collective-permute-start(bf16[768,256]{1,0:T(8,128)(2,1)} %param.7), channel_id=1, source_target_pairs={{2,0},{4,2},{6,4},{8,6},{10,8},{12,10},{14,12},{16,14},{18,16},{20... | collective-permute-start | bytes 1179656 | tf_op jit(solution)/shard_map/ppermute | solution.py:17
  14.5 0.7 broadcast_subtract_fusion
  15.2 0.7 iota_compare_fusion.1
  16.0 0.0 copy-done
  16.0 2.2 %convolution_convert_fusion = bf16[6,18,128,128]{3,1,2,0:T(8,128)(2,1)S(1)} fusion(bf16[6,6,128,128]{3,2,1,0:T(8,128)(2,1)S(1)} %copy-done, s32[6,6]{1,0:T(8,128)S(1)} %broadcast_subtract_fusion, pred[6,6]{1,0:T(8,128)(4,1)S(1)} %iota_compare_fusion.1), kind=kOutput, calls=%fused_computation.4 | convolution fusion | flops 23004432 | bytes 4718772 | tf_op jit(solution)/shard_map/bks,bkij->bsij/dot_general | solution.py:141
  18.2 0.0 copy-start.1
  18.2 0.0 collective-permute-done
  18.2 0.0 collective-permute-done.1
  18.2 0.1 pad_maximum_fusion
  18.3 0.0 copy-start.3
  18.3 0.0 copy-start.4
  18.4 0.0 copy-start.5
  18.4 1.1 fusion.8
  19.5 0.9 copy-done.1
  20.4 2.1 %collective-permute-start.2 = (bf16[384,256]{1,0:T(8,128)(2,1)S(1)}, bf16[384,256]{1,0:T(8,128)(2,1)S(1)}, u32[]{:S(2)}, u32[]{:S(2)}) collective-permute-start(bf16[384,256]{1,0:T(8,128)(2,1)S(1)} %dynamic-slice_convert_fusion), channel_id=1, source_target_pairs={{0,1},{1,0},{2,3},{3,2},{4,5},{5,4},{6,7},{7,6},{8,9},{9,8},{10,11... | collective-permute-start | bytes 589832 | tf_op jit(solution)/shard_map/ppermute | solution.py:100
  22.5 13.4 %collective-permute-done.2 = bf16[384,256]{1,0:T(8,128)(2,1)S(1)} collective-permute-done((bf16[384,256]{1,0:T(8,128)(2,1)S(1)}, bf16[384,256]{1,0:T(8,128)(2,1)S(1)}, u32[]{:S(2)}, u32[]{:S(2)}) %collective-permute-start.2) | collective-permute-done | bytes 196640 | tf_op jit(solution)/shard_map/ppermute | solution.py:100
  36.0 0.1 add_convert_fusion
  36.1 0.4 convert_reduce_fusion
  36.4 0.3 fusion.21
  36.7 0.2 convolution_convert_fusion.1
  37.0 2.5 %collective-permute-start.3 = (bf16[384,512]{1,0:T(8,128)(2,1)S(1)}, bf16[384,512]{1,0:T(8,128)(2,1)S(1)}, u32[]{:S(2)}, u32[]{:S(2)}) collective-permute-start(bf16[384,512]{1,0:T(8,128)(2,1)S(1)} %pad_maximum_fusion.2), channel_id=1, source_target_pairs={{0,1},{1,0},{2,3},{3,2},{4,5},{5,4},{6,7},{7,6},{8,9},{9,8},{10,11... | collective-permute-start | bytes 1179656 | tf_op jit(solution)/shard_map/ppermute | solution.py:100
  39.6 2.3 %collective-permute-start.4 = (f32[257,128]{1,0:T(8,128)S(1)}, f32[257,128]{1,0:T(8,128)S(1)}, u32[]{:S(2)}, u32[]{:S(2)}) collective-permute-start(f32[257,128]{1,0:T(8,128)S(1)} %fusion.12), channel_id=1, source_target_pairs={{0,2},{2,0},{4,6},{6,4},{8,10},{10,8},{12,14},{14,12},{16,18},{18,... | collective-permute-start | bytes 394760 | tf_op jit(solution)/shard_map/ppermute | solution.py:36
  42.0 0.8 collective-permute-done.4
  42.8 9.8 %collective-permute-start.7 = (f32[257,128]{1,0:T(8,128)S(1)}, f32[257,128]{1,0:T(8,128)S(1)}, u32[]{:S(2)}, u32[]{:S(2)}) collective-permute-start(f32[257,128]{1,0:T(8,128)S(1)} %fusion.14), channel_id=1, source_target_pairs={{0,192},{2,194},{4,196},{6,198},{8,200},{10,202},{12,204},{14,206}... | collective-permute-start | bytes 394760 | tf_op jit(solution)/shard_map/ppermute | solution.py:36
  52.6 5.0 %collective-permute-start.6 = (f32[257,128]{1,0:T(8,128)S(1)}, f32[257,128]{1,0:T(8,128)S(1)}, u32[]{:S(2)}, u32[]{:S(2)}) collective-permute-start(f32[257,128]{1,0:T(8,128)S(1)} %fusion.14), channel_id=1, source_target_pairs={{0,384},{2,386},{4,388},{6,390},{8,392},{10,394},{12,396},{14,398}... | collective-permute-start | bytes 394760 | tf_op jit(solution)/shard_map/ppermute | solution.py:36
  57.6 2.4 %collective-permute-start.5 = (f32[257,128]{1,0:T(8,128)S(1)}, f32[257,128]{1,0:T(8,128)S(1)}, u32[]{:S(2)}, u32[]{:S(2)}) collective-permute-start(f32[257,128]{1,0:T(8,128)S(1)} %fusion.14), channel_id=1, source_target_pairs={{0,576},{2,578},{4,580},{6,582},{8,584},{10,586},{12,588},{14,590}... | collective-permute-start | bytes 394760 | tf_op jit(solution)/shard_map/ppermute | solution.py:36
  60.0 0.0 collective-permute-done.3
  60.1 0.2 maximum_select_fusion.1
  60.3 3.5 %fusion.4 = f32[18,128,256]{2,1,0:T(8,128)S(1)} fusion(bf16[6,128,256,1]{2,1,0,3:T(8,128)(2,1)S(1)} %bitcast.38, bf16[6,18,128,128]{3,1,2,0:T(8,128)(2,1)} %copy-done.1), kind=kOutput, calls=%fused_computation.5 | convolution fusion | flops 905969664 | bytes 6291456 | tf_op jit(solution)/shard_map/bsij,bif->sjf/dot_general | solution.py:162
  63.8 0.1 slice.32
  63.9 3.1 %collective-permute-start.11 = (f32[6,128,256]{2,1,0:T(8,128)S(1)}, f32[6,128,256]{2,1,0:T(8,128)S(1)}, u32[]{:S(2)}, u32[]{:S(2)}) collective-permute-start(f32[6,128,256]{2,1,0:T(8,128)S(1)} %slice.32), channel_id=1, source_target_pairs={{2,0},{4,2},{6,4},{8,6},{10,8},{12,10},{14,12},{16,14},{18,16},{20... | collective-permute-start | bytes 2359304 | tf_op jit(solution)/shard_map/ppermute | solution.py:25
  67.0 0.0 collective-permute-done.7
  67.0 0.0 collective-permute-done.6
  67.0 0.0 collective-permute-done.5
  67.1 0.1 add_bitcast_fusion
  67.1 1.9 %collective-permute-start.8 = (f32[257,128]{1,0:T(8,128)S(1)}, f32[257,128]{1,0:T(8,128)S(1)}, u32[]{:S(2)}, u32[]{:S(2)}) collective-permute-start(f32[257,128]{1,0:T(8,128)S(1)} %add_bitcast_fusion), channel_id=1, source_target_pairs={{0,4},{2,6},{4,0},{6,2},{8,12},{10,14},{12,8},{14,10},{16,20},{18,... | collective-permute-start | bytes 394760 | tf_op jit(solution)/shard_map/ppermute | solution.py:36
  69.1 2.9 %collective-permute-start.12 = (bf16[6,128,256]{2,1,0:T(8,128)(2,1)S(1)}, bf16[6,128,256]{2,1,0:T(8,128)(2,1)S(1)}, u32[]{:S(2)}, u32[]{:S(2)}) collective-permute-start(bf16[6,128,256]{2,1,0:T(8,128)(2,1)S(1)} %slice.42), channel_id=1, source_target_pairs={{0,2},{2,4},{4,6},{6,8},{8,10},{10,12},{12,14},{14,16},{16,18},{18... | collective-permute-start | bytes 1179656 | tf_op jit(solution)/shard_map/ppermute | solution.py:25
  72.0 5.7 %collective-permute-done.8 = f32[257,128]{1,0:T(8,128)S(1)} collective-permute-done((f32[257,128]{1,0:T(8,128)S(1)}, f32[257,128]{1,0:T(8,128)S(1)}, u32[]{:S(2)}, u32[]{:S(2)}) %collective-permute-start.8) | collective-permute-done | bytes 131616 | tf_op jit(solution)/shard_map/ppermute | solution.py:36
  77.7 0.1 fusion.30
  77.8 2.6 %collective-permute-start.9 = (f32[257,128]{1,0:T(8,128)S(1)}, f32[257,128]{1,0:T(8,128)S(1)}, u32[]{:S(2)}, u32[]{:S(2)}) collective-permute-start(f32[257,128]{1,0:T(8,128)S(1)} %fusion.30), channel_id=1, source_target_pairs={{0,8},{2,10},{4,12},{6,14},{8,0},{10,2},{12,4},{14,6},{16,24},{18,... | collective-permute-start | bytes 394760 | tf_op jit(solution)/shard_map/ppermute | solution.py:36
  80.3 4.1 %collective-permute-done.9 = f32[257,128]{1,0:T(8,128)S(1)} collective-permute-done((f32[257,128]{1,0:T(8,128)S(1)}, f32[257,128]{1,0:T(8,128)S(1)}, u32[]{:S(2)}, u32[]{:S(2)}) %collective-permute-start.9) | collective-permute-done | bytes 131616 | tf_op jit(solution)/shard_map/ppermute | solution.py:36
  84.4 4.8 %collective-permute-start.10 = (f32[257,128]{1,0:T(8,128)S(1)}, f32[257,128]{1,0:T(8,128)S(1)}, u32[]{:S(2)}, u32[]{:S(2)}) collective-permute-start(f32[257,128]{1,0:T(8,128)S(1)} %add.145), channel_id=1, source_target_pairs={{0,1},{1,0},{2,3},{3,2},{4,5},{5,4},{6,7},{7,6},{8,9},{9,8},{10,11... | collective-permute-start | bytes 394760 | tf_op jit(solution)/shard_map/ppermute | solution.py:79
  89.2 5.0 %collective-permute-done.10 = f32[257,128]{1,0:T(8,128)S(1)} collective-permute-done((f32[257,128]{1,0:T(8,128)S(1)}, f32[257,128]{1,0:T(8,128)S(1)}, u32[]{:S(2)}, u32[]{:S(2)}) %collective-permute-start.10) | collective-permute-done | bytes 131616 | tf_op jit(solution)/shard_map/ppermute | solution.py:79
  94.2 0.0 collective-permute-done.12
  94.2 0.0 collective-permute-done.11
  94.2 0.2 fusion.11
  94.4 4.8 %collective-permute-start.15 = (f32[6,128,256]{2,1,0:T(8,128)S(1)}, f32[6,128,256]{2,1,0:T(8,128)S(1)}, u32[]{:S(2)}, u32[]{:S(2)}) collective-permute-start(f32[6,128,256]{2,1,0:T(8,128)S(1)} %fusion.11), channel_id=1, source_target_pairs={{0,1},{1,0},{2,3},{3,2},{4,5},{5,4},{6,7},{7,6},{8,9},{9,8},{10,11... | collective-permute-start | bytes 2359304 | tf_op jit(solution)/shard_map/ppermute | solution.py:110
  99.2 7.3 %collective-permute-start.13 = (f32[257,128]{1,0:T(8,128)S(1)}, f32[257,128]{1,0:T(8,128)S(1)}, u32[]{:S(2)}, u32[]{:S(2)}) collective-permute-start(f32[257,128]{1,0:T(8,128)S(1)} %add.146), channel_id=1, source_target_pairs={{0,16},{2,18},{4,20},{6,22},{8,24},{10,26},{12,28},{14,30},{16,0},... | collective-permute-start | bytes 394760 | tf_op jit(solution)/shard_map/ppermute | solution.py:36
  106.5 2.4 %collective-permute-done.13 = f32[257,128]{1,0:T(8,128)S(1)} collective-permute-done((f32[257,128]{1,0:T(8,128)S(1)}, f32[257,128]{1,0:T(8,128)S(1)}, u32[]{:S(2)}, u32[]{:S(2)}) %collective-permute-start.13) | collective-permute-done | bytes 131616 | tf_op jit(solution)/shard_map/ppermute | solution.py:36
  108.9 7.6 %collective-permute-start.14 = (f32[257,128]{1,0:T(8,128)S(1)}, f32[257,128]{1,0:T(8,128)S(1)}, u32[]{:S(2)}, u32[]{:S(2)}) collective-permute-start(f32[257,128]{1,0:T(8,128)S(1)} %add.149), channel_id=1, source_target_pairs={{0,32},{2,34},{4,36},{6,38},{8,40},{10,42},{12,44},{14,46},{16,48}... | collective-permute-start | bytes 394760 | tf_op jit(solution)/shard_map/ppermute | solution.py:36
  116.5 4.1 %collective-permute-done.14 = f32[257,128]{1,0:T(8,128)S(1)} collective-permute-done((f32[257,128]{1,0:T(8,128)S(1)}, f32[257,128]{1,0:T(8,128)S(1)}, u32[]{:S(2)}, u32[]{:S(2)}) %collective-permute-start.14) | collective-permute-done | bytes 131616 | tf_op jit(solution)/shard_map/ppermute | solution.py:36
  120.6 0.0 collective-permute-done.15
  120.6 0.8 add.151
  121.5 19.8 %collective-permute-start.17 = (f32[257,128]{1,0:T(8,128)S(1)}, f32[257,128]{1,0:T(8,128)S(1)}, u32[]{:S(2)}, u32[]{:S(2)}) collective-permute-start(f32[257,128]{1,0:T(8,128)S(1)} %add.150), channel_id=1, source_target_pairs={{0,128},{2,130},{4,132},{6,134},{8,136},{10,138},{12,140},{14,142}... | collective-permute-start | bytes 394760 | tf_op jit(solution)/shard_map/ppermute | solution.py:36
  141.3 1.9 %collective-permute-start.16 = (f32[257,128]{1,0:T(8,128)S(1)}, f32[257,128]{1,0:T(8,128)S(1)}, u32[]{:S(2)}, u32[]{:S(2)}) collective-permute-start(f32[257,128]{1,0:T(8,128)S(1)} %add.150), channel_id=1, source_target_pairs={{0,64},{2,66},{4,68},{6,70},{8,72},{10,74},{12,76},{14,78},{16,80}... | collective-permute-start | bytes 394760 | tf_op jit(solution)/shard_map/ppermute | solution.py:36
  143.3 0.2 collective-permute-done.17
  143.5 10.0 %collective-permute-done.16 = f32[257,128]{1,0:T(8,128)S(1)} collective-permute-done((f32[257,128]{1,0:T(8,128)S(1)}, f32[257,128]{1,0:T(8,128)S(1)}, u32[]{:S(2)}, u32[]{:S(2)}) %collective-permute-start.16) | collective-permute-done | bytes 131616 | tf_op jit(solution)/shard_map/ppermute | solution.py:36
  153.6 20.1 %collective-permute-start.18 = (f32[257,128]{1,0:T(8,128)S(1)}, f32[257,128]{1,0:T(8,128)S(1)}, u32[]{:S(2)}, u32[]{:S(2)}) collective-permute-start(f32[257,128]{1,0:T(8,128)S(1)} %select_add_fusion), channel_id=1, source_target_pairs={{0,2},{2,0},{4,6},{6,4},{8,10},{10,8},{12,14},{14,12},{16,18},{18,... | collective-permute-start | bytes 394760 | tf_op jit(solution)/shard_map/ppermute | solution.py:36
  173.7 0.9 maximum_select_fusion
  174.6 0.1 collective-permute-done.18
  174.7 0.6 slice_multiply_fusion.1
  175.2 0.7 slice_multiply_fusion
  (18 shorter events, 0.4 us)
Async XLA Ops:
  0.6 15.3 %copy-start = (bf16[6,6,128,128]{3,2,1,0:T(8,128)(2,1)S(1)}, bf16[6,6,128,128]{3,2,1,0:T(8,128)(2,1)}, u32[]{:S(2)}) copy-start(bf16[6,6,128,128]{3,2,1,0:T(8,128)(2,1)} %param.8) | copy-start | bytes 3538948
  0.6 17.6 %collective-permute-start = (bf16[768,256]{1,0:T(8,128)(2,1)}, bf16[768,256]{1,0:T(8,128)(2,1)S(1)}, u32[]{:S(2)}, u32[]{:S(2)}) collective-permute-start(bf16[768,256]{1,0:T(8,128)(2,1)} %param.7), channel_id=1, source_target_pairs={{0,2},{2,4},{4,6},{6,8},{8,10},{10,12},{12,14},{14,16},{16,18},{18... | collective-permute-start | bytes 1179656 | tf_op jit(solution)/shard_map/ppermute | solution.py:14
  5.4 12.8 %collective-permute-start.1 = (bf16[768,256]{1,0:T(8,128)(2,1)}, bf16[768,256]{1,0:T(8,128)(2,1)S(1)}, u32[]{:S(2)}, u32[]{:S(2)}) collective-permute-start(bf16[768,256]{1,0:T(8,128)(2,1)} %param.7), channel_id=1, source_target_pairs={{2,0},{4,2},{6,4},{8,6},{10,8},{12,10},{14,12},{16,14},{18,16},{20... | collective-permute-start | bytes 1179656 | tf_op jit(solution)/shard_map/ppermute | solution.py:17
  16.0 2.3 %copy-start.2 = (bf16[768,256]{1,0:T(8,128)(2,1)S(1)}, bf16[768,256]{1,0:T(8,128)(2,1)}, u32[]{:S(2)}) copy-start(bf16[768,256]{1,0:T(8,128)(2,1)} %param.7) | copy-start | bytes 1179652
  18.2 2.1 %copy-start.1 = (bf16[6,18,128,128]{3,1,2,0:T(8,128)(2,1)}, bf16[6,18,128,128]{3,1,2,0:T(8,128)(2,1)S(1)}, u32[]{:S(2)}) copy-start(bf16[6,18,128,128]{3,1,2,0:T(8,128)(2,1)S(1)} %convolution_convert_fusion) | copy-start | bytes 10616836
  18.3 17.7 %copy-start.3 = (bf16[256,256]{1,0:T(8,128)(2,1)S(1)}, bf16[256,256]{1,0:T(8,128)(2,1)}, u32[]{:S(2)}) copy-start(bf16[256,256]{1,0:T(8,128)(2,1)} %param.11) | copy-start | bytes 393220
  18.3 17.7 %copy-start.4 = (bf16[768,256]{1,0:T(8,128)(2,1)S(1)}, bf16[768,256]{1,0:T(8,128)(2,1)}, u32[]{:S(2)}) copy-start(bf16[768,256]{1,0:T(8,128)(2,1)} %param.13) | copy-start | bytes 1179652
  18.4 17.7 %copy-start.5 = (f32[256]{0:T(256)S(1)}, f32[256]{0:T(256)}, u32[]{:S(2)}) copy-start(f32[256]{0:T(256)} %param.12) | copy-start | bytes 3076
  20.4 15.6 %collective-permute-start.2 = (bf16[384,256]{1,0:T(8,128)(2,1)S(1)}, bf16[384,256]{1,0:T(8,128)(2,1)S(1)}, u32[]{:S(2)}, u32[]{:S(2)}) collective-permute-start(bf16[384,256]{1,0:T(8,128)(2,1)S(1)} %dynamic-slice_convert_fusion), channel_id=1, source_target_pairs={{0,1},{1,0},{2,3},{3,2},{4,5},{5,4},{6,7},{7,6},{8,9},{9,8},{10,11... | collective-permute-start | bytes 589832 | tf_op jit(solution)/shard_map/ppermute | solution.py:100
  37.0 23.1 %collective-permute-start.3 = (bf16[384,512]{1,0:T(8,128)(2,1)S(1)}, bf16[384,512]{1,0:T(8,128)(2,1)S(1)}, u32[]{:S(2)}, u32[]{:S(2)}) collective-permute-start(bf16[384,512]{1,0:T(8,128)(2,1)S(1)} %pad_maximum_fusion.2), channel_id=1, source_target_pairs={{0,1},{1,0},{2,3},{3,2},{4,5},{5,4},{6,7},{7,6},{8,9},{9,8},{10,11... | collective-permute-start | bytes 1179656 | tf_op jit(solution)/shard_map/ppermute | solution.py:100
  39.6 3.2 %collective-permute-start.4 = (f32[257,128]{1,0:T(8,128)S(1)}, f32[257,128]{1,0:T(8,128)S(1)}, u32[]{:S(2)}, u32[]{:S(2)}) collective-permute-start(f32[257,128]{1,0:T(8,128)S(1)} %fusion.12), channel_id=1, source_target_pairs={{0,2},{2,0},{4,6},{6,4},{8,10},{10,8},{12,14},{14,12},{16,18},{18,... | collective-permute-start | bytes 394760 | tf_op jit(solution)/shard_map/ppermute | solution.py:36
  42.8 24.1 %collective-permute-start.7 = (f32[257,128]{1,0:T(8,128)S(1)}, f32[257,128]{1,0:T(8,128)S(1)}, u32[]{:S(2)}, u32[]{:S(2)}) collective-permute-start(f32[257,128]{1,0:T(8,128)S(1)} %fusion.14), channel_id=1, source_target_pairs={{0,192},{2,194},{4,196},{6,198},{8,200},{10,202},{12,204},{14,206}... | collective-permute-start | bytes 394760 | tf_op jit(solution)/shard_map/ppermute | solution.py:36
  52.6 14.4 %collective-permute-start.6 = (f32[257,128]{1,0:T(8,128)S(1)}, f32[257,128]{1,0:T(8,128)S(1)}, u32[]{:S(2)}, u32[]{:S(2)}) collective-permute-start(f32[257,128]{1,0:T(8,128)S(1)} %fusion.14), channel_id=1, source_target_pairs={{0,384},{2,386},{4,388},{6,390},{8,392},{10,394},{12,396},{14,398}... | collective-permute-start | bytes 394760 | tf_op jit(solution)/shard_map/ppermute | solution.py:36
  57.6 9.3 %collective-permute-start.5 = (f32[257,128]{1,0:T(8,128)S(1)}, f32[257,128]{1,0:T(8,128)S(1)}, u32[]{:S(2)}, u32[]{:S(2)}) collective-permute-start(f32[257,128]{1,0:T(8,128)S(1)} %fusion.14), channel_id=1, source_target_pairs={{0,576},{2,578},{4,580},{6,582},{8,584},{10,586},{12,588},{14,590}... | collective-permute-start | bytes 394760 | tf_op jit(solution)/shard_map/ppermute | solution.py:36
  63.9 30.4 %collective-permute-start.11 = (f32[6,128,256]{2,1,0:T(8,128)S(1)}, f32[6,128,256]{2,1,0:T(8,128)S(1)}, u32[]{:S(2)}, u32[]{:S(2)}) collective-permute-start(f32[6,128,256]{2,1,0:T(8,128)S(1)} %slice.32), channel_id=1, source_target_pairs={{2,0},{4,2},{6,4},{8,6},{10,8},{12,10},{14,12},{16,14},{18,16},{20... | collective-permute-start | bytes 2359304 | tf_op jit(solution)/shard_map/ppermute | solution.py:25
  67.1 10.6 %collective-permute-start.8 = (f32[257,128]{1,0:T(8,128)S(1)}, f32[257,128]{1,0:T(8,128)S(1)}, u32[]{:S(2)}, u32[]{:S(2)}) collective-permute-start(f32[257,128]{1,0:T(8,128)S(1)} %add_bitcast_fusion), channel_id=1, source_target_pairs={{0,4},{2,6},{4,0},{6,2},{8,12},{10,14},{12,8},{14,10},{16,20},{18,... | collective-permute-start | bytes 394760 | tf_op jit(solution)/shard_map/ppermute | solution.py:36
  69.1 25.1 %collective-permute-start.12 = (bf16[6,128,256]{2,1,0:T(8,128)(2,1)S(1)}, bf16[6,128,256]{2,1,0:T(8,128)(2,1)S(1)}, u32[]{:S(2)}, u32[]{:S(2)}) collective-permute-start(bf16[6,128,256]{2,1,0:T(8,128)(2,1)S(1)} %slice.42), channel_id=1, source_target_pairs={{0,2},{2,4},{4,6},{6,8},{8,10},{10,12},{12,14},{14,16},{16,18},{18... | collective-permute-start | bytes 1179656 | tf_op jit(solution)/shard_map/ppermute | solution.py:25
  77.8 6.6 %collective-permute-start.9 = (f32[257,128]{1,0:T(8,128)S(1)}, f32[257,128]{1,0:T(8,128)S(1)}, u32[]{:S(2)}, u32[]{:S(2)}) collective-permute-start(f32[257,128]{1,0:T(8,128)S(1)} %fusion.30), channel_id=1, source_target_pairs={{0,8},{2,10},{4,12},{6,14},{8,0},{10,2},{12,4},{14,6},{16,24},{18,... | collective-permute-start | bytes 394760 | tf_op jit(solution)/shard_map/ppermute | solution.py:36
  84.4 9.8 %collective-permute-start.10 = (f32[257,128]{1,0:T(8,128)S(1)}, f32[257,128]{1,0:T(8,128)S(1)}, u32[]{:S(2)}, u32[]{:S(2)}) collective-permute-start(f32[257,128]{1,0:T(8,128)S(1)} %add.145), channel_id=1, source_target_pairs={{0,1},{1,0},{2,3},{3,2},{4,5},{5,4},{6,7},{7,6},{8,9},{9,8},{10,11... | collective-permute-start | bytes 394760 | tf_op jit(solution)/shard_map/ppermute | solution.py:79
  94.4 26.2 %collective-permute-start.15 = (f32[6,128,256]{2,1,0:T(8,128)S(1)}, f32[6,128,256]{2,1,0:T(8,128)S(1)}, u32[]{:S(2)}, u32[]{:S(2)}) collective-permute-start(f32[6,128,256]{2,1,0:T(8,128)S(1)} %fusion.11), channel_id=1, source_target_pairs={{0,1},{1,0},{2,3},{3,2},{4,5},{5,4},{6,7},{7,6},{8,9},{9,8},{10,11... | collective-permute-start | bytes 2359304 | tf_op jit(solution)/shard_map/ppermute | solution.py:110
  99.2 9.7 %collective-permute-start.13 = (f32[257,128]{1,0:T(8,128)S(1)}, f32[257,128]{1,0:T(8,128)S(1)}, u32[]{:S(2)}, u32[]{:S(2)}) collective-permute-start(f32[257,128]{1,0:T(8,128)S(1)} %add.146), channel_id=1, source_target_pairs={{0,16},{2,18},{4,20},{6,22},{8,24},{10,26},{12,28},{14,30},{16,0},... | collective-permute-start | bytes 394760 | tf_op jit(solution)/shard_map/ppermute | solution.py:36
  108.9 11.7 %collective-permute-start.14 = (f32[257,128]{1,0:T(8,128)S(1)}, f32[257,128]{1,0:T(8,128)S(1)}, u32[]{:S(2)}, u32[]{:S(2)}) collective-permute-start(f32[257,128]{1,0:T(8,128)S(1)} %add.149), channel_id=1, source_target_pairs={{0,32},{2,34},{4,36},{6,38},{8,40},{10,42},{12,44},{14,46},{16,48}... | collective-permute-start | bytes 394760 | tf_op jit(solution)/shard_map/ppermute | solution.py:36
  121.5 22.0 %collective-permute-start.17 = (f32[257,128]{1,0:T(8,128)S(1)}, f32[257,128]{1,0:T(8,128)S(1)}, u32[]{:S(2)}, u32[]{:S(2)}) collective-permute-start(f32[257,128]{1,0:T(8,128)S(1)} %add.150), channel_id=1, source_target_pairs={{0,128},{2,130},{4,132},{6,134},{8,136},{10,138},{12,140},{14,142}... | collective-permute-start | bytes 394760 | tf_op jit(solution)/shard_map/ppermute | solution.py:36
  141.3 12.2 %collective-permute-start.16 = (f32[257,128]{1,0:T(8,128)S(1)}, f32[257,128]{1,0:T(8,128)S(1)}, u32[]{:S(2)}, u32[]{:S(2)}) collective-permute-start(f32[257,128]{1,0:T(8,128)S(1)} %add.150), channel_id=1, source_target_pairs={{0,64},{2,66},{4,68},{6,70},{8,72},{10,74},{12,76},{14,78},{16,80}... | collective-permute-start | bytes 394760 | tf_op jit(solution)/shard_map/ppermute | solution.py:36
  153.6 21.1 %collective-permute-start.18 = (f32[257,128]{1,0:T(8,128)S(1)}, f32[257,128]{1,0:T(8,128)S(1)}, u32[]{:S(2)}, u32[]{:S(2)}) collective-permute-start(f32[257,128]{1,0:T(8,128)S(1)} %select_add_fusion), channel_id=1, source_target_pairs={{0,2},{2,0},{4,6},{6,4},{8,10},{10,8},{12,14},{14,12},{16,18},{18,... | collective-permute-start | bytes 394760 | tf_op jit(solution)/shard_map/ppermute | solution.py:36

commit v15 on v13

--- a/solution.py
+++ b/solution.py
@@ -78,8 +78,7 @@
     x = swapped_sum(x, "rows", count, y_stride, y_size, 2)
     x = x + lax.ppermute(x, "rep", [(0, 1), (1, 0)])
     x, tie = lax.optimization_barrier((x, tie))
-    x = swapped_sum(x, "rows", count, z_stride, z_size, 1)
-    x = swapped_sum(x, "rows", count, z_stride, z_size, 2)
+    x = ring_sum(x, "rows", count, z_stride, z_size // 3)
     x = three_way_sum(x, "rows", count, z_stride, z_size)
     other = moved(x, "rows", count, c_stride, c_size, lambda c: c ^ 1)
     joined = jnp.where(core == 0, jnp.concatenate([x, other], 1), jnp.concatenate([other, x], 1))

time: 173 us -> 177 us (1.023)
  the two profiles are of different devices: /device:TPU:68 before, /device:TPU:64 now
where the time goes in v15:
time: 177 us; the launch traced here: 176 us
  starting transfers between devices  95.8 us (54%)
  waiting for transfers between devices  60.4 us (34%)
  other arithmetic  9.64 us (5%)
  matrix products  7.72 us (4%)
    ppermute x12, starting transfers between devices, moved(): return lax.ppermute(x, axis, pairs)  56.5 us
    ppermute x12, waiting for transfers between devices, moved(): return lax.ppermute(x, axis, pairs)  30 us
    ppermute x1, waiting for transfers between devices, partner_sum(): return x + lax.ppermute(x, 'rep', [(0, 1), (1, 0)])  12.5 us
    ppermute x2, starting transfers between devices, partner_swap(): return lax.ppermute(x, 'rep', [(0, 1), (1, 0)])  12.3 us
    ppermute x2, starting transfers between devices, from_behind(): return lax.ppermute(x, axis, pairs)  10.1 us
    ppermute x2, waiting for transfers between devices, partner_swap(): return lax.ppermute(x, 'rep', [(0, 1), (1, 0)])  6.62 us
    ppermute x1, waiting for transfers between devices, extended(): lax.ppermute(lax.slice_in_dim(block, block.shape[dim] - width, None, axis...  6.38 us
    ppermute x1, starting transfers between devices, global_sum(): x = x + lax.ppermute(x, 'rep', [(0, 1), (1, 0)])  5.86 us
  transfers between devices with their start and end apart: 20, of which 10 were waited for; matrix products, arithmetic and copies ran while one was open for 8% of the time, Pallas kernels for 0%

profile of v15, /device:TPU:64, one launch (start us, length us, event | category | flops | bytes accessed | tf_op | source)
XLA Modules:
  0.0 175.8 jit_solution(15747569374321607183)
XLA Ops:
  0.6 0.0 copy-start
  0.6 4.2 %collective-permute-start.1 = (bf16[768,256]{1,0:T(8,128)(2,1)}, bf16[768,256]{1,0:T(8,128)(2,1)S(1)}, u32[]{:S(2)}, u32[]{:S(2)}) collective-permute-start(bf16[768,256]{1,0:T(8,128)(2,1)} %param.7), channel_id=1, source_target_pairs={{2,0},{4,2},{6,4},{8,6},{10,8},{12,10},{14,12},{16,14},{18,16},{20... | collective-permute-start | bytes 1179656 | tf_op jit(solution)/shard_map/ppermute | solution.py:17
  4.8 1.9 %collective-permute-start = (bf16[768,256]{1,0:T(8,128)(2,1)}, bf16[768,256]{1,0:T(8,128)(2,1)S(1)}, u32[]{:S(2)}, u32[]{:S(2)}) collective-permute-start(bf16[768,256]{1,0:T(8,128)(2,1)} %param.7), channel_id=1, source_target_pairs={{0,2},{2,4},{4,6},{6,8},{8,10},{10,12},{12,14},{14,16},{16,18},{18... | collective-permute-start | bytes 1179656 | tf_op jit(solution)/shard_map/ppermute | solution.py:14
  6.8 0.7 broadcast_subtract_fusion
  7.5 0.7 iota_compare_fusion.1
  8.2 2.2 %convolution_convert_fusion = bf16[6,18,128,128]{3,1,2,0:T(8,128)(2,1)S(1)} fusion(bf16[6,6,128,128]{3,2,1,0:T(8,128)(2,1)S(1)} %copy-done, s32[6,6]{1,0:T(8,128)S(1)} %broadcast_subtract_fusion, pred[6,6]{1,0:T(8,128)(4,1)S(1)} %iota_compare_fusion.1), kind=kOutput, calls=%fused_computation.4 | convolution fusion | flops 23004432 | bytes 4718772 | tf_op jit(solution)/shard_map/bks,bkij->bsij/dot_general | solution.py:130
  10.5 6.4 %collective-permute-done = bf16[768,256]{1,0:T(8,128)(2,1)S(1)} collective-permute-done((bf16[768,256]{1,0:T(8,128)(2,1)}, bf16[768,256]{1,0:T(8,128)(2,1)S(1)}, u32[]{:S(2)}, u32[]{:S(2)}) %collective-permute-start) | collective-permute-done | bytes 393248 | tf_op jit(solution)/shard_map/ppermute | solution.py:14
  16.8 0.1 pad_maximum_fusion
  16.9 0.0 copy-start.3
  16.9 0.0 copy-start.4
  16.9 0.0 copy-start.5
  17.0 1.1 fusion.8
  18.1 5.6 %collective-permute-start.2 = (bf16[384,256]{1,0:T(8,128)(2,1)S(1)}, bf16[384,256]{1,0:T(8,128)(2,1)S(1)}, u32[]{:S(2)}, u32[]{:S(2)}) collective-permute-start(bf16[384,256]{1,0:T(8,128)(2,1)S(1)} %dynamic-slice_convert_fusion), channel_id=1, source_target_pairs={{0,1},{1,0},{2,3},{3,2},{4,5},{5,4},{6,7},{7,6},{8,9},{9,8},{10,11... | collective-permute-start | bytes 589832 | tf_op jit(solution)/shard_map/ppermute | solution.py:89
  23.7 6.6 %collective-permute-done.2 = bf16[384,256]{1,0:T(8,128)(2,1)S(1)} collective-permute-done((bf16[384,256]{1,0:T(8,128)(2,1)S(1)}, bf16[384,256]{1,0:T(8,128)(2,1)S(1)}, u32[]{:S(2)}, u32[]{:S(2)}) %collective-permute-start.2) | collective-permute-done | bytes 196640 | tf_op jit(solution)/shard_map/ppermute | solution.py:89
  30.4 0.1 add_convert_fusion.1
  30.4 0.4 convert_reduce_fusion
  30.8 0.2 convolution_convert_fusion.1
  31.1 0.3 fusion.21
  31.4 6.7 %collective-permute-start.3 = (bf16[384,512]{1,0:T(8,128)(2,1)S(1)}, bf16[384,512]{1,0:T(8,128)(2,1)S(1)}, u32[]{:S(2)}, u32[]{:S(2)}) collective-permute-start(bf16[384,512]{1,0:T(8,128)(2,1)S(1)} %pad_maximum_fusion.3), channel_id=1, source_target_pairs={{0,1},{1,0},{2,3},{3,2},{4,5},{5,4},{6,7},{7,6},{8,9},{9,8},{10,11... | collective-permute-start | bytes 1179656 | tf_op jit(solution)/shard_map/ppermute | solution.py:89
  38.1 1.9 %collective-permute-start.4 = (f32[257,128]{1,0:T(8,128)S(1)}, f32[257,128]{1,0:T(8,128)S(1)}, u32[]{:S(2)}, u32[]{:S(2)}) collective-permute-start(f32[257,128]{1,0:T(8,128)S(1)} %fusion.12), channel_id=1, source_target_pairs={{0,2},{2,0},{4,6},{6,4},{8,10},{10,8},{12,14},{14,12},{16,18},{18,... | collective-permute-start | bytes 394760 | tf_op jit(solution)/shard_map/ppermute | solution.py:36
  40.1 1.2 collective-permute-done.4
  41.3 3.4 %collective-permute-start.7 = (f32[257,128]{1,0:T(8,128)S(1)}, f32[257,128]{1,0:T(8,128)S(1)}, u32[]{:S(2)}, u32[]{:S(2)}) collective-permute-start(f32[257,128]{1,0:T(8,128)S(1)} %fusion.14), channel_id=1, source_target_pairs={{0,192},{2,194},{4,196},{6,198},{8,200},{10,202},{12,204},{14,206}... | collective-permute-start | bytes 394760 | tf_op jit(solution)/shard_map/ppermute | solution.py:36
  44.8 4.6 %collective-permute-start.6 = (f32[257,128]{1,0:T(8,128)S(1)}, f32[257,128]{1,0:T(8,128)S(1)}, u32[]{:S(2)}, u32[]{:S(2)}) collective-permute-start(f32[257,128]{1,0:T(8,128)S(1)} %fusion.14), channel_id=1, source_target_pairs={{0,384},{2,386},{4,388},{6,390},{8,392},{10,394},{12,396},{14,398}... | collective-permute-start | bytes 394760 | tf_op jit(solution)/shard_map/ppermute | solution.py:36
  49.4 3.3 %collective-permute-start.5 = (f32[257,128]{1,0:T(8,128)S(1)}, f32[257,128]{1,0:T(8,128)S(1)}, u32[]{:S(2)}, u32[]{:S(2)}) collective-permute-start(f32[257,128]{1,0:T(8,128)S(1)} %fusion.14), channel_id=1, source_target_pairs={{0,576},{2,578},{4,580},{6,582},{8,584},{10,586},{12,588},{14,590}... | collective-permute-start | bytes 394760 | tf_op jit(solution)/shard_map/ppermute | solution.py:36
  52.7 0.0 collective-permute-done.3
  52.7 0.7 fusion.20
  53.5 0.2 maximum_select_fusion.1
  53.6 3.5 %fusion.4 = f32[18,128,256]{2,1,0:T(8,128)S(1)} fusion(bf16[6,128,256,1]{2,1,0,3:T(8,128)(2,1)S(1)} %bitcast.46, bf16[6,18,128,128]{3,1,2,0:T(8,128)(2,1)} %copy-done.1), kind=kOutput, calls=%fused_computation.5 | convolution fusion | flops 905969664 | bytes 6291456 | tf_op jit(solution)/shard_map/bsij,bif->sjf/dot_general | solution.py:151
  57.1 0.1 slice.32
  57.2 8.2 %collective-permute-start.11 = (f32[6,128,256]{2,1,0:T(8,128)S(1)}, f32[6,128,256]{2,1,0:T(8,128)S(1)}, u32[]{:S(2)}, u32[]{:S(2)}) collective-permute-start(f32[6,128,256]{2,1,0:T(8,128)S(1)} %slice.32), channel_id=1, source_target_pairs={{2,0},{4,2},{6,4},{8,6},{10,8},{12,10},{14,12},{16,14},{18,16},{20... | collective-permute-start | bytes 2359304 | tf_op jit(solution)/shard_map/ppermute | solution.py:25
  65.4 0.0 collective-permute-done.7
  65.5 0.0 collective-permute-done.5
  65.5 0.1 add_bitcast_fusion.1
  65.6 1.9 %collective-permute-start.8 = (f32[257,128]{1,0:T(8,128)S(1)}, f32[257,128]{1,0:T(8,128)S(1)}, u32[]{:S(2)}, u32[]{:S(2)}) collective-permute-start(f32[257,128]{1,0:T(8,128)S(1)} %add_bitcast_fusion.1), channel_id=1, source_target_pairs={{0,4},{2,6},{4,0},{6,2},{8,12},{10,14},{12,8},{14,10},{16,20},{18,... | collective-permute-start | bytes 394760 | tf_op jit(solution)/shard_map/ppermute | solution.py:36
  67.5 1.9 %collective-permute-start.12 = (bf16[6,128,256]{2,1,0:T(8,128)(2,1)S(1)}, bf16[6,128,256]{2,1,0:T(8,128)(2,1)S(1)}, u32[]{:S(2)}, u32[]{:S(2)}) collective-permute-start(bf16[6,128,256]{2,1,0:T(8,128)(2,1)S(1)} %slice.42), channel_id=1, source_target_pairs={{0,2},{2,4},{4,6},{6,8},{8,10},{10,12},{12,14},{14,16},{16,18},{18... | collective-permute-start | bytes 1179656 | tf_op jit(solution)/shard_map/ppermute | solution.py:25
  69.5 12.4 %collective-permute-done.8 = f32[257,128]{1,0:T(8,128)S(1)} collective-permute-done((f32[257,128]{1,0:T(8,128)S(1)}, f32[257,128]{1,0:T(8,128)S(1)}, u32[]{:S(2)}, u32[]{:S(2)}) %collective-permute-start.8) | collective-permute-done | bytes 131616 | tf_op jit(solution)/shard_map/ppermute | solution.py:36
  81.8 0.1 fusion.30
  81.9 2.2 %collective-permute-start.9 = (f32[257,128]{1,0:T(8,128)S(1)}, f32[257,128]{1,0:T(8,128)S(1)}, u32[]{:S(2)}, u32[]{:S(2)}) collective-permute-start(f32[257,128]{1,0:T(8,128)S(1)} %fusion.30), channel_id=1, source_target_pairs={{0,8},{2,10},{4,12},{6,14},{8,0},{10,2},{12,4},{14,6},{16,24},{18,... | collective-permute-start | bytes 394760 | tf_op jit(solution)/shard_map/ppermute | solution.py:36
  84.1 6.1 %collective-permute-done.9 = f32[257,128]{1,0:T(8,128)S(1)} collective-permute-done((f32[257,128]{1,0:T(8,128)S(1)}, f32[257,128]{1,0:T(8,128)S(1)}, u32[]{:S(2)}, u32[]{:S(2)}) %collective-permute-start.9) | collective-permute-done | bytes 131616 | tf_op jit(solution)/shard_map/ppermute | solution.py:36
  90.3 5.9 %collective-permute-start.10 = (f32[257,128]{1,0:T(8,128)S(1)}, f32[257,128]{1,0:T(8,128)S(1)}, u32[]{:S(2)}, u32[]{:S(2)}) collective-permute-start(f32[257,128]{1,0:T(8,128)S(1)} %add.179), channel_id=1, source_target_pairs={{0,1},{1,0},{2,3},{3,2},{4,5},{5,4},{6,7},{7,6},{8,9},{9,8},{10,11... | collective-permute-start | bytes 394760 | tf_op jit(solution)/shard_map/ppermute | solution.py:79
  96.1 4.9 %collective-permute-done.10 = f32[257,128]{1,0:T(8,128)S(1)} collective-permute-done((f32[257,128]{1,0:T(8,128)S(1)}, f32[257,128]{1,0:T(8,128)S(1)}, u32[]{:S(2)}, u32[]{:S(2)}) %collective-permute-start.10) | collective-permute-done | bytes 131616 | tf_op jit(solution)/shard_map/ppermute | solution.py:79
  101.1 0.0 collective-permute-done.12
  101.1 0.0 collective-permute-done.11
  101.1 0.2 fusion.11
  101.3 3.0 %collective-permute-start.16 = (f32[257,128]{1,0:T(8,128)S(1)}, f32[257,128]{1,0:T(8,128)S(1)}, u32[]{:S(2)}, u32[]{:S(2)}) collective-permute-start(f32[257,128]{1,0:T(8,128)S(1)} %add.180), channel_id=1, source_target_pairs={{0,16},{2,18},{4,20},{6,22},{8,24},{10,26},{12,28},{14,30},{16,32}... | collective-permute-start | bytes 394760 | tf_op jit(solution)/shard_map/ppermute | solution.py:36
  104.3 22.6 %collective-permute-start.15 = (f32[257,128]{1,0:T(8,128)S(1)}, f32[257,128]{1,0:T(8,128)S(1)}, u32[]{:S(2)}, u32[]{:S(2)}) collective-permute-start(f32[257,128]{1,0:T(8,128)S(1)} %add.180), channel_id=1, source_target_pairs={{0,32},{2,34},{4,36},{6,38},{8,40},{10,42},{12,44},{14,46},{16,48}... | collective-permute-start | bytes 394760 | tf_op jit(solution)/shard_map/ppermute | solution.py:36
  126.9 1.9 %collective-permute-start.14 = (f32[257,128]{1,0:T(8,128)S(1)}, f32[257,128]{1,0:T(8,128)S(1)}, u32[]{:S(2)}, u32[]{:S(2)}) collective-permute-start(f32[257,128]{1,0:T(8,128)S(1)} %add.180), channel_id=1, source_target_pairs={{0,48},{2,50},{4,52},{6,54},{8,56},{10,58},{12,60},{14,62},{16,0},... | collective-permute-start | bytes 394760 | tf_op jit(solution)/shard_map/ppermute | solution.py:36
  128.9 0.0 collective-permute-done.16
  128.9 5.5 %collective-permute-done.15 = f32[257,128]{1,0:T(8,128)S(1)} collective-permute-done((f32[257,128]{1,0:T(8,128)S(1)}, f32[257,128]{1,0:T(8,128)S(1)}, u32[]{:S(2)}, u32[]{:S(2)}) %collective-permute-start.15) | collective-permute-done | bytes 131616 | tf_op jit(solution)/shard_map/ppermute | solution.py:36
  134.4 4.4 %collective-permute-done.14 = f32[257,128]{1,0:T(8,128)S(1)} collective-permute-done((f32[257,128]{1,0:T(8,128)S(1)}, f32[257,128]{1,0:T(8,128)S(1)}, u32[]{:S(2)}, u32[]{:S(2)}) %collective-permute-start.14) | collective-permute-done | bytes 131616 | tf_op jit(solution)/shard_map/ppermute | solution.py:36
  138.8 0.7 add_bitcast_fusion
  139.6 1.9 %collective-permute-start.17 = (f32[257,128]{1,0:T(8,128)}, f32[257,128]{1,0:T(8,128)}, u32[]{:S(2)}, u32[]{:S(2)}) collective-permute-start(f32[257,128]{1,0:T(8,128)} %add_bitcast_fusion), channel_id=1, source_target_pairs={{0,64},{2,66},{4,68},{6,70},{8,72},{10,74},{12,76},{14,78},{16,80}... | collective-permute-start | bytes 394760 | tf_op jit(solution)/shard_map/ppermute | solution.py:36
  141.5 7.8 %collective-permute-start.18 = (f32[257,128]{1,0:T(8,128)}, f32[257,128]{1,0:T(8,128)}, u32[]{:S(2)}, u32[]{:S(2)}) collective-permute-start(f32[257,128]{1,0:T(8,128)} %add_bitcast_fusion), channel_id=1, source_target_pairs={{0,128},{2,130},{4,132},{6,134},{8,136},{10,138},{12,140},{14,142}... | collective-permute-start | bytes 394760 | tf_op jit(solution)/shard_map/ppermute | solution.py:36
  149.4 4.9 %collective-permute-start.13 = (f32[6,128,256]{2,1,0:T(8,128)S(1)}, f32[6,128,256]{2,1,0:T(8,128)S(1)}, u32[]{:S(2)}, u32[]{:S(2)}) collective-permute-start(f32[6,128,256]{2,1,0:T(8,128)S(1)} %fusion.11), channel_id=1, source_target_pairs={{0,1},{1,0},{2,3},{3,2},{4,5},{5,4},{6,7},{7,6},{8,9},{9,8},{10,11... | collective-permute-start | bytes 2359304 | tf_op jit(solution)/shard_map/ppermute | solution.py:99
  154.2 0.4 collective-permute-done.18
  154.6 1.7 select_add_fusion
  156.3 1.9 %collective-permute-start.19 = (f32[257,128]{1,0:T(8,128)}, f32[257,128]{1,0:T(8,128)S(1)}, u32[]{:S(2)}, u32[]{:S(2)}) collective-permute-start(f32[257,128]{1,0:T(8,128)} %select_add_fusion), channel_id=1, source_target_pairs={{0,2},{2,0},{4,6},{6,4},{8,10},{10,8},{12,14},{14,12},{16,18},{18,... | collective-permute-start | bytes 394760 | tf_op jit(solution)/shard_map/ppermute | solution.py:36
  158.3 1.9 %maximum_select_fusion = bf16[768,256]{1,0:T(8,128)(2,1)} fusion(bf16[384,256]{1,0:T(8,128)(2,1)} %get-tuple-element.11, bf16[384,256]{1,0:T(8,128)(2,1)S(1)} %get-tuple-element.12, pred[]{:T(512)S(6)} %eq.43), kind=kLoop, calls=%fused_computation.18 | loop fusion | flops 1769472 | bytes 786433 | tf_op jit(solution)/shard_map/jit(_where)/select_n | solution.py:93
  160.2 0.0 collective-permute-done.19
  160.2 1.0 maximum_select_fusion.2
  161.2 0.6 slice_multiply_fusion.1
  161.7 0.7 slice_multiply_fusion
  162.5 12.5 %collective-permute-done.13 = f32[6,128,256]{2,1,0:T(8,128)S(1)} collective-permute-done((f32[6,128,256]{2,1,0:T(8,128)S(1)}, f32[6,128,256]{2,1,0:T(8,128)S(1)}, u32[]{:S(2)}, u32[]{:S(2)}) %collective-permute-start.13) | collective-permute-done | bytes 786464 | tf_op jit(solution)/shard_map/ppermute | solution.py:99
  174.9 0.8 add_convert_fusion
  (20 shorter events, 0.3 us)
Async XLA Ops:
  0.6 7.6 %copy-start = (bf16[6,6,128,128]{3,2,1,0:T(8,128)(2,1)S(1)}, bf16[6,6,128,128]{3,2,1,0:T(8,128)(2,1)}, u32[]{:S(2)}) copy-start(bf16[6,6,128,128]{3,2,1,0:T(8,128)(2,1)} %param.8) | copy-start | bytes 3538948
  0.6 9.8 %collective-permute-start.1 = (bf16[768,256]{1,0:T(8,128)(2,1)}, bf16[768,256]{1,0:T(8,128)(2,1)S(1)}, u32[]{:S(2)}, u32[]{:S(2)}) collective-permute-start(bf16[768,256]{1,0:T(8,128)(2,1)} %param.7), channel_id=1, source_target_pairs={{2,0},{4,2},{6,4},{8,6},{10,8},{12,10},{14,12},{16,14},{18,16},{20... | collective-permute-start | bytes 1179656 | tf_op jit(solution)/shard_map/ppermute | solution.py:17
  4.8 12.0 %collective-permute-start = (bf16[768,256]{1,0:T(8,128)(2,1)}, bf16[768,256]{1,0:T(8,128)(2,1)S(1)}, u32[]{:S(2)}, u32[]{:S(2)}) collective-permute-start(bf16[768,256]{1,0:T(8,128)(2,1)} %param.7), channel_id=1, source_target_pairs={{0,2},{2,4},{4,6},{6,8},{8,10},{10,12},{12,14},{14,16},{16,18},{18... | collective-permute-start | bytes 1179656 | tf_op jit(solution)/shard_map/ppermute | solution.py:14
  8.2 8.6 %copy-start.2 = (bf16[768,256]{1,0:T(8,128)(2,1)S(1)}, bf16[768,256]{1,0:T(8,128)(2,1)}, u32[]{:S(2)}) copy-start(bf16[768,256]{1,0:T(8,128)(2,1)} %param.7) | copy-start | bytes 1179652
  10.4 7.6 %copy-start.1 = (bf16[6,18,128,128]{3,1,2,0:T(8,128)(2,1)}, bf16[6,18,128,128]{3,1,2,0:T(8,128)(2,1)S(1)}, u32[]{:S(2)}) copy-start(bf16[6,18,128,128]{3,1,2,0:T(8,128)(2,1)S(1)} %convolution_convert_fusion) | copy-start | bytes 10616836
  16.9 13.5 %copy-start.3 = (bf16[256,256]{1,0:T(8,128)(2,1)S(1)}, bf16[256,256]{1,0:T(8,128)(2,1)}, u32[]{:S(2)}) copy-start(bf16[256,256]{1,0:T(8,128)(2,1)} %param.11) | copy-start | bytes 393220
  16.9 13.5 %copy-start.4 = (bf16[768,256]{1,0:T(8,128)(2,1)S(1)}, bf16[768,256]{1,0:T(8,128)(2,1)}, u32[]{:S(2)}) copy-start(bf16[768,256]{1,0:T(8,128)(2,1)} %param.13) | copy-start | bytes 1179652
  16.9 13.5 %copy-start.5 = (f32[256]{0:T(256)S(1)}, f32[256]{0:T(256)}, u32[]{:S(2)}) copy-start(f32[256]{0:T(256)} %param.12) | copy-start | bytes 3076
  18.1 12.3 %collective-permute-start.2 = (bf16[384,256]{1,0:T(8,128)(2,1)S(1)}, bf16[384,256]{1,0:T(8,128)(2,1)S(1)}, u32[]{:S(2)}, u32[]{:S(2)}) collective-permute-start(bf16[384,256]{1,0:T(8,128)(2,1)S(1)} %dynamic-slice_convert_fusion), channel_id=1, source_target_pairs={{0,1},{1,0},{2,3},{3,2},{4,5},{5,4},{6,7},{7,6},{8,9},{9,8},{10,11... | collective-permute-start | bytes 589832 | tf_op jit(solution)/shard_map/ppermute | solution.py:89
  31.4 21.4 %collective-permute-start.3 = (bf16[384,512]{1,0:T(8,128)(2,1)S(1)}, bf16[384,512]{1,0:T(8,128)(2,1)S(1)}, u32[]{:S(2)}, u32[]{:S(2)}) collective-permute-start(bf16[384,512]{1,0:T(8,128)(2,1)S(1)} %pad_maximum_fusion.3), channel_id=1, source_target_pairs={{0,1},{1,0},{2,3},{3,2},{4,5},{5,4},{6,7},{7,6},{8,9},{9,8},{10,11... | collective-permute-start | bytes 1179656 | tf_op jit(solution)/shard_map/ppermute | solution.py:89
  38.1 3.2 %collective-permute-start.4 = (f32[257,128]{1,0:T(8,128)S(1)}, f32[257,128]{1,0:T(8,128)S(1)}, u32[]{:S(2)}, u32[]{:S(2)}) collective-permute-start(f32[257,128]{1,0:T(8,128)S(1)} %fusion.12), channel_id=1, source_target_pairs={{0,2},{2,0},{4,6},{6,4},{8,10},{10,8},{12,14},{14,12},{16,18},{18,... | collective-permute-start | bytes 394760 | tf_op jit(solution)/shard_map/ppermute | solution.py:36
  41.3 24.1 %collective-permute-start.7 = (f32[257,128]{1,0:T(8,128)S(1)}, f32[257,128]{1,0:T(8,128)S(1)}, u32[]{:S(2)}, u32[]{:S(2)}) collective-permute-start(f32[257,128]{1,0:T(8,128)S(1)} %fusion.14), channel_id=1, source_target_pairs={{0,192},{2,194},{4,196},{6,198},{8,200},{10,202},{12,204},{14,206}... | collective-permute-start | bytes 394760 | tf_op jit(solution)/shard_map/ppermute | solution.py:36
  44.8 20.7 %collective-permute-start.6 = (f32[257,128]{1,0:T(8,128)S(1)}, f32[257,128]{1,0:T(8,128)S(1)}, u32[]{:S(2)}, u32[]{:S(2)}) collective-permute-start(f32[257,128]{1,0:T(8,128)S(1)} %fusion.14), channel_id=1, source_target_pairs={{0,384},{2,386},{4,388},{6,390},{8,392},{10,394},{12,396},{14,398}... | collective-permute-start | bytes 394760 | tf_op jit(solution)/shard_map/ppermute | solution.py:36
  49.4 16.1 %collective-permute-start.5 = (f32[257,128]{1,0:T(8,128)S(1)}, f32[257,128]{1,0:T(8,128)S(1)}, u32[]{:S(2)}, u32[]{:S(2)}) collective-permute-start(f32[257,128]{1,0:T(8,128)S(1)} %fusion.14), channel_id=1, source_target_pairs={{0,576},{2,578},{4,580},{6,582},{8,584},{10,586},{12,588},{14,590}... | collective-permute-start | bytes 394760 | tf_op jit(solution)/shard_map/ppermute | solution.py:36
  57.2 43.9 %collective-permute-start.11 = (f32[6,128,256]{2,1,0:T(8,128)S(1)}, f32[6,128,256]{2,1,0:T(8,128)S(1)}, u32[]{:S(2)}, u32[]{:S(2)}) collective-permute-start(f32[6,128,256]{2,1,0:T(8,128)S(1)} %slice.32), channel_id=1, source_target_pairs={{2,0},{4,2},{6,4},{8,6},{10,8},{12,10},{14,12},{16,14},{18,16},{20... | collective-permute-start | bytes 2359304 | tf_op jit(solution)/shard_map/ppermute | solution.py:25
  65.6 16.3 %collective-permute-start.8 = (f32[257,128]{1,0:T(8,128)S(1)}, f32[257,128]{1,0:T(8,128)S(1)}, u32[]{:S(2)}, u32[]{:S(2)}) collective-permute-start(f32[257,128]{1,0:T(8,128)S(1)} %add_bitcast_fusion.1), channel_id=1, source_target_pairs={{0,4},{2,6},{4,0},{6,2},{8,12},{10,14},{12,8},{14,10},{16,20},{18,... | collective-permute-start | bytes 394760 | tf_op jit(solution)/shard_map/ppermute | solution.py:36
  67.5 33.5 %collective-permute-start.12 = (bf16[6,128,256]{2,1,0:T(8,128)(2,1)S(1)}, bf16[6,128,256]{2,1,0:T(8,128)(2,1)S(1)}, u32[]{:S(2)}, u32[]{:S(2)}) collective-permute-start(bf16[6,128,256]{2,1,0:T(8,128)(2,1)S(1)} %slice.42), channel_id=1, source_target_pairs={{0,2},{2,4},{4,6},{6,8},{8,10},{10,12},{12,14},{14,16},{16,18},{18... | collective-permute-start | bytes 1179656 | tf_op jit(solution)/shard_map/ppermute | solution.py:25
  81.9 8.3 %collective-permute-start.9 = (f32[257,128]{1,0:T(8,128)S(1)}, f32[257,128]{1,0:T(8,128)S(1)}, u32[]{:S(2)}, u32[]{:S(2)}) collective-permute-start(f32[257,128]{1,0:T(8,128)S(1)} %fusion.30), channel_id=1, source_target_pairs={{0,8},{2,10},{4,12},{6,14},{8,0},{10,2},{12,4},{14,6},{16,24},{18,... | collective-permute-start | bytes 394760 | tf_op jit(solution)/shard_map/ppermute | solution.py:36
  90.3 10.8 %collective-permute-start.10 = (f32[257,128]{1,0:T(8,128)S(1)}, f32[257,128]{1,0:T(8,128)S(1)}, u32[]{:S(2)}, u32[]{:S(2)}) collective-permute-start(f32[257,128]{1,0:T(8,128)S(1)} %add.179), channel_id=1, source_target_pairs={{0,1},{1,0},{2,3},{3,2},{4,5},{5,4},{6,7},{7,6},{8,9},{9,8},{10,11... | collective-permute-start | bytes 394760 | tf_op jit(solution)/shard_map/ppermute | solution.py:79
  101.3 27.6 %collective-permute-start.16 = (f32[257,128]{1,0:T(8,128)S(1)}, f32[257,128]{1,0:T(8,128)S(1)}, u32[]{:S(2)}, u32[]{:S(2)}) collective-permute-start(f32[257,128]{1,0:T(8,128)S(1)} %add.180), channel_id=1, source_target_pairs={{0,16},{2,18},{4,20},{6,22},{8,24},{10,26},{12,28},{14,30},{16,32}... | collective-permute-start | bytes 394760 | tf_op jit(solution)/shard_map/ppermute | solution.py:36
  104.3 30.1 %collective-permute-start.15 = (f32[257,128]{1,0:T(8,128)S(1)}, f32[257,128]{1,0:T(8,128)S(1)}, u32[]{:S(2)}, u32[]{:S(2)}) collective-permute-start(f32[257,128]{1,0:T(8,128)S(1)} %add.180), channel_id=1, source_target_pairs={{0,32},{2,34},{4,36},{6,38},{8,40},{10,42},{12,44},{14,46},{16,48}... | collective-permute-start | bytes 394760 | tf_op jit(solution)/shard_map/ppermute | solution.py:36
  126.9 11.9 %collective-permute-start.14 = (f32[257,128]{1,0:T(8,128)S(1)}, f32[257,128]{1,0:T(8,128)S(1)}, u32[]{:S(2)}, u32[]{:S(2)}) collective-permute-start(f32[257,128]{1,0:T(8,128)S(1)} %add.180), channel_id=1, source_target_pairs={{0,48},{2,50},{4,52},{6,54},{8,56},{10,58},{12,60},{14,62},{16,0},... | collective-permute-start | bytes 394760 | tf_op jit(solution)/shard_map/ppermute | solution.py:36
  139.6 14.7 %collective-permute-start.17 = (f32[257,128]{1,0:T(8,128)}, f32[257,128]{1,0:T(8,128)}, u32[]{:S(2)}, u32[]{:S(2)}) collective-permute-start(f32[257,128]{1,0:T(8,128)} %add_bitcast_fusion), channel_id=1, source_target_pairs={{0,64},{2,66},{4,68},{6,70},{8,72},{10,74},{12,76},{14,78},{16,80}... | collective-permute-start | bytes 394760 | tf_op jit(solution)/shard_map/ppermute | solution.py:36
  141.5 13.2 %collective-permute-start.18 = (f32[257,128]{1,0:T(8,128)}, f32[257,128]{1,0:T(8,128)}, u32[]{:S(2)}, u32[]{:S(2)}) collective-permute-start(f32[257,128]{1,0:T(8,128)} %add_bitcast_fusion), channel_id=1, source_target_pairs={{0,128},{2,130},{4,132},{6,134},{8,136},{10,138},{12,140},{14,142}... | collective-permute-start | bytes 394760 | tf_op jit(solution)/shard_map/ppermute | solution.py:36
  149.4 25.6 %collective-permute-start.13 = (f32[6,128,256]{2,1,0:T(8,128)S(1)}, f32[6,128,256]{2,1,0:T(8,128)S(1)}, u32[]{:S(2)}, u32[]{:S(2)}) collective-permute-start(f32[6,128,256]{2,1,0:T(8,128)S(1)} %fusion.11), channel_id=1, source_target_pairs={{0,1},{1,0},{2,3},{3,2},{4,5},{5,4},{6,7},{7,6},{8,9},{9,8},{10,11... | collective-permute-start | bytes 2359304 | tf_op jit(solution)/shard_map/ppermute | solution.py:99
  156.3 3.8 %collective-permute-start.19 = (f32[257,128]{1,0:T(8,128)}, f32[257,128]{1,0:T(8,128)S(1)}, u32[]{:S(2)}, u32[]{:S(2)}) collective-permute-start(f32[257,128]{1,0:T(8,128)} %select_add_fusion), channel_id=1, source_target_pairs={{0,2},{2,0},{4,6},{6,4},{8,10},{10,8},{12,14},{14,12},{16,18},{18,... | collective-permute-start | bytes 394760 | tf_op jit(solution)/shard_map/ppermute | solution.py:36

commit v16 on v14

--- a/solution.py
+++ b/solution.py
@@ -80,6 +80,7 @@
     x, tie = lax.optimization_barrier((x, tie))
     x = swapped_sum(x, "rows", count, z_stride, z_size, 1)
     x = swapped_sum(x, "rows", count, z_stride, z_size, 2)
+    x = three_way_sum(x, "rows", count, z_stride, z_size)
     return x, tie
 
 
@@ -90,7 +91,6 @@
     (x_stride, x_size), (z_stride, z_size), (y_stride, y_size), (c_stride, c_size) = ROW_AXES[count]
     core = (lax.axis_index("rows") // c_stride) % c_size
     x, tie = lax.optimization_barrier((x, tie))
-    x = three_way_sum(x, "rows", count, z_stride, z_size)
     other = moved(x, "rows", count, c_stride, c_size, lambda c: c ^ 1)
     joined = jnp.where(core == 0, jnp.concatenate([x, other], 1), jnp.concatenate([other, x], 1))
     return joined, tie

time: 177 us -> 177 us (level)
  no operation moved by 1% of the time
where the time goes in v16:
time: 177 us; the launch traced here: 176 us
  starting transfers between devices  114 us (64%)
  waiting for transfers between devices  46.1 us (26%)
  matrix products  7.72 us (4%)
  other arithmetic  6.17 us (3%)
    ppermute x11, starting transfers between devices, moved(): return lax.ppermute(x, axis, pairs)  79.5 us
    ppermute x11, waiting for transfers between devices, moved(): return lax.ppermute(x, axis, pairs)  27.7 us
    ppermute x2, waiting for transfers between devices, partner_swap(): return lax.ppermute(x, 'rep', [(0, 1), (1, 0)])  13.4 us
    ppermute x1, starting transfers between devices, extended(): lax.ppermute(lax.slice_in_dim(block, 0, width, axis=dim), axis, backward)  9.15 us
    ppermute x2, starting transfers between devices, from_behind(): return lax.ppermute(x, axis, pairs)  6.02 us
    ppermute x1, waiting for transfers between devices, global_sum(): x = x + lax.ppermute(x, 'rep', [(0, 1), (1, 0)])  4.96 us
    ppermute x1, starting transfers between devices, partner_sum(): return x + lax.ppermute(x, 'rep', [(0, 1), (1, 0)])  4.8 us
    ppermute x1, starting transfers between devices, global_sum(): x = x + lax.ppermute(x, 'rep', [(0, 1), (1, 0)])  4.8 us
  transfers between devices with their start and end apart: 19, of which 10 were waited for; matrix products, arithmetic and copies ran while one was open for 5% of the time, Pallas kernels for 0%

profile of v16, /device:TPU:1, one launch (start us, length us, event | category | flops | bytes accessed | tf_op | source)
XLA Modules:
  0.0 176.0 jit_solution(16566480051467965557)
XLA Ops:
  0.6 0.0 copy-start
  0.6 4.7 %collective-permute-start = (bf16[768,256]{1,0:T(8,128)(2,1)}, bf16[768,256]{1,0:T(8,128)(2,1)S(1)}, u32[]{:S(2)}, u32[]{:S(2)}) collective-permute-start(bf16[768,256]{1,0:T(8,128)(2,1)} %param.7), channel_id=1, source_target_pairs={{0,2},{2,4},{4,6},{6,8},{8,10},{10,12},{12,14},{14,16},{16,18},{18... | collective-permute-start | bytes 1179656 | tf_op jit(solution)/shard_map/ppermute | solution.py:14
  5.4 9.1 %collective-permute-start.1 = (bf16[768,256]{1,0:T(8,128)(2,1)}, bf16[768,256]{1,0:T(8,128)(2,1)S(1)}, u32[]{:S(2)}, u32[]{:S(2)}) collective-permute-start(bf16[768,256]{1,0:T(8,128)(2,1)} %param.7), channel_id=1, source_target_pairs={{2,0},{4,2},{6,4},{8,6},{10,8},{12,10},{14,12},{16,14},{18,16},{20... | collective-permute-start | bytes 1179656 | tf_op jit(solution)/shard_map/ppermute | solution.py:17
  14.5 0.7 broadcast_subtract_fusion
  15.2 0.7 iota_compare_fusion.1
  16.0 2.2 %convolution_convert_fusion = bf16[6,18,128,128]{3,1,2,0:T(8,128)(2,1)S(1)} fusion(bf16[6,6,128,128]{3,2,1,0:T(8,128)(2,1)S(1)} %copy-done, s32[6,6]{1,0:T(8,128)S(1)} %broadcast_subtract_fusion, pred[6,6]{1,0:T(8,128)(4,1)S(1)} %iota_compare_fusion.1), kind=kOutput, calls=%fused_computation.4 | convolution fusion | flops 23004432 | bytes 4718772 | tf_op jit(solution)/shard_map/bks,bkij->bsij/dot_general | solution.py:141
  18.2 0.0 copy-start.1
  18.2 0.0 collective-permute-done
  18.2 0.0 collective-permute-done.1
  18.2 0.1 pad_maximum_fusion
  18.3 0.0 copy-start.3
  18.3 0.0 copy-start.4
  18.4 0.0 copy-start.5
  18.4 1.1 fusion.8
  19.5 0.9 copy-done.1
  20.4 2.1 %collective-permute-start.2 = (bf16[384,256]{1,0:T(8,128)(2,1)S(1)}, bf16[384,256]{1,0:T(8,128)(2,1)S(1)}, u32[]{:S(2)}, u32[]{:S(2)}) collective-permute-start(bf16[384,256]{1,0:T(8,128)(2,1)S(1)} %dynamic-slice_convert_fusion), channel_id=1, source_target_pairs={{0,1},{1,0},{2,3},{3,2},{4,5},{5,4},{6,7},{7,6},{8,9},{9,8},{10,11... | collective-permute-start | bytes 589832 | tf_op jit(solution)/shard_map/ppermute | solution.py:100
  22.5 13.4 %collective-permute-done.2 = bf16[384,256]{1,0:T(8,128)(2,1)S(1)} collective-permute-done((bf16[384,256]{1,0:T(8,128)(2,1)S(1)}, bf16[384,256]{1,0:T(8,128)(2,1)S(1)}, u32[]{:S(2)}, u32[]{:S(2)}) %collective-permute-start.2) | collective-permute-done | bytes 196640 | tf_op jit(solution)/shard_map/ppermute | solution.py:100
  36.0 0.1 add_convert_fusion
  36.1 0.4 convert_reduce_fusion
  36.4 0.3 fusion.21
  36.7 0.2 convolution_convert_fusion.1
  37.0 2.5 %collective-permute-start.3 = (bf16[384,512]{1,0:T(8,128)(2,1)S(1)}, bf16[384,512]{1,0:T(8,128)(2,1)S(1)}, u32[]{:S(2)}, u32[]{:S(2)}) collective-permute-start(bf16[384,512]{1,0:T(8,128)(2,1)S(1)} %pad_maximum_fusion.2), channel_id=1, source_target_pairs={{0,1},{1,0},{2,3},{3,2},{4,5},{5,4},{6,7},{7,6},{8,9},{9,8},{10,11... | collective-permute-start | bytes 1179656 | tf_op jit(solution)/shard_map/ppermute | solution.py:100
  39.6 2.3 %collective-permute-start.4 = (f32[257,128]{1,0:T(8,128)S(1)}, f32[257,128]{1,0:T(8,128)S(1)}, u32[]{:S(2)}, u32[]{:S(2)}) collective-permute-start(f32[257,128]{1,0:T(8,128)S(1)} %fusion.12), channel_id=1, source_target_pairs={{0,2},{2,0},{4,6},{6,4},{8,10},{10,8},{12,14},{14,12},{16,18},{18,... | collective-permute-start | bytes 394760 | tf_op jit(solution)/shard_map/ppermute | solution.py:36
  42.0 0.8 collective-permute-done.4
  42.8 9.8 %collective-permute-start.7 = (f32[257,128]{1,0:T(8,128)S(1)}, f32[257,128]{1,0:T(8,128)S(1)}, u32[]{:S(2)}, u32[]{:S(2)}) collective-permute-start(f32[257,128]{1,0:T(8,128)S(1)} %fusion.14), channel_id=1, source_target_pairs={{0,192},{2,194},{4,196},{6,198},{8,200},{10,202},{12,204},{14,206}... | collective-permute-start | bytes 394760 | tf_op jit(solution)/shard_map/ppermute | solution.py:36
  52.6 5.0 %collective-permute-start.6 = (f32[257,128]{1,0:T(8,128)S(1)}, f32[257,128]{1,0:T(8,128)S(1)}, u32[]{:S(2)}, u32[]{:S(2)}) collective-permute-start(f32[257,128]{1,0:T(8,128)S(1)} %fusion.14), channel_id=1, source_target_pairs={{0,384},{2,386},{4,388},{6,390},{8,392},{10,394},{12,396},{14,398}... | collective-permute-start | bytes 394760 | tf_op jit(solution)/shard_map/ppermute | solution.py:36
  57.7 2.4 %collective-permute-start.5 = (f32[257,128]{1,0:T(8,128)S(1)}, f32[257,128]{1,0:T(8,128)S(1)}, u32[]{:S(2)}, u32[]{:S(2)}) collective-permute-start(f32[257,128]{1,0:T(8,128)S(1)} %fusion.14), channel_id=1, source_target_pairs={{0,576},{2,578},{4,580},{6,582},{8,584},{10,586},{12,588},{14,590}... | collective-permute-start | bytes 394760 | tf_op jit(solution)/shard_map/ppermute | solution.py:36
  60.0 0.0 collective-permute-done.3
  60.1 0.2 maximum_select_fusion.1
  60.2 3.5 %fusion.4 = f32[18,128,256]{2,1,0:T(8,128)S(1)} fusion(bf16[6,128,256,1]{2,1,0,3:T(8,128)(2,1)S(1)} %bitcast.38, bf16[6,18,128,128]{3,1,2,0:T(8,128)(2,1)} %copy-done.1), kind=kOutput, calls=%fused_computation.5 | convolution fusion | flops 905969664 | bytes 6291456 | tf_op jit(solution)/shard_map/bsij,bif->sjf/dot_general | solution.py:162
  63.8 0.1 slice.32
  63.8 3.1 %collective-permute-start.11 = (f32[6,128,256]{2,1,0:T(8,128)S(1)}, f32[6,128,256]{2,1,0:T(8,128)S(1)}, u32[]{:S(2)}, u32[]{:S(2)}) collective-permute-start(f32[6,128,256]{2,1,0:T(8,128)S(1)} %slice.32), channel_id=1, source_target_pairs={{2,0},{4,2},{6,4},{8,6},{10,8},{12,10},{14,12},{16,14},{18,16},{20... | collective-permute-start | bytes 2359304 | tf_op jit(solution)/shard_map/ppermute | solution.py:25
  67.0 0.0 collective-permute-done.7
  67.0 0.0 collective-permute-done.6
  67.0 0.0 collective-permute-done.5
  67.0 0.1 add_bitcast_fusion
  67.1 1.9 %collective-permute-start.8 = (f32[257,128]{1,0:T(8,128)S(1)}, f32[257,128]{1,0:T(8,128)S(1)}, u32[]{:S(2)}, u32[]{:S(2)}) collective-permute-start(f32[257,128]{1,0:T(8,128)S(1)} %add_bitcast_fusion), channel_id=1, source_target_pairs={{0,4},{2,6},{4,0},{6,2},{8,12},{10,14},{12,8},{14,10},{16,20},{18,... | collective-permute-start | bytes 394760 | tf_op jit(solution)/shard_map/ppermute | solution.py:36
  69.1 2.9 %collective-permute-start.12 = (bf16[6,128,256]{2,1,0:T(8,128)(2,1)S(1)}, bf16[6,128,256]{2,1,0:T(8,128)(2,1)S(1)}, u32[]{:S(2)}, u32[]{:S(2)}) collective-permute-start(bf16[6,128,256]{2,1,0:T(8,128)(2,1)S(1)} %slice.42), channel_id=1, source_target_pairs={{0,2},{2,4},{4,6},{6,8},{8,10},{10,12},{12,14},{14,16},{16,18},{18... | collective-permute-start | bytes 1179656 | tf_op jit(solution)/shard_map/ppermute | solution.py:25
  72.0 5.7 %collective-permute-done.8 = f32[257,128]{1,0:T(8,128)S(1)} collective-permute-done((f32[257,128]{1,0:T(8,128)S(1)}, f32[257,128]{1,0:T(8,128)S(1)}, u32[]{:S(2)}, u32[]{:S(2)}) %collective-permute-start.8) | collective-permute-done | bytes 131616 | tf_op jit(solution)/shard_map/ppermute | solution.py:36
  77.7 0.1 fusion.30
  77.8 2.6 %collective-permute-start.9 = (f32[257,128]{1,0:T(8,128)S(1)}, f32[257,128]{1,0:T(8,128)S(1)}, u32[]{:S(2)}, u32[]{:S(2)}) collective-permute-start(f32[257,128]{1,0:T(8,128)S(1)} %fusion.30), channel_id=1, source_target_pairs={{0,8},{2,10},{4,12},{6,14},{8,0},{10,2},{12,4},{14,6},{16,24},{18,... | collective-permute-start | bytes 394760 | tf_op jit(solution)/shard_map/ppermute | solution.py:36
  80.3 4.1 %collective-permute-done.9 = f32[257,128]{1,0:T(8,128)S(1)} collective-permute-done((f32[257,128]{1,0:T(8,128)S(1)}, f32[257,128]{1,0:T(8,128)S(1)}, u32[]{:S(2)}, u32[]{:S(2)}) %collective-permute-start.9) | collective-permute-done | bytes 131616 | tf_op jit(solution)/shard_map/ppermute | solution.py:36
  84.4 4.8 %collective-permute-start.10 = (f32[257,128]{1,0:T(8,128)S(1)}, f32[257,128]{1,0:T(8,128)S(1)}, u32[]{:S(2)}, u32[]{:S(2)}) collective-permute-start(f32[257,128]{1,0:T(8,128)S(1)} %add.146), channel_id=1, source_target_pairs={{0,1},{1,0},{2,3},{3,2},{4,5},{5,4},{6,7},{7,6},{8,9},{9,8},{10,11... | collective-permute-start | bytes 394760 | tf_op jit(solution)/shard_map/ppermute | solution.py:79
  89.2 5.0 %collective-permute-done.10 = f32[257,128]{1,0:T(8,128)S(1)} collective-permute-done((f32[257,128]{1,0:T(8,128)S(1)}, f32[257,128]{1,0:T(8,128)S(1)}, u32[]{:S(2)}, u32[]{:S(2)}) %collective-permute-start.10) | collective-permute-done | bytes 131616 | tf_op jit(solution)/shard_map/ppermute | solution.py:79
  94.2 0.0 collective-permute-done.12
  94.2 0.0 collective-permute-done.11
  94.2 0.2 fusion.11
  94.4 4.8 %collective-permute-start.17 = (f32[6,128,256]{2,1,0:T(8,128)S(1)}, f32[6,128,256]{2,1,0:T(8,128)S(1)}, u32[]{:S(2)}, u32[]{:S(2)}) collective-permute-start(f32[6,128,256]{2,1,0:T(8,128)S(1)} %fusion.11), channel_id=1, source_target_pairs={{0,1},{1,0},{2,3},{3,2},{4,5},{5,4},{6,7},{7,6},{8,9},{9,8},{10,11... | collective-permute-start | bytes 2359304 | tf_op jit(solution)/shard_map/ppermute | solution.py:110
  99.2 7.3 %collective-permute-start.13 = (f32[257,128]{1,0:T(8,128)S(1)}, f32[257,128]{1,0:T(8,128)S(1)}, u32[]{:S(2)}, u32[]{:S(2)}) collective-permute-start(f32[257,128]{1,0:T(8,128)S(1)} %add.147), channel_id=1, source_target_pairs={{0,16},{2,18},{4,20},{6,22},{8,24},{10,26},{12,28},{14,30},{16,0},... | collective-permute-start | bytes 394760 | tf_op jit(solution)/shard_map/ppermute | solution.py:36
  106.5 2.4 %collective-permute-done.13 = f32[257,128]{1,0:T(8,128)S(1)} collective-permute-done((f32[257,128]{1,0:T(8,128)S(1)}, f32[257,128]{1,0:T(8,128)S(1)}, u32[]{:S(2)}, u32[]{:S(2)}) %collective-permute-start.13) | collective-permute-done | bytes 131616 | tf_op jit(solution)/shard_map/ppermute | solution.py:36
  108.9 7.5 %collective-permute-start.14 = (f32[257,128]{1,0:T(8,128)S(1)}, f32[257,128]{1,0:T(8,128)S(1)}, u32[]{:S(2)}, u32[]{:S(2)}) collective-permute-start(f32[257,128]{1,0:T(8,128)S(1)} %add.150), channel_id=1, source_target_pairs={{0,32},{2,34},{4,36},{6,38},{8,40},{10,42},{12,44},{14,46},{16,48}... | collective-permute-start | bytes 394760 | tf_op jit(solution)/shard_map/ppermute | solution.py:36
  116.5 4.1 %collective-permute-done.14 = f32[257,128]{1,0:T(8,128)S(1)} collective-permute-done((f32[257,128]{1,0:T(8,128)S(1)}, f32[257,128]{1,0:T(8,128)S(1)}, u32[]{:S(2)}, u32[]{:S(2)}) %collective-permute-start.14) | collective-permute-done | bytes 131616 | tf_op jit(solution)/shard_map/ppermute | solution.py:36
  120.6 11.2 %collective-permute-start.16 = (f32[257,128]{1,0:T(8,128)S(1)}, f32[257,128]{1,0:T(8,128)S(1)}, u32[]{:S(2)}, u32[]{:S(2)}) collective-permute-start(f32[257,128]{1,0:T(8,128)S(1)} %add.151), channel_id=1, source_target_pairs={{0,128},{2,130},{4,132},{6,134},{8,136},{10,138},{12,140},{14,142}... | collective-permute-start | bytes 394760 | tf_op jit(solution)/shard_map/ppermute | solution.py:36
  131.8 1.9 %collective-permute-start.15 = (f32[257,128]{1,0:T(8,128)S(1)}, f32[257,128]{1,0:T(8,128)}, u32[]{:S(2)}, u32[]{:S(2)}) collective-permute-start(f32[257,128]{1,0:T(8,128)S(1)} %add.151), channel_id=1, source_target_pairs={{0,64},{2,66},{4,68},{6,70},{8,72},{10,74},{12,76},{14,78},{16,80}... | collective-permute-start | bytes 394760 | tf_op jit(solution)/shard_map/ppermute | solution.py:36
  133.8 3.9 %collective-permute-done.16 = f32[257,128]{1,0:T(8,128)S(1)} collective-permute-done((f32[257,128]{1,0:T(8,128)S(1)}, f32[257,128]{1,0:T(8,128)S(1)}, u32[]{:S(2)}, u32[]{:S(2)}) %collective-permute-start.16) | collective-permute-done | bytes 131616 | tf_op jit(solution)/shard_map/ppermute | solution.py:36
  137.7 6.6 %collective-permute-done.15 = f32[257,128]{1,0:T(8,128)} collective-permute-done((f32[257,128]{1,0:T(8,128)S(1)}, f32[257,128]{1,0:T(8,128)}, u32[]{:S(2)}, u32[]{:S(2)}) %collective-permute-start.15) | collective-permute-done | bytes 131616 | tf_op jit(solution)/shard_map/ppermute | solution.py:36
  144.3 0.9 select_add_fusion
  145.2 0.0 collective-permute-done.17
  145.2 0.8 add.154
  146.1 27.6 %collective-permute-start.18 = (f32[257,128]{1,0:T(8,128)S(1)}, f32[257,128]{1,0:T(8,128)S(1)}, u32[]{:S(2)}, u32[]{:S(2)}) collective-permute-start(f32[257,128]{1,0:T(8,128)S(1)} %select_add_fusion), channel_id=1, source_target_pairs={{0,2},{2,0},{4,6},{6,4},{8,10},{10,8},{12,14},{14,12},{16,18},{18,... | collective-permute-start | bytes 394760 | tf_op jit(solution)/shard_map/ppermute | solution.py:36
  173.7 0.9 maximum_select_fusion
  174.6 0.1 collective-permute-done.18
  174.7 0.6 slice_multiply_fusion.1
  175.2 0.7 slice_multiply_fusion
  (18 shorter events, 0.3 us)
Async XLA Ops:
  0.6 15.3 %copy-start = (bf16[6,6,128,128]{3,2,1,0:T(8,128)(2,1)S(1)}, bf16[6,6,128,128]{3,2,1,0:T(8,128)(2,1)}, u32[]{:S(2)}) copy-start(bf16[6,6,128,128]{3,2,1,0:T(8,128)(2,1)} %param.8) | copy-start | bytes 3538948
  0.6 17.6 %collective-permute-start = (bf16[768,256]{1,0:T(8,128)(2,1)}, bf16[768,256]{1,0:T(8,128)(2,1)S(1)}, u32[]{:S(2)}, u32[]{:S(2)}) collective-permute-start(bf16[768,256]{1,0:T(8,128)(2,1)} %param.7), channel_id=1, source_target_pairs={{0,2},{2,4},{4,6},{6,8},{8,10},{10,12},{12,14},{14,16},{16,18},{18... | collective-permute-start | bytes 1179656 | tf_op jit(solution)/shard_map/ppermute | solution.py:14
  5.4 12.8 %collective-permute-start.1 = (bf16[768,256]{1,0:T(8,128)(2,1)}, bf16[768,256]{1,0:T(8,128)(2,1)S(1)}, u32[]{:S(2)}, u32[]{:S(2)}) collective-permute-start(bf16[768,256]{1,0:T(8,128)(2,1)} %param.7), channel_id=1, source_target_pairs={{2,0},{4,2},{6,4},{8,6},{10,8},{12,10},{14,12},{16,14},{18,16},{20... | collective-permute-start | bytes 1179656 | tf_op jit(solution)/shard_map/ppermute | solution.py:17
  16.0 2.3 %copy-start.2 = (bf16[768,256]{1,0:T(8,128)(2,1)S(1)}, bf16[768,256]{1,0:T(8,128)(2,1)}, u32[]{:S(2)}) copy-start(bf16[768,256]{1,0:T(8,128)(2,1)} %param.7) | copy-start | bytes 1179652
  18.2 2.1 %copy-start.1 = (bf16[6,18,128,128]{3,1,2,0:T(8,128)(2,1)}, bf16[6,18,128,128]{3,1,2,0:T(8,128)(2,1)S(1)}, u32[]{:S(2)}) copy-start(bf16[6,18,128,128]{3,1,2,0:T(8,128)(2,1)S(1)} %convolution_convert_fusion) | copy-start | bytes 10616836
  18.3 17.7 %copy-start.3 = (bf16[256,256]{1,0:T(8,128)(2,1)S(1)}, bf16[256,256]{1,0:T(8,128)(2,1)}, u32[]{:S(2)}) copy-start(bf16[256,256]{1,0:T(8,128)(2,1)} %param.11) | copy-start | bytes 393220
  18.3 17.7 %copy-start.4 = (bf16[768,256]{1,0:T(8,128)(2,1)S(1)}, bf16[768,256]{1,0:T(8,128)(2,1)}, u32[]{:S(2)}) copy-start(bf16[768,256]{1,0:T(8,128)(2,1)} %param.13) | copy-start | bytes 1179652
  18.4 17.7 %copy-start.5 = (f32[256]{0:T(256)S(1)}, f32[256]{0:T(256)}, u32[]{:S(2)}) copy-start(f32[256]{0:T(256)} %param.12) | copy-start | bytes 3076
  20.4 15.6 %collective-permute-start.2 = (bf16[384,256]{1,0:T(8,128)(2,1)S(1)}, bf16[384,256]{1,0:T(8,128)(2,1)S(1)}, u32[]{:S(2)}, u32[]{:S(2)}) collective-permute-start(bf16[384,256]{1,0:T(8,128)(2,1)S(1)} %dynamic-slice_convert_fusion), channel_id=1, source_target_pairs={{0,1},{1,0},{2,3},{3,2},{4,5},{5,4},{6,7},{7,6},{8,9},{9,8},{10,11... | collective-permute-start | bytes 589832 | tf_op jit(solution)/shard_map/ppermute | solution.py:100
  37.0 23.1 %collective-permute-start.3 = (bf16[384,512]{1,0:T(8,128)(2,1)S(1)}, bf16[384,512]{1,0:T(8,128)(2,1)S(1)}, u32[]{:S(2)}, u32[]{:S(2)}) collective-permute-start(bf16[384,512]{1,0:T(8,128)(2,1)S(1)} %pad_maximum_fusion.2), channel_id=1, source_target_pairs={{0,1},{1,0},{2,3},{3,2},{4,5},{5,4},{6,7},{7,6},{8,9},{9,8},{10,11... | collective-permute-start | bytes 1179656 | tf_op jit(solution)/shard_map/ppermute | solution.py:100
  39.6 3.2 %collective-permute-start.4 = (f32[257,128]{1,0:T(8,128)S(1)}, f32[257,128]{1,0:T(8,128)S(1)}, u32[]{:S(2)}, u32[]{:S(2)}) collective-permute-start(f32[257,128]{1,0:T(8,128)S(1)} %fusion.12), channel_id=1, source_target_pairs={{0,2},{2,0},{4,6},{6,4},{8,10},{10,8},{12,14},{14,12},{16,18},{18,... | collective-permute-start | bytes 394760 | tf_op jit(solution)/shard_map/ppermute | solution.py:36
  42.8 24.1 %collective-permute-start.7 = (f32[257,128]{1,0:T(8,128)S(1)}, f32[257,128]{1,0:T(8,128)S(1)}, u32[]{:S(2)}, u32[]{:S(2)}) collective-permute-start(f32[257,128]{1,0:T(8,128)S(1)} %fusion.14), channel_id=1, source_target_pairs={{0,192},{2,194},{4,196},{6,198},{8,200},{10,202},{12,204},{14,206}... | collective-permute-start | bytes 394760 | tf_op jit(solution)/shard_map/ppermute | solution.py:36
  52.6 14.4 %collective-permute-start.6 = (f32[257,128]{1,0:T(8,128)S(1)}, f32[257,128]{1,0:T(8,128)S(1)}, u32[]{:S(2)}, u32[]{:S(2)}) collective-permute-start(f32[257,128]{1,0:T(8,128)S(1)} %fusion.14), channel_id=1, source_target_pairs={{0,384},{2,386},{4,388},{6,390},{8,392},{10,394},{12,396},{14,398}... | collective-permute-start | bytes 394760 | tf_op jit(solution)/shard_map/ppermute | solution.py:36
  57.7 9.3 %collective-permute-start.5 = (f32[257,128]{1,0:T(8,128)S(1)}, f32[257,128]{1,0:T(8,128)S(1)}, u32[]{:S(2)}, u32[]{:S(2)}) collective-permute-start(f32[257,128]{1,0:T(8,128)S(1)} %fusion.14), channel_id=1, source_target_pairs={{0,576},{2,578},{4,580},{6,582},{8,584},{10,586},{12,588},{14,590}... | collective-permute-start | bytes 394760 | tf_op jit(solution)/shard_map/ppermute | solution.py:36
  63.8 30.4 %collective-permute-start.11 = (f32[6,128,256]{2,1,0:T(8,128)S(1)}, f32[6,128,256]{2,1,0:T(8,128)S(1)}, u32[]{:S(2)}, u32[]{:S(2)}) collective-permute-start(f32[6,128,256]{2,1,0:T(8,128)S(1)} %slice.32), channel_id=1, source_target_pairs={{2,0},{4,2},{6,4},{8,6},{10,8},{12,10},{14,12},{16,14},{18,16},{20... | collective-permute-start | bytes 2359304 | tf_op jit(solution)/shard_map/ppermute | solution.py:25
  67.1 10.6 %collective-permute-start.8 = (f32[257,128]{1,0:T(8,128)S(1)}, f32[257,128]{1,0:T(8,128)S(1)}, u32[]{:S(2)}, u32[]{:S(2)}) collective-permute-start(f32[257,128]{1,0:T(8,128)S(1)} %add_bitcast_fusion), channel_id=1, source_target_pairs={{0,4},{2,6},{4,0},{6,2},{8,12},{10,14},{12,8},{14,10},{16,20},{18,... | collective-permute-start | bytes 394760 | tf_op jit(solution)/shard_map/ppermute | solution.py:36
  69.1 25.1 %collective-permute-start.12 = (bf16[6,128,256]{2,1,0:T(8,128)(2,1)S(1)}, bf16[6,128,256]{2,1,0:T(8,128)(2,1)S(1)}, u32[]{:S(2)}, u32[]{:S(2)}) collective-permute-start(bf16[6,128,256]{2,1,0:T(8,128)(2,1)S(1)} %slice.42), channel_id=1, source_target_pairs={{0,2},{2,4},{4,6},{6,8},{8,10},{10,12},{12,14},{14,16},{16,18},{18... | collective-permute-start | bytes 1179656 | tf_op jit(solution)/shard_map/ppermute | solution.py:25
  77.8 6.7 %collective-permute-start.9 = (f32[257,128]{1,0:T(8,128)S(1)}, f32[257,128]{1,0:T(8,128)S(1)}, u32[]{:S(2)}, u32[]{:S(2)}) collective-permute-start(f32[257,128]{1,0:T(8,128)S(1)} %fusion.30), channel_id=1, source_target_pairs={{0,8},{2,10},{4,12},{6,14},{8,0},{10,2},{12,4},{14,6},{16,24},{18,... | collective-permute-start | bytes 394760 | tf_op jit(solution)/shard_map/ppermute | solution.py:36
  84.4 9.8 %collective-permute-start.10 = (f32[257,128]{1,0:T(8,128)S(1)}, f32[257,128]{1,0:T(8,128)S(1)}, u32[]{:S(2)}, u32[]{:S(2)}) collective-permute-start(f32[257,128]{1,0:T(8,128)S(1)} %add.146), channel_id=1, source_target_pairs={{0,1},{1,0},{2,3},{3,2},{4,5},{5,4},{6,7},{7,6},{8,9},{9,8},{10,11... | collective-permute-start | bytes 394760 | tf_op jit(solution)/shard_map/ppermute | solution.py:79
  94.4 50.8 %collective-permute-start.17 = (f32[6,128,256]{2,1,0:T(8,128)S(1)}, f32[6,128,256]{2,1,0:T(8,128)S(1)}, u32[]{:S(2)}, u32[]{:S(2)}) collective-permute-start(f32[6,128,256]{2,1,0:T(8,128)S(1)} %fusion.11), channel_id=1, source_target_pairs={{0,1},{1,0},{2,3},{3,2},{4,5},{5,4},{6,7},{7,6},{8,9},{9,8},{10,11... | collective-permute-start | bytes 2359304 | tf_op jit(solution)/shard_map/ppermute | solution.py:110
  99.2 9.7 %collective-permute-start.13 = (f32[257,128]{1,0:T(8,128)S(1)}, f32[257,128]{1,0:T(8,128)S(1)}, u32[]{:S(2)}, u32[]{:S(2)}) collective-permute-start(f32[257,128]{1,0:T(8,128)S(1)} %add.147), channel_id=1, source_target_pairs={{0,16},{2,18},{4,20},{6,22},{8,24},{10,26},{12,28},{14,30},{16,0},... | collective-permute-start | bytes 394760 | tf_op jit(solution)/shard_map/ppermute | solution.py:36
  108.9 11.7 %collective-permute-start.14 = (f32[257,128]{1,0:T(8,128)S(1)}, f32[257,128]{1,0:T(8,128)S(1)}, u32[]{:S(2)}, u32[]{:S(2)}) collective-permute-start(f32[257,128]{1,0:T(8,128)S(1)} %add.150), channel_id=1, source_target_pairs={{0,32},{2,34},{4,36},{6,38},{8,40},{10,42},{12,44},{14,46},{16,48}... | collective-permute-start | bytes 394760 | tf_op jit(solution)/shard_map/ppermute | solution.py:36
  120.6 17.1 %collective-permute-start.16 = (f32[257,128]{1,0:T(8,128)S(1)}, f32[257,128]{1,0:T(8,128)S(1)}, u32[]{:S(2)}, u32[]{:S(2)}) collective-permute-start(f32[257,128]{1,0:T(8,128)S(1)} %add.151), channel_id=1, source_target_pairs={{0,128},{2,130},{4,132},{6,134},{8,136},{10,138},{12,140},{14,142}... | collective-permute-start | bytes 394760 | tf_op jit(solution)/shard_map/ppermute | solution.py:36
  131.8 12.5 %collective-permute-start.15 = (f32[257,128]{1,0:T(8,128)S(1)}, f32[257,128]{1,0:T(8,128)}, u32[]{:S(2)}, u32[]{:S(2)}) collective-permute-start(f32[257,128]{1,0:T(8,128)S(1)} %add.151), channel_id=1, source_target_pairs={{0,64},{2,66},{4,68},{6,70},{8,72},{10,74},{12,76},{14,78},{16,80}... | collective-permute-start | bytes 394760 | tf_op jit(solution)/shard_map/ppermute | solution.py:36
  146.1 28.6 %collective-permute-start.18 = (f32[257,128]{1,0:T(8,128)S(1)}, f32[257,128]{1,0:T(8,128)S(1)}, u32[]{:S(2)}, u32[]{:S(2)}) collective-permute-start(f32[257,128]{1,0:T(8,128)S(1)} %select_add_fusion), channel_id=1, source_target_pairs={{0,2},{2,0},{4,6},{6,4},{8,10},{10,8},{12,14},{14,12},{16,18},{18,... | collective-permute-start | bytes 394760 | tf_op jit(solution)/shard_map/ppermute | solution.py:36
